TPU v7x, 128 devices: a whole 4x4x4 slice. The times are simulated.
128 devices in a mesh: head: 4 (over x_hi, core), blk: 32 (over y, x_lo, z).
Axes of the slice: x: 4 (x_hi: 2, x_lo: 2; x = x_hi * 2 + x_lo), y: 4, z: 4, core: 2. Of those that a mesh axis runs over, the one named last changes fastest.
Arguments:
- queries: bfloat16 [24576, 32, 128], P(('blk', 'head')), may hold values from -6 to 6
- rotated_keys: bfloat16 [24576, 8, 128], P(('blk', 'head')), may hold values from -6 to 6
- value_vectors: bfloat16 [24576, 8, 128], P(('blk', 'head')), may hold values from -6 to 6
- block_list: int32 [8, 192, 8], replicated, may hold values from 0 to 191, as said below
- grad_out: bfloat16 [24576, 32, 128], P(('blk', 'head')), may hold values from -6 to 6
Outputs:
- attn_out: bfloat16 [24576, 32, 128], P(('blk', 'head'))
- grad_queries: bfloat16 [24576, 32, 128], P(('blk', 'head'))
- key_gradient: bfloat16 [24576, 8, 128], P(('blk', 'head'))
- value_gradient: bfloat16 [24576, 8, 128], P(('blk', 'head'))
Inputs may be any that keep to these rules, and one draw needn't show every extreme that they name: Slot 0 of block_list[g, b, :] is b itself; every other slot names a distinct block below b or repeats b. For one head g, the blocks listed by the 6 query blocks of a run (blocks r * 6 to (r + 1) * 6 - 1) lie in that run or, for each earlier run, in one single block of it; the last query block of every run but the first lists a block of the run before.
All inputs are finite; a program needn't handle non-finite values.
Results may differ from a plain program's by a relative error of at most 0.035.
Values may be sent and summed in bfloat16 or wider, within the bound.
No kernel may reach another device: no remote copies, remote signals or barrier semaphores. Data moves between devices by JAX's collectives and lax.ppermute only.
A program may use at most 192 MiB of HBM per device.

v0:
```python
import jax
import jax.numpy as jnp
from jax import lax
from jax.sharding import PartitionSpec as P
from jax.experimental import pallas as pl
from jax.experimental.pallas import tpu as pltpu

BLOCK_TOKENS = 128
TOPK = 8


def to_heads(x):
    return lax.all_to_all(x, "head", split_axis=1, concat_axis=0, tiled=True)


def from_heads(x):
    return lax.all_to_all(x, "head", split_axis=0, concat_axis=1, tiled=True)


def attention_kernel(src_ref, base_ref, *refs):
    k_refs = refs[:TOPK]
    v_refs = refs[TOPK:2 * TOPK]
    q_ref, do_ref, kpos_ref = refs[2 * TOPK:2 * TOPK + 3]
    o_ref, dq_ref, dk_ref, dv_ref = refs[2 * TOPK + 3:]
    g = pl.program_id(0)
    b = pl.program_id(1)
    blocks = pl.num_programs(1)

    @pl.when((g == 0) & (b == 0))
    def _():
        dk_ref[...] = jnp.zeros_like(dk_ref)
        dv_ref[...] = jnp.zeros_like(dv_ref)

    head_width = k_refs[0].shape[-1]
    group_width = q_ref.shape[-1] // head_width
    scale = head_width ** (-0.5)
    keys = jnp.concatenate([r[...] for r in k_refs], axis=0)
    values = jnp.concatenate([r[...] for r in v_refs], axis=0)
    query_pos = base_ref[b] + lax.broadcasted_iota(jnp.int32, (BLOCK_TOKENS, 1), 0)
    allowed = kpos_ref[...] <= query_pos
    nt = (((1,), (1,)), ((), ()))
    tn = (((0,), (0,)), ((), ()))
    dk = None
    dv = None
    for j in range(group_width):
        cols = slice(j * head_width, (j + 1) * head_width)
        qj = q_ref[:, cols]
        gj = do_ref[:, cols]
        s = lax.dot_general(qj, keys, nt, preferred_element_type=jnp.float32) * scale
        s = jnp.where(allowed, s, -jnp.inf)
        m = jnp.max(s, axis=-1, keepdims=True)
        lt = m + jnp.log(jnp.sum(jnp.exp(s - m), axis=-1, keepdims=True))
        p = jnp.exp(s - lt)
        pb = p.astype(jnp.bfloat16)
        o = jnp.dot(pb, values, preferred_element_type=jnp.float32).astype(jnp.bfloat16)
        o_ref[:, cols] = o
        rd = jnp.sum(gj.astype(jnp.float32) * o.astype(jnp.float32), axis=-1, keepdims=True)
        dp = lax.dot_general(gj, values, nt, preferred_element_type=jnp.float32)
        ds = (p * (dp - rd)).astype(jnp.bfloat16)
        dq = jnp.dot(ds, keys, preferred_element_type=jnp.float32) * scale
        dq_ref[:, cols] = dq.astype(jnp.bfloat16)
        dkj = lax.dot_general(ds, qj, tn, preferred_element_type=jnp.float32)
        dvj = lax.dot_general(pb, gj, tn, preferred_element_type=jnp.float32)
        dk = dkj if dk is None else dk + dkj
        dv = dvj if dv is None else dv + dvj
    dk = dk * scale
    row = (g * blocks + b) * TOPK
    for s in range(TOPK):
        t = src_ref[row + s]
        rows = slice(s * BLOCK_TOKENS, (s + 1) * BLOCK_TOKENS)
        dk_ref[t, g] = dk_ref[t, g] + dk[rows]
        dv_ref[t, g] = dv_ref[t, g] + dv[rows]


def attend(slot_src, query_base, table, q2, do2, key_pos):
    groups = table.shape[2]
    block_ids = q2.shape[0] // BLOCK_TOKENS
    targets = table.shape[0]
    head_width = table.shape[-1]
    row_width = q2.shape[1] // groups

    def slot_spec(s, kv):
        def index(g, b, src, base):
            return (src[(g * block_ids + b) * TOPK + s], kv, g, 0, 0)

        return pl.BlockSpec((None, None, None, BLOCK_TOKENS, head_width), index)

    row_spec = pl.BlockSpec((BLOCK_TOKENS, row_width), lambda g, b, src, base: (b, g))
    pos_spec = pl.BlockSpec((None, None, 1, TOPK * BLOCK_TOKENS), lambda g, b, src, base: (g, b, 0, 0))
    acc_spec = pl.BlockSpec(
        (targets, groups, BLOCK_TOKENS, head_width), lambda g, b, src, base: (0, 0, 0, 0)
    )
    in_specs = (
        [slot_spec(s, 0) for s in range(TOPK)]
        + [slot_spec(s, 1) for s in range(TOPK)]
        + [row_spec, row_spec, pos_spec]
    )
    out_shape = (
        jax.ShapeDtypeStruct(q2.shape, jnp.bfloat16),
        jax.ShapeDtypeStruct(q2.shape, jnp.bfloat16),
        jax.ShapeDtypeStruct((targets, groups, BLOCK_TOKENS, head_width), jnp.float32),
        jax.ShapeDtypeStruct((targets, groups, BLOCK_TOKENS, head_width), jnp.float32),
    )
    grid_spec = pltpu.PrefetchScalarGridSpec(
        num_scalar_prefetch=2,
        grid=(groups, block_ids),
        in_specs=in_specs,
        out_specs=(row_spec, row_spec, acc_spec, acc_spec),
    )
    return pl.pallas_call(
        attention_kernel,
        grid_spec=grid_spec,
        out_shape=out_shape,
        compiler_params=pltpu.CompilerParams(
            dimension_semantics=("arbitrary", "arbitrary"),
            vmem_limit_bytes=48 * 1024 * 1024,
        ),
    )(slot_src, query_base, *([table] * (2 * TOPK)), q2, do2, key_pos)


def on_device(queries, rotated_keys, value_vectors, block_list, grad_out):
    query_h = to_heads(queries)
    key_h = to_heads(rotated_keys)
    value_h = to_heads(value_vectors)
    grad_h = to_heads(grad_out)
    run_len, head_count, head_width = query_h.shape
    groups = key_h.shape[1]
    block_ids = run_len // BLOCK_TOKENS
    peers = lax.axis_size("blk")
    rank = lax.axis_index("blk")
    head_rank = lax.axis_index("head")
    offsets = jnp.arange(BLOCK_TOKENS, dtype=jnp.int32)
    block_range = jnp.arange(block_ids, dtype=jnp.int32)
    peer_range = jnp.arange(peers, dtype=jnp.int32)

    lists_here = lax.dynamic_slice_in_dim(block_list, head_rank * groups, groups, 0)
    lists_mine = lax.dynamic_slice_in_dim(lists_here, rank * block_ids, block_ids, 1)
    by_run = lists_here.reshape(groups, peers, block_ids * TOPK)
    in_mine = (by_run // block_ids) == rank
    named = jnp.max(jnp.where(in_mine, by_run % block_ids, -1), axis=-1)
    present = (named >= 0) & (peer_range != rank)[None, :]
    pick_send = (named[:, :, None] == block_range).astype(jnp.bfloat16)

    kv_local = jnp.transpose(
        jnp.stack([key_h, value_h]).reshape(2, block_ids, BLOCK_TOKENS, groups, head_width),
        (1, 0, 3, 2, 4),
    )
    send = jnp.einsum(
        "grb,bkgtd->rkgtd", pick_send, kv_local, preferred_element_type=jnp.float32
    ).astype(jnp.bfloat16)
    recv = lax.all_to_all(send, "blk", split_axis=0, concat_axis=0, tiled=True)
    table = jnp.concatenate([recv, kv_local], axis=0)

    owner = lists_mine // block_ids
    slot_src = jnp.where(owner == rank, peers + lists_mine % block_ids, owner)
    slot_ids = jnp.arange(TOPK, dtype=jnp.int32)
    earlier = slot_ids[None, :] < slot_ids[:, None]
    repeated = jnp.any((lists_mine[..., :, None] == lists_mine[..., None, :]) & earlier, axis=-1)
    key_pos = lists_mine[..., None] * BLOCK_TOKENS + offsets
    key_pos = jnp.where(repeated[..., None], jnp.int32(2**30), key_pos)
    key_pos = key_pos.reshape(groups, block_ids, 1, TOPK * BLOCK_TOKENS)
    query_base = (rank * block_ids + block_range) * BLOCK_TOKENS

    q2 = query_h.reshape(run_len, head_count * head_width)
    do2 = grad_h.reshape(run_len, head_count * head_width)
    o2, dq2, dk_acc, dv_acc = attend(
        slot_src.reshape(-1), query_base, table, q2, do2, key_pos
    )
    attn_h = o2.reshape(run_len, head_count, head_width)
    query_grad_h = dq2.reshape(run_len, head_count, head_width)

    acc = jnp.stack([dk_acc, dv_acc], axis=1)
    remote = acc[:peers].astype(jnp.bfloat16)
    local = acc[peers:].astype(jnp.bfloat16)
    back = lax.all_to_all(remote, "blk", split_axis=0, concat_axis=0, tiled=True)
    take_back = pick_send * present[..., None].astype(jnp.bfloat16)
    total = local.astype(jnp.float32) + jnp.einsum(
        "grl,rkgtd->lkgtd", take_back, back, preferred_element_type=jnp.float32
    )
    total = jnp.transpose(total.astype(jnp.bfloat16), (1, 0, 3, 2, 4))
    key_grad_h = total[0].reshape(run_len, groups, head_width)
    value_grad_h = total[1].reshape(run_len, groups, head_width)
    return (
        from_heads(attn_h),
        from_heads(query_grad_h),
        from_heads(key_grad_h),
        from_heads(value_grad_h),
    )


def solution(mesh):
    in_specs = (
        P(("blk", "head"), None, None),
        P(("blk", "head"), None, None),
        P(("blk", "head"), None, None),
        P(),
        P(("blk", "head"), None, None),
    )
    out_specs = (
        P(("blk", "head"), None, None),
        P(("blk", "head"), None, None),
        P(("blk", "head"), None, None),
        P(("blk", "head"), None, None),
    )
    return jax.shard_map(
        on_device, mesh=mesh, in_specs=in_specs, out_specs=out_specs, check_vma=False
    )
```

profile of v0, /device:TPU:0, one launch (start us, length us, event | category | flops | bytes accessed | tf_op | source)
XLA Modules:
  0.0 354.0 jit_solution(4708095961584398446)
XLA Ops:
  0.6 1.9 copy.96
  2.6 4.4 %all-to-all-start = ((bf16[192,8,128]{2,0,1:T(8,128)(2,1)}), bf16[192,8,128]{2,0,1:T(8,128)(2,1)S(1)}, u32[]{:S(2)}, u32[]{:S(2)}) async-start(bf16[192,8,128]{2,0,1:T(8,128)(2,1)} %copy.96), calls=%async_computation | async-start | bytes 786432 | tf_op jit(solution)/shard_map/all_to_all | solution.py:13
  6.9 1.8 copy.98
  8.7 7.2 %all-to-all-done = bf16[192,8,128]{2,0,1:T(8,128)(2,1)S(1)} async-done(((bf16[192,8,128]{2,0,1:T(8,128)(2,1)}), bf16[192,8,128]{2,0,1:T(8,128)(2,1)S(1)}, u32[]{:S(2)}, u32[]{:S(2)}) %all-to-all-start) | async-done | bytes 393248 | tf_op jit(solution)/shard_map/all_to_all | solution.py:13
  15.9 3.5 all-to-all-start.1
  19.4 1.8 copy.104
  21.1 7.1 %all-to-all-done.1 = bf16[192,8,128]{2,0,1:T(8,128)(2,1)S(1)} async-done(((bf16[192,8,128]{2,0,1:T(8,128)(2,1)}), bf16[192,8,128]{2,0,1:T(8,128)(2,1)S(1)}, u32[]{:S(2)}, u32[]{:S(2)}) %all-to-all-start.1) | async-done | bytes 393248 | tf_op jit(solution)/shard_map/all_to_all | solution.py:13
  28.3 3.6 %all-to-all-start.3 = ((bf16[192,32,128]{2,0,1:T(8,128)(2,1)}), bf16[192,32,128]{2,0,1:T(8,128)(2,1)S(1)}, u32[]{:S(2)}, u32[]{:S(2)}) async-start(bf16[192,32,128]{2,0,1:T(8,128)(2,1)} %copy.104), calls=%async_computation.3 | async-start | bytes 3145728 | tf_op jit(solution)/shard_map/all_to_all | solution.py:13
  31.8 1.8 copy.106
  33.6 19.8 %all-to-all-done.3 = bf16[192,32,128]{2,0,1:T(8,128)(2,1)S(1)} async-done(((bf16[192,32,128]{2,0,1:T(8,128)(2,1)}), bf16[192,32,128]{2,0,1:T(8,128)(2,1)S(1)}, u32[]{:S(2)}, u32[]{:S(2)}) %all-to-all-start.3) | async-done | bytes 1572896 | tf_op jit(solution)/shard_map/all_to_all | solution.py:13
  53.4 3.6 %all-to-all-start.4 = ((bf16[192,32,128]{2,0,1:T(8,128)(2,1)}), bf16[192,32,128]{2,0,1:T(8,128)(2,1)S(1)}, u32[]{:S(2)}, u32[]{:S(2)}) async-start(bf16[192,32,128]{2,0,1:T(8,128)(2,1)} %copy.106), calls=%async_computation.4 | async-start | bytes 3145728 | tf_op jit(solution)/shard_map/all_to_all | solution.py:13
  62.3 3.6 %copy.150 = bf16[2,2,128,128,32]{3,2,0,1,4:T(8,128)(2,1)} copy(bf16[2,2,128,128,32]{3,4,2,1,0:T(8,128)(2,1)S(1)} %fusion.5) | data formatting | bytes 8388608 | tf_op jit(solution)/shard_map/grb,bkgtd->rkgtd/dot_general | solution.py:148
  65.9 12.6 %all-to-all-done.4 = bf16[192,32,128]{2,0,1:T(8,128)(2,1)S(1)} async-done(((bf16[192,32,128]{2,0,1:T(8,128)(2,1)}), bf16[192,32,128]{2,0,1:T(8,128)(2,1)S(1)}, u32[]{:S(2)}, u32[]{:S(2)}) %all-to-all-start.4) | async-done | bytes 1572896 | tf_op jit(solution)/shard_map/all_to_all | solution.py:13
  78.5 8.7 %all-to-all-start.2 = ((bf16[32,2,2,128,128]{4,3,2,1,0:T(8,128)(2,1)}), bf16[32,2,2,128,128]{4,3,2,1,0:T(8,128)(2,1)}, u32[]{:S(2)}, u32[]{:S(2)}) async-start(bf16[32,2,2,128,128]{4,3,2,1,0:T(8,128)(2,1)} %bitcast.85), calls=%async_computation.2 | async-start | bytes 8388608 | tf_op jit(solution)/shard_map/all_to_all | solution.py:151
  89.1 2.2 copy.153
  93.3 1.9 copy_bitcast_fusion
  95.3 50.1 %all-to-all-done.2 = bf16[32,2,2,128,128]{4,3,2,1,0:T(8,128)(2,1)} async-done(((bf16[32,2,2,128,128]{4,3,2,1,0:T(8,128)(2,1)}), bf16[32,2,2,128,128]{4,3,2,1,0:T(8,128)(2,1)}, u32[]{:S(2)}, u32[]{:S(2)}) %all-to-all-start.2) | async-done | bytes 4194336 | tf_op jit(solution)/shard_map/all_to_all | solution.py:151
  145.4 5.1 %pad_maximum_fusion.1.refs_0_.refs_1_.refs_2_.refs_3_.refs_4_.refs_5_.refs_6_.refs_7_.refs_8_.refs_9_.refs_10_.refs_11_.refs_12_.refs_13_.refs_14_.refs_15_ = bf16[38,2,2,128,128]{4,3,2,1,0:T(8,128)(2,1)} fusion(bf16[6,2,2,128,128]{4,3,2,1,0:T(8,128)(2,1)} %bitcast.94, bf16[32,2,2,128,128]{4,3,2,1,0:T(8,128)(2,1)} %all-to-all-done.2), kind=kLoop, calls=%fused_computation.3 | loop fusion | flops 2490368 | bytes 9961472 | tf_op jit(solution)/shard_map/concatenate | solution.py:152
  150.5 54.9 %shard_map.84 = (bf16[768,1024]{1,0:T(8,128)(2,1)S(1)}, bf16[768,1024]{1,0:T(8,128)(2,1)S(1)}, f32[38,2,128,128]{3,2,1,0:T(8,128)}, f32[38,2,128,128]{3,2,1,0:T(8,128)}) custom-call(s32[96]{0:T(128)S(1)} %reshape.100.src_ref, s32[6]{0:T(128)S(1)} %add_multiply_fusion.base_ref, ...), custom_call_target="tpu_custom_call" | custom-call | tf_op jit(solution)/shard_map/pallas_call | solution.py:110
  207.0 4.8 %all-to-all-start.6 = ((bf16[768,8,128]{2,1,0:T(8,128)(2,1)}), bf16[768,8,128]{2,1,0:T(8,128)(2,1)S(1)}, u32[]{:S(2)}, u32[]{:S(2)}) async-start(bf16[768,8,128]{2,1,0:T(8,128)(2,1)} %bitcast.91), calls=%async_computation.6 | async-start | bytes 3145728 | tf_op jit(solution)/shard_map/all_to_all | solution.py:17
  211.8 4.2 %fusion = bf16[32,2,2,128,128]{4,3,2,0,1:T(8,128)(2,1)S(1)} fusion(f32[38,1,2,128,128]{4,3,2,0,1:T(8,128)} %bitcast.83, f32[38,1,2,128,128]{4,3,2,0,1:T(8,128)} %bitcast.81), kind=kLoop, calls=%fused_computation.1 | loop fusion | flops 2097152 | bytes 14155776 | tf_op jit(solution)/shard_map/convert.1
  216.0 2.3 copy.114
  218.3 15.1 %all-to-all-done.6 = bf16[768,8,128]{2,1,0:T(8,128)(2,1)S(1)} async-done(((bf16[768,8,128]{2,1,0:T(8,128)(2,1)}), bf16[768,8,128]{2,1,0:T(8,128)(2,1)S(1)}, u32[]{:S(2)}, u32[]{:S(2)}) %all-to-all-start.6) | async-done | bytes 1572896 | tf_op jit(solution)/shard_map/all_to_all | solution.py:17
  233.4 4.9 %all-to-all-start.7 = ((bf16[32,2,2,128,128]{4,3,2,1,0:T(8,128)(2,1)}), bf16[32,2,2,128,128]{4,3,2,1,0:T(8,128)(2,1)}, u32[]{:S(2)}, u32[]{:S(2)}) async-start(bf16[32,2,2,128,128]{4,3,2,1,0:T(8,128)(2,1)} %copy.114), calls=%async_computation.7 | async-start | bytes 8388608 | tf_op jit(solution)/shard_map/all_to_all | solution.py:175
  239.9 59.5 %all-to-all-done.7 = bf16[32,2,2,128,128]{4,3,2,1,0:T(8,128)(2,1)} async-done(((bf16[32,2,2,128,128]{4,3,2,1,0:T(8,128)(2,1)}), bf16[32,2,2,128,128]{4,3,2,1,0:T(8,128)(2,1)}, u32[]{:S(2)}, u32[]{:S(2)}) %all-to-all-start.7) | async-done | bytes 4194336 | tf_op jit(solution)/shard_map/all_to_all | solution.py:175
  299.4 5.4 %all-to-all-start.5 = ((bf16[768,8,128]{2,1,0:T(8,128)(2,1)}), bf16[768,8,128]{2,1,0:T(8,128)(2,1)S(1)}, u32[]{:S(2)}, u32[]{:S(2)}) async-start(bf16[768,8,128]{2,1,0:T(8,128)(2,1)} %bitcast.90), calls=%async_computation.5 | async-start | bytes 3145728 | tf_op jit(solution)/shard_map/all_to_all | solution.py:17
  304.8 4.5 %fusion.2 = f32[2,2,128,128,6]{3,4,2,1,0:T(8,128)S(1)} fusion(bf16[32,2,2,128,128]{4,3,2,1,0:T(8,128)(2,1)} %all-to-all-done.7, s32[2,32]{1,0:T(2,128)S(1)} %reduce_max.18, bf16[2,32]{1,0:T(2,128)(2,1)S(1)} %and_convert_fusion), kind=kOutput, calls=%fused_computation.5 | convolution fusion | flops 25166592 | bytes 5767552 | tf_op jit(solution)/shard_map/grl,rkgtd->lkgtd/dot_general | solution.py:177
  313.1 13.3 %all-to-all-done.5 = bf16[768,8,128]{2,1,0:T(8,128)(2,1)S(1)} async-done(((bf16[768,8,128]{2,1,0:T(8,128)(2,1)}), bf16[768,8,128]{2,1,0:T(8,128)(2,1)S(1)}, u32[]{:S(2)}, u32[]{:S(2)}) %all-to-all-start.5) | async-done | bytes 1572896 | tf_op jit(solution)/shard_map/all_to_all | solution.py:17
  326.4 3.5 all-to-all-start.9
  332.1 6.7 %all-to-all-done.9 = bf16[768,2,128]{2,1,0:T(2,128)(2,1)S(1)} async-done(((bf16[768,2,128]{2,1,0:T(2,128)(2,1)}), bf16[768,2,128]{2,1,0:T(2,128)(2,1)S(1)}, u32[]{:S(2)}, u32[]{:S(2)}) %all-to-all-start.9) | async-done | bytes 393248 | tf_op jit(solution)/shard_map/all_to_all | solution.py:17
  338.8 4.1 %all-to-all-start.8 = ((bf16[768,2,128]{2,1,0:T(2,128)(2,1)}), bf16[768,2,128]{2,1,0:T(2,128)(2,1)}, u32[]{:S(2)}, u32[]{:S(2)}) async-start(bf16[768,2,128]{2,1,0:T(2,128)(2,1)} %copy.118), calls=%async_computation.8 | async-start | bytes 786432 | tf_op jit(solution)/shard_map/all_to_all | solution.py:17
  346.8 5.1 %all-to-all-done.8 = bf16[768,2,128]{2,1,0:T(2,128)(2,1)} async-done(((bf16[768,2,128]{2,1,0:T(2,128)(2,1)}), bf16[768,2,128]{2,1,0:T(2,128)(2,1)}, u32[]{:S(2)}, u32[]{:S(2)}) %all-to-all-start.8) | async-done | bytes 393248 | tf_op jit(solution)/shard_map/all_to_all | solution.py:17
  (49 shorter events, 24.3 us)
Async XLA Ops:
  0.6 18.7 %copy-start = (bf16[192,32,128]{2,1,0:T(8,128)(2,1)S(1)}, bf16[192,32,128]{2,1,0:T(8,128)(2,1)}, u32[]{:S(2)}) copy-start(bf16[192,32,128]{2,1,0:T(8,128)(2,1)} %param.5) | copy-start | bytes 4718596
  2.6 13.3 %all-to-all-start = ((bf16[192,8,128]{2,0,1:T(8,128)(2,1)}), bf16[192,8,128]{2,0,1:T(8,128)(2,1)S(1)}, u32[]{:S(2)}, u32[]{:S(2)}) async-start(bf16[192,8,128]{2,0,1:T(8,128)(2,1)} %copy.96), calls=%async_computation | async-start | bytes 786432 | tf_op jit(solution)/shard_map/all_to_all | solution.py:13
  15.9 3.5 copy-start.2
  15.9 12.4 %all-to-all-start.1 = ((bf16[192,8,128]{2,0,1:T(8,128)(2,1)}), bf16[192,8,128]{2,0,1:T(8,128)(2,1)S(1)}, u32[]{:S(2)}, u32[]{:S(2)}) async-start(bf16[192,8,128]{2,0,1:T(8,128)(2,1)} %copy.98), calls=%async_computation.1 | async-start | bytes 786432 | tf_op jit(solution)/shard_map/all_to_all | solution.py:13
  21.1 10.7 %copy-start.1 = (bf16[192,32,128]{2,1,0:T(8,128)(2,1)S(1)}, bf16[192,32,128]{2,1,0:T(8,128)(2,1)}, u32[]{:S(2)}) copy-start(bf16[192,32,128]{2,1,0:T(8,128)(2,1)} %param.9) | copy-start | bytes 4718596
  28.3 5.3 %copy-start.3 = (bf16[192,8,128]{2,0,1:T(8,128)(2,1)}, bf16[192,8,128]{2,0,1:T(8,128)(2,1)S(1)}, u32[]{:S(2)}) copy-start(bf16[192,8,128]{2,0,1:T(8,128)(2,1)S(1)} %all-to-all-done.1) | copy-start | bytes 1179652
  28.3 25.1 %all-to-all-start.3 = ((bf16[192,32,128]{2,0,1:T(8,128)(2,1)}), bf16[192,32,128]{2,0,1:T(8,128)(2,1)S(1)}, u32[]{:S(2)}, u32[]{:S(2)}) async-start(bf16[192,32,128]{2,0,1:T(8,128)(2,1)} %copy.104), calls=%async_computation.3 | async-start | bytes 3145728 | tf_op jit(solution)/shard_map/all_to_all | solution.py:13
  53.4 25.1 %all-to-all-start.4 = ((bf16[192,32,128]{2,0,1:T(8,128)(2,1)}), bf16[192,32,128]{2,0,1:T(8,128)(2,1)S(1)}, u32[]{:S(2)}, u32[]{:S(2)}) async-start(bf16[192,32,128]{2,0,1:T(8,128)(2,1)} %copy.106), calls=%async_computation.4 | async-start | bytes 3145728 | tf_op jit(solution)/shard_map/all_to_all | solution.py:13
  78.5 66.9 %all-to-all-start.2 = ((bf16[32,2,2,128,128]{4,3,2,1,0:T(8,128)(2,1)}), bf16[32,2,2,128,128]{4,3,2,1,0:T(8,128)(2,1)}, u32[]{:S(2)}, u32[]{:S(2)}) async-start(bf16[32,2,2,128,128]{4,3,2,1,0:T(8,128)(2,1)} %bitcast.85), calls=%async_computation.2 | async-start | bytes 8388608 | tf_op jit(solution)/shard_map/all_to_all | solution.py:151
  207.0 26.4 %all-to-all-start.6 = ((bf16[768,8,128]{2,1,0:T(8,128)(2,1)}), bf16[768,8,128]{2,1,0:T(8,128)(2,1)S(1)}, u32[]{:S(2)}, u32[]{:S(2)}) async-start(bf16[768,8,128]{2,1,0:T(8,128)(2,1)} %bitcast.91), calls=%async_computation.6 | async-start | bytes 3145728 | tf_op jit(solution)/shard_map/all_to_all | solution.py:17
  233.4 66.0 %all-to-all-start.7 = ((bf16[32,2,2,128,128]{4,3,2,1,0:T(8,128)(2,1)}), bf16[32,2,2,128,128]{4,3,2,1,0:T(8,128)(2,1)}, u32[]{:S(2)}, u32[]{:S(2)}) async-start(bf16[32,2,2,128,128]{4,3,2,1,0:T(8,128)(2,1)} %copy.114), calls=%async_computation.7 | async-start | bytes 8388608 | tf_op jit(solution)/shard_map/all_to_all | solution.py:175
  299.4 27.0 %all-to-all-start.5 = ((bf16[768,8,128]{2,1,0:T(8,128)(2,1)}), bf16[768,8,128]{2,1,0:T(8,128)(2,1)S(1)}, u32[]{:S(2)}, u32[]{:S(2)}) async-start(bf16[768,8,128]{2,1,0:T(8,128)(2,1)} %bitcast.90), calls=%async_computation.5 | async-start | bytes 3145728 | tf_op jit(solution)/shard_map/all_to_all | solution.py:17
  326.4 12.4 %all-to-all-start.9 = ((bf16[768,2,128]{2,1,0:T(2,128)(2,1)}), bf16[768,2,128]{2,1,0:T(2,128)(2,1)S(1)}, u32[]{:S(2)}, u32[]{:S(2)}) async-start(bf16[768,2,128]{2,1,0:T(2,128)(2,1)} %copy.122), calls=%async_computation.9 | async-start | bytes 786432 | tf_op jit(solution)/shard_map/all_to_all | solution.py:17
  338.8 13.1 %all-to-all-start.8 = ((bf16[768,2,128]{2,1,0:T(2,128)(2,1)}), bf16[768,2,128]{2,1,0:T(2,128)(2,1)}, u32[]{:S(2)}, u32[]{:S(2)}) async-start(bf16[768,2,128]{2,1,0:T(2,128)(2,1)} %copy.118), calls=%async_computation.8 | async-start | bytes 786432 | tf_op jit(solution)/shard_map/all_to_all | solution.py:17
where the time goes:
time: 356 us; the launch traced here: 354 us
  waiting for transfers between devices  197 us (55%)
  Pallas kernels  54.9 us (15%)
  starting transfers between devices  46.4 us (13%)
  local copies, waits for them, and re-layouts  35.3 us (10%)
  other arithmetic  14.2 us (4%)
  matrix products  5.84 us (2%)
    all_to_all x1, waiting for transfers between devices, on_device(): lax.all_to_all(remote, 'blk', split_axis=0, concat_axis=0, tiled=True)  59.5 us
    pallas_call x1, Pallas kernels, attend(): pl.pallas_call(attention_kernel, grid_spec=grid_spec, out_shape=out_shape...  54.9 us
    all_to_all x1, waiting for transfers between devices, on_device(): recv = lax.all_to_all(send, 'blk', split_axis=0, concat_axis=0, tiled=True)  50.1 us
    all_to_all x4, waiting for transfers between devices, to_heads(): return lax.all_to_all(x, 'head', split_axis=1, concat_axis=0, tiled=True)  46.7 us
    all_to_all x4, waiting for transfers between devices, from_heads(): return lax.all_to_all(x, 'head', split_axis=0, concat_axis=1, tiled=True)  40.2 us
    all_to_all x4, starting transfers between devices, from_heads(): return lax.all_to_all(x, 'head', split_axis=0, concat_axis=1, tiled=True)  17.8 us
    all_to_all x4, starting transfers between devices, to_heads(): return lax.all_to_all(x, 'head', split_axis=1, concat_axis=0, tiled=True)  15 us
    unnamed x16, local copies, waits for them, and re-layouts  12.4 us
  transfers between devices with their start and end apart: 10, of which 10 were waited for; matrix products, arithmetic and copies ran while one was open for 13% of the time, Pallas kernels for 0%

commit v1 on v0

--- a/solution.py
+++ b/solution.py
@@ -22,11 +22,9 @@
     v_refs = refs[TOPK:2 * TOPK]
     q_ref, do_ref, kpos_ref = refs[2 * TOPK:2 * TOPK + 3]
     o_ref, dq_ref, dk_ref, dv_ref = refs[2 * TOPK + 3:]
-    g = pl.program_id(0)
-    b = pl.program_id(1)
-    blocks = pl.num_programs(1)
-
-    @pl.when((g == 0) & (b == 0))
+    b = pl.program_id(0)
+
+    @pl.when(b == 0)
     def _():
         dk_ref[...] = jnp.zeros_like(dk_ref)
         dv_ref[...] = jnp.zeros_like(dv_ref)
@@ -64,55 +62,52 @@
         dk = dkj if dk is None else dk + dkj
         dv = dvj if dv is None else dv + dvj
     dk = dk * scale
-    row = (g * blocks + b) * TOPK
     for s in range(TOPK):
-        t = src_ref[row + s]
+        t = src_ref[b * TOPK + s]
         rows = slice(s * BLOCK_TOKENS, (s + 1) * BLOCK_TOKENS)
-        dk_ref[t, g] = dk_ref[t, g] + dk[rows]
-        dv_ref[t, g] = dv_ref[t, g] + dv[rows]
-
-
-def attend(slot_src, query_base, table, q2, do2, key_pos):
-    groups = table.shape[2]
+        dk_ref[t] = dk_ref[t] + dk[rows]
+        dv_ref[t] = dv_ref[t] + dv[rows]
+
+
+def attend(slot_src, query_base, table, q2, do2, key_pos, group, groups):
     block_ids = q2.shape[0] // BLOCK_TOKENS
     targets = table.shape[0]
     head_width = table.shape[-1]
     row_width = q2.shape[1] // groups
 
     def slot_spec(s, kv):
-        def index(g, b, src, base):
-            return (src[(g * block_ids + b) * TOPK + s], kv, g, 0, 0)
-
-        return pl.BlockSpec((None, None, None, BLOCK_TOKENS, head_width), index)
-
-    row_spec = pl.BlockSpec((BLOCK_TOKENS, row_width), lambda g, b, src, base: (b, g))
-    pos_spec = pl.BlockSpec((None, None, 1, TOPK * BLOCK_TOKENS), lambda g, b, src, base: (g, b, 0, 0))
-    acc_spec = pl.BlockSpec(
-        (targets, groups, BLOCK_TOKENS, head_width), lambda g, b, src, base: (0, 0, 0, 0)
-    )
+        def index(b, src, base):
+            return (src[b * TOPK + s], kv, 0, 0)
+
+        return pl.BlockSpec((None, None, BLOCK_TOKENS, head_width), index)
+
+    in_row = pl.BlockSpec((BLOCK_TOKENS, row_width), lambda b, src, base: (b, group))
+    out_row = pl.BlockSpec((BLOCK_TOKENS, row_width), lambda b, src, base: (b, 0))
+    pos_spec = pl.BlockSpec((None, 1, TOPK * BLOCK_TOKENS), lambda b, src, base: (b, 0, 0))
+    acc_spec = pl.BlockSpec((targets, BLOCK_TOKENS, head_width), lambda b, src, base: (0, 0, 0))
     in_specs = (
         [slot_spec(s, 0) for s in range(TOPK)]
         + [slot_spec(s, 1) for s in range(TOPK)]
-        + [row_spec, row_spec, pos_spec]
+        + [in_row, in_row, pos_spec]
     )
     out_shape = (
-        jax.ShapeDtypeStruct(q2.shape, jnp.bfloat16),
-        jax.ShapeDtypeStruct(q2.shape, jnp.bfloat16),
-        jax.ShapeDtypeStruct((targets, groups, BLOCK_TOKENS, head_width), jnp.float32),
-        jax.ShapeDtypeStruct((targets, groups, BLOCK_TOKENS, head_width), jnp.float32),
+        jax.ShapeDtypeStruct((q2.shape[0], row_width), jnp.bfloat16),
+        jax.ShapeDtypeStruct((q2.shape[0], row_width), jnp.bfloat16),
+        jax.ShapeDtypeStruct((targets, BLOCK_TOKENS, head_width), jnp.float32),
+        jax.ShapeDtypeStruct((targets, BLOCK_TOKENS, head_width), jnp.float32),
     )
     grid_spec = pltpu.PrefetchScalarGridSpec(
         num_scalar_prefetch=2,
-        grid=(groups, block_ids),
+        grid=(block_ids,),
         in_specs=in_specs,
-        out_specs=(row_spec, row_spec, acc_spec, acc_spec),
+        out_specs=(out_row, out_row, acc_spec, acc_spec),
     )
     return pl.pallas_call(
         attention_kernel,
         grid_spec=grid_spec,
         out_shape=out_shape,
         compiler_params=pltpu.CompilerParams(
-            dimension_semantics=("arbitrary", "arbitrary"),
+            dimension_semantics=("arbitrary",),
             vmem_limit_bytes=48 * 1024 * 1024,
         ),
     )(slot_src, query_base, *([table] * (2 * TOPK)), q2, do2, key_pos)
@@ -125,6 +120,7 @@
     grad_h = to_heads(grad_out)
     run_len, head_count, head_width = query_h.shape
     groups = key_h.shape[1]
+    group_width = head_count // groups
     block_ids = run_len // BLOCK_TOKENS
     peers = lax.axis_size("blk")
     rank = lax.axis_index("blk")
@@ -140,17 +136,12 @@
     named = jnp.max(jnp.where(in_mine, by_run % block_ids, -1), axis=-1)
     present = (named >= 0) & (peer_range != rank)[None, :]
     pick_send = (named[:, :, None] == block_range).astype(jnp.bfloat16)
+    take_back = pick_send * present[..., None].astype(jnp.bfloat16)
 
     kv_local = jnp.transpose(
         jnp.stack([key_h, value_h]).reshape(2, block_ids, BLOCK_TOKENS, groups, head_width),
-        (1, 0, 3, 2, 4),
-    )
-    send = jnp.einsum(
-        "grb,bkgtd->rkgtd", pick_send, kv_local, preferred_element_type=jnp.float32
-    ).astype(jnp.bfloat16)
-    recv = lax.all_to_all(send, "blk", split_axis=0, concat_axis=0, tiled=True)
-    table = jnp.concatenate([recv, kv_local], axis=0)
-
+        (3, 1, 0, 2, 4),
+    )
     owner = lists_mine // block_ids
     slot_src = jnp.where(owner == rank, peers + lists_mine % block_ids, owner)
     slot_ids = jnp.arange(TOPK, dtype=jnp.int32)
@@ -163,28 +154,40 @@
 
     q2 = query_h.reshape(run_len, head_count * head_width)
     do2 = grad_h.reshape(run_len, head_count * head_width)
-    o2, dq2, dk_acc, dv_acc = attend(
-        slot_src.reshape(-1), query_base, table, q2, do2, key_pos
-    )
-    attn_h = o2.reshape(run_len, head_count, head_width)
-    query_grad_h = dq2.reshape(run_len, head_count, head_width)
-
-    acc = jnp.stack([dk_acc, dv_acc], axis=1)
-    remote = acc[:peers].astype(jnp.bfloat16)
-    local = acc[peers:].astype(jnp.bfloat16)
-    back = lax.all_to_all(remote, "blk", split_axis=0, concat_axis=0, tiled=True)
-    take_back = pick_send * present[..., None].astype(jnp.bfloat16)
-    total = local.astype(jnp.float32) + jnp.einsum(
-        "grl,rkgtd->lkgtd", take_back, back, preferred_element_type=jnp.float32
-    )
-    total = jnp.transpose(total.astype(jnp.bfloat16), (1, 0, 3, 2, 4))
-    key_grad_h = total[0].reshape(run_len, groups, head_width)
-    value_grad_h = total[1].reshape(run_len, groups, head_width)
+    outs, query_grads, key_grads, value_grads = [], [], [], []
+    for g in range(groups):
+        send = jnp.einsum(
+            "rb,bktd->rktd", pick_send[g], kv_local[g], preferred_element_type=jnp.float32
+        ).astype(jnp.bfloat16)
+        recv = lax.all_to_all(send, "blk", split_axis=0, concat_axis=0, tiled=True)
+        table = jnp.concatenate([recv, kv_local[g]], axis=0)
+        o_g, dq_g, dk_acc, dv_acc = attend(
+            slot_src[g].reshape(-1), query_base, table, q2, do2, key_pos[g], g, groups
+        )
+        outs.append(o_g)
+        query_grads.append(dq_g)
+        acc = jnp.stack([dk_acc, dv_acc], axis=1)
+        remote = acc[:peers].astype(jnp.bfloat16)
+        local = acc[peers:].astype(jnp.bfloat16)
+        back = lax.all_to_all(remote, "blk", split_axis=0, concat_axis=0, tiled=True)
+        total = local.astype(jnp.float32) + jnp.einsum(
+            "rl,rktd->lktd", take_back[g], back, preferred_element_type=jnp.float32
+        )
+        total = total.astype(jnp.bfloat16)
+        key_grads.append(total[:, 0])
+        value_grads.append(total[:, 1])
+
+    def heads_layout(parts):
+        return jnp.concatenate(parts, axis=1).reshape(run_len, head_count, head_width)
+
+    def group_layout(parts):
+        return jnp.stack(parts, axis=2).reshape(run_len, groups, head_width)
+
     return (
-        from_heads(attn_h),
-        from_heads(query_grad_h),
-        from_heads(key_grad_h),
-        from_heads(value_grad_h),
+        from_heads(heads_layout(outs)),
+        from_heads(heads_layout(query_grads)),
+        from_heads(group_layout(key_grads)),
+        from_heads(group_layout(value_grads)),
     )
 
 

time: 356 us -> 350 us (0.983)
  waiting for transfers between devices: 197 us -> 165 us
  starting transfers between devices: 46.4 us -> 56.7 us
  local copies, waits for them, and re-layouts: 35.3 us -> 41.9 us
  other arithmetic: 14.2 us -> 19.6 us
    all_to_all x1 -> x2, waiting for transfers between devices: 50.1 us -> 27.6 us  [on_device(): recv = lax.all_to_all(send, 'blk', split_axis=0, concat_axis=0, tiled=True)]
    all_to_all x1 -> x2, waiting for transfers between devices: 59.5 us -> 47.2 us  [on_device(): lax.all_to_all(remote, 'blk', split_axis=0, concat_axis=0, tiled=True)]
    unnamed x16 -> x42, local copies, waits for them, and re-layouts: 12.4 us -> 19.8 us
    all_to_all x1 -> x2, starting transfers between devices: 4.87 us -> 11.8 us  [on_device(): lax.all_to_all(remote, 'blk', split_axis=0, concat_axis=0, tiled=True)]
    all_to_all x1 -> x2, starting transfers between devices: 8.71 us -> 13.3 us  [on_device(): recv = lax.all_to_all(send, 'blk', split_axis=0, concat_axis=0, tiled=True)]
    all_to_all x6 -> x4, local copies, waits for them, and re-layouts: 3.98 us -> 7.67 us  [from_heads(): return lax.all_to_all(x, 'head', split_axis=0, concat_axis=1, tiled=True)]
    another operation x1 -> x4, other arithmetic: 4.16 us -> 7.81 us
    pallas_call x1 -> x2, Pallas kernels: 54.9 us -> 56.5 us  [attend(): pl.pallas_call(attention_kernel, grid_spec=grid_spec, out_shape=out_shape...]
  transfers between devices with their start and end apart: 10 -> 12, of which waited for: 10 -> 11; matrix products, arithmetic and copies ran while one was open for 13% -> 15% of each run, Pallas kernels for 0% -> 8%
where the time goes in v1:
time: 350 us; the launch traced here: 348 us
  waiting for transfers between devices  165 us (47%)
  starting transfers between devices  56.7 us (16%)
  Pallas kernels  56.5 us (16%)
  local copies, waits for them, and re-layouts  41.9 us (12%)
  other arithmetic  19.6 us (6%)
  matrix products  7.36 us (2%)
    pallas_call x2, Pallas kernels, attend(): pl.pallas_call(attention_kernel, grid_spec=grid_spec, out_shape=out_shape...  56.5 us
    all_to_all x4, waiting for transfers between devices, to_heads(): return lax.all_to_all(x, 'head', split_axis=1, concat_axis=0, tiled=True)  48.4 us
    all_to_all x2, waiting for transfers between devices, on_device(): lax.all_to_all(remote, 'blk', split_axis=0, concat_axis=0, tiled=True)  47.2 us
    all_to_all x4, waiting for transfers between devices, from_heads(): return lax.all_to_all(x, 'head', split_axis=0, concat_axis=1, tiled=True)  41.6 us
    all_to_all x2, waiting for transfers between devices, on_device(): recv = lax.all_to_all(send, 'blk', split_axis=0, concat_axis=0, tiled=True)  27.6 us
    unnamed x42, local copies, waits for them, and re-layouts  19.8 us
    all_to_all x4, starting transfers between devices, from_heads(): return lax.all_to_all(x, 'head', split_axis=0, concat_axis=1, tiled=True)  15.9 us
    all_to_all x4, starting transfers between devices, to_heads(): return lax.all_to_all(x, 'head', split_axis=1, concat_axis=0, tiled=True)  15.6 us
  transfers between devices with their start and end apart: 12, of which 11 were waited for; matrix products, arithmetic and copies ran while one was open for 15% of the time, Pallas kernels for 8%

profile of v1, /device:TPU:0, one launch (start us, length us, event | category | flops | bytes accessed | tf_op | source)
XLA Modules:
  0.0 348.1 jit_solution(14570452547233218809)
XLA Ops:
  2.6 4.4 %all-to-all-start = ((bf16[192,8,128]{2,0,1:T(8,128)(2,1)}), bf16[192,8,128]{2,0,1:T(8,128)(2,1)S(1)}, u32[]{:S(2)}, u32[]{:S(2)}) async-start(bf16[192,8,128]{2,0,1:T(8,128)(2,1)} %copy.83), calls=%async_computation | async-start | bytes 786432 | tf_op jit(solution)/shard_map/all_to_all | solution.py:13
  8.7 7.2 %all-to-all-done = bf16[192,8,128]{2,0,1:T(8,128)(2,1)S(1)} async-done(((bf16[192,8,128]{2,0,1:T(8,128)(2,1)}), bf16[192,8,128]{2,0,1:T(8,128)(2,1)S(1)}, u32[]{:S(2)}, u32[]{:S(2)}) %all-to-all-start) | async-done | bytes 393248 | tf_op jit(solution)/shard_map/all_to_all | solution.py:13
  15.9 4.1 %all-to-all-start.1 = ((bf16[192,8,128]{2,0,1:T(8,128)(2,1)}), bf16[192,8,128]{2,0,1:T(8,128)(2,1)}, u32[]{:S(2)}, u32[]{:S(2)}) async-start(bf16[192,8,128]{2,0,1:T(8,128)(2,1)} %copy.85), calls=%async_computation.1 | async-start | bytes 786432 | tf_op jit(solution)/shard_map/all_to_all | solution.py:13
  21.8 7.2 %all-to-all-done.1 = bf16[192,8,128]{2,0,1:T(8,128)(2,1)} async-done(((bf16[192,8,128]{2,0,1:T(8,128)(2,1)}), bf16[192,8,128]{2,0,1:T(8,128)(2,1)}, u32[]{:S(2)}, u32[]{:S(2)}) %all-to-all-start.1) | async-done | bytes 393248 | tf_op jit(solution)/shard_map/all_to_all | solution.py:13
  29.0 3.6 %all-to-all-start.4 = ((bf16[192,32,128]{2,0,1:T(8,128)(2,1)}), bf16[192,32,128]{2,0,1:T(8,128)(2,1)S(1)}, u32[]{:S(2)}, u32[]{:S(2)}) async-start(bf16[192,32,128]{2,0,1:T(8,128)(2,1)} %copy.91), calls=%async_computation.4 | async-start | bytes 3145728 | tf_op jit(solution)/shard_map/all_to_all | solution.py:13
  34.3 19.8 %all-to-all-done.4 = bf16[192,32,128]{2,0,1:T(8,128)(2,1)S(1)} async-done(((bf16[192,32,128]{2,0,1:T(8,128)(2,1)}), bf16[192,32,128]{2,0,1:T(8,128)(2,1)S(1)}, u32[]{:S(2)}, u32[]{:S(2)}) %all-to-all-start.4) | async-done | bytes 1572896 | tf_op jit(solution)/shard_map/all_to_all | solution.py:13
  54.1 3.6 %all-to-all-start.3 = ((bf16[192,32,128]{2,0,1:T(8,128)(2,1)}), bf16[192,32,128]{2,0,1:T(8,128)(2,1)S(1)}, u32[]{:S(2)}, u32[]{:S(2)}) async-start(bf16[192,32,128]{2,0,1:T(8,128)(2,1)} %copy.89), calls=%async_computation.3 | async-start | bytes 3145728 | tf_op jit(solution)/shard_map/all_to_all | solution.py:13
  65.0 14.3 %all-to-all-done.3 = bf16[192,32,128]{2,0,1:T(8,128)(2,1)S(1)} async-done(((bf16[192,32,128]{2,0,1:T(8,128)(2,1)}), bf16[192,32,128]{2,0,1:T(8,128)(2,1)S(1)}, u32[]{:S(2)}, u32[]{:S(2)}) %all-to-all-start.3) | async-done | bytes 1572896 | tf_op jit(solution)/shard_map/all_to_all | solution.py:13
  80.4 8.4 %all-to-all-start.2 = ((bf16[32,2,128,128]{3,2,1,0:T(8,128)(2,1)}), bf16[32,2,128,128]{3,2,1,0:T(8,128)(2,1)S(1)}, u32[]{:S(2)}, u32[]{:S(2)}) async-start(bf16[32,2,128,128]{3,2,1,0:T(8,128)(2,1)} %copy.142), calls=%async_computation.2 | async-start | bytes 4194304 | tf_op jit(solution)/shard_map/all_to_all | solution.py:162
  91.7 27.6 %all-to-all-done.2 = bf16[32,2,128,128]{3,2,1,0:T(8,128)(2,1)S(1)} async-done(((bf16[32,2,128,128]{3,2,1,0:T(8,128)(2,1)}), bf16[32,2,128,128]{3,2,1,0:T(8,128)(2,1)S(1)}, u32[]{:S(2)}, u32[]{:S(2)}) %all-to-all-start.2) | async-done | bytes 2097184 | tf_op jit(solution)/shard_map/all_to_all | solution.py:162
  120.7 4.9 %all-to-all-start.5 = ((bf16[32,2,128,128]{3,2,1,0:T(8,128)(2,1)}), bf16[32,2,128,128]{3,2,1,0:T(8,128)(2,1)}, u32[]{:S(2)}, u32[]{:S(2)}) async-start(bf16[32,2,128,128]{3,2,1,0:T(8,128)(2,1)} %copy.141), calls=%async_computation.5 | async-start | bytes 4194304 | tf_op jit(solution)/shard_map/all_to_all | solution.py:162
  127.5 2.4 copy.92
  135.7 28.4 %shard_map.84 = (bf16[768,512]{1,0:T(8,128)(2,1)S(1)}, bf16[768,512]{1,0:T(8,128)(2,1)S(1)}, f32[38,128,128]{2,1,0:T(8,128)}, f32[38,128,128]{2,1,0:T(8,128)}) custom-call(s32[48]{0:T(128)S(1)} %reshape_squeeze.6.src_ref, s32[6]{0:T(128)S(1)} %add_multiply_fusion.base_ref, ...), custom_call_target="tpu_custom_call" | custom-call | tf_op jit(solution)/shard_map/pallas_call | solution.py:105
  165.9 3.4 pad_maximum_fusion.3.refs_0_.refs_1_.refs_2_.refs_3_.refs_4_.refs_5_.refs_6_.refs_7_.refs_8_.refs_9_.refs_10_.refs_11_.refs_12_.refs_13_.refs_14_.refs_15_
  169.3 28.1 %shard_map.85 = (bf16[768,512]{1,0:T(8,128)(2,1)S(1)}, bf16[768,512]{1,0:T(8,128)(2,1)S(1)}, f32[38,128,128]{2,1,0:T(8,128)}, f32[38,128,128]{2,1,0:T(8,128)}) custom-call(s32[48]{0:T(128)S(1)} %reshape_squeeze.7.src_ref, s32[6]{0:T(128)S(1)} %add_multiply_fusion.base_ref, ...), custom_call_target="tpu_custom_call" | custom-call | tf_op jit(solution)/shard_map/pallas_call | solution.py:105
  201.2 4.7 %all-to-all-start.7 = ((bf16[768,8,128]{2,1,0:T(8,128)(2,1)}), bf16[768,8,128]{2,1,0:T(8,128)(2,1)}, u32[]{:S(2)}, u32[]{:S(2)}) async-start(bf16[768,8,128]{2,1,0:T(8,128)(2,1)} %bitcast.109), calls=%async_computation.7 | async-start | bytes 3145728 | tf_op jit(solution)/shard_map/all_to_all | solution.py:17
  209.4 17.9 %all-to-all-done.7 = bf16[768,8,128]{2,1,0:T(8,128)(2,1)} async-done(((bf16[768,8,128]{2,1,0:T(8,128)(2,1)}), bf16[768,8,128]{2,1,0:T(8,128)(2,1)}, u32[]{:S(2)}, u32[]{:S(2)}) %all-to-all-start.7) | async-done | bytes 1572896 | tf_op jit(solution)/shard_map/all_to_all | solution.py:17
  227.3 7.0 %all-to-all-start.8 = ((bf16[32,2,128,128]{3,2,1,0:T(8,128)(2,1)}), bf16[32,2,128,128]{3,2,1,0:T(8,128)(2,1)}, u32[]{:S(2)}, u32[]{:S(2)}) async-start(bf16[32,2,128,128]{3,2,1,0:T(8,128)(2,1)} %copy.101), calls=%async_computation.8 | async-start | bytes 4194304 | tf_op jit(solution)/shard_map/all_to_all | solution.py:172
  234.4 2.6 fusion
  238.5 26.4 %all-to-all-done.8 = bf16[32,2,128,128]{3,2,1,0:T(8,128)(2,1)} async-done(((bf16[32,2,128,128]{3,2,1,0:T(8,128)(2,1)}), bf16[32,2,128,128]{3,2,1,0:T(8,128)(2,1)}, u32[]{:S(2)}, u32[]{:S(2)}) %all-to-all-start.8) | async-done | bytes 2097184 | tf_op jit(solution)/shard_map/all_to_all | solution.py:172
  264.9 4.8 %all-to-all-start.9 = ((bf16[32,2,128,128]{3,2,1,0:T(8,128)(2,1)}), bf16[32,2,128,128]{3,2,1,0:T(8,128)(2,1)}, u32[]{:S(2)}, u32[]{:S(2)}) async-start(bf16[32,2,128,128]{3,2,1,0:T(8,128)(2,1)} %copy.104), calls=%async_computation.9 | async-start | bytes 4194304 | tf_op jit(solution)/shard_map/all_to_all | solution.py:172
  269.7 3.0 copy.119
  272.7 2.8 fusion.4
  275.5 20.8 %all-to-all-done.9 = bf16[32,2,128,128]{3,2,1,0:T(8,128)(2,1)} async-done(((bf16[32,2,128,128]{3,2,1,0:T(8,128)(2,1)}), bf16[32,2,128,128]{3,2,1,0:T(8,128)(2,1)}, u32[]{:S(2)}, u32[]{:S(2)}) %all-to-all-start.9) | async-done | bytes 2097184 | tf_op jit(solution)/shard_map/all_to_all | solution.py:172
  296.3 4.3 %all-to-all-start.6 = ((bf16[768,8,128]{2,1,0:T(8,128)(2,1)}), bf16[768,8,128]{2,1,0:T(8,128)(2,1)}, u32[]{:S(2)}, u32[]{:S(2)}) async-start(bf16[768,8,128]{2,1,0:T(8,128)(2,1)} %bitcast.108), calls=%async_computation.6 | async-start | bytes 3145728 | tf_op jit(solution)/shard_map/all_to_all | solution.py:17
  302.4 3.0 fusion.2
  307.6 14.8 %all-to-all-done.6 = bf16[768,8,128]{2,1,0:T(8,128)(2,1)} async-done(((bf16[768,8,128]{2,1,0:T(8,128)(2,1)}), bf16[768,8,128]{2,1,0:T(8,128)(2,1)}, u32[]{:S(2)}, u32[]{:S(2)}) %all-to-all-start.6) | async-done | bytes 1572896 | tf_op jit(solution)/shard_map/all_to_all | solution.py:17
  322.3 3.5 all-to-all-start.11
  328.1 6.6 %all-to-all-done.11 = bf16[768,2,128]{2,1,0:T(2,128)(2,1)S(1)} async-done(((bf16[768,2,128]{2,1,0:T(2,128)(2,1)}), bf16[768,2,128]{2,1,0:T(2,128)(2,1)S(1)}, u32[]{:S(2)}, u32[]{:S(2)}) %all-to-all-start.11) | async-done | bytes 393248 | tf_op jit(solution)/shard_map/all_to_all | solution.py:17
  334.7 3.5 all-to-all-start.10
  338.2 2.8 copy.145
  341.0 2.8 copy.146
  (90 shorter events, 48.3 us)
Async XLA Ops:
  0.6 19.4 %copy-start.15 = (bf16[192,32,128]{2,1,0:T(8,128)(2,1)S(1)}, bf16[192,32,128]{2,1,0:T(8,128)(2,1)}, u32[]{:S(2)}) copy-start(bf16[192,32,128]{2,1,0:T(8,128)(2,1)} %param.9) | copy-start | bytes 4718596
  2.6 13.3 %all-to-all-start = ((bf16[192,8,128]{2,0,1:T(8,128)(2,1)}), bf16[192,8,128]{2,0,1:T(8,128)(2,1)S(1)}, u32[]{:S(2)}, u32[]{:S(2)}) async-start(bf16[192,8,128]{2,0,1:T(8,128)(2,1)} %copy.83), calls=%async_computation | async-start | bytes 786432 | tf_op jit(solution)/shard_map/all_to_all | solution.py:13
  15.9 13.1 %all-to-all-start.1 = ((bf16[192,8,128]{2,0,1:T(8,128)(2,1)}), bf16[192,8,128]{2,0,1:T(8,128)(2,1)}, u32[]{:S(2)}, u32[]{:S(2)}) async-start(bf16[192,8,128]{2,0,1:T(8,128)(2,1)} %copy.85), calls=%async_computation.1 | async-start | bytes 786432 | tf_op jit(solution)/shard_map/all_to_all | solution.py:13
  21.8 10.8 %copy-start.16 = (bf16[192,32,128]{2,1,0:T(8,128)(2,1)S(1)}, bf16[192,32,128]{2,1,0:T(8,128)(2,1)}, u32[]{:S(2)}) copy-start(bf16[192,32,128]{2,1,0:T(8,128)(2,1)} %param.5) | copy-start | bytes 4718596
  29.0 25.1 %all-to-all-start.4 = ((bf16[192,32,128]{2,0,1:T(8,128)(2,1)}), bf16[192,32,128]{2,0,1:T(8,128)(2,1)S(1)}, u32[]{:S(2)}, u32[]{:S(2)}) async-start(bf16[192,32,128]{2,0,1:T(8,128)(2,1)} %copy.91), calls=%async_computation.4 | async-start | bytes 3145728 | tf_op jit(solution)/shard_map/all_to_all | solution.py:13
  54.1 7.0 %copy-start.9 = (bf16[192,32,128]{2,0,1:T(8,128)(2,1)}, bf16[192,32,128]{2,0,1:T(8,128)(2,1)S(1)}, u32[]{:S(2)}) copy-start(bf16[192,32,128]{2,0,1:T(8,128)(2,1)S(1)} %all-to-all-done.4) | copy-start | bytes 4718596
  54.1 25.1 %all-to-all-start.3 = ((bf16[192,32,128]{2,0,1:T(8,128)(2,1)}), bf16[192,32,128]{2,0,1:T(8,128)(2,1)S(1)}, u32[]{:S(2)}, u32[]{:S(2)}) async-start(bf16[192,32,128]{2,0,1:T(8,128)(2,1)} %copy.89), calls=%async_computation.3 | async-start | bytes 3145728 | tf_op jit(solution)/shard_map/all_to_all | solution.py:13
  61.3 0.7 copy-start.13
  61.3 27.5 %copy-start.12 = (bf16[6,2,128,128]{3,2,1,0:T(8,128)(2,1)}, bf16[6,2,128,128]{3,2,1,0:T(8,128)(2,1)S(1)}, u32[]{:S(2)}) copy-start(bf16[6,2,128,128]{3,2,1,0:T(8,128)(2,1)S(1)} %get-tuple-element.23) | copy-start | bytes 1179652
  79.2 1.1 copy-start.10
  80.4 39.0 %all-to-all-start.2 = ((bf16[32,2,128,128]{3,2,1,0:T(8,128)(2,1)}), bf16[32,2,128,128]{3,2,1,0:T(8,128)(2,1)S(1)}, u32[]{:S(2)}, u32[]{:S(2)}) async-start(bf16[32,2,128,128]{3,2,1,0:T(8,128)(2,1)} %copy.142), calls=%async_computation.2 | async-start | bytes 4194304 | tf_op jit(solution)/shard_map/all_to_all | solution.py:162
  119.4 1.4 copy-start.7
  120.7 45.2 %all-to-all-start.5 = ((bf16[32,2,128,128]{3,2,1,0:T(8,128)(2,1)}), bf16[32,2,128,128]{3,2,1,0:T(8,128)(2,1)}, u32[]{:S(2)}, u32[]{:S(2)}) async-start(bf16[32,2,128,128]{3,2,1,0:T(8,128)(2,1)} %copy.141), calls=%async_computation.5 | async-start | bytes 4194304 | tf_op jit(solution)/shard_map/all_to_all | solution.py:162
  129.9 1.4 copy-start.11
  132.4 1.6 copy-start.8
  132.4 1.6 copy-start.14
  164.1 0.9 copy-start
  165.0 0.9 copy-start.2
  169.3 28.1 %copy-start.1 = (bf16[768,512]{1,0:T(8,128)(2,1)S(1)}, bf16[768,512]{1,0:T(8,128)(2,1)}, u32[]{:S(2)}) copy-start(bf16[768,512]{1,0:T(8,128)(2,1)} %copy-done) | copy-start | bytes 2359300
  169.3 28.1 %copy-start.3 = (bf16[768,512]{1,0:T(8,128)(2,1)S(1)}, bf16[768,512]{1,0:T(8,128)(2,1)}, u32[]{:S(2)}) copy-start(bf16[768,512]{1,0:T(8,128)(2,1)} %copy-done.2) | copy-start | bytes 2359300
  201.2 4.7 %copy-start.4 = (f32[38,128,128]{2,1,0:T(8,128)S(1)}, f32[38,128,128]{2,1,0:T(8,128)}, u32[]{:S(2)}) copy-start(f32[38,128,128]{2,1,0:T(8,128)} %get-tuple-element.16) | copy-start | bytes 7471108
  201.2 26.1 %all-to-all-start.7 = ((bf16[768,8,128]{2,1,0:T(8,128)(2,1)}), bf16[768,8,128]{2,1,0:T(8,128)(2,1)}, u32[]{:S(2)}, u32[]{:S(2)}) async-start(bf16[768,8,128]{2,1,0:T(8,128)(2,1)} %bitcast.109), calls=%async_computation.7 | async-start | bytes 3145728 | tf_op jit(solution)/shard_map/all_to_all | solution.py:17
  227.3 37.6 %all-to-all-start.8 = ((bf16[32,2,128,128]{3,2,1,0:T(8,128)(2,1)}), bf16[32,2,128,128]{3,2,1,0:T(8,128)(2,1)}, u32[]{:S(2)}, u32[]{:S(2)}) async-start(bf16[32,2,128,128]{3,2,1,0:T(8,128)(2,1)} %copy.101), calls=%async_computation.8 | async-start | bytes 4194304 | tf_op jit(solution)/shard_map/all_to_all | solution.py:172
  264.9 31.4 %all-to-all-start.9 = ((bf16[32,2,128,128]{3,2,1,0:T(8,128)(2,1)}), bf16[32,2,128,128]{3,2,1,0:T(8,128)(2,1)}, u32[]{:S(2)}, u32[]{:S(2)}) async-start(bf16[32,2,128,128]{3,2,1,0:T(8,128)(2,1)} %copy.104), calls=%async_computation.9 | async-start | bytes 4194304 | tf_op jit(solution)/shard_map/all_to_all | solution.py:172
  296.3 26.0 %all-to-all-start.6 = ((bf16[768,8,128]{2,1,0:T(8,128)(2,1)}), bf16[768,8,128]{2,1,0:T(8,128)(2,1)}, u32[]{:S(2)}, u32[]{:S(2)}) async-start(bf16[768,8,128]{2,1,0:T(8,128)(2,1)} %bitcast.108), calls=%async_computation.6 | async-start | bytes 3145728 | tf_op jit(solution)/shard_map/all_to_all | solution.py:17
  300.7 4.7 %copy-start.6 = (f32[38,128,128]{2,1,0:T(8,128)S(1)}, f32[38,128,128]{2,1,0:T(8,128)}, u32[]{:S(2)}) copy-start(f32[38,128,128]{2,1,0:T(8,128)} %get-tuple-element.19) | copy-start | bytes 7471108
  302.0 3.4 copy-start.5
  322.3 12.4 %all-to-all-start.11 = ((bf16[768,2,128]{2,1,0:T(2,128)(2,1)}), bf16[768,2,128]{2,1,0:T(2,128)(2,1)S(1)}, u32[]{:S(2)}, u32[]{:S(2)}) async-start(bf16[768,2,128]{2,1,0:T(2,128)(2,1)} %pad_maximum_fusion.5), calls=%async_computation.11 | async-start | bytes 786432 | tf_op jit(solution)/shard_map/all_to_all | solution.py:17
  334.7 12.4 %all-to-all-start.10 = ((bf16[768,2,128]{2,1,0:T(2,128)(2,1)}), bf16[768,2,128]{2,1,0:T(2,128)(2,1)S(1)}, u32[]{:S(2)}, u32[]{:S(2)}) async-start(bf16[768,2,128]{2,1,0:T(2,128)(2,1)} %pad_maximum_fusion.4), calls=%async_computation.10 | async-start | bytes 786432 | tf_op jit(solution)/shard_map/all_to_all | solution.py:17

commit v2 on v1

--- a/solution.py
+++ b/solution.py
@@ -9,12 +9,13 @@
 TOPK = 8
 
 
-def to_heads(x):
-    return lax.all_to_all(x, "head", split_axis=1, concat_axis=0, tiled=True)
-
-
-def from_heads(x):
-    return lax.all_to_all(x, "head", split_axis=0, concat_axis=1, tiled=True)
+def to_heads(*xs):
+    return lax.all_to_all(jnp.stack(xs), "head", split_axis=2, concat_axis=1, tiled=True)
+
+
+def from_heads(*xs):
+    both = lax.all_to_all(jnp.stack(xs), "head", split_axis=1, concat_axis=2, tiled=True)
+    return tuple(both[i] for i in range(len(xs)))
 
 
 def attention_kernel(src_ref, base_ref, *refs):
@@ -69,11 +70,12 @@
         dv_ref[t] = dv_ref[t] + dv[rows]
 
 
-def attend(slot_src, query_base, table, q2, do2, key_pos, group, groups):
-    block_ids = q2.shape[0] // BLOCK_TOKENS
+def attend(slot_src, query_base, table, qg2, key_pos, group, groups):
+    run_len = qg2.shape[1]
+    block_ids = run_len // BLOCK_TOKENS
     targets = table.shape[0]
     head_width = table.shape[-1]
-    row_width = q2.shape[1] // groups
+    row_width = qg2.shape[2] // groups
 
     def slot_spec(s, kv):
         def index(b, src, base):
@@ -81,18 +83,19 @@
 
         return pl.BlockSpec((None, None, BLOCK_TOKENS, head_width), index)
 
-    in_row = pl.BlockSpec((BLOCK_TOKENS, row_width), lambda b, src, base: (b, group))
+    q_row = pl.BlockSpec((None, BLOCK_TOKENS, row_width), lambda b, src, base: (0, b, group))
+    do_row = pl.BlockSpec((None, BLOCK_TOKENS, row_width), lambda b, src, base: (1, b, group))
     out_row = pl.BlockSpec((BLOCK_TOKENS, row_width), lambda b, src, base: (b, 0))
     pos_spec = pl.BlockSpec((None, 1, TOPK * BLOCK_TOKENS), lambda b, src, base: (b, 0, 0))
     acc_spec = pl.BlockSpec((targets, BLOCK_TOKENS, head_width), lambda b, src, base: (0, 0, 0))
     in_specs = (
         [slot_spec(s, 0) for s in range(TOPK)]
         + [slot_spec(s, 1) for s in range(TOPK)]
-        + [in_row, in_row, pos_spec]
+        + [q_row, do_row, pos_spec]
     )
     out_shape = (
-        jax.ShapeDtypeStruct((q2.shape[0], row_width), jnp.bfloat16),
-        jax.ShapeDtypeStruct((q2.shape[0], row_width), jnp.bfloat16),
+        jax.ShapeDtypeStruct((run_len, row_width), jnp.bfloat16),
+        jax.ShapeDtypeStruct((run_len, row_width), jnp.bfloat16),
         jax.ShapeDtypeStruct((targets, BLOCK_TOKENS, head_width), jnp.float32),
         jax.ShapeDtypeStruct((targets, BLOCK_TOKENS, head_width), jnp.float32),
     )
@@ -110,16 +113,14 @@
             dimension_semantics=("arbitrary",),
             vmem_limit_bytes=48 * 1024 * 1024,
         ),
-    )(slot_src, query_base, *([table] * (2 * TOPK)), q2, do2, key_pos)
+    )(slot_src, query_base, *([table] * (2 * TOPK)), qg2, qg2, key_pos)
 
 
 def on_device(queries, rotated_keys, value_vectors, block_list, grad_out):
-    query_h = to_heads(queries)
-    key_h = to_heads(rotated_keys)
-    value_h = to_heads(value_vectors)
-    grad_h = to_heads(grad_out)
-    run_len, head_count, head_width = query_h.shape
-    groups = key_h.shape[1]
+    kv_h = to_heads(rotated_keys, value_vectors)
+    qg_h = to_heads(queries, grad_out)
+    _, run_len, head_count, head_width = qg_h.shape
+    groups = kv_h.shape[2]
     group_width = head_count // groups
     block_ids = run_len // BLOCK_TOKENS
     peers = lax.axis_size("blk")
@@ -139,8 +140,7 @@
     take_back = pick_send * present[..., None].astype(jnp.bfloat16)
 
     kv_local = jnp.transpose(
-        jnp.stack([key_h, value_h]).reshape(2, block_ids, BLOCK_TOKENS, groups, head_width),
-        (3, 1, 0, 2, 4),
+        kv_h.reshape(2, block_ids, BLOCK_TOKENS, groups, head_width), (3, 1, 0, 2, 4)
     )
     owner = lists_mine // block_ids
     slot_src = jnp.where(owner == rank, peers + lists_mine % block_ids, owner)
@@ -152,8 +152,7 @@
     key_pos = key_pos.reshape(groups, block_ids, 1, TOPK * BLOCK_TOKENS)
     query_base = (rank * block_ids + block_range) * BLOCK_TOKENS
 
-    q2 = query_h.reshape(run_len, head_count * head_width)
-    do2 = grad_h.reshape(run_len, head_count * head_width)
+    qg2 = qg_h.reshape(2, run_len, head_count * head_width)
     outs, query_grads, key_grads, value_grads = [], [], [], []
     for g in range(groups):
         send = jnp.einsum(
@@ -162,7 +161,7 @@
         recv = lax.all_to_all(send, "blk", split_axis=0, concat_axis=0, tiled=True)
         table = jnp.concatenate([recv, kv_local[g]], axis=0)
         o_g, dq_g, dk_acc, dv_acc = attend(
-            slot_src[g].reshape(-1), query_base, table, q2, do2, key_pos[g], g, groups
+            slot_src[g].reshape(-1), query_base, table, qg2, key_pos[g], g, groups
         )
         outs.append(o_g)
         query_grads.append(dq_g)
@@ -183,12 +182,9 @@
     def group_layout(parts):
         return jnp.stack(parts, axis=2).reshape(run_len, groups, head_width)
 
-    return (
-        from_heads(heads_layout(outs)),
-        from_heads(heads_layout(query_grads)),
-        from_heads(group_layout(key_grads)),
-        from_heads(group_layout(value_grads)),
-    )
+    attn_out, grad_queries = from_heads(heads_layout(outs), heads_layout(query_grads))
+    key_gradient, value_gradient = from_heads(group_layout(key_grads), group_layout(value_grads))
+    return attn_out, grad_queries, key_gradient, value_gradient
 
 
 def solution(mesh):

time: 350 us -> 295 us (0.84)
  waiting for transfers between devices: 165 us -> 123 us
  starting transfers between devices: 56.7 us -> 45.6 us
  local copies, waits for them, and re-layouts: 41.9 us -> 35.5 us
  other arithmetic: 19.6 us -> 25.4 us
    all_to_all x2, waiting for transfers between devices: 47.2 us -> 19.4 us  [on_device(): lax.all_to_all(remote, 'blk', split_axis=0, concat_axis=0, tiled=True)]
    unnamed x42 -> x28, local copies, waits for them, and re-layouts: 19.8 us -> 3.22 us
    all_to_all x8 -> x4, starting transfers between devices: 31.5 us -> 16.5 us  [the longest x2 8.42 us: from_heads(): lax.all_to_all(jnp.stack(xs), 'head', split_axis=1, concat_axis=2, tiled=...]
    all_to_all x8 -> x4, waiting for transfers between devices: 90 us -> 75.8 us  [the longest x2 41 us: to_heads(): lax.all_to_all(jnp.stack(xs), 'head', split_axis=2, concat_axis=1, tiled=...]
    slice x2 -> x8, local copies, waits for them, and re-layouts: 0.06 us -> 7.56 us  [the longest x6 7.51 us: from_heads(): return tuple((both[i] for i in range(len(xs))))]
    all_to_all x8 -> x2, local copies, waits for them, and re-layouts: 12.2 us -> 5.1 us  [to_heads(): lax.all_to_all(jnp.stack(xs), 'head', split_axis=2, concat_axis=1, tiled=...]
    another operation x4 -> x6, other arithmetic: 7.81 us -> 14.4 us  [the longest x2 5.88 us: from_heads(): jnp.stack(xs)]
    reshape x0 -> x2, local copies, waits for them, and re-layouts: none -> 5.96 us  [the longest x1 5.89 us: on_device(): qg2 = qg_h.reshape(2, run_len, head_count * head_width)]
  transfers between devices with their start and end apart: 12 -> 8, of which waited for: 11 -> 6; matrix products, arithmetic and copies ran while one was open for 15% -> 21% of each run, Pallas kernels for 8% -> 19%
where the time goes in v2:
time: 295 us; the launch traced here: 293 us
  waiting for transfers between devices  123 us (42%)
  Pallas kernels  55.2 us (19%)
  starting transfers between devices  45.6 us (15%)
  local copies, waits for them, and re-layouts  35.5 us (12%)
  other arithmetic  25.4 us (9%)
  matrix products  7.68 us (3%)
    pallas_call x2, Pallas kernels, attend(): pl.pallas_call(attention_kernel, grid_spec=grid_spec, out_shape=out_shape...  55.2 us
    all_to_all x2, waiting for transfers between devices, to_heads(): lax.all_to_all(jnp.stack(xs), 'head', split_axis=2, concat_axis=1, tiled=...  41 us
    all_to_all x2, waiting for transfers between devices, from_heads(): lax.all_to_all(jnp.stack(xs), 'head', split_axis=1, concat_axis=2, tiled=...  34.8 us
    all_to_all x2, waiting for transfers between devices, on_device(): recv = lax.all_to_all(send, 'blk', split_axis=0, concat_axis=0, tiled=True)  27.6 us
    all_to_all x2, waiting for transfers between devices, on_device(): lax.all_to_all(remote, 'blk', split_axis=0, concat_axis=0, tiled=True)  19.4 us
    all_to_all x2, starting transfers between devices, on_device(): lax.all_to_all(remote, 'blk', split_axis=0, concat_axis=0, tiled=True)  15.6 us
    all_to_all x2, starting transfers between devices, on_device(): recv = lax.all_to_all(send, 'blk', split_axis=0, concat_axis=0, tiled=True)  13.5 us
    all_to_all x2, starting transfers between devices, from_heads(): lax.all_to_all(jnp.stack(xs), 'head', split_axis=1, concat_axis=2, tiled=...  8.42 us
  transfers between devices with their start and end apart: 8, of which 6 were waited for; matrix products, arithmetic and copies ran while one was open for 21% of the time, Pallas kernels for 19%

profile of v2, /device:TPU:0, one launch (start us, length us, event | category | flops | bytes accessed | tf_op | source)
XLA Modules:
  0.0 293.3 jit_solution(14936936053186600534)
XLA Ops:
  3.0 4.4 %all-to-all-start = ((bf16[2,192,8,128]{3,1,0,2:T(8,128)(2,1)}), bf16[2,192,8,128]{3,1,0,2:T(8,128)(2,1)S(1)}, u32[]{:S(2)}, u32[]{:S(2)}) async-start(bf16[2,192,8,128]{3,1,0,2:T(8,128)(2,1)} %pad_maximum_fusion.6), calls=%async_computation | async-start | bytes 1572864 | tf_op jit(solution)/shard_map/all_to_all | solution.py:13
  7.4 2.6 copy_bitcast_fusion.3
  10.0 2.0 pad_maximum_fusion.2
  11.9 8.6 %all-to-all-done = bf16[2,192,8,128]{3,1,0,2:T(8,128)(2,1)S(1)} async-done(((bf16[2,192,8,128]{3,1,0,2:T(8,128)(2,1)}), bf16[2,192,8,128]{3,1,0,2:T(8,128)(2,1)S(1)}, u32[]{:S(2)}, u32[]{:S(2)}) %all-to-all-start) | async-done | bytes 786464 | tf_op jit(solution)/shard_map/all_to_all | solution.py:13
  21.4 3.7 %all-to-all-start.2 = ((bf16[2,192,32,128]{3,1,0,2:T(8,128)(2,1)}), bf16[2,192,32,128]{3,1,0,2:T(8,128)(2,1)S(1)}, u32[]{:S(2)}, u32[]{:S(2)}) async-start(bf16[2,192,32,128]{3,1,0,2:T(8,128)(2,1)} %pad_maximum_fusion.2), calls=%async_computation.2 | async-start | bytes 6291456 | tf_op jit(solution)/shard_map/all_to_all | solution.py:13
  29.0 2.1 copy.160
  31.1 32.4 %all-to-all-done.2 = bf16[2,192,32,128]{3,1,0,2:T(8,128)(2,1)S(1)} async-done(((bf16[2,192,32,128]{3,1,0,2:T(8,128)(2,1)}), bf16[2,192,32,128]{3,1,0,2:T(8,128)(2,1)S(1)}, u32[]{:S(2)}, u32[]{:S(2)}) %all-to-all-start.2) | async-done | bytes 3145760 | tf_op jit(solution)/shard_map/all_to_all | solution.py:13
  63.5 8.6 %all-to-all-start.1 = ((bf16[32,2,128,128]{3,2,1,0:T(8,128)(2,1)}), bf16[32,2,128,128]{3,2,1,0:T(8,128)(2,1)}, u32[]{:S(2)}, u32[]{:S(2)}) async-start(bf16[32,2,128,128]{3,2,1,0:T(8,128)(2,1)} %copy.160), calls=%async_computation.1 | async-start | bytes 4194304 | tf_op jit(solution)/shard_map/all_to_all | solution.py:161
  72.9 2.2 copy.159
  75.0 27.6 %all-to-all-done.1 = bf16[32,2,128,128]{3,2,1,0:T(8,128)(2,1)} async-done(((bf16[32,2,128,128]{3,2,1,0:T(8,128)(2,1)}), bf16[32,2,128,128]{3,2,1,0:T(8,128)(2,1)}, u32[]{:S(2)}, u32[]{:S(2)}) %all-to-all-start.1) | async-done | bytes 2097184 | tf_op jit(solution)/shard_map/all_to_all | solution.py:161
  102.6 5.0 %all-to-all-start.3 = ((bf16[32,2,128,128]{3,2,1,0:T(8,128)(2,1)}), bf16[32,2,128,128]{3,2,1,0:T(8,128)(2,1)}, u32[]{:S(2)}, u32[]{:S(2)}) async-start(bf16[32,2,128,128]{3,2,1,0:T(8,128)(2,1)} %copy.159), calls=%async_computation.3 | async-start | bytes 4194304 | tf_op jit(solution)/shard_map/all_to_all | solution.py:161
  109.3 3.9 %copy.161 = bf16[2,192,4,8,128]{4,3,1,2,0:T(8,128)(2,1)} copy(bf16[2,192,4,8,128]{4,1,0,3,2:T(8,128)(2,1)S(1)} %bitcast.99) | data formatting | bytes 6291456 | tf_op jit(solution)/shard_map/all_to_all | solution.py:13
  113.2 5.9 %reshape.80.refs_16_.refs_17_ = bf16[2,768,1024]{2,1,0:T(8,128)(2,1)} reshape(bf16[2,4,192,8,128]{4,3,2,1,0:T(8,128)(2,1)} %bitcast.100) | data formatting | bytes 6291456 | tf_op jit(solution)/shard_map/reshape | solution.py:155
  119.1 3.3 %pad_maximum_fusion.4.refs_0_.refs_1_.refs_2_.refs_3_.refs_4_.refs_5_.refs_6_.refs_7_.refs_8_.refs_9_.refs_10_.refs_11_.refs_12_.refs_13_.refs_14_.refs_15_ = bf16[38,2,128,128]{3,2,1,0:T(8,128)(2,1)} fusion(bf16[6,2,128,128]{3,2,1,0:T(8,128)(2,1)S(1)} %copy-done.10, bf16[32,2,128,128]{3,2,1,0:T(8,128)(2,1)} %all-to-all-done.1), kind=kLoop, calls=%fused_computation.9 | loop fusion | flops 1245184 | bytes 4980736 | tf_op jit(solution)/shard_map/concatenate | solution.py:162
  122.4 27.5 %shard_map.84 = (bf16[768,512]{1,0:T(8,128)(2,1)S(1)}, bf16[768,512]{1,0:T(8,128)(2,1)S(1)}, f32[38,128,128]{2,1,0:T(8,128)S(1)}, f32[38,128,128]{2,1,0:T(8,128)}) custom-call(s32[48]{0:T(128)S(1)} %reshape_squeeze.6.src_ref, s32[6]{0:T(128)S(1)} %add_multiply_fusion.base_ref, ...), custom_call_target="tpu_custom_call" | custom-call | tf_op jit(solution)/shard_map/pallas_call | solution.py:108
  149.9 2.2 fusion.1
  152.1 1.7 copy.116
  153.8 8.0 %all-to-all-start.5 = ((bf16[32,2,128,128]{3,2,1,0:T(8,128)(2,1)}), bf16[32,2,128,128]{3,2,1,0:T(8,128)(2,1)}, u32[]{:S(2)}, u32[]{:S(2)}) async-start(bf16[32,2,128,128]{3,2,1,0:T(8,128)(2,1)} %copy.116), calls=%async_computation.5 | async-start | bytes 4194304 | tf_op jit(solution)/shard_map/all_to_all | solution.py:171
  162.0 3.4 %pad_maximum_fusion.5.refs_0_.refs_1_.refs_2_.refs_3_.refs_4_.refs_5_.refs_6_.refs_7_.refs_8_.refs_9_.refs_10_.refs_11_.refs_12_.refs_13_.refs_14_.refs_15_ = bf16[38,2,128,128]{3,2,1,0:T(8,128)(2,1)} fusion(bf16[6,2,128,128]{3,2,1,0:T(8,128)(2,1)} %copy-done.8, bf16[32,2,128,128]{3,2,1,0:T(8,128)(2,1)} %all-to-all-done.3), kind=kLoop, calls=%fused_computation.10 | loop fusion | flops 1245184 | bytes 4980736 | tf_op jit(solution)/shard_map/concatenate | solution.py:162
  165.4 27.7 %shard_map.85 = (bf16[768,512]{1,0:T(8,128)(2,1)S(1)}, bf16[768,512]{1,0:T(8,128)(2,1)S(1)}, f32[38,128,128]{2,1,0:T(8,128)S(1)}, f32[38,128,128]{2,1,0:T(8,128)}) custom-call(s32[48]{0:T(128)S(1)} %reshape_squeeze.7.src_ref, s32[6]{0:T(128)S(1)} %add_multiply_fusion.base_ref, ...), custom_call_target="tpu_custom_call" | custom-call | tf_op jit(solution)/shard_map/pallas_call | solution.py:108
  193.1 3.4 %fusion = bf16[32,2,128,128]{3,2,0,1:T(8,128)(2,1)S(1)} fusion(f32[38,1,128,128]{3,2,0,1:T(8,128)} %bitcast.103, f32[38,1,128,128]{3,2,0,1:T(8,128)S(1)} %bitcast.95), kind=kLoop, calls=%fused_computation.1 | loop fusion | flops 1048576 | bytes 7077888 | tf_op jit(solution)/shard_map/convert.1
  198.1 7.5 %all-to-all-start.6 = ((bf16[32,2,128,128]{3,2,1,0:T(8,128)(2,1)}), bf16[32,2,128,128]{3,2,1,0:T(8,128)(2,1)}, u32[]{:S(2)}, u32[]{:S(2)}) async-start(bf16[32,2,128,128]{3,2,1,0:T(8,128)(2,1)} %copy.119), calls=%async_computation.6 | async-start | bytes 4194304 | tf_op jit(solution)/shard_map/all_to_all | solution.py:171
  209.3 2.2 pad_maximum_fusion.3
  211.5 19.4 %all-to-all-done.6 = bf16[32,2,128,128]{3,2,1,0:T(8,128)(2,1)} async-done(((bf16[32,2,128,128]{3,2,1,0:T(8,128)(2,1)}), bf16[32,2,128,128]{3,2,1,0:T(8,128)(2,1)}, u32[]{:S(2)}, u32[]{:S(2)}) %all-to-all-start.6) | async-done | bytes 2097184 | tf_op jit(solution)/shard_map/all_to_all | solution.py:171
  230.9 4.9 %all-to-all-start.4 = ((bf16[2,768,8,128]{3,2,0,1:T(8,128)(2,1)}), bf16[2,768,8,128]{3,2,0,1:T(8,128)(2,1)}, u32[]{:S(2)}, u32[]{:S(2)}) async-start(bf16[2,768,8,128]{3,2,0,1:T(8,128)(2,1)} %pad_maximum_fusion.3), calls=%async_computation.4 | async-start | bytes 6291456 | tf_op jit(solution)/shard_map/all_to_all | solution.py:17
  235.9 3.0 %fusion.4 = f32[6,2,128,128]{3,0,2,1:T(8,128)S(1)} fusion(bf16[32,2,128,128]{3,2,1,0:T(8,128)(2,1)} %all-to-all-done.5, bf16[2,32,6]{1,2,0:T(8,128)(2,1)S(1)} %broadcast_select_fusion), kind=kOutput, calls=%fused_computation.13 | convolution fusion | flops 12582912 | bytes 2885632 | tf_op jit(solution)/shard_map/rl,rktd->lktd/dot_general | solution.py:172
  239.7 3.2 %fusion.2 = f32[6,2,128,128]{3,0,2,1:T(8,128)S(1)} fusion(bf16[32,2,128,128]{3,2,1,0:T(8,128)(2,1)} %all-to-all-done.6, bf16[2,32,6]{1,2,0:T(8,128)(2,1)S(1)} %broadcast_select_fusion), kind=kOutput, calls=%fused_computation.11 | convolution fusion | flops 12582912 | bytes 2885632 | tf_op jit(solution)/shard_map/rl,rktd->lktd/dot_general | solution.py:172
  243.7 3.7 %maximum_maximum_fusion = bf16[2,768,2,128]{3,2,0,1:T(2,128)(2,1)} fusion(bf16[1,768,1,128]{3,2,0,1:T(2,128)(2,1)S(1)} %copy.125, bf16[1,768,1,128]{3,2,0,1:T(2,128)(2,1)S(1)} %copy.124, bf16[1,768,1,128]{3,2,0,1:T(2,128)(2,1)S(1)} %copy.123, bf16[1,768,1,128]{3,2,0,1:T(2,128)(2,1)S(1)} %copy.122), kind=kLoop, calls=%fused_computation.26 | loop fusion | flops 3145728 | bytes 1572864 | tf_op jit(solution)/shard_map/stack | solution.py:17
  247.4 26.7 %all-to-all-done.4 = bf16[2,768,8,128]{3,2,0,1:T(8,128)(2,1)} async-done(((bf16[2,768,8,128]{3,2,0,1:T(8,128)(2,1)}), bf16[2,768,8,128]{3,2,0,1:T(8,128)(2,1)}, u32[]{:S(2)}, u32[]{:S(2)}) %all-to-all-start.4) | async-done | bytes 3145760 | tf_op jit(solution)/shard_map/all_to_all | solution.py:17
  274.1 3.5 %all-to-all-start.7 = ((bf16[2,768,2,128]{3,2,0,1:T(2,128)(2,1)}), bf16[2,768,2,128]{3,2,0,1:T(2,128)(2,1)S(1)}, u32[]{:S(2)}, u32[]{:S(2)}) async-start(bf16[2,768,2,128]{3,2,0,1:T(2,128)(2,1)} %maximum_maximum_fusion), calls=%async_computation.7 | async-start | bytes 1572864 | tf_op jit(solution)/shard_map/all_to_all | solution.py:17
  277.6 2.1 fusion.18
  282.5 8.2 %all-to-all-done.7 = bf16[2,768,2,128]{3,2,0,1:T(2,128)(2,1)S(1)} async-done(((bf16[2,768,2,128]{3,2,0,1:T(2,128)(2,1)}), bf16[2,768,2,128]{3,2,0,1:T(2,128)(2,1)S(1)}, u32[]{:S(2)}, u32[]{:S(2)}) %all-to-all-start.7) | async-done | bytes 786464 | tf_op jit(solution)/shard_map/all_to_all | solution.py:17
  (76 shorter events, 21.8 us)
Async XLA Ops:
  0.6 6.7 %copy-start.12 = (bf16[192,32,128]{2,1,0:T(8,128)(2,1)S(1)}, bf16[192,32,128]{2,1,0:T(8,128)(2,1)}, u32[]{:S(2)}) copy-start(bf16[192,32,128]{2,1,0:T(8,128)(2,1)} %param.9) | copy-start | bytes 4718596
  3.0 17.5 %all-to-all-start = ((bf16[2,192,8,128]{3,1,0,2:T(8,128)(2,1)}), bf16[2,192,8,128]{3,1,0,2:T(8,128)(2,1)S(1)}, u32[]{:S(2)}, u32[]{:S(2)}) async-start(bf16[2,192,8,128]{3,1,0,2:T(8,128)(2,1)} %pad_maximum_fusion.6), calls=%async_computation | async-start | bytes 1572864 | tf_op jit(solution)/shard_map/all_to_all | solution.py:13
  20.5 0.9 copy-start.11
  21.4 42.1 %all-to-all-start.2 = ((bf16[2,192,32,128]{3,1,0,2:T(8,128)(2,1)}), bf16[2,192,32,128]{3,1,0,2:T(8,128)(2,1)S(1)}, u32[]{:S(2)}, u32[]{:S(2)}) async-start(bf16[2,192,32,128]{3,1,0,2:T(8,128)(2,1)} %pad_maximum_fusion.2), calls=%async_computation.2 | async-start | bytes 6291456 | tf_op jit(solution)/shard_map/all_to_all | solution.py:13
  27.4 0.7 copy-start.9
  27.5 44.6 %copy-start.8 = (bf16[6,2,128,128]{3,2,1,0:T(8,128)(2,1)}, bf16[6,2,128,128]{3,2,1,0:T(8,128)(2,1)S(1)}, u32[]{:S(2)}) copy-start(bf16[6,2,128,128]{3,2,1,0:T(8,128)(2,1)S(1)} %get-tuple-element.27) | copy-start | bytes 1179652
  63.5 39.1 %all-to-all-start.1 = ((bf16[32,2,128,128]{3,2,1,0:T(8,128)(2,1)}), bf16[32,2,128,128]{3,2,1,0:T(8,128)(2,1)}, u32[]{:S(2)}, u32[]{:S(2)}) async-start(bf16[32,2,128,128]{3,2,1,0:T(8,128)(2,1)} %copy.160), calls=%async_computation.1 | async-start | bytes 4194304 | tf_op jit(solution)/shard_map/all_to_all | solution.py:161
  102.6 51.2 %all-to-all-start.3 = ((bf16[32,2,128,128]{3,2,1,0:T(8,128)(2,1)}), bf16[32,2,128,128]{3,2,1,0:T(8,128)(2,1)}, u32[]{:S(2)}, u32[]{:S(2)}) async-start(bf16[32,2,128,128]{3,2,1,0:T(8,128)(2,1)} %copy.159), calls=%async_computation.3 | async-start | bytes 4194304 | tf_op jit(solution)/shard_map/all_to_all | solution.py:161
  113.2 5.9 %copy-start.10 = (bf16[6,2,128,128]{3,2,1,0:T(8,128)(2,1)S(1)}, bf16[6,2,128,128]{3,2,1,0:T(8,128)(2,1)}, u32[]{:S(2)}) copy-start(bf16[6,2,128,128]{3,2,1,0:T(8,128)(2,1)} %copy-done.9) | copy-start | bytes 1179652
  149.9 2.2 copy-start.2
  153.8 44.3 %all-to-all-start.5 = ((bf16[32,2,128,128]{3,2,1,0:T(8,128)(2,1)}), bf16[32,2,128,128]{3,2,1,0:T(8,128)(2,1)}, u32[]{:S(2)}, u32[]{:S(2)}) async-start(bf16[32,2,128,128]{3,2,1,0:T(8,128)(2,1)} %copy.116), calls=%async_computation.5 | async-start | bytes 4194304 | tf_op jit(solution)/shard_map/all_to_all | solution.py:171
  193.1 3.4 %copy-start = (f32[38,128,128]{2,1,0:T(8,128)}, f32[38,128,128]{2,1,0:T(8,128)S(1)}, u32[]{:S(2)}) copy-start(f32[38,128,128]{2,1,0:T(8,128)S(1)} %get-tuple-element.18) | copy-start | bytes 7471108
  193.1 3.4 %copy-start.3 = (bf16[768,512]{1,0:T(8,128)(2,1)}, bf16[768,512]{1,0:T(8,128)(2,1)S(1)}, u32[]{:S(2)}) copy-start(bf16[768,512]{1,0:T(8,128)(2,1)S(1)} %get-tuple-element.15) | copy-start | bytes 2359300
  193.1 3.4 %copy-start.5 = (bf16[768,512]{1,0:T(8,128)(2,1)}, bf16[768,512]{1,0:T(8,128)(2,1)S(1)}, u32[]{:S(2)}) copy-start(bf16[768,512]{1,0:T(8,128)(2,1)S(1)} %get-tuple-element.13) | copy-start | bytes 2359300
  198.1 32.8 %all-to-all-start.6 = ((bf16[32,2,128,128]{3,2,1,0:T(8,128)(2,1)}), bf16[32,2,128,128]{3,2,1,0:T(8,128)(2,1)}, u32[]{:S(2)}, u32[]{:S(2)}) async-start(bf16[32,2,128,128]{3,2,1,0:T(8,128)(2,1)} %copy.119), calls=%async_computation.6 | async-start | bytes 4194304 | tf_op jit(solution)/shard_map/all_to_all | solution.py:171
  207.2 1.1 copy-start.4
  230.9 43.2 %all-to-all-start.4 = ((bf16[2,768,8,128]{3,2,0,1:T(8,128)(2,1)}), bf16[2,768,8,128]{3,2,0,1:T(8,128)(2,1)}, u32[]{:S(2)}, u32[]{:S(2)}) async-start(bf16[2,768,8,128]{3,2,0,1:T(8,128)(2,1)} %pad_maximum_fusion.3), calls=%async_computation.4 | async-start | bytes 6291456 | tf_op jit(solution)/shard_map/all_to_all | solution.py:17
  235.8 3.0 %copy-start.6 = (f32[38,128,128]{2,1,0:T(8,128)S(1)}, f32[38,128,128]{2,1,0:T(8,128)}, u32[]{:S(2)}) copy-start(f32[38,128,128]{2,1,0:T(8,128)} %get-tuple-element.17) | copy-start | bytes 7471108
  239.0 3.8 %copy-start.7 = (f32[38,128,128]{2,1,0:T(8,128)S(1)}, f32[38,128,128]{2,1,0:T(8,128)}, u32[]{:S(2)}) copy-start(f32[38,128,128]{2,1,0:T(8,128)} %get-tuple-element.19) | copy-start | bytes 7471108
  239.1 3.8 %copy-start.1 = (f32[38,128,128]{2,1,0:T(8,128)S(1)}, f32[38,128,128]{2,1,0:T(8,128)}, u32[]{:S(2)}) copy-start(f32[38,128,128]{2,1,0:T(8,128)} %copy-done) | copy-start | bytes 7471108
  274.1 16.6 %all-to-all-start.7 = ((bf16[2,768,2,128]{3,2,0,1:T(2,128)(2,1)}), bf16[2,768,2,128]{3,2,0,1:T(2,128)(2,1)S(1)}, u32[]{:S(2)}, u32[]{:S(2)}) async-start(bf16[2,768,2,128]{3,2,0,1:T(2,128)(2,1)} %maximum_maximum_fusion), calls=%async_computation.7 | async-start | bytes 1572864 | tf_op jit(solution)/shard_map/all_to_all | solution.py:17

commit v3 on v2

--- a/solution.py
+++ b/solution.py
@@ -9,12 +9,33 @@
 TOPK = 8
 
 
+def exchange(x, part_axis, out_axis):
+    size = lax.axis_size("head")
+    here = lax.axis_index("head")
+    pieces = []
+    for k in range(size):
+        piece = lax.dynamic_index_in_dim(x, (here + k) % size, axis=part_axis, keepdims=False)
+        if k:
+            piece = lax.ppermute(piece, "head", [(i, (i + k) % size) for i in range(size)])
+        pieces.append(piece)
+    ordered = jnp.stack([pieces[(-s) % size] for s in range(size)], axis=out_axis)
+    return jnp.roll(ordered, here, axis=out_axis)
+
+
 def to_heads(*xs):
-    return lax.all_to_all(jnp.stack(xs), "head", split_axis=2, concat_axis=1, tiled=True)
+    size = lax.axis_size("head")
+    x = jnp.stack(xs)
+    n, tok, heads, d = x.shape
+    x = x.reshape(n, tok, size, heads // size, d)
+    return exchange(x, 2, 1).reshape(n, size * tok, heads // size, d)
 
 
 def from_heads(*xs):
-    both = lax.all_to_all(jnp.stack(xs), "head", split_axis=1, concat_axis=2, tiled=True)
+    size = lax.axis_size("head")
+    x = jnp.stack(xs)
+    n, run, part, d = x.shape
+    x = x.reshape(n, size, run // size, part, d)
+    both = exchange(x, 1, 2).reshape(n, run // size, size * part, d)
     return tuple(both[i] for i in range(len(xs)))
 
 

time: 295 us -> 274 us (0.929)
  waiting for transfers between devices: 123 us -> 87.8 us
  local copies, waits for them, and re-layouts: 35.5 us -> 59.9 us
  starting transfers between devices: 45.6 us -> 40.4 us
  other arithmetic: 25.4 us -> 20.5 us
    all_to_all x4 -> x0, waiting for transfers between devices: 75.8 us -> none  [the longest x2 41 us: to_heads(): lax.all_to_all(jnp.stack(xs), 'head', split_axis=2, concat_axis=1, tiled=...]
    ppermute x0 -> x12, waiting for transfers between devices: none -> 68.1 us  [exchange(): lax.ppermute(piece, 'head', [(i, (i + k) % size) for i in range(size)])]
    unnamed x28 -> x48, local copies, waits for them, and re-layouts: 3.22 us -> 31.1 us
    all_to_all x2, waiting for transfers between devices: 19.4 us -> 1.63 us  [on_device(): lax.all_to_all(remote, 'blk', split_axis=0, concat_axis=0, tiled=True)]
    all_to_all x4 -> x0, starting transfers between devices: 16.5 us -> none  [the longest x2 8.42 us: from_heads(): lax.all_to_all(jnp.stack(xs), 'head', split_axis=1, concat_axis=2, tiled=...]
    ppermute x0 -> x12, starting transfers between devices: none -> 11.6 us  [exchange(): lax.ppermute(piece, 'head', [(i, (i + k) % size) for i in range(size)])]
    another operation x6 -> x3, other arithmetic: 14.4 us -> 4.89 us  [the longest x2 5.88 us: from_heads(): jnp.stack(xs)]
    all_to_all x2, waiting for transfers between devices: 27.6 us -> 18.1 us  [on_device(): recv = lax.all_to_all(send, 'blk', split_axis=0, concat_axis=0, tiled=True)]
  transfers between devices with their start and end apart: 8 -> 16, of which waited for: 6 -> 10; matrix products, arithmetic and copies ran while one was open for 21% -> 26% of each run, Pallas kernels for 19% -> 20%
where the time goes in v3:
time: 274 us; the launch traced here: 273 us
  waiting for transfers between devices  87.8 us (32%)
  local copies, waits for them, and re-layouts  59.9 us (22%)
  Pallas kernels  54.8 us (20%)
  starting transfers between devices  40.4 us (15%)
  other arithmetic  20.5 us (7%)
  matrix products  8.34 us (3%)
    ppermute x12, waiting for transfers between devices, exchange(): lax.ppermute(piece, 'head', [(i, (i + k) % size) for i in range(size)])  68.1 us
    pallas_call x2, Pallas kernels, attend(): pl.pallas_call(attention_kernel, grid_spec=grid_spec, out_shape=out_shape...  54.8 us
    unnamed x48, local copies, waits for them, and re-layouts  31.1 us
    all_to_all x2, waiting for transfers between devices, on_device(): recv = lax.all_to_all(send, 'blk', split_axis=0, concat_axis=0, tiled=True)  18.1 us
    all_to_all x2, starting transfers between devices, on_device(): recv = lax.all_to_all(send, 'blk', split_axis=0, concat_axis=0, tiled=True)  14.5 us
    all_to_all x2, starting transfers between devices, on_device(): lax.all_to_all(remote, 'blk', split_axis=0, concat_axis=0, tiled=True)  14.2 us
    ppermute x12, starting transfers between devices, exchange(): lax.ppermute(piece, 'head', [(i, (i + k) % size) for i in range(size)])  11.6 us
    concatenate x2, other arithmetic, on_device(): table = jnp.concatenate([recv, kv_local[g]], axis=0)  6.81 us
  transfers between devices with their start and end apart: 16, of which 10 were waited for; matrix products, arithmetic and copies ran while one was open for 26% of the time, Pallas kernels for 20%

profile of v3, /device:TPU:0, one launch (start us, length us, event | category | flops | bytes accessed | tf_op | source)
XLA Modules:
  0.0 272.7 jit_solution(3121828551450333432)
XLA Ops:
  2.9 2.6 collective-permute-start
  10.7 5.3 %collective-permute-done.1 = bf16[2,192,2,128]{3,1,2,0:T(8,128)(2,1)S(1)} collective-permute-done((bf16[2,192,2,128]{3,1,2,0:T(8,128)(2,1)S(1)}, bf16[2,192,2,128]{3,1,2,0:T(8,128)(2,1)S(1)}, u32[]{:S(2)}, u32[]{:S(2)}) %collective-permute-start.1) | collective-permute-done | bytes 196640 | tf_op jit(solution)/shard_map/ppermute | solution.py:19
  18.7 2.2 copy.121
  20.9 9.6 %all-to-all-start = ((bf16[32,2,128,128]{3,2,1,0:T(8,128)(2,1)}), bf16[32,2,128,128]{3,2,1,0:T(8,128)(2,1)}, u32[]{:S(2)}, u32[]{:S(2)}) async-start(bf16[32,2,128,128]{3,2,1,0:T(8,128)(2,1)} %copy.121), calls=%async_computation | async-start | bytes 4194304 | tf_op jit(solution)/shard_map/all_to_all | solution.py:182
  32.0 2.7 collective-permute-start.4
  41.7 18.1 %all-to-all-done = bf16[32,2,128,128]{3,2,1,0:T(8,128)(2,1)} async-done(((bf16[32,2,128,128]{3,2,1,0:T(8,128)(2,1)}), bf16[32,2,128,128]{3,2,1,0:T(8,128)(2,1)}, u32[]{:S(2)}, u32[]{:S(2)}) %all-to-all-start) | async-done | bytes 2097184 | tf_op jit(solution)/shard_map/all_to_all | solution.py:182
  59.8 5.0 %all-to-all-start.1 = ((bf16[32,2,128,128]{3,2,1,0:T(8,128)(2,1)}), bf16[32,2,128,128]{3,2,1,0:T(8,128)(2,1)}, u32[]{:S(2)}, u32[]{:S(2)}) async-start(bf16[32,2,128,128]{3,2,1,0:T(8,128)(2,1)} %copy.120), calls=%async_computation.1 | async-start | bytes 4194304 | tf_op jit(solution)/shard_map/all_to_all | solution.py:182
  64.7 6.2 %collective-permute-done.3 = bf16[2,192,8,128]{3,2,1,0:T(8,128)(2,1)} collective-permute-done((bf16[2,192,8,128]{3,2,1,0:T(8,128)(2,1)}, bf16[2,192,8,128]{3,2,1,0:T(8,128)(2,1)}, u32[]{:S(2)}, u32[]{:S(2)}) %collective-permute-start.3) | collective-permute-done | bytes 786464 | tf_op jit(solution)/shard_map/ppermute | solution.py:19
  70.9 2.2 bitcast_dynamic-update-slice_fusion.12
  73.1 19.2 %collective-permute-done.4 = bf16[2,192,8,128]{3,2,1,0:T(8,128)(2,1)} collective-permute-done((bf16[2,192,8,128]{3,2,1,0:T(8,128)(2,1)}, bf16[2,192,8,128]{3,2,1,0:T(8,128)(2,1)}, u32[]{:S(2)}, u32[]{:S(2)}) %collective-permute-start.4) | collective-permute-done | bytes 786464 | tf_op jit(solution)/shard_map/ppermute | solution.py:19
  92.2 2.2 bitcast_dynamic-update-slice_fusion.10
  94.4 2.2 bitcast_dynamic-update-slice_fusion.8
  97.6 2.2 bitcast_dynamic-update-slice_fusion.13
  99.8 2.2 bitcast_dynamic-update-slice_fusion.11
  106.3 3.3 %reshape_reshape.7.refs_16_.refs_17_ = bf16[2,768,1024]{2,1,0:T(8,128)(2,1)} reshape(bf16[2,4,192,8,128]{4,3,2,1,0:T(8,128)(2,1)S(1)} %constant_dynamic-slice_fusion.5) | data formatting | bytes 6291456 | tf_op jit(solution)/shard_map/reshape;reshape | solution.py:176
  109.6 3.4 %pad_maximum_fusion.2.refs_0_.refs_1_.refs_2_.refs_3_.refs_4_.refs_5_.refs_6_.refs_7_.refs_8_.refs_9_.refs_10_.refs_11_.refs_12_.refs_13_.refs_14_.refs_15_ = bf16[38,2,128,128]{3,2,1,0:T(8,128)(2,1)} fusion(bf16[6,2,128,128]{3,2,1,0:T(8,128)(2,1)} %copy-done.8, bf16[32,2,128,128]{3,2,1,0:T(8,128)(2,1)} %all-to-all-done), kind=kLoop, calls=%fused_computation.14 | loop fusion | flops 1245184 | bytes 4980736 | tf_op jit(solution)/shard_map/concatenate | solution.py:183
  113.0 27.3 %shard_map.84 = (bf16[768,512]{1,0:T(8,128)(2,1)S(1)}, bf16[768,512]{1,0:T(8,128)(2,1)S(1)}, f32[38,128,128]{2,1,0:T(8,128)S(1)}, f32[38,128,128]{2,1,0:T(8,128)}) custom-call(s32[48]{0:T(128)S(1)} %reshape_squeeze.6.src_ref, s32[6]{0:T(128)S(1)} %add_multiply_fusion.base_ref, ...), custom_call_target="tpu_custom_call" | custom-call | tf_op jit(solution)/shard_map/pallas_call | solution.py:129
  140.4 2.2 fusion.1
  144.2 6.9 %all-to-all-start.2 = ((bf16[32,2,128,128]{3,2,1,0:T(8,128)(2,1)}), bf16[32,2,128,128]{3,2,1,0:T(8,128)(2,1)}, u32[]{:S(2)}, u32[]{:S(2)}) async-start(bf16[32,2,128,128]{3,2,1,0:T(8,128)(2,1)} %copy.80), calls=%async_computation.2 | async-start | bytes 4194304 | tf_op jit(solution)/shard_map/all_to_all | solution.py:192
  151.2 3.4 %pad_maximum_fusion.3.refs_0_.refs_1_.refs_2_.refs_3_.refs_4_.refs_5_.refs_6_.refs_7_.refs_8_.refs_9_.refs_10_.refs_11_.refs_12_.refs_13_.refs_14_.refs_15_ = bf16[38,2,128,128]{3,2,1,0:T(8,128)(2,1)} fusion(bf16[6,2,128,128]{3,2,1,0:T(8,128)(2,1)} %get-tuple-element.37, bf16[32,2,128,128]{3,2,1,0:T(8,128)(2,1)} %all-to-all-done.1), kind=kLoop, calls=%fused_computation.15 | loop fusion | flops 1245184 | bytes 4980736 | tf_op jit(solution)/shard_map/concatenate | solution.py:183
  154.6 27.4 %shard_map.85 = (bf16[768,512]{1,0:T(8,128)(2,1)S(1)}, bf16[768,512]{1,0:T(8,128)(2,1)S(1)}, f32[38,128,128]{2,1,0:T(8,128)S(1)}, f32[38,128,128]{2,1,0:T(8,128)}) custom-call(s32[48]{0:T(128)S(1)} %reshape_squeeze.7.src_ref, s32[6]{0:T(128)S(1)} %add_multiply_fusion.base_ref, ...), custom_call_target="tpu_custom_call" | custom-call | tf_op jit(solution)/shard_map/pallas_call | solution.py:129
  190.7 2.6 fusion
  196.9 8.0 %collective-permute-done.6 = bf16[2,192,8,128]{3,2,1,0:T(8,128)(2,1)S(1)} collective-permute-done((bf16[2,192,8,128]{3,2,1,0:T(8,128)(2,1)}, bf16[2,192,8,128]{3,2,1,0:T(8,128)(2,1)S(1)}, u32[]{:S(2)}, u32[]{:S(2)}) %collective-permute-start.6) | collective-permute-done | bytes 786464 | tf_op jit(solution)/shard_map/ppermute | solution.py:19
  205.9 19.1 %collective-permute-done.7 = bf16[2,192,8,128]{3,2,1,0:T(8,128)(2,1)} collective-permute-done((bf16[2,192,8,128]{3,2,1,0:T(8,128)(2,1)}, bf16[2,192,8,128]{3,2,1,0:T(8,128)(2,1)}, u32[]{:S(2)}, u32[]{:S(2)}) %collective-permute-start.7) | collective-permute-done | bytes 786464 | tf_op jit(solution)/shard_map/ppermute | solution.py:19
  225.0 2.2 bitcast_dynamic-update-slice_fusion.2
  227.2 7.2 %all-to-all-start.3 = ((bf16[32,2,128,128]{3,2,1,0:T(8,128)(2,1)}), bf16[32,2,128,128]{3,2,1,0:T(8,128)(2,1)}, u32[]{:S(2)}, u32[]{:S(2)}) async-start(bf16[32,2,128,128]{3,2,1,0:T(8,128)(2,1)} %copy.83), calls=%async_computation.3 | async-start | bytes 4194304 | tf_op jit(solution)/shard_map/all_to_all | solution.py:192
  236.5 2.2 bitcast_dynamic-update-slice_fusion.7
  244.0 4.1 %dynamic-slice_bitcast_fusion = (bf16[192,32,128]{2,1,0:T(8,128)(2,1)}, bf16[192,32,128]{2,1,0:T(8,128)(2,1)}) fusion(bf16[2,192,8,8,128]{4,3,2,1,0:T(8,128)(2,1)} %bitcast_dynamic-update-slice_fusion.1, s32[]{:T(128)S(6)} %add.172, s32[]{:T(128)S(6)} %select_n.163), kind=kLoop, calls=%fused_computation.20 | loop fusion | bytes 6291464 | tf_op jit(solution)/shard_map/squeeze | solution.py:39
  248.1 3.0 %fusion.4 = f32[6,2,128,128]{3,0,2,1:T(8,128)S(1)} fusion(bf16[32,2,128,128]{3,2,1,0:T(8,128)(2,1)} %all-to-all-done.2, bf16[2,32,6]{1,2,0:T(8,128)(2,1)S(1)} %broadcast_select_fusion), kind=kOutput, calls=%fused_computation.18 | convolution fusion | flops 12582912 | bytes 2885632 | tf_op jit(solution)/shard_map/rl,rktd->lktd/dot_general | solution.py:193
  252.9 2.8 %fusion.2 = f32[6,2,128,128]{3,0,2,1:T(8,128)S(1)} fusion(bf16[32,2,128,128]{3,2,1,0:T(8,128)(2,1)} %all-to-all-done.3, bf16[2,32,6]{1,2,0:T(8,128)(2,1)S(1)} %broadcast_select_fusion), kind=kOutput, calls=%fused_computation.16 | convolution fusion | flops 12582912 | bytes 2885632 | tf_op jit(solution)/shard_map/rl,rktd->lktd/dot_general | solution.py:193
  257.6 2.5 collective-permute-start.10
  261.2 7.8 %collective-permute-done.10 = bf16[2,192,2,128]{3,2,1,0:T(2,128)(2,1)S(1)} collective-permute-done((bf16[2,192,2,128]{3,2,1,0:T(2,128)(2,1)S(1)}, bf16[2,192,2,128]{3,2,1,0:T(2,128)(2,1)S(1)}, u32[]{:S(2)}, u32[]{:S(2)}) %collective-permute-start.10) | collective-permute-done | bytes 196640 | tf_op jit(solution)/shard_map/ppermute | solution.py:19
  (111 shorter events, 54.4 us)
Async XLA Ops:
  2.9 7.8 %collective-permute-start = (bf16[2,192,2,128]{3,1,2,0:T(8,128)(2,1)S(1)}, bf16[2,192,2,128]{3,1,2,0:T(8,128)(2,1)S(1)}, u32[]{:S(2)}, u32[]{:S(2)}) collective-permute-start(bf16[2,192,2,128]{3,1,2,0:T(8,128)(2,1)S(1)} %get-tuple-element.40), channel_id=1, source_target_pairs={{0,96},{32,0},{64,32},{96,64},{1,97},{33,1},{65,33},{97,65},{2,98}... | collective-permute-start | bytes 589832 | tf_op jit(solution)/shard_map/ppermute | solution.py:19
  5.5 10.5 %collective-permute-start.1 = (bf16[2,192,2,128]{3,1,2,0:T(8,128)(2,1)S(1)}, bf16[2,192,2,128]{3,1,2,0:T(8,128)(2,1)S(1)}, u32[]{:S(2)}, u32[]{:S(2)}) collective-permute-start(bf16[2,192,2,128]{3,1,2,0:T(8,128)(2,1)S(1)} %get-tuple-element.39), channel_id=1, source_target_pairs={{0,64},{32,96},{64,0},{96,32},{1,65},{33,97},{65,1},{97,33},{2,66}... | collective-permute-start | bytes 589832 | tf_op jit(solution)/shard_map/ppermute | solution.py:19
  6.2 9.9 %collective-permute-start.2 = (bf16[2,192,2,128]{3,1,2,0:T(8,128)(2,1)S(1)}, bf16[2,192,2,128]{3,1,2,0:T(8,128)(2,1)S(1)}, u32[]{:S(2)}, u32[]{:S(2)}) collective-permute-start(bf16[2,192,2,128]{3,1,2,0:T(8,128)(2,1)S(1)} %get-tuple-element.38), channel_id=1, source_target_pairs={{0,32},{32,64},{64,96},{96,0},{1,33},{33,65},{65,97},{97,1},{2,34}... | collective-permute-start | bytes 589832 | tf_op jit(solution)/shard_map/ppermute | solution.py:19
  17.2 0.7 copy-start.8
  20.9 9.6 %copy-start.4 = (bf16[192,32,128]{2,1,0:T(8,128)(2,1)S(1)}, bf16[192,32,128]{2,1,0:T(8,128)(2,1)}, u32[]{:S(2)}) copy-start(bf16[192,32,128]{2,1,0:T(8,128)(2,1)} %param.9) | copy-start | bytes 4718596
  20.9 9.6 %copy-start.5 = (bf16[192,32,128]{2,1,0:T(8,128)(2,1)S(1)}, bf16[192,32,128]{2,1,0:T(8,128)(2,1)}, u32[]{:S(2)}) copy-start(bf16[192,32,128]{2,1,0:T(8,128)(2,1)} %param.5) | copy-start | bytes 4718596
  20.9 38.9 %all-to-all-start = ((bf16[32,2,128,128]{3,2,1,0:T(8,128)(2,1)}), bf16[32,2,128,128]{3,2,1,0:T(8,128)(2,1)}, u32[]{:S(2)}, u32[]{:S(2)}) async-start(bf16[32,2,128,128]{3,2,1,0:T(8,128)(2,1)} %copy.121), calls=%async_computation | async-start | bytes 4194304 | tf_op jit(solution)/shard_map/all_to_all | solution.py:182
  32.0 38.9 %collective-permute-start.3 = (bf16[2,192,8,128]{3,2,1,0:T(8,128)(2,1)}, bf16[2,192,8,128]{3,2,1,0:T(8,128)(2,1)}, u32[]{:S(2)}, u32[]{:S(2)}) collective-permute-start(bf16[2,192,8,128]{3,2,1,0:T(8,128)(2,1)} %get-tuple-element.28), channel_id=1, source_target_pairs={{0,96},{32,0},{64,32},{96,64},{1,97},{33,1},{65,33},{97,65},{2,98}... | collective-permute-start | bytes 2359304 | tf_op jit(solution)/shard_map/ppermute | solution.py:19
  32.0 60.2 %collective-permute-start.4 = (bf16[2,192,8,128]{3,2,1,0:T(8,128)(2,1)}, bf16[2,192,8,128]{3,2,1,0:T(8,128)(2,1)}, u32[]{:S(2)}, u32[]{:S(2)}) collective-permute-start(bf16[2,192,8,128]{3,2,1,0:T(8,128)(2,1)} %get-tuple-element.29), channel_id=1, source_target_pairs={{0,64},{32,96},{64,0},{96,32},{1,65},{33,97},{65,1},{97,33},{2,66}... | collective-permute-start | bytes 2359304 | tf_op jit(solution)/shard_map/ppermute | solution.py:19
  34.8 59.7 %collective-permute-start.5 = (bf16[2,192,8,128]{3,2,1,0:T(8,128)(2,1)}, bf16[2,192,8,128]{3,2,1,0:T(8,128)(2,1)}, u32[]{:S(2)}, u32[]{:S(2)}) collective-permute-start(bf16[2,192,8,128]{3,2,1,0:T(8,128)(2,1)} %get-tuple-element.27), channel_id=1, source_target_pairs={{0,32},{32,64},{64,96},{96,0},{1,33},{33,65},{65,97},{97,1},{2,34}... | collective-permute-start | bytes 2359304 | tf_op jit(solution)/shard_map/ppermute | solution.py:19
  59.8 84.5 %all-to-all-start.1 = ((bf16[32,2,128,128]{3,2,1,0:T(8,128)(2,1)}), bf16[32,2,128,128]{3,2,1,0:T(8,128)(2,1)}, u32[]{:S(2)}, u32[]{:S(2)}) async-start(bf16[32,2,128,128]{3,2,1,0:T(8,128)(2,1)} %copy.120), calls=%async_computation.1 | async-start | bytes 4194304 | tf_op jit(solution)/shard_map/all_to_all | solution.py:182
  140.3 2.3 copy-start.2
  144.2 82.9 %all-to-all-start.2 = ((bf16[32,2,128,128]{3,2,1,0:T(8,128)(2,1)}), bf16[32,2,128,128]{3,2,1,0:T(8,128)(2,1)}, u32[]{:S(2)}, u32[]{:S(2)}) async-start(bf16[32,2,128,128]{3,2,1,0:T(8,128)(2,1)} %copy.80), calls=%async_computation.2 | async-start | bytes 4194304 | tf_op jit(solution)/shard_map/all_to_all | solution.py:192
  154.6 27.4 %copy-start.3 = (bf16[768,512]{1,0:T(8,128)(2,1)S(1)}, bf16[768,512]{1,0:T(8,128)(2,1)}, u32[]{:S(2)}) copy-start(bf16[768,512]{1,0:T(8,128)(2,1)} %copy-done.2) | copy-start | bytes 2359300
  182.0 1.9 copy-start
  185.1 1.7 copy-start.7
  188.3 16.6 %collective-permute-start.6 = (bf16[2,192,8,128]{3,2,1,0:T(8,128)(2,1)}, bf16[2,192,8,128]{3,2,1,0:T(8,128)(2,1)S(1)}, u32[]{:S(2)}, u32[]{:S(2)}) collective-permute-start(bf16[2,192,8,128]{3,2,1,0:T(8,128)(2,1)} %get-tuple-element.26), channel_id=1, source_target_pairs={{0,96},{32,0},{64,32},{96,64},{1,97},{33,1},{65,33},{97,65},{2,98}... | collective-permute-start | bytes 2359304 | tf_op jit(solution)/shard_map/ppermute | solution.py:19
  188.3 36.6 %collective-permute-start.7 = (bf16[2,192,8,128]{3,2,1,0:T(8,128)(2,1)}, bf16[2,192,8,128]{3,2,1,0:T(8,128)(2,1)}, u32[]{:S(2)}, u32[]{:S(2)}) collective-permute-start(bf16[2,192,8,128]{3,2,1,0:T(8,128)(2,1)} %get-tuple-element.25), channel_id=1, source_target_pairs={{0,64},{32,96},{64,0},{96,32},{1,65},{33,97},{65,1},{97,33},{2,66}... | collective-permute-start | bytes 2359304 | tf_op jit(solution)/shard_map/ppermute | solution.py:19
  190.5 43.9 %collective-permute-start.8 = (bf16[2,192,8,128]{3,2,1,0:T(8,128)(2,1)}, bf16[2,192,8,128]{3,2,1,0:T(8,128)(2,1)}, u32[]{:S(2)}, u32[]{:S(2)}) collective-permute-start(bf16[2,192,8,128]{3,2,1,0:T(8,128)(2,1)} %get-tuple-element.24), channel_id=1, source_target_pairs={{0,32},{32,64},{64,96},{96,0},{1,33},{33,65},{65,97},{97,1},{2,34}... | collective-permute-start | bytes 2359304 | tf_op jit(solution)/shard_map/ppermute | solution.py:19
  227.2 25.8 %all-to-all-start.3 = ((bf16[32,2,128,128]{3,2,1,0:T(8,128)(2,1)}), bf16[32,2,128,128]{3,2,1,0:T(8,128)(2,1)}, u32[]{:S(2)}, u32[]{:S(2)}) async-start(bf16[32,2,128,128]{3,2,1,0:T(8,128)(2,1)} %copy.83), calls=%async_computation.3 | async-start | bytes 4194304 | tf_op jit(solution)/shard_map/all_to_all | solution.py:192
  248.1 3.0 %copy-start.6 = (f32[38,128,128]{2,1,0:T(8,128)S(1)}, f32[38,128,128]{2,1,0:T(8,128)}, u32[]{:S(2)}) copy-start(f32[38,128,128]{2,1,0:T(8,128)} %get-tuple-element.17) | copy-start | bytes 7471108
  251.3 4.5 %copy-start.1 = (f32[38,128,128]{2,1,0:T(8,128)S(1)}, f32[38,128,128]{2,1,0:T(8,128)}, u32[]{:S(2)}) copy-start(f32[38,128,128]{2,1,0:T(8,128)} %copy-done) | copy-start | bytes 7471108
  257.4 3.5 %collective-permute-start.9 = (bf16[2,192,2,128]{3,2,1,0:T(2,128)(2,1)S(1)}, bf16[2,192,2,128]{3,2,1,0:T(2,128)(2,1)S(1)}, u32[]{:S(2)}, u32[]{:S(2)}) collective-permute-start(bf16[2,192,2,128]{3,2,1,0:T(2,128)(2,1)S(1)} %bitcast.174), channel_id=1, source_target_pairs={{0,96},{32,0},{64,32},{96,64},{1,97},{33,1},{65,33},{97,65},{2,98}... | collective-permute-start | bytes 589832 | tf_op jit(solution)/shard_map/ppermute | solution.py:19
  257.6 11.3 %collective-permute-start.10 = (bf16[2,192,2,128]{3,2,1,0:T(2,128)(2,1)S(1)}, bf16[2,192,2,128]{3,2,1,0:T(2,128)(2,1)S(1)}, u32[]{:S(2)}, u32[]{:S(2)}) collective-permute-start(bf16[2,192,2,128]{3,2,1,0:T(2,128)(2,1)S(1)} %bitcast.175), channel_id=1, source_target_pairs={{0,64},{32,96},{64,0},{96,32},{1,65},{33,97},{65,1},{97,33},{2,66}... | collective-permute-start | bytes 589832 | tf_op jit(solution)/shard_map/ppermute | solution.py:19
  260.4 9.5 %collective-permute-start.11 = (bf16[2,192,2,128]{3,2,1,0:T(2,128)(2,1)S(1)}, bf16[2,192,2,128]{3,2,1,0:T(2,128)(2,1)S(1)}, u32[]{:S(2)}, u32[]{:S(2)}) collective-permute-start(bf16[2,192,2,128]{3,2,1,0:T(2,128)(2,1)S(1)} %bitcast.176), channel_id=1, source_target_pairs={{0,32},{32,64},{64,96},{96,0},{1,33},{33,65},{65,97},{97,1},{2,34}... | collective-permute-start | bytes 589832 | tf_op jit(solution)/shard_map/ppermute | solution.py:19

commit v4 on v3

--- a/solution.py
+++ b/solution.py
@@ -174,7 +174,7 @@
     query_base = (rank * block_ids + block_range) * BLOCK_TOKENS
 
     qg2 = qg_h.reshape(2, run_len, head_count * head_width)
-    outs, query_grads, key_grads, value_grads = [], [], [], []
+    outs, query_grads, backs, locals_ = [], [], [], []
     for g in range(groups):
         send = jnp.einsum(
             "rb,bktd->rktd", pick_send[g], kv_local[g], preferred_element_type=jnp.float32
@@ -189,21 +189,27 @@
         acc = jnp.stack([dk_acc, dv_acc], axis=1)
         remote = acc[:peers].astype(jnp.bfloat16)
         local = acc[peers:].astype(jnp.bfloat16)
-        back = lax.all_to_all(remote, "blk", split_axis=0, concat_axis=0, tiled=True)
-        total = local.astype(jnp.float32) + jnp.einsum(
-            "rl,rktd->lktd", take_back[g], back, preferred_element_type=jnp.float32
+        backs.append(lax.all_to_all(remote, "blk", split_axis=0, concat_axis=0, tiled=True))
+        locals_.append(local)
+
+    def heads_layout(parts):
+        return jnp.concatenate(parts, axis=1).reshape(run_len, head_count, head_width)
+
+    def group_layout(parts):
+        return jnp.stack(parts, axis=2).reshape(run_len, groups, head_width)
+
+    attn_all, query_grad_all, backs[-1] = lax.optimization_barrier(
+        (heads_layout(outs), heads_layout(query_grads), backs[-1])
+    )
+    key_grads, value_grads = [], []
+    for g in range(groups):
+        total = locals_[g].astype(jnp.float32) + jnp.einsum(
+            "rl,rktd->lktd", take_back[g], backs[g], preferred_element_type=jnp.float32
         )
         total = total.astype(jnp.bfloat16)
         key_grads.append(total[:, 0])
         value_grads.append(total[:, 1])
-
-    def heads_layout(parts):
-        return jnp.concatenate(parts, axis=1).reshape(run_len, head_count, head_width)
-
-    def group_layout(parts):
-        return jnp.stack(parts, axis=2).reshape(run_len, groups, head_width)
-
-    attn_out, grad_queries = from_heads(heads_layout(outs), heads_layout(query_grads))
+    attn_out, grad_queries = from_heads(attn_all, query_grad_all)
     key_gradient, value_gradient = from_heads(group_layout(key_grads), group_layout(value_grads))
     return attn_out, grad_queries, key_gradient, value_gradient
 

time: 274 us -> 274 us (level)
  local copies, waits for them, and re-layouts: 59.9 us -> 41.3 us
  waiting for transfers between devices: 87.8 us -> 97.6 us
  other arithmetic: 20.5 us -> 25.8 us
    unnamed x48 -> x61, local copies, waits for them, and re-layouts: 31.1 us -> 17.4 us
    all_to_all x2, waiting for transfers between devices: 1.63 us -> 13.9 us  [on_device(): lax.all_to_all(remote, 'blk', split_axis=0, concat_axis=0, tiled=True)]
    unnamed x3 -> x6, other arithmetic: 2.96 us -> 5.92 us
  transfers between devices with their start and end apart: 16 -> 16, of which waited for: 10 -> 11; matrix products, arithmetic and copies ran while one was open for 26% -> 21% of each run, Pallas kernels for 20% -> 20%
where the time goes in v4:
time: 274 us; the launch traced here: 272 us
  waiting for transfers between devices  97.6 us (36%)
  Pallas kernels  54.9 us (20%)
  starting transfers between devices  43.1 us (16%)
  local copies, waits for them, and re-layouts  41.3 us (15%)
  other arithmetic  25.8 us (9%)
  matrix products  8.5 us (3%)
    ppermute x12, waiting for transfers between devices, exchange(): lax.ppermute(piece, 'head', [(i, (i + k) % size) for i in range(size)])  65.6 us
    pallas_call x2, Pallas kernels, attend(): pl.pallas_call(attention_kernel, grid_spec=grid_spec, out_shape=out_shape...  54.9 us
    all_to_all x2, waiting for transfers between devices, on_device(): recv = lax.all_to_all(send, 'blk', split_axis=0, concat_axis=0, tiled=True)  18.2 us
    unnamed x61, local copies, waits for them, and re-layouts  17.4 us
    all_to_all x2, starting transfers between devices, on_device(): lax.all_to_all(remote, 'blk', split_axis=0, concat_axis=0, tiled=True)  14.8 us
    all_to_all x2, starting transfers between devices, on_device(): recv = lax.all_to_all(send, 'blk', split_axis=0, concat_axis=0, tiled=True)  14.5 us
    all_to_all x2, waiting for transfers between devices, on_device(): lax.all_to_all(remote, 'blk', split_axis=0, concat_axis=0, tiled=True)  13.9 us
    ppermute x12, starting transfers between devices, exchange(): lax.ppermute(piece, 'head', [(i, (i + k) % size) for i in range(size)])  13.7 us
  transfers between devices with their start and end apart: 16, of which 11 were waited for; matrix products, arithmetic and copies ran while one was open for 21% of the time, Pallas kernels for 20%

profile of v4, /device:TPU:0, one launch (start us, length us, event | category | flops | bytes accessed | tf_op | source)
XLA Modules:
  0.0 272.5 jit_solution(15343609319478170919)
XLA Ops:
  2.9 2.6 collective-permute-start
  10.7 5.3 %collective-permute-done.1 = bf16[2,192,2,128]{3,1,2,0:T(8,128)(2,1)S(1)} collective-permute-done((bf16[2,192,2,128]{3,1,2,0:T(8,128)(2,1)S(1)}, bf16[2,192,2,128]{3,1,2,0:T(8,128)(2,1)S(1)}, u32[]{:S(2)}, u32[]{:S(2)}) %collective-permute-start.1) | collective-permute-done | bytes 196640 | tf_op jit(solution)/shard_map/ppermute | solution.py:19
  20.9 9.6 %all-to-all-start.1 = ((bf16[32,2,128,128]{3,2,1,0:T(8,128)(2,1)}), bf16[32,2,128,128]{3,2,1,0:T(8,128)(2,1)}, u32[]{:S(2)}, u32[]{:S(2)}) async-start(bf16[32,2,128,128]{3,2,1,0:T(8,128)(2,1)} %copy.120), calls=%async_computation.1 | async-start | bytes 4194304 | tf_op jit(solution)/shard_map/all_to_all | solution.py:182
  32.0 2.7 %collective-permute-start.4 = (bf16[2,192,8,128]{3,2,1,0:T(8,128)(2,1)}, bf16[2,192,8,128]{3,2,1,0:T(8,128)(2,1)}, u32[]{:S(2)}, u32[]{:S(2)}) collective-permute-start(bf16[2,192,8,128]{3,2,1,0:T(8,128)(2,1)} %get-tuple-element.35), channel_id=1, source_target_pairs={{0,64},{32,96},{64,0},{96,32},{1,65},{33,97},{65,1},{97,33},{2,66}... | collective-permute-start | bytes 2359304 | tf_op jit(solution)/shard_map/ppermute | solution.py:19
  39.4 2.2 copy.121
  41.6 18.2 %all-to-all-done.1 = bf16[32,2,128,128]{3,2,1,0:T(8,128)(2,1)} async-done(((bf16[32,2,128,128]{3,2,1,0:T(8,128)(2,1)}), bf16[32,2,128,128]{3,2,1,0:T(8,128)(2,1)}, u32[]{:S(2)}, u32[]{:S(2)}) %all-to-all-start.1) | async-done | bytes 2097184 | tf_op jit(solution)/shard_map/all_to_all | solution.py:182
  59.8 4.9 %all-to-all-start = ((bf16[32,2,128,128]{3,2,1,0:T(8,128)(2,1)}), bf16[32,2,128,128]{3,2,1,0:T(8,128)(2,1)}, u32[]{:S(2)}, u32[]{:S(2)}) async-start(bf16[32,2,128,128]{3,2,1,0:T(8,128)(2,1)} %copy.121), calls=%async_computation | async-start | bytes 4194304 | tf_op jit(solution)/shard_map/all_to_all | solution.py:182
  64.7 6.2 %collective-permute-done.3 = bf16[2,192,8,128]{3,2,1,0:T(8,128)(2,1)} collective-permute-done((bf16[2,192,8,128]{3,2,1,0:T(8,128)(2,1)}, bf16[2,192,8,128]{3,2,1,0:T(8,128)(2,1)}, u32[]{:S(2)}, u32[]{:S(2)}) %collective-permute-start.3) | collective-permute-done | bytes 786464 | tf_op jit(solution)/shard_map/ppermute | solution.py:19
  70.9 2.2 bitcast_dynamic-update-slice_fusion.10
  73.1 19.2 %collective-permute-done.4 = bf16[2,192,8,128]{3,2,1,0:T(8,128)(2,1)} collective-permute-done((bf16[2,192,8,128]{3,2,1,0:T(8,128)(2,1)}, bf16[2,192,8,128]{3,2,1,0:T(8,128)(2,1)}, u32[]{:S(2)}, u32[]{:S(2)}) %collective-permute-start.4) | collective-permute-done | bytes 786464 | tf_op jit(solution)/shard_map/ppermute | solution.py:19
  92.2 2.2 bitcast_dynamic-update-slice_fusion.8
  97.6 2.2 bitcast_dynamic-update-slice_fusion.11
  99.8 2.2 bitcast_dynamic-update-slice_fusion.9
  106.2 3.4 %reshape_reshape.7.refs_16_.refs_17_ = bf16[2,768,1024]{2,1,0:T(8,128)(2,1)} reshape(bf16[2,4,192,8,128]{4,3,2,1,0:T(8,128)(2,1)S(1)} %constant_dynamic-slice_fusion.6) | data formatting | bytes 6291456 | tf_op jit(solution)/shard_map/reshape;reshape | solution.py:176
  109.6 3.4 %pad_maximum_fusion.2.refs_0_.refs_1_.refs_2_.refs_3_.refs_4_.refs_5_.refs_6_.refs_7_.refs_8_.refs_9_.refs_10_.refs_11_.refs_12_.refs_13_.refs_14_.refs_15_ = bf16[38,2,128,128]{3,2,1,0:T(8,128)(2,1)} fusion(bf16[6,2,128,128]{3,2,1,0:T(8,128)(2,1)} %copy-done.12, bf16[32,2,128,128]{3,2,1,0:T(8,128)(2,1)} %all-to-all-done.1), kind=kLoop, calls=%fused_computation.22 | loop fusion | flops 1245184 | bytes 4980736 | tf_op jit(solution)/shard_map/concatenate | solution.py:183
  113.0 27.5 %shard_map.85 = (bf16[768,512]{1,0:T(8,128)(2,1)S(1)}, bf16[768,512]{1,0:T(8,128)(2,1)S(1)}, f32[38,128,128]{2,1,0:T(8,128)S(1)}, f32[38,128,128]{2,1,0:T(8,128)}) custom-call(s32[48]{0:T(128)S(1)} %reshape_squeeze.7.src_ref, s32[6]{0:T(128)S(1)} %add_multiply_fusion.base_ref, ...), custom_call_target="tpu_custom_call" | custom-call | tf_op jit(solution)/shard_map/pallas_call | solution.py:129
  140.5 2.4 maximum_convert_fusion
  144.7 6.6 %all-to-all-start.2 = ((bf16[32,2,128,128]{3,2,1,0:T(8,128)(2,1)}), bf16[32,2,128,128]{3,2,1,0:T(8,128)(2,1)}, u32[]{:S(2)}, u32[]{:S(2)}) async-start(bf16[32,2,128,128]{3,2,1,0:T(8,128)(2,1)} %copy.80), calls=%async_computation.2 | async-start | bytes 4194304 | tf_op jit(solution)/shard_map/all_to_all | solution.py:192
  151.5 3.4 %pad_maximum_fusion.1.refs_0_.refs_1_.refs_2_.refs_3_.refs_4_.refs_5_.refs_6_.refs_7_.refs_8_.refs_9_.refs_10_.refs_11_.refs_12_.refs_13_.refs_14_.refs_15_ = bf16[38,2,128,128]{3,2,1,0:T(8,128)(2,1)} fusion(bf16[6,2,128,128]{3,2,1,0:T(8,128)(2,1)} %get-tuple-element.42, bf16[32,2,128,128]{3,2,1,0:T(8,128)(2,1)} %all-to-all-done), kind=kLoop, calls=%fused_computation.21 | loop fusion | flops 1245184 | bytes 4980736 | tf_op jit(solution)/shard_map/concatenate | solution.py:183
  154.9 27.4 %shard_map.84 = (bf16[768,512]{1,0:T(8,128)(2,1)S(1)}, bf16[768,512]{1,0:T(8,128)(2,1)S(1)}, f32[38,128,128]{2,1,0:T(8,128)S(1)}, f32[38,128,128]{2,1,0:T(8,128)}) custom-call(s32[48]{0:T(128)S(1)} %reshape_squeeze.6.src_ref, s32[6]{0:T(128)S(1)} %add_multiply_fusion.base_ref, ...), custom_call_target="tpu_custom_call" | custom-call | tf_op jit(solution)/shard_map/pallas_call | solution.py:129
  182.4 3.4 %fusion = bf16[32,2,128,128]{3,2,0,1:T(8,128)(2,1)S(1)} fusion(f32[38,1,128,128]{3,2,0,1:T(8,128)} %bitcast.168, f32[38,1,128,128]{3,2,0,1:T(8,128)S(1)} %bitcast.150), kind=kLoop, calls=%fused_computation.18 | loop fusion | flops 1048576 | bytes 7077888 | tf_op jit(solution)/shard_map/convert.2
  187.4 8.2 %all-to-all-start.3 = ((bf16[32,2,128,128]{3,2,1,0:T(8,128)(2,1)}), bf16[32,2,128,128]{3,2,1,0:T(8,128)(2,1)}, u32[]{:S(2)}, u32[]{:S(2)}) async-start(bf16[32,2,128,128]{3,2,1,0:T(8,128)(2,1)} %copy.81), calls=%async_computation.3 | async-start | bytes 4194304 | tf_op jit(solution)/shard_map/all_to_all | solution.py:192
  195.6 2.6 maximum_bitcast_fusion
  202.0 13.9 %all-to-all-done.3 = bf16[32,2,128,128]{3,2,1,0:T(8,128)(2,1)} async-done(((bf16[32,2,128,128]{3,2,1,0:T(8,128)(2,1)}), bf16[32,2,128,128]{3,2,1,0:T(8,128)(2,1)}, u32[]{:S(2)}, u32[]{:S(2)}) %all-to-all-start.3) | async-done | bytes 2097184 | tf_op jit(solution)/shard_map/all_to_all | solution.py:192
  215.8 3.0 %fusion.3 = f32[6,2,128,128]{3,0,2,1:T(8,128)S(1)} fusion(bf16[32,2,128,128]{3,2,1,0:T(8,128)(2,1)} %all-to-all-done.3, bf16[2,32,6]{1,2,0:T(8,128)(2,1)S(1)} %broadcast_select_fusion), kind=kOutput, calls=%fused_computation.25 | convolution fusion | flops 12582912 | bytes 2885632 | tf_op jit(solution)/shard_map/rl,rktd->lktd/dot_general | solution.py:206
  220.0 3.0 %fusion.1 = f32[6,2,128,128]{3,0,2,1:T(8,128)S(1)} fusion(bf16[32,2,128,128]{3,2,1,0:T(8,128)(2,1)} %all-to-all-done.2, bf16[2,32,6]{1,2,0:T(8,128)(2,1)S(1)} %broadcast_select_fusion), kind=kOutput, calls=%fused_computation.23 | convolution fusion | flops 12582912 | bytes 2885632 | tf_op jit(solution)/shard_map/rl,rktd->lktd/dot_general | solution.py:206
  224.8 2.9 %collective-permute-start.6 = (bf16[2,192,8,128]{3,2,1,0:T(8,128)(2,1)S(1)}, bf16[2,192,8,128]{3,2,1,0:T(8,128)(2,1)S(1)}, u32[]{:S(2)}, u32[]{:S(2)}) collective-permute-start(bf16[2,192,8,128]{3,2,1,0:T(8,128)(2,1)S(1)} %copy-done.14), channel_id=1, source_target_pairs={{0,96},{32,0},{64,32},{96,64},{1,97},{33,1},{65,33},{97,65},{2,98}... | collective-permute-start | bytes 2359304 | tf_op jit(solution)/shard_map/ppermute | solution.py:19
  227.7 3.3 %collective-permute-start.7 = (bf16[2,192,8,128]{3,2,1,0:T(8,128)(2,1)S(1)}, bf16[2,192,8,128]{3,2,1,0:T(8,128)(2,1)S(1)}, u32[]{:S(2)}, u32[]{:S(2)}) collective-permute-start(bf16[2,192,8,128]{3,2,1,0:T(8,128)(2,1)S(1)} %copy-done.13), channel_id=1, source_target_pairs={{0,64},{32,96},{64,0},{96,32},{1,65},{33,97},{65,1},{97,33},{2,66}... | collective-permute-start | bytes 2359304 | tf_op jit(solution)/shard_map/ppermute | solution.py:19
  233.5 3.1 %collective-permute-done.11 = bf16[2,192,2,128]{3,2,1,0:T(2,128)(2,1)S(1)} collective-permute-done((bf16[2,192,2,128]{3,2,1,0:T(2,128)(2,1)S(1)}, bf16[2,192,2,128]{3,2,1,0:T(2,128)(2,1)S(1)}, u32[]{:S(2)}, u32[]{:S(2)}) %collective-permute-start.11) | collective-permute-done | bytes 196640 | tf_op jit(solution)/shard_map/ppermute | solution.py:19
  239.5 10.5 %collective-permute-done.6 = bf16[2,192,8,128]{3,2,1,0:T(8,128)(2,1)S(1)} collective-permute-done((bf16[2,192,8,128]{3,2,1,0:T(8,128)(2,1)S(1)}, bf16[2,192,8,128]{3,2,1,0:T(8,128)(2,1)S(1)}, u32[]{:S(2)}, u32[]{:S(2)}) %collective-permute-start.6) | collective-permute-done | bytes 786464 | tf_op jit(solution)/shard_map/ppermute | solution.py:19
  250.2 16.7 %collective-permute-done.7 = bf16[2,192,8,128]{3,2,1,0:T(8,128)(2,1)S(1)} collective-permute-done((bf16[2,192,8,128]{3,2,1,0:T(8,128)(2,1)S(1)}, bf16[2,192,8,128]{3,2,1,0:T(8,128)(2,1)S(1)}, u32[]{:S(2)}, u32[]{:S(2)}) %collective-permute-start.7) | collective-permute-done | bytes 786464 | tf_op jit(solution)/shard_map/ppermute | solution.py:19
  270.0 2.4 dynamic-slice_bitcast_fusion
  (127 shorter events, 44.5 us)
Async XLA Ops:
  2.9 7.8 %collective-permute-start = (bf16[2,192,2,128]{3,1,2,0:T(8,128)(2,1)S(1)}, bf16[2,192,2,128]{3,1,2,0:T(8,128)(2,1)S(1)}, u32[]{:S(2)}, u32[]{:S(2)}) collective-permute-start(bf16[2,192,2,128]{3,1,2,0:T(8,128)(2,1)S(1)} %get-tuple-element.46), channel_id=1, source_target_pairs={{0,96},{32,0},{64,32},{96,64},{1,97},{33,1},{65,33},{97,65},{2,98}... | collective-permute-start | bytes 589832 | tf_op jit(solution)/shard_map/ppermute | solution.py:19
  5.5 10.5 %collective-permute-start.1 = (bf16[2,192,2,128]{3,1,2,0:T(8,128)(2,1)S(1)}, bf16[2,192,2,128]{3,1,2,0:T(8,128)(2,1)S(1)}, u32[]{:S(2)}, u32[]{:S(2)}) collective-permute-start(bf16[2,192,2,128]{3,1,2,0:T(8,128)(2,1)S(1)} %get-tuple-element.45), channel_id=1, source_target_pairs={{0,64},{32,96},{64,0},{96,32},{1,65},{33,97},{65,1},{97,33},{2,66}... | collective-permute-start | bytes 589832 | tf_op jit(solution)/shard_map/ppermute | solution.py:19
  6.2 9.9 %collective-permute-start.2 = (bf16[2,192,2,128]{3,1,2,0:T(8,128)(2,1)S(1)}, bf16[2,192,2,128]{3,1,2,0:T(8,128)(2,1)S(1)}, u32[]{:S(2)}, u32[]{:S(2)}) collective-permute-start(bf16[2,192,2,128]{3,1,2,0:T(8,128)(2,1)S(1)} %get-tuple-element.44), channel_id=1, source_target_pairs={{0,32},{32,64},{64,96},{96,0},{1,33},{33,65},{65,97},{97,1},{2,34}... | collective-permute-start | bytes 589832 | tf_op jit(solution)/shard_map/ppermute | solution.py:19
  20.9 9.6 %copy-start.9 = (bf16[192,32,128]{2,1,0:T(8,128)(2,1)S(1)}, bf16[192,32,128]{2,1,0:T(8,128)(2,1)}, u32[]{:S(2)}) copy-start(bf16[192,32,128]{2,1,0:T(8,128)(2,1)} %param.9) | copy-start | bytes 4718596
  20.9 9.6 %copy-start.10 = (bf16[192,32,128]{2,1,0:T(8,128)(2,1)S(1)}, bf16[192,32,128]{2,1,0:T(8,128)(2,1)}, u32[]{:S(2)}) copy-start(bf16[192,32,128]{2,1,0:T(8,128)(2,1)} %param.5) | copy-start | bytes 4718596
  20.9 38.9 %all-to-all-start.1 = ((bf16[32,2,128,128]{3,2,1,0:T(8,128)(2,1)}), bf16[32,2,128,128]{3,2,1,0:T(8,128)(2,1)}, u32[]{:S(2)}, u32[]{:S(2)}) async-start(bf16[32,2,128,128]{3,2,1,0:T(8,128)(2,1)} %copy.120), calls=%async_computation.1 | async-start | bytes 4194304 | tf_op jit(solution)/shard_map/all_to_all | solution.py:182
  32.0 38.9 %collective-permute-start.3 = (bf16[2,192,8,128]{3,2,1,0:T(8,128)(2,1)}, bf16[2,192,8,128]{3,2,1,0:T(8,128)(2,1)}, u32[]{:S(2)}, u32[]{:S(2)}) collective-permute-start(bf16[2,192,8,128]{3,2,1,0:T(8,128)(2,1)} %get-tuple-element.34), channel_id=1, source_target_pairs={{0,96},{32,0},{64,32},{96,64},{1,97},{33,1},{65,33},{97,65},{2,98}... | collective-permute-start | bytes 2359304 | tf_op jit(solution)/shard_map/ppermute | solution.py:19
  32.0 60.2 %collective-permute-start.4 = (bf16[2,192,8,128]{3,2,1,0:T(8,128)(2,1)}, bf16[2,192,8,128]{3,2,1,0:T(8,128)(2,1)}, u32[]{:S(2)}, u32[]{:S(2)}) collective-permute-start(bf16[2,192,8,128]{3,2,1,0:T(8,128)(2,1)} %get-tuple-element.35), channel_id=1, source_target_pairs={{0,64},{32,96},{64,0},{96,32},{1,65},{33,97},{65,1},{97,33},{2,66}... | collective-permute-start | bytes 2359304 | tf_op jit(solution)/shard_map/ppermute | solution.py:19
  34.7 59.7 %collective-permute-start.5 = (bf16[2,192,8,128]{3,2,1,0:T(8,128)(2,1)}, bf16[2,192,8,128]{3,2,1,0:T(8,128)(2,1)}, u32[]{:S(2)}, u32[]{:S(2)}) collective-permute-start(bf16[2,192,8,128]{3,2,1,0:T(8,128)(2,1)} %get-tuple-element.33), channel_id=1, source_target_pairs={{0,32},{32,64},{64,96},{96,0},{1,33},{33,65},{65,97},{97,1},{2,34}... | collective-permute-start | bytes 2359304 | tf_op jit(solution)/shard_map/ppermute | solution.py:19
  59.8 85.0 %all-to-all-start = ((bf16[32,2,128,128]{3,2,1,0:T(8,128)(2,1)}), bf16[32,2,128,128]{3,2,1,0:T(8,128)(2,1)}, u32[]{:S(2)}, u32[]{:S(2)}) async-start(bf16[32,2,128,128]{3,2,1,0:T(8,128)(2,1)} %copy.121), calls=%async_computation | async-start | bytes 4194304 | tf_op jit(solution)/shard_map/all_to_all | solution.py:182
  140.5 2.4 copy-start.2
  144.7 42.6 %all-to-all-start.2 = ((bf16[32,2,128,128]{3,2,1,0:T(8,128)(2,1)}), bf16[32,2,128,128]{3,2,1,0:T(8,128)(2,1)}, u32[]{:S(2)}, u32[]{:S(2)}) async-start(bf16[32,2,128,128]{3,2,1,0:T(8,128)(2,1)} %copy.80), calls=%async_computation.2 | async-start | bytes 4194304 | tf_op jit(solution)/shard_map/all_to_all | solution.py:192
  182.4 3.4 %copy-start = (f32[38,128,128]{2,1,0:T(8,128)}, f32[38,128,128]{2,1,0:T(8,128)S(1)}, u32[]{:S(2)}) copy-start(f32[38,128,128]{2,1,0:T(8,128)S(1)} %get-tuple-element.23) | copy-start | bytes 7471108
  182.4 3.4 %copy-start.3 = (bf16[768,512]{1,0:T(8,128)(2,1)}, bf16[768,512]{1,0:T(8,128)(2,1)S(1)}, u32[]{:S(2)}) copy-start(bf16[768,512]{1,0:T(8,128)(2,1)S(1)} %get-tuple-element.15) | copy-start | bytes 2359300
  182.4 3.4 %copy-start.4 = (bf16[768,512]{1,0:T(8,128)(2,1)}, bf16[768,512]{1,0:T(8,128)(2,1)S(1)}, u32[]{:S(2)}) copy-start(bf16[768,512]{1,0:T(8,128)(2,1)S(1)} %get-tuple-element.17) | copy-start | bytes 2359300
  187.4 28.4 %all-to-all-start.3 = ((bf16[32,2,128,128]{3,2,1,0:T(8,128)(2,1)}), bf16[32,2,128,128]{3,2,1,0:T(8,128)(2,1)}, u32[]{:S(2)}, u32[]{:S(2)}) async-start(bf16[32,2,128,128]{3,2,1,0:T(8,128)(2,1)} %copy.81), calls=%async_computation.3 | async-start | bytes 4194304 | tf_op jit(solution)/shard_map/all_to_all | solution.py:192
  198.7 1.5 copy-start.5
  199.1 1.5 copy-start.7
  215.8 3.0 %copy-start.1 = (f32[38,128,128]{2,1,0:T(8,128)S(1)}, f32[38,128,128]{2,1,0:T(8,128)}, u32[]{:S(2)}) copy-start(f32[38,128,128]{2,1,0:T(8,128)} %copy-done) | copy-start | bytes 7471108
  220.0 3.0 %copy-start.11 = (f32[38,128,128]{2,1,0:T(8,128)S(1)}, f32[38,128,128]{2,1,0:T(8,128)}, u32[]{:S(2)}) copy-start(f32[38,128,128]{2,1,0:T(8,128)} %get-tuple-element.20) | copy-start | bytes 7471108
  223.0 27.0 %slice-start = ((s8[6291456]{0:T(1024)(128)(4,1)}), s8[4194304]{0:T(1024)(128)(4,1)S(1)}, s32[]{:S(2)}) async-start(s8[6291456]{0:T(1024)(128)(4,1)} %bitcast.173), calls=%async_computation.4 | async-start | bytes 8388608
  223.2 1.6 copy-start.14
  223.2 4.5 %copy-start.13 = (bf16[2,192,8,128]{3,2,1,0:T(8,128)(2,1)S(1)}, bf16[2,192,8,128]{3,2,1,0:T(8,128)(2,1)}, u32[]{:S(2)}) copy-start(bf16[2,192,8,128]{3,2,1,0:T(8,128)(2,1)} %get-tuple-element.32) | copy-start | bytes 2359300
  223.2 26.7 %slice-start.1 = ((s8[6291456]{0:T(1024)(128)(4,1)}), s8[2097152]{0:T(1024)(128)(4,1)S(1)}, s32[]{:S(2)}) async-start(s8[6291456]{0:T(1024)(128)(4,1)} %bitcast.173), calls=%async_computation.5 | async-start | bytes 4194304
  223.6 7.6 %collective-permute-start.9 = (bf16[2,192,2,128]{3,2,1,0:T(2,128)(2,1)S(1)}, bf16[2,192,2,128]{3,2,1,0:T(2,128)(2,1)S(1)}, u32[]{:S(2)}, u32[]{:S(2)}) collective-permute-start(bf16[2,192,2,128]{3,2,1,0:T(2,128)(2,1)S(1)} %bitcast.185), channel_id=1, source_target_pairs={{0,96},{32,0},{64,32},{96,64},{1,97},{33,1},{65,33},{97,65},{2,98}... | collective-permute-start | bytes 589832 | tf_op jit(solution)/shard_map/ppermute | solution.py:19
  223.9 9.3 %collective-permute-start.10 = (bf16[2,192,2,128]{3,2,1,0:T(2,128)(2,1)S(1)}, bf16[2,192,2,128]{3,2,1,0:T(2,128)(2,1)S(1)}, u32[]{:S(2)}, u32[]{:S(2)}) collective-permute-start(bf16[2,192,2,128]{3,2,1,0:T(2,128)(2,1)S(1)} %bitcast.183), channel_id=1, source_target_pairs={{0,64},{32,96},{64,0},{96,32},{1,65},{33,97},{65,1},{97,33},{2,66}... | collective-permute-start | bytes 589832 | tf_op jit(solution)/shard_map/ppermute | solution.py:19
  224.4 12.2 %collective-permute-start.11 = (bf16[2,192,2,128]{3,2,1,0:T(2,128)(2,1)S(1)}, bf16[2,192,2,128]{3,2,1,0:T(2,128)(2,1)S(1)}, u32[]{:S(2)}, u32[]{:S(2)}) collective-permute-start(bf16[2,192,2,128]{3,2,1,0:T(2,128)(2,1)S(1)} %bitcast.184), channel_id=1, source_target_pairs={{0,32},{32,64},{64,96},{96,0},{1,33},{33,65},{65,97},{97,1},{2,34}... | collective-permute-start | bytes 589832 | tf_op jit(solution)/shard_map/ppermute | solution.py:19
  224.8 25.2 %collective-permute-start.6 = (bf16[2,192,8,128]{3,2,1,0:T(8,128)(2,1)S(1)}, bf16[2,192,8,128]{3,2,1,0:T(8,128)(2,1)S(1)}, u32[]{:S(2)}, u32[]{:S(2)}) collective-permute-start(bf16[2,192,8,128]{3,2,1,0:T(8,128)(2,1)S(1)} %copy-done.14), channel_id=1, source_target_pairs={{0,96},{32,0},{64,32},{96,64},{1,97},{33,1},{65,33},{97,65},{2,98}... | collective-permute-start | bytes 2359304 | tf_op jit(solution)/shard_map/ppermute | solution.py:19
  227.7 39.2 %collective-permute-start.7 = (bf16[2,192,8,128]{3,2,1,0:T(8,128)(2,1)S(1)}, bf16[2,192,8,128]{3,2,1,0:T(8,128)(2,1)S(1)}, u32[]{:S(2)}, u32[]{:S(2)}) collective-permute-start(bf16[2,192,8,128]{3,2,1,0:T(8,128)(2,1)S(1)} %copy-done.13), channel_id=1, source_target_pairs={{0,64},{32,96},{64,0},{96,32},{1,65},{33,97},{65,1},{97,33},{2,66}... | collective-permute-start | bytes 2359304 | tf_op jit(solution)/shard_map/ppermute | solution.py:19
  231.3 37.3 %collective-permute-start.8 = (bf16[2,192,8,128]{3,2,1,0:T(8,128)(2,1)S(1)}, bf16[2,192,8,128]{3,2,1,0:T(8,128)(2,1)S(1)}, u32[]{:S(2)}, u32[]{:S(2)}) collective-permute-start(bf16[2,192,8,128]{3,2,1,0:T(8,128)(2,1)S(1)} %get-tuple-element.30), channel_id=1, source_target_pairs={{0,32},{32,64},{64,96},{96,0},{1,33},{33,65},{65,97},{97,1},{2,34}... | collective-permute-start | bytes 2359304 | tf_op jit(solution)/shard_map/ppermute | solution.py:19
  239.5 29.4 %copy-start.6 = (bf16[96,8,8,128]{3,2,1,0:T(8,128)(2,1)S(1)}, bf16[96,8,8,128]{3,2,1,0:T(8,128)(2,1)}, u32[]{:S(2)}) copy-start(bf16[96,8,8,128]{3,2,1,0:T(8,128)(2,1)} %copy-done.5) | copy-start | bytes 4718596
  239.5 29.4 %copy-start.8 = (bf16[96,8,8,128]{3,2,1,0:T(8,128)(2,1)S(1)}, bf16[96,8,8,128]{3,2,1,0:T(8,128)(2,1)}, u32[]{:S(2)}) copy-start(bf16[96,8,8,128]{3,2,1,0:T(8,128)(2,1)} %copy-done.7) | copy-start | bytes 4718596
  (1 other events, 0.7 us)

commit v5 on v4

--- a/solution.py
+++ b/solution.py
@@ -39,11 +39,11 @@
     return tuple(both[i] for i in range(len(xs)))
 
 
-def attention_kernel(src_ref, base_ref, *refs):
+def attention_kernel(src_ref, base_ref, peer_ref, *refs):
     k_refs = refs[:TOPK]
     v_refs = refs[TOPK:2 * TOPK]
-    q_ref, do_ref, kpos_ref = refs[2 * TOPK:2 * TOPK + 3]
-    o_ref, dq_ref, dk_ref, dv_ref = refs[2 * TOPK + 3:]
+    q_lo, q_hi, do_lo, do_hi, kpos_ref = refs[2 * TOPK:2 * TOPK + 5]
+    o_ref, dq_ref, dk_ref, dv_ref = refs[2 * TOPK + 5:]
     b = pl.program_id(0)
 
     @pl.when(b == 0)
@@ -52,7 +52,7 @@
         dv_ref[...] = jnp.zeros_like(dv_ref)
 
     head_width = k_refs[0].shape[-1]
-    group_width = q_ref.shape[-1] // head_width
+    group_width = q_lo.shape[-1] // head_width
     scale = head_width ** (-0.5)
     keys = jnp.concatenate([r[...] for r in k_refs], axis=0)
     values = jnp.concatenate([r[...] for r in v_refs], axis=0)
@@ -64,8 +64,8 @@
     dv = None
     for j in range(group_width):
         cols = slice(j * head_width, (j + 1) * head_width)
-        qj = q_ref[:, cols]
-        gj = do_ref[:, cols]
+        qj = jnp.concatenate([q_lo[:, cols], q_hi[:, cols]], axis=0)
+        gj = jnp.concatenate([do_lo[:, cols], do_hi[:, cols]], axis=0)
         s = lax.dot_general(qj, keys, nt, preferred_element_type=jnp.float32) * scale
         s = jnp.where(allowed, s, -jnp.inf)
         m = jnp.max(s, axis=-1, keepdims=True)
@@ -91,28 +91,36 @@
         dv_ref[t] = dv_ref[t] + dv[rows]
 
 
-def attend(slot_src, query_base, table, qg2, key_pos, group, groups):
-    run_len = qg2.shape[1]
+def attend(slot_src, query_base, peer_of, table, pieces, key_pos, group, groups):
+    piece_len = pieces.shape[2]
+    run_len = pieces.shape[0] * piece_len
     block_ids = run_len // BLOCK_TOKENS
     targets = table.shape[0]
     head_width = table.shape[-1]
-    row_width = qg2.shape[2] // groups
+    row_width = pieces.shape[-1] // groups
+    half = BLOCK_TOKENS // 2
+    per_piece = piece_len // half
+
+    def half_spec(which, part):
+        def index(b, src, base, peer):
+            i = 2 * b + part
+            return (peer[i // per_piece], which, i % per_piece, group)
+
+        return pl.BlockSpec((None, None, half, row_width), index)
 
     def slot_spec(s, kv):
-        def index(b, src, base):
+        def index(b, src, base, peer):
             return (src[b * TOPK + s], kv, 0, 0)
 
         return pl.BlockSpec((None, None, BLOCK_TOKENS, head_width), index)
 
-    q_row = pl.BlockSpec((None, BLOCK_TOKENS, row_width), lambda b, src, base: (0, b, group))
-    do_row = pl.BlockSpec((None, BLOCK_TOKENS, row_width), lambda b, src, base: (1, b, group))
-    out_row = pl.BlockSpec((BLOCK_TOKENS, row_width), lambda b, src, base: (b, 0))
-    pos_spec = pl.BlockSpec((None, 1, TOPK * BLOCK_TOKENS), lambda b, src, base: (b, 0, 0))
-    acc_spec = pl.BlockSpec((targets, BLOCK_TOKENS, head_width), lambda b, src, base: (0, 0, 0))
+    out_row = pl.BlockSpec((BLOCK_TOKENS, row_width), lambda b, src, base, peer: (b, 0))
+    pos_spec = pl.BlockSpec((None, 1, TOPK * BLOCK_TOKENS), lambda b, src, base, peer: (b, 0, 0))
+    acc_spec = pl.BlockSpec((targets, BLOCK_TOKENS, head_width), lambda b, src, base, peer: (0, 0, 0))
     in_specs = (
         [slot_spec(s, 0) for s in range(TOPK)]
         + [slot_spec(s, 1) for s in range(TOPK)]
-        + [q_row, do_row, pos_spec]
+        + [half_spec(0, 0), half_spec(0, 1), half_spec(1, 0), half_spec(1, 1), pos_spec]
     )
     out_shape = (
         jax.ShapeDtypeStruct((run_len, row_width), jnp.bfloat16),
@@ -121,7 +129,7 @@
         jax.ShapeDtypeStruct((targets, BLOCK_TOKENS, head_width), jnp.float32),
     )
     grid_spec = pltpu.PrefetchScalarGridSpec(
-        num_scalar_prefetch=2,
+        num_scalar_prefetch=3,
         grid=(block_ids,),
         in_specs=in_specs,
         out_specs=(out_row, out_row, acc_spec, acc_spec),
@@ -134,15 +142,28 @@
             dimension_semantics=("arbitrary",),
             vmem_limit_bytes=48 * 1024 * 1024,
         ),
-    )(slot_src, query_base, *([table] * (2 * TOPK)), qg2, qg2, key_pos)
+    )(slot_src, query_base, peer_of, *([table] * (2 * TOPK)), *([pieces] * 4), key_pos)
 
 
 def on_device(queries, rotated_keys, value_vectors, block_list, grad_out):
     kv_h = to_heads(rotated_keys, value_vectors)
-    qg_h = to_heads(queries, grad_out)
-    _, run_len, head_count, head_width = qg_h.shape
+    size = lax.axis_size("head")
+    here = lax.axis_index("head")
+    tok, head_count, head_width = queries.shape
+    run_len = size * tok
     groups = kv_h.shape[2]
-    group_width = head_count // groups
+    group_width = head_count // size // groups
+    qg = jnp.stack([queries, grad_out]).reshape(2, tok, size, head_count // size * head_width)
+    qg = jnp.transpose(qg, (2, 0, 1, 3))
+    pieces = []
+    for k in range(size):
+        piece = lax.dynamic_index_in_dim(qg, (here + k) % size, axis=0, keepdims=False)
+        if k:
+            piece = lax.ppermute(piece, "head", [(i, (i + k) % size) for i in range(size)])
+        pieces.append(piece)
+    qg_pieces = jnp.stack(pieces)
+    peer_of = (here - jnp.arange(size, dtype=jnp.int32)) % size
+    head_count = head_count // size
     block_ids = run_len // BLOCK_TOKENS
     peers = lax.axis_size("blk")
     rank = lax.axis_index("blk")
@@ -173,7 +194,6 @@
     key_pos = key_pos.reshape(groups, block_ids, 1, TOPK * BLOCK_TOKENS)
     query_base = (rank * block_ids + block_range) * BLOCK_TOKENS
 
-    qg2 = qg_h.reshape(2, run_len, head_count * head_width)
     outs, query_grads, backs, locals_ = [], [], [], []
     for g in range(groups):
         send = jnp.einsum(
@@ -182,7 +202,7 @@
         recv = lax.all_to_all(send, "blk", split_axis=0, concat_axis=0, tiled=True)
         table = jnp.concatenate([recv, kv_local[g]], axis=0)
         o_g, dq_g, dk_acc, dv_acc = attend(
-            slot_src[g].reshape(-1), query_base, table, qg2, key_pos[g], g, groups
+            slot_src[g].reshape(-1), query_base, peer_of, table, qg_pieces, key_pos[g], g, groups
         )
         outs.append(o_g)
         query_grads.append(dq_g)

time: 274 us -> 267 us (0.974)
  local copies, waits for them, and re-layouts: 41.3 us -> 32.4 us
  starting transfers between devices: 43.1 us -> 46.9 us
    ppermute x12 -> x9, waiting for transfers between devices: 65.6 us -> 36.4 us  [exchange(): lax.ppermute(piece, 'head', [(i, (i + k) % size) for i in range(size)])]
    ppermute x0 -> x3, waiting for transfers between devices: none -> 22.3 us  [on_device(): lax.ppermute(piece, 'head', [(i, (i + k) % size) for i in range(size)])]
    unnamed x61 -> x55, local copies, waits for them, and re-layouts: 17.4 us -> 7.81 us
    all_to_all x2, waiting for transfers between devices: 13.9 us -> 22.8 us  [on_device(): lax.all_to_all(remote, 'blk', split_axis=0, concat_axis=0, tiled=True)]
    ppermute x0 -> x3, starting transfers between devices: none -> 4.54 us  [on_device(): lax.ppermute(piece, 'head', [(i, (i + k) % size) for i in range(size)])]
    all_to_all x2, waiting for transfers between devices: 18.2 us -> 13.7 us  [on_device(): recv = lax.all_to_all(send, 'blk', split_axis=0, concat_axis=0, tiled=True)]
    another operation x1 -> x3, local copies, waits for them, and re-layouts: 3.38 us -> 7.45 us  [on_device(): jnp.stack([queries, grad_out])]
    another operation x2 -> x3, other arithmetic: 5.82 us -> 9.04 us
  transfers between devices with their start and end apart: 16 -> 16, of which waited for: 11 -> 10; matrix products, arithmetic and copies ran while one was open for 21% -> 17% of each run, Pallas kernels for 20% -> 21%
where the time goes in v5:
time: 267 us; the launch traced here: 263 us
  waiting for transfers between devices  95.1 us (36%)
  Pallas kernels  56 us (21%)
  starting transfers between devices  46.9 us (18%)
  local copies, waits for them, and re-layouts  32.4 us (12%)
  other arithmetic  23.8 us (9%)
  matrix products  7.5 us (3%)
    pallas_call x2, Pallas kernels, attend(): pl.pallas_call(attention_kernel, grid_spec=grid_spec, out_shape=out_shape...  56 us
    ppermute x9, waiting for transfers between devices, exchange(): lax.ppermute(piece, 'head', [(i, (i + k) % size) for i in range(size)])  36.4 us
    all_to_all x2, waiting for transfers between devices, on_device(): lax.all_to_all(remote, 'blk', split_axis=0, concat_axis=0, tiled=True)  22.8 us
    ppermute x3, waiting for transfers between devices, on_device(): lax.ppermute(piece, 'head', [(i, (i + k) % size) for i in range(size)])  22.3 us
    all_to_all x2, starting transfers between devices, on_device(): lax.all_to_all(remote, 'blk', split_axis=0, concat_axis=0, tiled=True)  15.5 us
    all_to_all x2, waiting for transfers between devices, on_device(): recv = lax.all_to_all(send, 'blk', split_axis=0, concat_axis=0, tiled=True)  13.7 us
    ppermute x9, starting transfers between devices, exchange(): lax.ppermute(piece, 'head', [(i, (i + k) % size) for i in range(size)])  13.6 us
    all_to_all x2, starting transfers between devices, on_device(): recv = lax.all_to_all(send, 'blk', split_axis=0, concat_axis=0, tiled=True)  13.3 us
  transfers between devices with their start and end apart: 16, of which 10 were waited for; matrix products, arithmetic and copies ran while one was open for 17% of the time, Pallas kernels for 21%

profile of v5, /device:TPU:0, one launch (start us, length us, event | category | flops | bytes accessed | tf_op | source)
XLA Modules:
  0.0 263.1 jit_solution(17868613353884959788)
XLA Ops:
  3.0 3.2 %collective-permute-start.1 = (bf16[2,192,2,128]{3,1,2,0:T(8,128)(2,1)S(1)}, bf16[2,192,2,128]{3,1,2,0:T(8,128)(2,1)S(1)}, u32[]{:S(2)}, u32[]{:S(2)}) collective-permute-start(bf16[2,192,2,128]{3,1,2,0:T(8,128)(2,1)S(1)} %get-tuple-element.46), channel_id=1, source_target_pairs={{0,64},{32,96},{64,0},{96,32},{1,65},{33,97},{65,1},{97,33},{2,66}... | collective-permute-start | bytes 589832 | tf_op jit(solution)/shard_map/ppermute | solution.py:19
  6.2 2.9 %collective-permute-start = (bf16[2,192,2,128]{3,1,2,0:T(8,128)(2,1)S(1)}, bf16[2,192,2,128]{3,1,2,0:T(8,128)(2,1)S(1)}, u32[]{:S(2)}, u32[]{:S(2)}) collective-permute-start(bf16[2,192,2,128]{3,1,2,0:T(8,128)(2,1)S(1)} %get-tuple-element.47), channel_id=1, source_target_pairs={{0,96},{32,0},{64,32},{96,64},{1,97},{33,1},{65,33},{97,65},{2,98}... | collective-permute-start | bytes 589832 | tf_op jit(solution)/shard_map/ppermute | solution.py:19
  11.4 3.6 %collective-permute-done = bf16[2,192,2,128]{3,1,2,0:T(8,128)(2,1)S(1)} collective-permute-done((bf16[2,192,2,128]{3,1,2,0:T(8,128)(2,1)S(1)}, bf16[2,192,2,128]{3,1,2,0:T(8,128)(2,1)S(1)}, u32[]{:S(2)}, u32[]{:S(2)}) %collective-permute-start) | collective-permute-done | bytes 196640 | tf_op jit(solution)/shard_map/ppermute | solution.py:19
  16.3 2.2 copy.130
  18.5 8.4 %all-to-all-start.1 = ((bf16[32,2,128,128]{3,2,1,0:T(8,128)(2,1)}), bf16[32,2,128,128]{3,2,1,0:T(8,128)(2,1)S(1)}, u32[]{:S(2)}, u32[]{:S(2)}) async-start(bf16[32,2,128,128]{3,2,1,0:T(8,128)(2,1)} %copy.130), calls=%async_computation.1 | async-start | bytes 4194304 | tf_op jit(solution)/shard_map/all_to_all | solution.py:202
  26.8 3.5 %stack.121 = bf16[1,192,4,1024]{3,2,1,0:T(4,128)(2,1)} reshape(bf16[192,32,128]{2,1,0:T(8,128)(2,1)} %param.5) | data formatting | bytes 3145728 | tf_op jit(solution)/shard_map/stack | solution.py:156
  30.3 3.5 %stack.122 = bf16[1,192,4,1024]{3,2,1,0:T(4,128)(2,1)} reshape(bf16[192,32,128]{2,1,0:T(8,128)(2,1)} %param.9) | data formatting | bytes 3145728 | tf_op jit(solution)/shard_map/stack | solution.py:156
  33.8 2.0 copy_dynamic-update-slice_fusion.1
  38.0 3.7 %collective-permute-start.5 = (bf16[2,192,1024]{2,1,0:T(8,128)(2,1)}, bf16[2,192,1024]{2,1,0:T(8,128)(2,1)}, u32[]{:S(2)}, u32[]{:S(2)}) collective-permute-start(bf16[2,192,1024]{2,1,0:T(8,128)(2,1)} %get-tuple-element.34), channel_id=1, source_target_pairs={{0,96},{32,0},{64,32},{96,64},{1,97},{33,1},{65,33},{97,65},{2,98}... | collective-permute-start | bytes 2359304 | tf_op jit(solution)/shard_map/ppermute | solution.py:162
  43.3 2.2 copy.131
  45.6 13.7 %all-to-all-done.1 = bf16[32,2,128,128]{3,2,1,0:T(8,128)(2,1)S(1)} async-done(((bf16[32,2,128,128]{3,2,1,0:T(8,128)(2,1)}), bf16[32,2,128,128]{3,2,1,0:T(8,128)(2,1)S(1)}, u32[]{:S(2)}, u32[]{:S(2)}) %all-to-all-start.1) | async-done | bytes 2097184 | tf_op jit(solution)/shard_map/all_to_all | solution.py:202
  59.3 4.9 %all-to-all-start = ((bf16[32,2,128,128]{3,2,1,0:T(8,128)(2,1)}), bf16[32,2,128,128]{3,2,1,0:T(8,128)(2,1)}, u32[]{:S(2)}, u32[]{:S(2)}) async-start(bf16[32,2,128,128]{3,2,1,0:T(8,128)(2,1)} %copy.131), calls=%async_computation | async-start | bytes 4194304 | tf_op jit(solution)/shard_map/all_to_all | solution.py:202
  66.7 18.5 %collective-permute-done.4 = bf16[2,192,1024]{2,1,0:T(8,128)(2,1)} collective-permute-done((bf16[2,192,1024]{2,1,0:T(8,128)(2,1)}, bf16[2,192,1024]{2,1,0:T(8,128)(2,1)}, u32[]{:S(2)}, u32[]{:S(2)}) %collective-permute-start.4) | collective-permute-done | bytes 786464 | tf_op jit(solution)/shard_map/ppermute | solution.py:162
  85.2 3.0 %collective-permute-done.3 = bf16[2,192,1024]{2,1,0:T(8,128)(2,1)} collective-permute-done((bf16[2,192,1024]{2,1,0:T(8,128)(2,1)}, bf16[2,192,1024]{2,1,0:T(8,128)(2,1)}, u32[]{:S(2)}, u32[]{:S(2)}) %collective-permute-start.3) | collective-permute-done | bytes 786464 | tf_op jit(solution)/shard_map/ppermute | solution.py:162
  88.2 3.2 %pad_maximum_fusion.1.refs_16_.refs_17_.refs_18_.refs_19_ = bf16[4,2,192,1024]{3,2,1,0:T(8,128)(2,1)} fusion(bf16[1,2,192,1024]{3,2,1,0:T(8,128)(2,1)} %bitcast.21, bf16[1,2,192,1024]{3,2,1,0:T(8,128)(2,1)} %bitcast.19, bf16[1,2,192,1024]{3,2,1,0:T(8,128)(2,1)} %bitcast.17, bf16[1,2,192,1024]{3,2,1,0:T(8,128)(2,1)} %get-tuple-element.33), kind=kLoop, calls=%fused_computation.13 | loop fusion | flops 4718592 | bytes 6291456 | tf_op jit(solution)/shard_map/stack | solution.py:164
  93.1 28.1 %shard_map.85 = (bf16[768,512]{1,0:T(8,128)(2,1)S(1)}, bf16[768,512]{1,0:T(8,128)(2,1)S(1)}, f32[38,128,128]{2,1,0:T(8,128)S(1)}, f32[38,128,128]{2,1,0:T(8,128)}) custom-call(s32[48]{0:T(128)S(1)} %reshape_squeeze.7.src_ref, s32[6]{0:T(128)S(1)} %add_multiply_fusion.base_ref, s32[4]{0:T(128)S(1)} %and_select_fusion.peer_ref, ...), custom_call_target="tpu_custom_call" | custom-call | tf_op jit(solution)/shard_map/pallas_call | solution.py:137
  121.1 2.4 maximum_convert_fusion
  125.3 7.4 %all-to-all-start.2 = ((bf16[32,2,128,128]{3,2,1,0:T(8,128)(2,1)}), bf16[32,2,128,128]{3,2,1,0:T(8,128)(2,1)}, u32[]{:S(2)}, u32[]{:S(2)}) async-start(bf16[32,2,128,128]{3,2,1,0:T(8,128)(2,1)} %copy.88), calls=%async_computation.2 | async-start | bytes 4194304 | tf_op jit(solution)/shard_map/all_to_all | solution.py:212
  132.9 3.4 %pad_maximum_fusion.2.refs_0_.refs_1_.refs_2_.refs_3_.refs_4_.refs_5_.refs_6_.refs_7_.refs_8_.refs_9_.refs_10_.refs_11_.refs_12_.refs_13_.refs_14_.refs_15_ = bf16[38,2,128,128]{3,2,1,0:T(8,128)(2,1)} fusion(bf16[6,2,128,128]{3,2,1,0:T(8,128)(2,1)} %copy-done.11, bf16[32,2,128,128]{3,2,1,0:T(8,128)(2,1)} %all-to-all-done), kind=kLoop, calls=%fused_computation.14 | loop fusion | flops 1245184 | bytes 4980736 | tf_op jit(solution)/shard_map/concatenate | solution.py:203
  136.3 28.0 %shard_map.84 = (bf16[768,512]{1,0:T(8,128)(2,1)S(1)}, bf16[768,512]{1,0:T(8,128)(2,1)S(1)}, f32[38,128,128]{2,1,0:T(8,128)S(1)}, f32[38,128,128]{2,1,0:T(8,128)}) custom-call(s32[48]{0:T(128)S(1)} %reshape_squeeze.6.src_ref, s32[6]{0:T(128)S(1)} %add_multiply_fusion.base_ref, s32[4]{0:T(128)S(1)} %and_select_fusion.peer_ref, ...), custom_call_target="tpu_custom_call" | custom-call | tf_op jit(solution)/shard_map/pallas_call | solution.py:137
  164.3 3.4 %fusion = bf16[32,2,128,128]{3,2,0,1:T(8,128)(2,1)S(1)} fusion(f32[38,1,128,128]{3,2,0,1:T(8,128)} %bitcast.148, f32[38,1,128,128]{3,2,0,1:T(8,128)S(1)} %bitcast.136), kind=kLoop, calls=%fused_computation.10 | loop fusion | flops 1048576 | bytes 7077888 | tf_op jit(solution)/shard_map/convert.2
  169.3 8.1 %all-to-all-start.3 = ((bf16[32,2,128,128]{3,2,1,0:T(8,128)(2,1)}), bf16[32,2,128,128]{3,2,1,0:T(8,128)(2,1)}, u32[]{:S(2)}, u32[]{:S(2)}) async-start(bf16[32,2,128,128]{3,2,1,0:T(8,128)(2,1)} %copy.89), calls=%async_computation.3 | async-start | bytes 4194304 | tf_op jit(solution)/shard_map/all_to_all | solution.py:212
  177.4 2.6 maximum_bitcast_fusion
  183.8 22.8 %all-to-all-done.3 = bf16[32,2,128,128]{3,2,1,0:T(8,128)(2,1)} async-done(((bf16[32,2,128,128]{3,2,1,0:T(8,128)(2,1)}), bf16[32,2,128,128]{3,2,1,0:T(8,128)(2,1)}, u32[]{:S(2)}, u32[]{:S(2)}) %all-to-all-start.3) | async-done | bytes 2097184 | tf_op jit(solution)/shard_map/all_to_all | solution.py:212
  206.5 3.0 %fusion.3 = f32[6,2,128,128]{3,0,2,1:T(8,128)S(1)} fusion(bf16[32,2,128,128]{3,2,1,0:T(8,128)(2,1)} %all-to-all-done.3, bf16[2,32,6]{1,2,0:T(8,128)(2,1)S(1)} %broadcast_select_fusion), kind=kOutput, calls=%fused_computation.18 | convolution fusion | flops 12582912 | bytes 2885632 | tf_op jit(solution)/shard_map/rl,rktd->lktd/dot_general | solution.py:226
  210.7 3.0 %fusion.1 = f32[6,2,128,128]{3,0,2,1:T(8,128)S(1)} fusion(bf16[32,2,128,128]{3,2,1,0:T(8,128)(2,1)} %all-to-all-done.2, bf16[2,32,6]{1,2,0:T(8,128)(2,1)S(1)} %broadcast_select_fusion), kind=kOutput, calls=%fused_computation.16 | convolution fusion | flops 12582912 | bytes 2885632 | tf_op jit(solution)/shard_map/rl,rktd->lktd/dot_general | solution.py:226
  220.1 2.3 collective-permute-start.7
  222.7 2.5 collective-permute-done.10
  225.5 2.4 collective-permute-done.11
  230.8 10.4 %collective-permute-done.6 = bf16[2,192,8,128]{3,2,1,0:T(8,128)(2,1)S(1)} collective-permute-done((bf16[2,192,8,128]{3,2,1,0:T(8,128)(2,1)S(1)}, bf16[2,192,8,128]{3,2,1,0:T(8,128)(2,1)S(1)}, u32[]{:S(2)}, u32[]{:S(2)}) %collective-permute-start.6) | collective-permute-done | bytes 786464 | tf_op jit(solution)/shard_map/ppermute | solution.py:19
  241.5 17.4 %collective-permute-done.7 = bf16[2,192,8,128]{3,2,1,0:T(8,128)(2,1)S(1)} collective-permute-done((bf16[2,192,8,128]{3,2,1,0:T(8,128)(2,1)S(1)}, bf16[2,192,8,128]{3,2,1,0:T(8,128)(2,1)S(1)}, u32[]{:S(2)}, u32[]{:S(2)}) %collective-permute-start.7) | collective-permute-done | bytes 786464 | tf_op jit(solution)/shard_map/ppermute | solution.py:19
  260.6 2.4 dynamic-slice_bitcast_fusion
  (121 shorter events, 33.7 us)
Async XLA Ops:
  2.9 12.2 %collective-permute-start.2 = (bf16[2,192,2,128]{3,1,2,0:T(8,128)(2,1)S(1)}, bf16[2,192,2,128]{3,1,2,0:T(8,128)(2,1)S(1)}, u32[]{:S(2)}, u32[]{:S(2)}) collective-permute-start(bf16[2,192,2,128]{3,1,2,0:T(8,128)(2,1)S(1)} %get-tuple-element.45), channel_id=1, source_target_pairs={{0,32},{32,64},{64,96},{96,0},{1,33},{33,65},{65,97},{97,1},{2,34}... | collective-permute-start | bytes 589832 | tf_op jit(solution)/shard_map/ppermute | solution.py:19
  3.0 12.1 %collective-permute-start.1 = (bf16[2,192,2,128]{3,1,2,0:T(8,128)(2,1)S(1)}, bf16[2,192,2,128]{3,1,2,0:T(8,128)(2,1)S(1)}, u32[]{:S(2)}, u32[]{:S(2)}) collective-permute-start(bf16[2,192,2,128]{3,1,2,0:T(8,128)(2,1)S(1)} %get-tuple-element.46), channel_id=1, source_target_pairs={{0,64},{32,96},{64,0},{96,32},{1,65},{33,97},{65,1},{97,33},{2,66}... | collective-permute-start | bytes 589832 | tf_op jit(solution)/shard_map/ppermute | solution.py:19
  6.2 8.8 %collective-permute-start = (bf16[2,192,2,128]{3,1,2,0:T(8,128)(2,1)S(1)}, bf16[2,192,2,128]{3,1,2,0:T(8,128)(2,1)S(1)}, u32[]{:S(2)}, u32[]{:S(2)}) collective-permute-start(bf16[2,192,2,128]{3,1,2,0:T(8,128)(2,1)S(1)} %get-tuple-element.47), channel_id=1, source_target_pairs={{0,96},{32,0},{64,32},{96,64},{1,97},{33,1},{65,33},{97,65},{2,98}... | collective-permute-start | bytes 589832 | tf_op jit(solution)/shard_map/ppermute | solution.py:19
  15.5 27.1 %copy-start.11 = (bf16[6,2,128,128]{3,2,1,0:T(8,128)(2,1)}, bf16[6,2,128,128]{3,2,1,0:T(8,128)(2,1)S(1)}, u32[]{:S(2)}) copy-start(bf16[6,2,128,128]{3,2,1,0:T(8,128)(2,1)S(1)} %get-tuple-element.43) | copy-start | bytes 1179652
  18.5 40.8 %all-to-all-start.1 = ((bf16[32,2,128,128]{3,2,1,0:T(8,128)(2,1)}), bf16[32,2,128,128]{3,2,1,0:T(8,128)(2,1)S(1)}, u32[]{:S(2)}, u32[]{:S(2)}) async-start(bf16[32,2,128,128]{3,2,1,0:T(8,128)(2,1)} %copy.130), calls=%async_computation.1 | async-start | bytes 4194304 | tf_op jit(solution)/shard_map/all_to_all | solution.py:202
  33.8 2.0 copy-start.10
  38.0 28.7 %collective-permute-start.5 = (bf16[2,192,1024]{2,1,0:T(8,128)(2,1)}, bf16[2,192,1024]{2,1,0:T(8,128)(2,1)}, u32[]{:S(2)}, u32[]{:S(2)}) collective-permute-start(bf16[2,192,1024]{2,1,0:T(8,128)(2,1)} %get-tuple-element.34), channel_id=1, source_target_pairs={{0,96},{32,0},{64,32},{96,64},{1,97},{33,1},{65,33},{97,65},{2,98}... | collective-permute-start | bytes 2359304 | tf_op jit(solution)/shard_map/ppermute | solution.py:162
  41.8 43.4 %collective-permute-start.4 = (bf16[2,192,1024]{2,1,0:T(8,128)(2,1)}, bf16[2,192,1024]{2,1,0:T(8,128)(2,1)}, u32[]{:S(2)}, u32[]{:S(2)}) collective-permute-start(bf16[2,192,1024]{2,1,0:T(8,128)(2,1)} %get-tuple-element.35), channel_id=1, source_target_pairs={{0,64},{32,96},{64,0},{96,32},{1,65},{33,97},{65,1},{97,33},{2,66}... | collective-permute-start | bytes 2359304 | tf_op jit(solution)/shard_map/ppermute | solution.py:162
  42.6 45.6 %collective-permute-start.3 = (bf16[2,192,1024]{2,1,0:T(8,128)(2,1)}, bf16[2,192,1024]{2,1,0:T(8,128)(2,1)}, u32[]{:S(2)}, u32[]{:S(2)}) collective-permute-start(bf16[2,192,1024]{2,1,0:T(8,128)(2,1)} %get-tuple-element.36), channel_id=1, source_target_pairs={{0,32},{32,64},{64,96},{96,0},{1,33},{33,65},{65,97},{97,1},{2,34}... | collective-permute-start | bytes 2359304 | tf_op jit(solution)/shard_map/ppermute | solution.py:162
  59.3 66.0 %all-to-all-start = ((bf16[32,2,128,128]{3,2,1,0:T(8,128)(2,1)}), bf16[32,2,128,128]{3,2,1,0:T(8,128)(2,1)}, u32[]{:S(2)}, u32[]{:S(2)}) async-start(bf16[32,2,128,128]{3,2,1,0:T(8,128)(2,1)} %copy.131), calls=%async_computation | async-start | bytes 4194304 | tf_op jit(solution)/shard_map/all_to_all | solution.py:202
  121.1 2.4 copy-start.2
  125.3 44.0 %all-to-all-start.2 = ((bf16[32,2,128,128]{3,2,1,0:T(8,128)(2,1)}), bf16[32,2,128,128]{3,2,1,0:T(8,128)(2,1)}, u32[]{:S(2)}, u32[]{:S(2)}) async-start(bf16[32,2,128,128]{3,2,1,0:T(8,128)(2,1)} %copy.88), calls=%async_computation.2 | async-start | bytes 4194304 | tf_op jit(solution)/shard_map/all_to_all | solution.py:212
  164.3 3.4 %copy-start = (f32[38,128,128]{2,1,0:T(8,128)}, f32[38,128,128]{2,1,0:T(8,128)S(1)}, u32[]{:S(2)}) copy-start(f32[38,128,128]{2,1,0:T(8,128)S(1)} %get-tuple-element.23) | copy-start | bytes 7471108
  164.3 3.4 %copy-start.3 = (bf16[768,512]{1,0:T(8,128)(2,1)}, bf16[768,512]{1,0:T(8,128)(2,1)S(1)}, u32[]{:S(2)}) copy-start(bf16[768,512]{1,0:T(8,128)(2,1)S(1)} %get-tuple-element.15) | copy-start | bytes 2359300
  164.3 3.4 %copy-start.4 = (bf16[768,512]{1,0:T(8,128)(2,1)}, bf16[768,512]{1,0:T(8,128)(2,1)S(1)}, u32[]{:S(2)}) copy-start(bf16[768,512]{1,0:T(8,128)(2,1)S(1)} %get-tuple-element.17) | copy-start | bytes 2359300
  169.3 37.2 %all-to-all-start.3 = ((bf16[32,2,128,128]{3,2,1,0:T(8,128)(2,1)}), bf16[32,2,128,128]{3,2,1,0:T(8,128)(2,1)}, u32[]{:S(2)}, u32[]{:S(2)}) async-start(bf16[32,2,128,128]{3,2,1,0:T(8,128)(2,1)} %copy.89), calls=%async_computation.3 | async-start | bytes 4194304 | tf_op jit(solution)/shard_map/all_to_all | solution.py:212
  180.5 1.5 copy-start.5
  181.0 1.5 copy-start.7
  206.5 3.0 %copy-start.1 = (f32[38,128,128]{2,1,0:T(8,128)S(1)}, f32[38,128,128]{2,1,0:T(8,128)}, u32[]{:S(2)}) copy-start(f32[38,128,128]{2,1,0:T(8,128)} %copy-done) | copy-start | bytes 7471108
  210.7 3.0 %copy-start.9 = (f32[38,128,128]{2,1,0:T(8,128)S(1)}, f32[38,128,128]{2,1,0:T(8,128)}, u32[]{:S(2)}) copy-start(f32[38,128,128]{2,1,0:T(8,128)} %get-tuple-element.20) | copy-start | bytes 7471108
  213.7 27.5 %slice-start = ((s8[6291456]{0:T(1024)(128)(4,1)}), s8[4194304]{0:T(1024)(128)(4,1)S(1)}, s32[]{:S(2)}) async-start(s8[6291456]{0:T(1024)(128)(4,1)} %bitcast.153), calls=%async_computation.4 | async-start | bytes 8388608
  213.9 4.6 %copy-start.13 = (bf16[2,192,8,128]{3,2,1,0:T(8,128)(2,1)S(1)}, bf16[2,192,8,128]{3,2,1,0:T(8,128)(2,1)}, u32[]{:S(2)}) copy-start(bf16[2,192,8,128]{3,2,1,0:T(8,128)(2,1)} %get-tuple-element.31) | copy-start | bytes 2359300
  213.9 6.2 %copy-start.12 = (bf16[2,192,8,128]{3,2,1,0:T(8,128)(2,1)S(1)}, bf16[2,192,8,128]{3,2,1,0:T(8,128)(2,1)}, u32[]{:S(2)}) copy-start(bf16[2,192,8,128]{3,2,1,0:T(8,128)(2,1)} %get-tuple-element.32) | copy-start | bytes 2359300
  214.0 27.2 %slice-start.1 = ((s8[6291456]{0:T(1024)(128)(4,1)}), s8[2097152]{0:T(1024)(128)(4,1)S(1)}, s32[]{:S(2)}) async-start(s8[6291456]{0:T(1024)(128)(4,1)} %bitcast.153), calls=%async_computation.5 | async-start | bytes 4194304
  214.8 5.4 %collective-permute-start.9 = (bf16[2,192,2,128]{3,2,1,0:T(2,128)(2,1)S(1)}, bf16[2,192,2,128]{3,2,1,0:T(2,128)(2,1)S(1)}, u32[]{:S(2)}, u32[]{:S(2)}) collective-permute-start(bf16[2,192,2,128]{3,2,1,0:T(2,128)(2,1)S(1)} %bitcast.165), channel_id=1, source_target_pairs={{0,96},{32,0},{64,32},{96,64},{1,97},{33,1},{65,33},{97,65},{2,98}... | collective-permute-start | bytes 589832 | tf_op jit(solution)/shard_map/ppermute | solution.py:19
  214.8 10.4 %collective-permute-start.10 = (bf16[2,192,2,128]{3,2,1,0:T(2,128)(2,1)S(1)}, bf16[2,192,2,128]{3,2,1,0:T(2,128)(2,1)S(1)}, u32[]{:S(2)}, u32[]{:S(2)}) collective-permute-start(bf16[2,192,2,128]{3,2,1,0:T(2,128)(2,1)S(1)} %bitcast.164), channel_id=1, source_target_pairs={{0,64},{32,96},{64,0},{96,32},{1,65},{33,97},{65,1},{97,33},{2,66}... | collective-permute-start | bytes 589832 | tf_op jit(solution)/shard_map/ppermute | solution.py:19
  216.6 11.3 %collective-permute-start.11 = (bf16[2,192,2,128]{3,2,1,0:T(2,128)(2,1)S(1)}, bf16[2,192,2,128]{3,2,1,0:T(2,128)(2,1)S(1)}, u32[]{:S(2)}, u32[]{:S(2)}) collective-permute-start(bf16[2,192,2,128]{3,2,1,0:T(2,128)(2,1)S(1)} %bitcast.163), channel_id=1, source_target_pairs={{0,32},{32,64},{64,96},{96,0},{1,33},{33,65},{65,97},{97,1},{2,34}... | collective-permute-start | bytes 589832 | tf_op jit(solution)/shard_map/ppermute | solution.py:19
  216.6 42.6 %collective-permute-start.8 = (bf16[2,192,8,128]{3,2,1,0:T(8,128)(2,1)S(1)}, bf16[2,192,8,128]{3,2,1,0:T(8,128)(2,1)S(1)}, u32[]{:S(2)}, u32[]{:S(2)}) collective-permute-start(bf16[2,192,8,128]{3,2,1,0:T(8,128)(2,1)S(1)} %get-tuple-element.30), channel_id=1, source_target_pairs={{0,32},{32,64},{64,96},{96,0},{1,33},{33,65},{65,97},{97,1},{2,34}... | collective-permute-start | bytes 2359304 | tf_op jit(solution)/shard_map/ppermute | solution.py:19
  218.6 22.6 %collective-permute-start.6 = (bf16[2,192,8,128]{3,2,1,0:T(8,128)(2,1)S(1)}, bf16[2,192,8,128]{3,2,1,0:T(8,128)(2,1)S(1)}, u32[]{:S(2)}, u32[]{:S(2)}) collective-permute-start(bf16[2,192,8,128]{3,2,1,0:T(8,128)(2,1)S(1)} %copy-done.13), channel_id=1, source_target_pairs={{0,96},{32,0},{64,32},{96,64},{1,97},{33,1},{65,33},{97,65},{2,98}... | collective-permute-start | bytes 2359304 | tf_op jit(solution)/shard_map/ppermute | solution.py:19
  220.1 38.8 %collective-permute-start.7 = (bf16[2,192,8,128]{3,2,1,0:T(8,128)(2,1)S(1)}, bf16[2,192,8,128]{3,2,1,0:T(8,128)(2,1)S(1)}, u32[]{:S(2)}, u32[]{:S(2)}) collective-permute-start(bf16[2,192,8,128]{3,2,1,0:T(8,128)(2,1)S(1)} %copy-done.12), channel_id=1, source_target_pairs={{0,64},{32,96},{64,0},{96,32},{1,65},{33,97},{65,1},{97,33},{2,66}... | collective-permute-start | bytes 2359304 | tf_op jit(solution)/shard_map/ppermute | solution.py:19
  230.8 28.7 %copy-start.6 = (bf16[96,8,8,128]{3,2,1,0:T(8,128)(2,1)S(1)}, bf16[96,8,8,128]{3,2,1,0:T(8,128)(2,1)}, u32[]{:S(2)}) copy-start(bf16[96,8,8,128]{3,2,1,0:T(8,128)(2,1)} %copy-done.5) | copy-start | bytes 4718596
  230.8 28.7 %copy-start.8 = (bf16[96,8,8,128]{3,2,1,0:T(8,128)(2,1)S(1)}, bf16[96,8,8,128]{3,2,1,0:T(8,128)(2,1)}, u32[]{:S(2)}) copy-start(bf16[96,8,8,128]{3,2,1,0:T(8,128)(2,1)} %copy-done.7) | copy-start | bytes 4718596

commit v6 on v5

--- a/solution.py
+++ b/solution.py
@@ -22,9 +22,8 @@
     return jnp.roll(ordered, here, axis=out_axis)
 
 
-def to_heads(*xs):
-    size = lax.axis_size("head")
-    x = jnp.stack(xs)
+def to_heads(x):
+    size = lax.axis_size("head")
     n, tok, heads, d = x.shape
     x = x.reshape(n, tok, size, heads // size, d)
     return exchange(x, 2, 1).reshape(n, size * tok, heads // size, d)
@@ -146,15 +145,16 @@
 
 
 def on_device(queries, rotated_keys, value_vectors, block_list, grad_out):
-    kv_h = to_heads(rotated_keys, value_vectors)
     size = lax.axis_size("head")
     here = lax.axis_index("head")
     tok, head_count, head_width = queries.shape
     run_len = size * tok
-    groups = kv_h.shape[2]
+    groups = rotated_keys.shape[1] // size
     group_width = head_count // size // groups
     qg = jnp.stack([queries, grad_out]).reshape(2, tok, size, head_count // size * head_width)
     qg = jnp.transpose(qg, (2, 0, 1, 3))
+    kv, qg = lax.optimization_barrier((jnp.stack([rotated_keys, value_vectors]), qg))
+    kv_h = to_heads(kv)
     pieces = []
     for k in range(size):
         piece = lax.dynamic_index_in_dim(qg, (here + k) % size, axis=0, keepdims=False)

time: 267 us -> 276 us (1.034)
  local copies, waits for them, and re-layouts: 32.4 us -> 41.1 us
  starting transfers between devices: 46.9 us -> 42.6 us
  waiting for transfers between devices: 95.1 us -> 98.3 us
    all_to_all x2, waiting for transfers between devices: 22.8 us -> 13.9 us  [on_device(): lax.all_to_all(remote, 'blk', split_axis=0, concat_axis=0, tiled=True)]
    unnamed x55 -> x68, local copies, waits for them, and re-layouts: 7.81 us -> 15.8 us
    all_to_all x2, waiting for transfers between devices: 13.7 us -> 21.4 us  [on_device(): recv = lax.all_to_all(send, 'blk', split_axis=0, concat_axis=0, tiled=True)]
    ppermute x3, waiting for transfers between devices: 22.3 us -> 25.1 us  [on_device(): lax.ppermute(piece, 'head', [(i, (i + k) % size) for i in range(size)])]
    ppermute x9, starting transfers between devices: 13.6 us -> 10.8 us  [exchange(): lax.ppermute(piece, 'head', [(i, (i + k) % size) for i in range(size)])]
    another operation x3 -> x4, local copies, waits for them, and re-layouts: 7.45 us -> 4.84 us  [on_device(): jnp.stack([queries, grad_out])]
    another operation x2 -> x3, other arithmetic: 5.82 us -> 6.77 us
  transfers between devices with their start and end apart: 16 -> 16, of which waited for: 10 -> 9; matrix products, arithmetic and copies ran while one was open for 17% -> 15% of each run, Pallas kernels for 21% -> 21%
where the time goes in v6:
time: 276 us; the launch traced here: 273 us
  waiting for transfers between devices  98.3 us (36%)
  Pallas kernels  56.4 us (20%)
  starting transfers between devices  42.6 us (15%)
  local copies, waits for them, and re-layouts  41.1 us (15%)
  other arithmetic  25.2 us (9%)
  matrix products  7.5 us (3%)
    pallas_call x2, Pallas kernels, attend(): pl.pallas_call(attention_kernel, grid_spec=grid_spec, out_shape=out_shape...  56.4 us
    ppermute x9, waiting for transfers between devices, exchange(): lax.ppermute(piece, 'head', [(i, (i + k) % size) for i in range(size)])  37.8 us
    ppermute x3, waiting for transfers between devices, on_device(): lax.ppermute(piece, 'head', [(i, (i + k) % size) for i in range(size)])  25.1 us
    all_to_all x2, waiting for transfers between devices, on_device(): recv = lax.all_to_all(send, 'blk', split_axis=0, concat_axis=0, tiled=True)  21.4 us
    unnamed x68, local copies, waits for them, and re-layouts  15.8 us
    all_to_all x2, starting transfers between devices, on_device(): recv = lax.all_to_all(send, 'blk', split_axis=0, concat_axis=0, tiled=True)  14.6 us
    all_to_all x2, starting transfers between devices, on_device(): lax.all_to_all(remote, 'blk', split_axis=0, concat_axis=0, tiled=True)  14.3 us
    all_to_all x2, waiting for transfers between devices, on_device(): lax.all_to_all(remote, 'blk', split_axis=0, concat_axis=0, tiled=True)  13.9 us
  transfers between devices with their start and end apart: 16, of which 9 were waited for; matrix products, arithmetic and copies ran while one was open for 15% of the time, Pallas kernels for 21%

profile of v6, /device:TPU:0, one launch (start us, length us, event | category | flops | bytes accessed | tf_op | source)
XLA Modules:
  0.0 272.6 jit_solution(3500117940888979685)
XLA Ops:
  0.7 2.4 stack.117
  7.5 1.8 constant_dynamic-slice_fusion.8
  10.0 2.5 collective-permute-start
  18.5 4.4 %collective-permute-done.1 = bf16[2,192,2,128]{3,1,2,0:T(8,128)(2,1)} collective-permute-done((bf16[2,192,2,128]{3,1,2,0:T(8,128)(2,1)}, bf16[2,192,2,128]{3,1,2,0:T(8,128)(2,1)}, u32[]{:S(2)}, u32[]{:S(2)}) %collective-permute-start.1) | collective-permute-done | bytes 196640 | tf_op jit(solution)/shard_map/ppermute | solution.py:19
  33.7 2.2 copy.142
  35.9 9.0 %all-to-all-start.1 = ((bf16[32,2,128,128]{3,2,1,0:T(8,128)(2,1)}), bf16[32,2,128,128]{3,2,1,0:T(8,128)(2,1)}, u32[]{:S(2)}, u32[]{:S(2)}) async-start(bf16[32,2,128,128]{3,2,1,0:T(8,128)(2,1)} %copy.142), calls=%async_computation.1 | async-start | bytes 4194304 | tf_op jit(solution)/shard_map/all_to_all | solution.py:202
  46.7 2.7 %collective-permute-start.4 = (bf16[2,192,1024]{2,1,0:T(8,128)(2,1)}, bf16[2,192,1024]{2,1,0:T(8,128)(2,1)S(1)}, u32[]{:S(2)}, u32[]{:S(2)}) collective-permute-start(bf16[2,192,1024]{2,1,0:T(8,128)(2,1)} %get-tuple-element.39), channel_id=1, source_target_pairs={{0,64},{32,96},{64,0},{96,32},{1,65},{33,97},{65,1},{97,33},{2,66}... | collective-permute-start | bytes 2359304 | tf_op jit(solution)/shard_map/ppermute | solution.py:162
  50.4 2.3 copy.143
  52.7 21.4 %all-to-all-done.1 = bf16[32,2,128,128]{3,2,1,0:T(8,128)(2,1)} async-done(((bf16[32,2,128,128]{3,2,1,0:T(8,128)(2,1)}), bf16[32,2,128,128]{3,2,1,0:T(8,128)(2,1)}, u32[]{:S(2)}, u32[]{:S(2)}) %all-to-all-start.1) | async-done | bytes 2097184 | tf_op jit(solution)/shard_map/all_to_all | solution.py:202
  74.1 5.6 %all-to-all-start = ((bf16[32,2,128,128]{3,2,1,0:T(8,128)(2,1)}), bf16[32,2,128,128]{3,2,1,0:T(8,128)(2,1)}, u32[]{:S(2)}, u32[]{:S(2)}) async-start(bf16[32,2,128,128]{3,2,1,0:T(8,128)(2,1)} %copy.143), calls=%async_computation | async-start | bytes 4194304 | tf_op jit(solution)/shard_map/all_to_all | solution.py:202
  81.4 4.0 %collective-permute-done.5 = bf16[2,192,1024]{2,1,0:T(8,128)(2,1)S(1)} collective-permute-done((bf16[2,192,1024]{2,1,0:T(8,128)(2,1)}, bf16[2,192,1024]{2,1,0:T(8,128)(2,1)S(1)}, u32[]{:S(2)}, u32[]{:S(2)}) %collective-permute-start.5) | collective-permute-done | bytes 786464 | tf_op jit(solution)/shard_map/ppermute | solution.py:162
  85.3 21.1 %collective-permute-done.4 = bf16[2,192,1024]{2,1,0:T(8,128)(2,1)S(1)} collective-permute-done((bf16[2,192,1024]{2,1,0:T(8,128)(2,1)}, bf16[2,192,1024]{2,1,0:T(8,128)(2,1)S(1)}, u32[]{:S(2)}, u32[]{:S(2)}) %collective-permute-start.4) | collective-permute-done | bytes 786464 | tf_op jit(solution)/shard_map/ppermute | solution.py:162
  106.5 1.8 pad_maximum_fusion.1.refs_16_.refs_17_.refs_18_.refs_19_
  108.3 3.3 %pad_maximum_fusion.3.refs_0_.refs_1_.refs_2_.refs_3_.refs_4_.refs_5_.refs_6_.refs_7_.refs_8_.refs_9_.refs_10_.refs_11_.refs_12_.refs_13_.refs_14_.refs_15_ = bf16[38,2,128,128]{3,2,1,0:T(8,128)(2,1)} fusion(bf16[6,2,128,128]{3,2,1,0:T(8,128)(2,1)S(1)} %copy-done.13, bf16[32,2,128,128]{3,2,1,0:T(8,128)(2,1)} %all-to-all-done.1), kind=kLoop, calls=%fused_computation.16 | loop fusion | flops 1245184 | bytes 4980736 | tf_op jit(solution)/shard_map/concatenate | solution.py:203
  111.6 28.3 %shard_map.85 = (bf16[768,512]{1,0:T(8,128)(2,1)S(1)}, bf16[768,512]{1,0:T(8,128)(2,1)S(1)}, f32[38,128,128]{2,1,0:T(8,128)S(1)}, f32[38,128,128]{2,1,0:T(8,128)}) custom-call(s32[48]{0:T(128)S(1)} %reshape_squeeze.7.src_ref, s32[6]{0:T(128)S(1)} %add_multiply_fusion.base_ref, s32[4]{0:T(128)S(1)} %and_select_fusion.peer_ref, ...), custom_call_target="tpu_custom_call" | custom-call | tf_op jit(solution)/shard_map/pallas_call | solution.py:136
  139.9 2.4 maximum_convert_fusion
  144.0 6.4 %all-to-all-start.2 = ((bf16[32,2,128,128]{3,2,1,0:T(8,128)(2,1)}), bf16[32,2,128,128]{3,2,1,0:T(8,128)(2,1)}, u32[]{:S(2)}, u32[]{:S(2)}) async-start(bf16[32,2,128,128]{3,2,1,0:T(8,128)(2,1)} %copy.92), calls=%async_computation.2 | async-start | bytes 4194304 | tf_op jit(solution)/shard_map/all_to_all | solution.py:212
  150.6 3.4 %pad_maximum_fusion.2.refs_0_.refs_1_.refs_2_.refs_3_.refs_4_.refs_5_.refs_6_.refs_7_.refs_8_.refs_9_.refs_10_.refs_11_.refs_12_.refs_13_.refs_14_.refs_15_ = bf16[38,2,128,128]{3,2,1,0:T(8,128)(2,1)} fusion(bf16[6,2,128,128]{3,2,1,0:T(8,128)(2,1)} %copy-done.11, bf16[32,2,128,128]{3,2,1,0:T(8,128)(2,1)} %all-to-all-done), kind=kLoop, calls=%fused_computation.15 | loop fusion | flops 1245184 | bytes 4980736 | tf_op jit(solution)/shard_map/concatenate | solution.py:203
  154.0 28.2 %shard_map.84 = (bf16[768,512]{1,0:T(8,128)(2,1)S(1)}, bf16[768,512]{1,0:T(8,128)(2,1)S(1)}, f32[38,128,128]{2,1,0:T(8,128)S(1)}, f32[38,128,128]{2,1,0:T(8,128)}) custom-call(s32[48]{0:T(128)S(1)} %reshape_squeeze.6.src_ref, s32[6]{0:T(128)S(1)} %add_multiply_fusion.base_ref, s32[4]{0:T(128)S(1)} %and_select_fusion.peer_ref, ...), custom_call_target="tpu_custom_call" | custom-call | tf_op jit(solution)/shard_map/pallas_call | solution.py:136
  182.2 3.4 %fusion = bf16[32,2,128,128]{3,2,0,1:T(8,128)(2,1)S(1)} fusion(f32[38,1,128,128]{3,2,0,1:T(8,128)} %bitcast.155, f32[38,1,128,128]{3,2,0,1:T(8,128)S(1)} %bitcast.143), kind=kLoop, calls=%fused_computation.10 | loop fusion | flops 1048576 | bytes 7077888 | tf_op jit(solution)/shard_map/convert.2
  187.2 7.9 %all-to-all-start.3 = ((bf16[32,2,128,128]{3,2,1,0:T(8,128)(2,1)}), bf16[32,2,128,128]{3,2,1,0:T(8,128)(2,1)}, u32[]{:S(2)}, u32[]{:S(2)}) async-start(bf16[32,2,128,128]{3,2,1,0:T(8,128)(2,1)} %copy.93), calls=%async_computation.3 | async-start | bytes 4194304 | tf_op jit(solution)/shard_map/all_to_all | solution.py:212
  195.1 2.6 maximum_bitcast_fusion.1
  201.5 13.9 %all-to-all-done.3 = bf16[32,2,128,128]{3,2,1,0:T(8,128)(2,1)} async-done(((bf16[32,2,128,128]{3,2,1,0:T(8,128)(2,1)}), bf16[32,2,128,128]{3,2,1,0:T(8,128)(2,1)}, u32[]{:S(2)}, u32[]{:S(2)}) %all-to-all-start.3) | async-done | bytes 2097184 | tf_op jit(solution)/shard_map/all_to_all | solution.py:212
  215.4 3.0 %fusion.3 = f32[6,2,128,128]{3,0,2,1:T(8,128)S(1)} fusion(bf16[32,2,128,128]{3,2,1,0:T(8,128)(2,1)} %all-to-all-done.3, bf16[2,32,6]{1,2,0:T(8,128)(2,1)S(1)} %broadcast_select_fusion), kind=kOutput, calls=%fused_computation.19 | convolution fusion | flops 12582912 | bytes 2885632 | tf_op jit(solution)/shard_map/rl,rktd->lktd/dot_general | solution.py:226
  219.6 3.0 %fusion.1 = f32[6,2,128,128]{3,0,2,1:T(8,128)S(1)} fusion(bf16[32,2,128,128]{3,2,1,0:T(8,128)(2,1)} %all-to-all-done.2, bf16[2,32,6]{1,2,0:T(8,128)(2,1)S(1)} %broadcast_select_fusion), kind=kOutput, calls=%fused_computation.17 | convolution fusion | flops 12582912 | bytes 2885632 | tf_op jit(solution)/shard_map/rl,rktd->lktd/dot_general | solution.py:226
  223.7 2.2 collective-permute-start.10
  227.4 1.8 collective-permute-start.6
  229.5 1.8 collective-permute-start.7
  231.6 3.2 %collective-permute-done.10 = bf16[2,192,2,128]{3,2,1,0:T(2,128)(2,1)S(1)} collective-permute-done((bf16[2,192,2,128]{3,2,1,0:T(2,128)(2,1)S(1)}, bf16[2,192,2,128]{3,2,1,0:T(2,128)(2,1)S(1)}, u32[]{:S(2)}, u32[]{:S(2)}) %collective-permute-start.10) | collective-permute-done | bytes 196640 | tf_op jit(solution)/shard_map/ppermute | solution.py:19
  239.6 8.7 %collective-permute-done.6 = bf16[2,192,8,128]{3,2,1,0:T(8,128)(2,1)S(1)} collective-permute-done((bf16[2,192,8,128]{3,2,1,0:T(8,128)(2,1)S(1)}, bf16[2,192,8,128]{3,2,1,0:T(8,128)(2,1)S(1)}, u32[]{:S(2)}, u32[]{:S(2)}) %collective-permute-start.6) | collective-permute-done | bytes 786464 | tf_op jit(solution)/shard_map/ppermute | solution.py:19
  248.6 19.8 %collective-permute-done.7 = bf16[2,192,8,128]{3,2,1,0:T(8,128)(2,1)S(1)} collective-permute-done((bf16[2,192,8,128]{3,2,1,0:T(8,128)(2,1)S(1)}, bf16[2,192,8,128]{3,2,1,0:T(8,128)(2,1)S(1)}, u32[]{:S(2)}, u32[]{:S(2)}) %collective-permute-start.7) | collective-permute-done | bytes 786464 | tf_op jit(solution)/shard_map/ppermute | solution.py:19
  270.2 2.4 dynamic-slice_bitcast_fusion
  (136 shorter events, 44.4 us)
Async XLA Ops:
  5.1 2.0 copy-start.10
  10.0 7.8 %collective-permute-start = (bf16[2,192,2,128]{3,1,2,0:T(8,128)(2,1)}, bf16[2,192,2,128]{3,1,2,0:T(8,128)(2,1)S(1)}, u32[]{:S(2)}, u32[]{:S(2)}) collective-permute-start(bf16[2,192,2,128]{3,1,2,0:T(8,128)(2,1)} %bitcast.137), channel_id=1, source_target_pairs={{0,96},{32,0},{64,32},{96,64},{1,97},{33,1},{65,33},{97,65},{2,98}... | collective-permute-start | bytes 589832 | tf_op jit(solution)/shard_map/ppermute | solution.py:19
  13.2 9.7 %collective-permute-start.1 = (bf16[2,192,2,128]{3,1,2,0:T(8,128)(2,1)}, bf16[2,192,2,128]{3,1,2,0:T(8,128)(2,1)}, u32[]{:S(2)}, u32[]{:S(2)}) collective-permute-start(bf16[2,192,2,128]{3,1,2,0:T(8,128)(2,1)} %bitcast.136), channel_id=1, source_target_pairs={{0,64},{32,96},{64,0},{96,32},{1,65},{33,97},{65,1},{97,33},{2,66}... | collective-permute-start | bytes 589832 | tf_op jit(solution)/shard_map/ppermute | solution.py:19
  14.5 10.0 %collective-permute-start.2 = (bf16[2,192,2,128]{3,1,2,0:T(8,128)(2,1)}, bf16[2,192,2,128]{3,1,2,0:T(8,128)(2,1)}, u32[]{:S(2)}, u32[]{:S(2)}) collective-permute-start(bf16[2,192,2,128]{3,1,2,0:T(8,128)(2,1)} %bitcast.135), channel_id=1, source_target_pairs={{0,32},{32,64},{64,96},{96,0},{1,33},{33,65},{65,97},{97,1},{2,34}... | collective-permute-start | bytes 589832 | tf_op jit(solution)/shard_map/ppermute | solution.py:19
  32.2 17.4 %copy-start.11 = (bf16[6,2,128,128]{3,2,1,0:T(8,128)(2,1)}, bf16[6,2,128,128]{3,2,1,0:T(8,128)(2,1)S(1)}, u32[]{:S(2)}) copy-start(bf16[6,2,128,128]{3,2,1,0:T(8,128)(2,1)S(1)} %get-tuple-element.47) | copy-start | bytes 1179652
  35.9 38.2 %all-to-all-start.1 = ((bf16[32,2,128,128]{3,2,1,0:T(8,128)(2,1)}), bf16[32,2,128,128]{3,2,1,0:T(8,128)(2,1)}, u32[]{:S(2)}, u32[]{:S(2)}) async-start(bf16[32,2,128,128]{3,2,1,0:T(8,128)(2,1)} %copy.142), calls=%async_computation.1 | async-start | bytes 4194304 | tf_op jit(solution)/shard_map/all_to_all | solution.py:202
  46.7 38.7 %collective-permute-start.5 = (bf16[2,192,1024]{2,1,0:T(8,128)(2,1)}, bf16[2,192,1024]{2,1,0:T(8,128)(2,1)S(1)}, u32[]{:S(2)}, u32[]{:S(2)}) collective-permute-start(bf16[2,192,1024]{2,1,0:T(8,128)(2,1)} %get-tuple-element.38), channel_id=1, source_target_pairs={{0,96},{32,0},{64,32},{96,64},{1,97},{33,1},{65,33},{97,65},{2,98}... | collective-permute-start | bytes 2359304 | tf_op jit(solution)/shard_map/ppermute | solution.py:162
  46.7 59.8 %collective-permute-start.4 = (bf16[2,192,1024]{2,1,0:T(8,128)(2,1)}, bf16[2,192,1024]{2,1,0:T(8,128)(2,1)S(1)}, u32[]{:S(2)}, u32[]{:S(2)}) collective-permute-start(bf16[2,192,1024]{2,1,0:T(8,128)(2,1)} %get-tuple-element.39), channel_id=1, source_target_pairs={{0,64},{32,96},{64,0},{96,32},{1,65},{33,97},{65,1},{97,33},{2,66}... | collective-permute-start | bytes 2359304 | tf_op jit(solution)/shard_map/ppermute | solution.py:162
  49.4 57.1 %collective-permute-start.3 = (bf16[2,192,1024]{2,1,0:T(8,128)(2,1)}, bf16[2,192,1024]{2,1,0:T(8,128)(2,1)S(1)}, u32[]{:S(2)}, u32[]{:S(2)}) collective-permute-start(bf16[2,192,1024]{2,1,0:T(8,128)(2,1)} %get-tuple-element.40), channel_id=1, source_target_pairs={{0,32},{32,64},{64,96},{96,0},{1,33},{33,65},{65,97},{97,1},{2,34}... | collective-permute-start | bytes 2359304 | tf_op jit(solution)/shard_map/ppermute | solution.py:162
  52.7 53.8 %copy-start.14 = (bf16[1,2,192,1024]{3,2,1,0:T(8,128)(2,1)S(1)}, bf16[1,2,192,1024]{3,2,1,0:T(8,128)(2,1)}, u32[]{:S(2)}) copy-start(bf16[1,2,192,1024]{3,2,1,0:T(8,128)(2,1)} %get-tuple-element.37) | copy-start | bytes 2359300
  74.1 69.9 %all-to-all-start = ((bf16[32,2,128,128]{3,2,1,0:T(8,128)(2,1)}), bf16[32,2,128,128]{3,2,1,0:T(8,128)(2,1)}, u32[]{:S(2)}, u32[]{:S(2)}) async-start(bf16[32,2,128,128]{3,2,1,0:T(8,128)(2,1)} %copy.143), calls=%async_computation | async-start | bytes 4194304 | tf_op jit(solution)/shard_map/all_to_all | solution.py:202
  106.5 1.8 copy-start.13
  139.9 2.4 copy-start.2
  144.0 43.2 %all-to-all-start.2 = ((bf16[32,2,128,128]{3,2,1,0:T(8,128)(2,1)}), bf16[32,2,128,128]{3,2,1,0:T(8,128)(2,1)}, u32[]{:S(2)}, u32[]{:S(2)}) async-start(bf16[32,2,128,128]{3,2,1,0:T(8,128)(2,1)} %copy.92), calls=%async_computation.2 | async-start | bytes 4194304 | tf_op jit(solution)/shard_map/all_to_all | solution.py:212
  182.2 3.4 %copy-start = (f32[38,128,128]{2,1,0:T(8,128)}, f32[38,128,128]{2,1,0:T(8,128)S(1)}, u32[]{:S(2)}) copy-start(f32[38,128,128]{2,1,0:T(8,128)S(1)} %get-tuple-element.27) | copy-start | bytes 7471108
  182.2 3.4 %copy-start.3 = (bf16[768,512]{1,0:T(8,128)(2,1)}, bf16[768,512]{1,0:T(8,128)(2,1)S(1)}, u32[]{:S(2)}) copy-start(bf16[768,512]{1,0:T(8,128)(2,1)S(1)} %get-tuple-element.19) | copy-start | bytes 2359300
  182.2 3.4 %copy-start.4 = (bf16[768,512]{1,0:T(8,128)(2,1)}, bf16[768,512]{1,0:T(8,128)(2,1)S(1)}, u32[]{:S(2)}) copy-start(bf16[768,512]{1,0:T(8,128)(2,1)S(1)} %get-tuple-element.21) | copy-start | bytes 2359300
  187.2 28.2 %all-to-all-start.3 = ((bf16[32,2,128,128]{3,2,1,0:T(8,128)(2,1)}), bf16[32,2,128,128]{3,2,1,0:T(8,128)(2,1)}, u32[]{:S(2)}, u32[]{:S(2)}) async-start(bf16[32,2,128,128]{3,2,1,0:T(8,128)(2,1)} %copy.93), calls=%async_computation.3 | async-start | bytes 4194304 | tf_op jit(solution)/shard_map/all_to_all | solution.py:212
  215.4 3.0 %copy-start.1 = (f32[38,128,128]{2,1,0:T(8,128)S(1)}, f32[38,128,128]{2,1,0:T(8,128)}, u32[]{:S(2)}) copy-start(f32[38,128,128]{2,1,0:T(8,128)} %copy-done) | copy-start | bytes 7471108
  219.5 3.0 %copy-start.9 = (f32[38,128,128]{2,1,0:T(8,128)S(1)}, f32[38,128,128]{2,1,0:T(8,128)}, u32[]{:S(2)}) copy-start(f32[38,128,128]{2,1,0:T(8,128)} %get-tuple-element.24) | copy-start | bytes 7471108
  222.6 25.8 %slice-start = ((s8[6291456]{0:T(1024)(128)(4,1)}), s8[4194304]{0:T(1024)(128)(4,1)S(1)}, s32[]{:S(2)}) async-start(s8[6291456]{0:T(1024)(128)(4,1)} %bitcast.161), calls=%async_computation.4 | async-start | bytes 8388608
  222.8 4.6 %copy-start.17 = (bf16[2,192,8,128]{3,2,1,0:T(8,128)(2,1)S(1)}, bf16[2,192,8,128]{3,2,1,0:T(8,128)(2,1)}, u32[]{:S(2)}) copy-start(bf16[2,192,8,128]{3,2,1,0:T(8,128)(2,1)} %get-tuple-element.35) | copy-start | bytes 2359300
  222.8 6.7 %copy-start.16 = (bf16[2,192,8,128]{3,2,1,0:T(8,128)(2,1)S(1)}, bf16[2,192,8,128]{3,2,1,0:T(8,128)(2,1)}, u32[]{:S(2)}) copy-start(bf16[2,192,8,128]{3,2,1,0:T(8,128)(2,1)} %get-tuple-element.36) | copy-start | bytes 2359300
  222.8 25.5 %slice-start.1 = ((s8[6291456]{0:T(1024)(128)(4,1)}), s8[2097152]{0:T(1024)(128)(4,1)S(1)}, s32[]{:S(2)}) async-start(s8[6291456]{0:T(1024)(128)(4,1)} %bitcast.161), calls=%async_computation.5 | async-start | bytes 4194304
  223.6 5.9 %collective-permute-start.9 = (bf16[2,192,2,128]{3,2,1,0:T(2,128)(2,1)S(1)}, bf16[2,192,2,128]{3,2,1,0:T(2,128)(2,1)S(1)}, u32[]{:S(2)}, u32[]{:S(2)}) collective-permute-start(bf16[2,192,2,128]{3,2,1,0:T(2,128)(2,1)S(1)} %bitcast.176), channel_id=1, source_target_pairs={{0,96},{32,0},{64,32},{96,64},{1,97},{33,1},{65,33},{97,65},{2,98}... | collective-permute-start | bytes 589832 | tf_op jit(solution)/shard_map/ppermute | solution.py:19
  223.7 11.1 %collective-permute-start.10 = (bf16[2,192,2,128]{3,2,1,0:T(2,128)(2,1)S(1)}, bf16[2,192,2,128]{3,2,1,0:T(2,128)(2,1)S(1)}, u32[]{:S(2)}, u32[]{:S(2)}) collective-permute-start(bf16[2,192,2,128]{3,2,1,0:T(2,128)(2,1)S(1)} %bitcast.175), channel_id=1, source_target_pairs={{0,64},{32,96},{64,0},{96,32},{1,65},{33,97},{65,1},{97,33},{2,66}... | collective-permute-start | bytes 589832 | tf_op jit(solution)/shard_map/ppermute | solution.py:19
  225.9 10.9 %collective-permute-start.11 = (bf16[2,192,2,128]{3,2,1,0:T(2,128)(2,1)S(1)}, bf16[2,192,2,128]{3,2,1,0:T(2,128)(2,1)S(1)}, u32[]{:S(2)}, u32[]{:S(2)}) collective-permute-start(bf16[2,192,2,128]{3,2,1,0:T(2,128)(2,1)S(1)} %bitcast.174), channel_id=1, source_target_pairs={{0,32},{32,64},{64,96},{96,0},{1,33},{33,65},{65,97},{97,1},{2,34}... | collective-permute-start | bytes 589832 | tf_op jit(solution)/shard_map/ppermute | solution.py:19
  226.0 42.7 %collective-permute-start.8 = (bf16[2,192,8,128]{3,2,1,0:T(8,128)(2,1)S(1)}, bf16[2,192,8,128]{3,2,1,0:T(8,128)(2,1)S(1)}, u32[]{:S(2)}, u32[]{:S(2)}) collective-permute-start(bf16[2,192,8,128]{3,2,1,0:T(8,128)(2,1)S(1)} %get-tuple-element.34), channel_id=1, source_target_pairs={{0,32},{32,64},{64,96},{96,0},{1,33},{33,65},{65,97},{97,1},{2,34}... | collective-permute-start | bytes 2359304 | tf_op jit(solution)/shard_map/ppermute | solution.py:19
  227.4 20.9 %collective-permute-start.6 = (bf16[2,192,8,128]{3,2,1,0:T(8,128)(2,1)S(1)}, bf16[2,192,8,128]{3,2,1,0:T(8,128)(2,1)S(1)}, u32[]{:S(2)}, u32[]{:S(2)}) collective-permute-start(bf16[2,192,8,128]{3,2,1,0:T(8,128)(2,1)S(1)} %copy-done.17), channel_id=1, source_target_pairs={{0,96},{32,0},{64,32},{96,64},{1,97},{33,1},{65,33},{97,65},{2,98}... | collective-permute-start | bytes 2359304 | tf_op jit(solution)/shard_map/ppermute | solution.py:19
  229.5 39.0 %collective-permute-start.7 = (bf16[2,192,8,128]{3,2,1,0:T(8,128)(2,1)S(1)}, bf16[2,192,8,128]{3,2,1,0:T(8,128)(2,1)S(1)}, u32[]{:S(2)}, u32[]{:S(2)}) collective-permute-start(bf16[2,192,8,128]{3,2,1,0:T(8,128)(2,1)S(1)} %copy-done.16), channel_id=1, source_target_pairs={{0,64},{32,96},{64,0},{96,32},{1,65},{33,97},{65,1},{97,33},{2,66}... | collective-permute-start | bytes 2359304 | tf_op jit(solution)/shard_map/ppermute | solution.py:19
  239.6 29.4 %copy-start.6 = (bf16[96,8,8,128]{3,2,1,0:T(8,128)(2,1)S(1)}, bf16[96,8,8,128]{3,2,1,0:T(8,128)(2,1)}, u32[]{:S(2)}) copy-start(bf16[96,8,8,128]{3,2,1,0:T(8,128)(2,1)} %copy-done.5) | copy-start | bytes 4718596
  239.6 29.4 %copy-start.8 = (bf16[96,8,8,128]{3,2,1,0:T(8,128)(2,1)S(1)}, bf16[96,8,8,128]{3,2,1,0:T(8,128)(2,1)}, u32[]{:S(2)}) copy-start(bf16[96,8,8,128]{3,2,1,0:T(8,128)(2,1)} %copy-done.7) | copy-start | bytes 4718596
  (6 other events, 7.5 us)

commit v7 on v5

--- a/solution.py
+++ b/solution.py
@@ -66,11 +66,11 @@
         cols = slice(j * head_width, (j + 1) * head_width)
         qj = jnp.concatenate([q_lo[:, cols], q_hi[:, cols]], axis=0)
         gj = jnp.concatenate([do_lo[:, cols], do_hi[:, cols]], axis=0)
-        s = lax.dot_general(qj, keys, nt, preferred_element_type=jnp.float32) * scale
+        s = lax.dot_general(qj, keys, nt, preferred_element_type=jnp.float32)
         s = jnp.where(allowed, s, -jnp.inf)
         m = jnp.max(s, axis=-1, keepdims=True)
-        lt = m + jnp.log(jnp.sum(jnp.exp(s - m), axis=-1, keepdims=True))
-        p = jnp.exp(s - lt)
+        e = jnp.exp((s - m) * scale)
+        p = e * (1.0 / jnp.sum(e, axis=-1, keepdims=True))
         pb = p.astype(jnp.bfloat16)
         o = jnp.dot(pb, values, preferred_element_type=jnp.float32).astype(jnp.bfloat16)
         o_ref[:, cols] = o

time: 267 us -> 267 us (level)
  no operation moved by 1% of the time
where the time goes in v7:
time: 267 us; the launch traced here: 263 us
  waiting for transfers between devices  95.1 us (36%)
  Pallas kernels  56.3 us (21%)
  starting transfers between devices  46.9 us (18%)
  local copies, waits for them, and re-layouts  32.4 us (12%)
  other arithmetic  23.8 us (9%)
  matrix products  7.5 us (3%)
    pallas_call x2, Pallas kernels, attend(): pl.pallas_call(attention_kernel, grid_spec=grid_spec, out_shape=out_shape...  56.3 us
    ppermute x9, waiting for transfers between devices, exchange(): lax.ppermute(piece, 'head', [(i, (i + k) % size) for i in range(size)])  36.4 us
    all_to_all x2, waiting for transfers between devices, on_device(): lax.all_to_all(remote, 'blk', split_axis=0, concat_axis=0, tiled=True)  22.7 us
    ppermute x3, waiting for transfers between devices, on_device(): lax.ppermute(piece, 'head', [(i, (i + k) % size) for i in range(size)])  22.3 us
    all_to_all x2, starting transfers between devices, on_device(): lax.all_to_all(remote, 'blk', split_axis=0, concat_axis=0, tiled=True)  15.5 us
    all_to_all x2, waiting for transfers between devices, on_device(): recv = lax.all_to_all(send, 'blk', split_axis=0, concat_axis=0, tiled=True)  13.7 us
    ppermute x9, starting transfers between devices, exchange(): lax.ppermute(piece, 'head', [(i, (i + k) % size) for i in range(size)])  13.6 us
    all_to_all x2, starting transfers between devices, on_device(): recv = lax.all_to_all(send, 'blk', split_axis=0, concat_axis=0, tiled=True)  13.3 us
  transfers between devices with their start and end apart: 16, of which 10 were waited for; matrix products, arithmetic and copies ran while one was open for 17% of the time, Pallas kernels for 21%

profile of v7, /device:TPU:0, one launch (start us, length us, event | category | flops | bytes accessed | tf_op | source)
XLA Modules:
  0.0 263.3 jit_solution(17856966449727618677)
XLA Ops:
  3.0 3.2 %collective-permute-start.1 = (bf16[2,192,2,128]{3,1,2,0:T(8,128)(2,1)S(1)}, bf16[2,192,2,128]{3,1,2,0:T(8,128)(2,1)S(1)}, u32[]{:S(2)}, u32[]{:S(2)}) collective-permute-start(bf16[2,192,2,128]{3,1,2,0:T(8,128)(2,1)S(1)} %get-tuple-element.46), channel_id=1, source_target_pairs={{0,64},{32,96},{64,0},{96,32},{1,65},{33,97},{65,1},{97,33},{2,66}... | collective-permute-start | bytes 589832 | tf_op jit(solution)/shard_map/ppermute | solution.py:19
  6.2 2.9 %collective-permute-start = (bf16[2,192,2,128]{3,1,2,0:T(8,128)(2,1)S(1)}, bf16[2,192,2,128]{3,1,2,0:T(8,128)(2,1)S(1)}, u32[]{:S(2)}, u32[]{:S(2)}) collective-permute-start(bf16[2,192,2,128]{3,1,2,0:T(8,128)(2,1)S(1)} %get-tuple-element.47), channel_id=1, source_target_pairs={{0,96},{32,0},{64,32},{96,64},{1,97},{33,1},{65,33},{97,65},{2,98}... | collective-permute-start | bytes 589832 | tf_op jit(solution)/shard_map/ppermute | solution.py:19
  11.4 3.6 %collective-permute-done = bf16[2,192,2,128]{3,1,2,0:T(8,128)(2,1)S(1)} collective-permute-done((bf16[2,192,2,128]{3,1,2,0:T(8,128)(2,1)S(1)}, bf16[2,192,2,128]{3,1,2,0:T(8,128)(2,1)S(1)}, u32[]{:S(2)}, u32[]{:S(2)}) %collective-permute-start) | collective-permute-done | bytes 196640 | tf_op jit(solution)/shard_map/ppermute | solution.py:19
  16.3 2.2 copy.130
  18.5 8.4 %all-to-all-start.1 = ((bf16[32,2,128,128]{3,2,1,0:T(8,128)(2,1)}), bf16[32,2,128,128]{3,2,1,0:T(8,128)(2,1)S(1)}, u32[]{:S(2)}, u32[]{:S(2)}) async-start(bf16[32,2,128,128]{3,2,1,0:T(8,128)(2,1)} %copy.130), calls=%async_computation.1 | async-start | bytes 4194304 | tf_op jit(solution)/shard_map/all_to_all | solution.py:202
  26.8 3.5 %stack.121 = bf16[1,192,4,1024]{3,2,1,0:T(4,128)(2,1)} reshape(bf16[192,32,128]{2,1,0:T(8,128)(2,1)} %param.5) | data formatting | bytes 3145728 | tf_op jit(solution)/shard_map/stack | solution.py:156
  30.3 3.5 %stack.122 = bf16[1,192,4,1024]{3,2,1,0:T(4,128)(2,1)} reshape(bf16[192,32,128]{2,1,0:T(8,128)(2,1)} %param.9) | data formatting | bytes 3145728 | tf_op jit(solution)/shard_map/stack | solution.py:156
  33.8 2.0 copy_dynamic-update-slice_fusion.1
  38.0 3.7 %collective-permute-start.5 = (bf16[2,192,1024]{2,1,0:T(8,128)(2,1)}, bf16[2,192,1024]{2,1,0:T(8,128)(2,1)}, u32[]{:S(2)}, u32[]{:S(2)}) collective-permute-start(bf16[2,192,1024]{2,1,0:T(8,128)(2,1)} %get-tuple-element.34), channel_id=1, source_target_pairs={{0,96},{32,0},{64,32},{96,64},{1,97},{33,1},{65,33},{97,65},{2,98}... | collective-permute-start | bytes 2359304 | tf_op jit(solution)/shard_map/ppermute | solution.py:162
  43.3 2.2 copy.131
  45.6 13.7 %all-to-all-done.1 = bf16[32,2,128,128]{3,2,1,0:T(8,128)(2,1)S(1)} async-done(((bf16[32,2,128,128]{3,2,1,0:T(8,128)(2,1)}), bf16[32,2,128,128]{3,2,1,0:T(8,128)(2,1)S(1)}, u32[]{:S(2)}, u32[]{:S(2)}) %all-to-all-start.1) | async-done | bytes 2097184 | tf_op jit(solution)/shard_map/all_to_all | solution.py:202
  59.3 4.9 %all-to-all-start = ((bf16[32,2,128,128]{3,2,1,0:T(8,128)(2,1)}), bf16[32,2,128,128]{3,2,1,0:T(8,128)(2,1)}, u32[]{:S(2)}, u32[]{:S(2)}) async-start(bf16[32,2,128,128]{3,2,1,0:T(8,128)(2,1)} %copy.131), calls=%async_computation | async-start | bytes 4194304 | tf_op jit(solution)/shard_map/all_to_all | solution.py:202
  66.7 18.5 %collective-permute-done.4 = bf16[2,192,1024]{2,1,0:T(8,128)(2,1)} collective-permute-done((bf16[2,192,1024]{2,1,0:T(8,128)(2,1)}, bf16[2,192,1024]{2,1,0:T(8,128)(2,1)}, u32[]{:S(2)}, u32[]{:S(2)}) %collective-permute-start.4) | collective-permute-done | bytes 786464 | tf_op jit(solution)/shard_map/ppermute | solution.py:162
  85.2 3.0 %collective-permute-done.3 = bf16[2,192,1024]{2,1,0:T(8,128)(2,1)} collective-permute-done((bf16[2,192,1024]{2,1,0:T(8,128)(2,1)}, bf16[2,192,1024]{2,1,0:T(8,128)(2,1)}, u32[]{:S(2)}, u32[]{:S(2)}) %collective-permute-start.3) | collective-permute-done | bytes 786464 | tf_op jit(solution)/shard_map/ppermute | solution.py:162
  88.2 3.2 %pad_maximum_fusion.1.refs_16_.refs_17_.refs_18_.refs_19_ = bf16[4,2,192,1024]{3,2,1,0:T(8,128)(2,1)} fusion(bf16[1,2,192,1024]{3,2,1,0:T(8,128)(2,1)} %bitcast.21, bf16[1,2,192,1024]{3,2,1,0:T(8,128)(2,1)} %bitcast.19, bf16[1,2,192,1024]{3,2,1,0:T(8,128)(2,1)} %bitcast.17, bf16[1,2,192,1024]{3,2,1,0:T(8,128)(2,1)} %get-tuple-element.33), kind=kLoop, calls=%fused_computation.13 | loop fusion | flops 4718592 | bytes 6291456 | tf_op jit(solution)/shard_map/stack | solution.py:164
  93.1 28.2 %shard_map.85 = (bf16[768,512]{1,0:T(8,128)(2,1)S(1)}, bf16[768,512]{1,0:T(8,128)(2,1)S(1)}, f32[38,128,128]{2,1,0:T(8,128)S(1)}, f32[38,128,128]{2,1,0:T(8,128)}) custom-call(s32[48]{0:T(128)S(1)} %reshape_squeeze.7.src_ref, s32[6]{0:T(128)S(1)} %add_multiply_fusion.base_ref, s32[4]{0:T(128)S(1)} %and_select_fusion.peer_ref, ...), custom_call_target="tpu_custom_call" | custom-call | tf_op jit(solution)/shard_map/pallas_call | solution.py:137
  121.2 2.4 maximum_convert_fusion
  125.4 7.4 %all-to-all-start.2 = ((bf16[32,2,128,128]{3,2,1,0:T(8,128)(2,1)}), bf16[32,2,128,128]{3,2,1,0:T(8,128)(2,1)}, u32[]{:S(2)}, u32[]{:S(2)}) async-start(bf16[32,2,128,128]{3,2,1,0:T(8,128)(2,1)} %copy.88), calls=%async_computation.2 | async-start | bytes 4194304 | tf_op jit(solution)/shard_map/all_to_all | solution.py:212
  133.0 3.4 %pad_maximum_fusion.2.refs_0_.refs_1_.refs_2_.refs_3_.refs_4_.refs_5_.refs_6_.refs_7_.refs_8_.refs_9_.refs_10_.refs_11_.refs_12_.refs_13_.refs_14_.refs_15_ = bf16[38,2,128,128]{3,2,1,0:T(8,128)(2,1)} fusion(bf16[6,2,128,128]{3,2,1,0:T(8,128)(2,1)} %copy-done.11, bf16[32,2,128,128]{3,2,1,0:T(8,128)(2,1)} %all-to-all-done), kind=kLoop, calls=%fused_computation.14 | loop fusion | flops 1245184 | bytes 4980736 | tf_op jit(solution)/shard_map/concatenate | solution.py:203
  136.4 28.1 %shard_map.84 = (bf16[768,512]{1,0:T(8,128)(2,1)S(1)}, bf16[768,512]{1,0:T(8,128)(2,1)S(1)}, f32[38,128,128]{2,1,0:T(8,128)S(1)}, f32[38,128,128]{2,1,0:T(8,128)}) custom-call(s32[48]{0:T(128)S(1)} %reshape_squeeze.6.src_ref, s32[6]{0:T(128)S(1)} %add_multiply_fusion.base_ref, s32[4]{0:T(128)S(1)} %and_select_fusion.peer_ref, ...), custom_call_target="tpu_custom_call" | custom-call | tf_op jit(solution)/shard_map/pallas_call | solution.py:137
  164.6 3.4 %fusion = bf16[32,2,128,128]{3,2,0,1:T(8,128)(2,1)S(1)} fusion(f32[38,1,128,128]{3,2,0,1:T(8,128)} %bitcast.148, f32[38,1,128,128]{3,2,0,1:T(8,128)S(1)} %bitcast.136), kind=kLoop, calls=%fused_computation.10 | loop fusion | flops 1048576 | bytes 7077888 | tf_op jit(solution)/shard_map/convert.2
  169.6 8.1 %all-to-all-start.3 = ((bf16[32,2,128,128]{3,2,1,0:T(8,128)(2,1)}), bf16[32,2,128,128]{3,2,1,0:T(8,128)(2,1)}, u32[]{:S(2)}, u32[]{:S(2)}) async-start(bf16[32,2,128,128]{3,2,1,0:T(8,128)(2,1)} %copy.89), calls=%async_computation.3 | async-start | bytes 4194304 | tf_op jit(solution)/shard_map/all_to_all | solution.py:212
  177.7 2.6 maximum_bitcast_fusion
  184.0 22.7 %all-to-all-done.3 = bf16[32,2,128,128]{3,2,1,0:T(8,128)(2,1)} async-done(((bf16[32,2,128,128]{3,2,1,0:T(8,128)(2,1)}), bf16[32,2,128,128]{3,2,1,0:T(8,128)(2,1)}, u32[]{:S(2)}, u32[]{:S(2)}) %all-to-all-start.3) | async-done | bytes 2097184 | tf_op jit(solution)/shard_map/all_to_all | solution.py:212
  206.8 3.0 %fusion.3 = f32[6,2,128,128]{3,0,2,1:T(8,128)S(1)} fusion(bf16[32,2,128,128]{3,2,1,0:T(8,128)(2,1)} %all-to-all-done.3, bf16[2,32,6]{1,2,0:T(8,128)(2,1)S(1)} %broadcast_select_fusion), kind=kOutput, calls=%fused_computation.18 | convolution fusion | flops 12582912 | bytes 2885632 | tf_op jit(solution)/shard_map/rl,rktd->lktd/dot_general | solution.py:226
  211.0 3.0 %fusion.1 = f32[6,2,128,128]{3,0,2,1:T(8,128)S(1)} fusion(bf16[32,2,128,128]{3,2,1,0:T(8,128)(2,1)} %all-to-all-done.2, bf16[2,32,6]{1,2,0:T(8,128)(2,1)S(1)} %broadcast_select_fusion), kind=kOutput, calls=%fused_computation.16 | convolution fusion | flops 12582912 | bytes 2885632 | tf_op jit(solution)/shard_map/rl,rktd->lktd/dot_general | solution.py:226
  220.4 2.3 collective-permute-start.7
  222.9 2.5 collective-permute-done.10
  225.8 2.4 collective-permute-done.11
  231.0 10.4 %collective-permute-done.6 = bf16[2,192,8,128]{3,2,1,0:T(8,128)(2,1)S(1)} collective-permute-done((bf16[2,192,8,128]{3,2,1,0:T(8,128)(2,1)S(1)}, bf16[2,192,8,128]{3,2,1,0:T(8,128)(2,1)S(1)}, u32[]{:S(2)}, u32[]{:S(2)}) %collective-permute-start.6) | collective-permute-done | bytes 786464 | tf_op jit(solution)/shard_map/ppermute | solution.py:19
  241.7 17.5 %collective-permute-done.7 = bf16[2,192,8,128]{3,2,1,0:T(8,128)(2,1)S(1)} collective-permute-done((bf16[2,192,8,128]{3,2,1,0:T(8,128)(2,1)S(1)}, bf16[2,192,8,128]{3,2,1,0:T(8,128)(2,1)S(1)}, u32[]{:S(2)}, u32[]{:S(2)}) %collective-permute-start.7) | collective-permute-done | bytes 786464 | tf_op jit(solution)/shard_map/ppermute | solution.py:19
  260.9 2.4 dynamic-slice_bitcast_fusion
  (121 shorter events, 33.7 us)
Async XLA Ops:
  2.9 12.2 %collective-permute-start.2 = (bf16[2,192,2,128]{3,1,2,0:T(8,128)(2,1)S(1)}, bf16[2,192,2,128]{3,1,2,0:T(8,128)(2,1)S(1)}, u32[]{:S(2)}, u32[]{:S(2)}) collective-permute-start(bf16[2,192,2,128]{3,1,2,0:T(8,128)(2,1)S(1)} %get-tuple-element.45), channel_id=1, source_target_pairs={{0,32},{32,64},{64,96},{96,0},{1,33},{33,65},{65,97},{97,1},{2,34}... | collective-permute-start | bytes 589832 | tf_op jit(solution)/shard_map/ppermute | solution.py:19
  3.0 12.1 %collective-permute-start.1 = (bf16[2,192,2,128]{3,1,2,0:T(8,128)(2,1)S(1)}, bf16[2,192,2,128]{3,1,2,0:T(8,128)(2,1)S(1)}, u32[]{:S(2)}, u32[]{:S(2)}) collective-permute-start(bf16[2,192,2,128]{3,1,2,0:T(8,128)(2,1)S(1)} %get-tuple-element.46), channel_id=1, source_target_pairs={{0,64},{32,96},{64,0},{96,32},{1,65},{33,97},{65,1},{97,33},{2,66}... | collective-permute-start | bytes 589832 | tf_op jit(solution)/shard_map/ppermute | solution.py:19
  6.2 8.8 %collective-permute-start = (bf16[2,192,2,128]{3,1,2,0:T(8,128)(2,1)S(1)}, bf16[2,192,2,128]{3,1,2,0:T(8,128)(2,1)S(1)}, u32[]{:S(2)}, u32[]{:S(2)}) collective-permute-start(bf16[2,192,2,128]{3,1,2,0:T(8,128)(2,1)S(1)} %get-tuple-element.47), channel_id=1, source_target_pairs={{0,96},{32,0},{64,32},{96,64},{1,97},{33,1},{65,33},{97,65},{2,98}... | collective-permute-start | bytes 589832 | tf_op jit(solution)/shard_map/ppermute | solution.py:19
  15.5 27.1 %copy-start.11 = (bf16[6,2,128,128]{3,2,1,0:T(8,128)(2,1)}, bf16[6,2,128,128]{3,2,1,0:T(8,128)(2,1)S(1)}, u32[]{:S(2)}) copy-start(bf16[6,2,128,128]{3,2,1,0:T(8,128)(2,1)S(1)} %get-tuple-element.43) | copy-start | bytes 1179652
  18.5 40.8 %all-to-all-start.1 = ((bf16[32,2,128,128]{3,2,1,0:T(8,128)(2,1)}), bf16[32,2,128,128]{3,2,1,0:T(8,128)(2,1)S(1)}, u32[]{:S(2)}, u32[]{:S(2)}) async-start(bf16[32,2,128,128]{3,2,1,0:T(8,128)(2,1)} %copy.130), calls=%async_computation.1 | async-start | bytes 4194304 | tf_op jit(solution)/shard_map/all_to_all | solution.py:202
  33.8 2.0 copy-start.10
  38.0 28.7 %collective-permute-start.5 = (bf16[2,192,1024]{2,1,0:T(8,128)(2,1)}, bf16[2,192,1024]{2,1,0:T(8,128)(2,1)}, u32[]{:S(2)}, u32[]{:S(2)}) collective-permute-start(bf16[2,192,1024]{2,1,0:T(8,128)(2,1)} %get-tuple-element.34), channel_id=1, source_target_pairs={{0,96},{32,0},{64,32},{96,64},{1,97},{33,1},{65,33},{97,65},{2,98}... | collective-permute-start | bytes 2359304 | tf_op jit(solution)/shard_map/ppermute | solution.py:162
  41.8 43.4 %collective-permute-start.4 = (bf16[2,192,1024]{2,1,0:T(8,128)(2,1)}, bf16[2,192,1024]{2,1,0:T(8,128)(2,1)}, u32[]{:S(2)}, u32[]{:S(2)}) collective-permute-start(bf16[2,192,1024]{2,1,0:T(8,128)(2,1)} %get-tuple-element.35), channel_id=1, source_target_pairs={{0,64},{32,96},{64,0},{96,32},{1,65},{33,97},{65,1},{97,33},{2,66}... | collective-permute-start | bytes 2359304 | tf_op jit(solution)/shard_map/ppermute | solution.py:162
  42.6 45.6 %collective-permute-start.3 = (bf16[2,192,1024]{2,1,0:T(8,128)(2,1)}, bf16[2,192,1024]{2,1,0:T(8,128)(2,1)}, u32[]{:S(2)}, u32[]{:S(2)}) collective-permute-start(bf16[2,192,1024]{2,1,0:T(8,128)(2,1)} %get-tuple-element.36), channel_id=1, source_target_pairs={{0,32},{32,64},{64,96},{96,0},{1,33},{33,65},{65,97},{97,1},{2,34}... | collective-permute-start | bytes 2359304 | tf_op jit(solution)/shard_map/ppermute | solution.py:162
  59.3 66.1 %all-to-all-start = ((bf16[32,2,128,128]{3,2,1,0:T(8,128)(2,1)}), bf16[32,2,128,128]{3,2,1,0:T(8,128)(2,1)}, u32[]{:S(2)}, u32[]{:S(2)}) async-start(bf16[32,2,128,128]{3,2,1,0:T(8,128)(2,1)} %copy.131), calls=%async_computation | async-start | bytes 4194304 | tf_op jit(solution)/shard_map/all_to_all | solution.py:202
  121.2 2.4 copy-start.2
  125.4 44.1 %all-to-all-start.2 = ((bf16[32,2,128,128]{3,2,1,0:T(8,128)(2,1)}), bf16[32,2,128,128]{3,2,1,0:T(8,128)(2,1)}, u32[]{:S(2)}, u32[]{:S(2)}) async-start(bf16[32,2,128,128]{3,2,1,0:T(8,128)(2,1)} %copy.88), calls=%async_computation.2 | async-start | bytes 4194304 | tf_op jit(solution)/shard_map/all_to_all | solution.py:212
  164.5 3.4 %copy-start = (f32[38,128,128]{2,1,0:T(8,128)}, f32[38,128,128]{2,1,0:T(8,128)S(1)}, u32[]{:S(2)}) copy-start(f32[38,128,128]{2,1,0:T(8,128)S(1)} %get-tuple-element.23) | copy-start | bytes 7471108
  164.5 3.4 %copy-start.3 = (bf16[768,512]{1,0:T(8,128)(2,1)}, bf16[768,512]{1,0:T(8,128)(2,1)S(1)}, u32[]{:S(2)}) copy-start(bf16[768,512]{1,0:T(8,128)(2,1)S(1)} %get-tuple-element.15) | copy-start | bytes 2359300
  164.5 3.4 %copy-start.4 = (bf16[768,512]{1,0:T(8,128)(2,1)}, bf16[768,512]{1,0:T(8,128)(2,1)S(1)}, u32[]{:S(2)}) copy-start(bf16[768,512]{1,0:T(8,128)(2,1)S(1)} %get-tuple-element.17) | copy-start | bytes 2359300
  169.6 37.2 %all-to-all-start.3 = ((bf16[32,2,128,128]{3,2,1,0:T(8,128)(2,1)}), bf16[32,2,128,128]{3,2,1,0:T(8,128)(2,1)}, u32[]{:S(2)}, u32[]{:S(2)}) async-start(bf16[32,2,128,128]{3,2,1,0:T(8,128)(2,1)} %copy.89), calls=%async_computation.3 | async-start | bytes 4194304 | tf_op jit(solution)/shard_map/all_to_all | solution.py:212
  180.7 1.5 copy-start.5
  181.2 1.5 copy-start.7
  206.8 3.0 %copy-start.1 = (f32[38,128,128]{2,1,0:T(8,128)S(1)}, f32[38,128,128]{2,1,0:T(8,128)}, u32[]{:S(2)}) copy-start(f32[38,128,128]{2,1,0:T(8,128)} %copy-done) | copy-start | bytes 7471108
  210.9 3.0 %copy-start.9 = (f32[38,128,128]{2,1,0:T(8,128)S(1)}, f32[38,128,128]{2,1,0:T(8,128)}, u32[]{:S(2)}) copy-start(f32[38,128,128]{2,1,0:T(8,128)} %get-tuple-element.20) | copy-start | bytes 7471108
  213.9 27.5 %slice-start = ((s8[6291456]{0:T(1024)(128)(4,1)}), s8[4194304]{0:T(1024)(128)(4,1)S(1)}, s32[]{:S(2)}) async-start(s8[6291456]{0:T(1024)(128)(4,1)} %bitcast.153), calls=%async_computation.4 | async-start | bytes 8388608
  214.2 4.6 %copy-start.13 = (bf16[2,192,8,128]{3,2,1,0:T(8,128)(2,1)S(1)}, bf16[2,192,8,128]{3,2,1,0:T(8,128)(2,1)}, u32[]{:S(2)}) copy-start(bf16[2,192,8,128]{3,2,1,0:T(8,128)(2,1)} %get-tuple-element.31) | copy-start | bytes 2359300
  214.2 6.2 %copy-start.12 = (bf16[2,192,8,128]{3,2,1,0:T(8,128)(2,1)S(1)}, bf16[2,192,8,128]{3,2,1,0:T(8,128)(2,1)}, u32[]{:S(2)}) copy-start(bf16[2,192,8,128]{3,2,1,0:T(8,128)(2,1)} %get-tuple-element.32) | copy-start | bytes 2359300
  214.2 27.2 %slice-start.1 = ((s8[6291456]{0:T(1024)(128)(4,1)}), s8[2097152]{0:T(1024)(128)(4,1)S(1)}, s32[]{:S(2)}) async-start(s8[6291456]{0:T(1024)(128)(4,1)} %bitcast.153), calls=%async_computation.5 | async-start | bytes 4194304
  215.0 5.4 %collective-permute-start.9 = (bf16[2,192,2,128]{3,2,1,0:T(2,128)(2,1)S(1)}, bf16[2,192,2,128]{3,2,1,0:T(2,128)(2,1)S(1)}, u32[]{:S(2)}, u32[]{:S(2)}) collective-permute-start(bf16[2,192,2,128]{3,2,1,0:T(2,128)(2,1)S(1)} %bitcast.165), channel_id=1, source_target_pairs={{0,96},{32,0},{64,32},{96,64},{1,97},{33,1},{65,33},{97,65},{2,98}... | collective-permute-start | bytes 589832 | tf_op jit(solution)/shard_map/ppermute | solution.py:19
  215.1 10.4 %collective-permute-start.10 = (bf16[2,192,2,128]{3,2,1,0:T(2,128)(2,1)S(1)}, bf16[2,192,2,128]{3,2,1,0:T(2,128)(2,1)S(1)}, u32[]{:S(2)}, u32[]{:S(2)}) collective-permute-start(bf16[2,192,2,128]{3,2,1,0:T(2,128)(2,1)S(1)} %bitcast.164), channel_id=1, source_target_pairs={{0,64},{32,96},{64,0},{96,32},{1,65},{33,97},{65,1},{97,33},{2,66}... | collective-permute-start | bytes 589832 | tf_op jit(solution)/shard_map/ppermute | solution.py:19
  216.9 11.3 %collective-permute-start.11 = (bf16[2,192,2,128]{3,2,1,0:T(2,128)(2,1)S(1)}, bf16[2,192,2,128]{3,2,1,0:T(2,128)(2,1)S(1)}, u32[]{:S(2)}, u32[]{:S(2)}) collective-permute-start(bf16[2,192,2,128]{3,2,1,0:T(2,128)(2,1)S(1)} %bitcast.163), channel_id=1, source_target_pairs={{0,32},{32,64},{64,96},{96,0},{1,33},{33,65},{65,97},{97,1},{2,34}... | collective-permute-start | bytes 589832 | tf_op jit(solution)/shard_map/ppermute | solution.py:19
  216.9 42.6 %collective-permute-start.8 = (bf16[2,192,8,128]{3,2,1,0:T(8,128)(2,1)S(1)}, bf16[2,192,8,128]{3,2,1,0:T(8,128)(2,1)S(1)}, u32[]{:S(2)}, u32[]{:S(2)}) collective-permute-start(bf16[2,192,8,128]{3,2,1,0:T(8,128)(2,1)S(1)} %get-tuple-element.30), channel_id=1, source_target_pairs={{0,32},{32,64},{64,96},{96,0},{1,33},{33,65},{65,97},{97,1},{2,34}... | collective-permute-start | bytes 2359304 | tf_op jit(solution)/shard_map/ppermute | solution.py:19
  218.8 22.6 %collective-permute-start.6 = (bf16[2,192,8,128]{3,2,1,0:T(8,128)(2,1)S(1)}, bf16[2,192,8,128]{3,2,1,0:T(8,128)(2,1)S(1)}, u32[]{:S(2)}, u32[]{:S(2)}) collective-permute-start(bf16[2,192,8,128]{3,2,1,0:T(8,128)(2,1)S(1)} %copy-done.13), channel_id=1, source_target_pairs={{0,96},{32,0},{64,32},{96,64},{1,97},{33,1},{65,33},{97,65},{2,98}... | collective-permute-start | bytes 2359304 | tf_op jit(solution)/shard_map/ppermute | solution.py:19
  220.4 38.8 %collective-permute-start.7 = (bf16[2,192,8,128]{3,2,1,0:T(8,128)(2,1)S(1)}, bf16[2,192,8,128]{3,2,1,0:T(8,128)(2,1)S(1)}, u32[]{:S(2)}, u32[]{:S(2)}) collective-permute-start(bf16[2,192,8,128]{3,2,1,0:T(8,128)(2,1)S(1)} %copy-done.12), channel_id=1, source_target_pairs={{0,64},{32,96},{64,0},{96,32},{1,65},{33,97},{65,1},{97,33},{2,66}... | collective-permute-start | bytes 2359304 | tf_op jit(solution)/shard_map/ppermute | solution.py:19
  231.0 28.7 %copy-start.6 = (bf16[96,8,8,128]{3,2,1,0:T(8,128)(2,1)S(1)}, bf16[96,8,8,128]{3,2,1,0:T(8,128)(2,1)}, u32[]{:S(2)}) copy-start(bf16[96,8,8,128]{3,2,1,0:T(8,128)(2,1)} %copy-done.5) | copy-start | bytes 4718596
  231.0 28.7 %copy-start.8 = (bf16[96,8,8,128]{3,2,1,0:T(8,128)(2,1)S(1)}, bf16[96,8,8,128]{3,2,1,0:T(8,128)(2,1)}, u32[]{:S(2)}) copy-start(bf16[96,8,8,128]{3,2,1,0:T(8,128)(2,1)} %copy-done.7) | copy-start | bytes 4718596

commit v8 on v7

--- a/solution.py
+++ b/solution.py
@@ -194,7 +194,7 @@
     key_pos = key_pos.reshape(groups, block_ids, 1, TOPK * BLOCK_TOKENS)
     query_base = (rank * block_ids + block_range) * BLOCK_TOKENS
 
-    outs, query_grads, backs, locals_ = [], [], [], []
+    outs, backs, locals_ = [], [], []
     for g in range(groups):
         send = jnp.einsum(
             "rb,bktd->rktd", pick_send[g], kv_local[g], preferred_element_type=jnp.float32
@@ -204,23 +204,18 @@
         o_g, dq_g, dk_acc, dv_acc = attend(
             slot_src[g].reshape(-1), query_base, peer_of, table, qg_pieces, key_pos[g], g, groups
         )
-        outs.append(o_g)
-        query_grads.append(dq_g)
+        size_ = lax.axis_size("head")
+        pair = jnp.stack([o_g, dq_g]).reshape(2, size_, run_len // size_, o_g.shape[-1])
+        outs.append(exchange(pair, 1, 1))
         acc = jnp.stack([dk_acc, dv_acc], axis=1)
         remote = acc[:peers].astype(jnp.bfloat16)
         local = acc[peers:].astype(jnp.bfloat16)
         backs.append(lax.all_to_all(remote, "blk", split_axis=0, concat_axis=0, tiled=True))
         locals_.append(local)
 
-    def heads_layout(parts):
-        return jnp.concatenate(parts, axis=1).reshape(run_len, head_count, head_width)
-
     def group_layout(parts):
         return jnp.stack(parts, axis=2).reshape(run_len, groups, head_width)
 
-    attn_all, query_grad_all, backs[-1] = lax.optimization_barrier(
-        (heads_layout(outs), heads_layout(query_grads), backs[-1])
-    )
     key_grads, value_grads = [], []
     for g in range(groups):
         total = locals_[g].astype(jnp.float32) + jnp.einsum(
@@ -229,7 +224,9 @@
         total = total.astype(jnp.bfloat16)
         key_grads.append(total[:, 0])
         value_grads.append(total[:, 1])
-    attn_out, grad_queries = from_heads(attn_all, query_grad_all)
+    both = jnp.transpose(jnp.stack(outs), (1, 3, 2, 0, 4))
+    both = both.reshape(2, run_len // size, size * head_count, head_width)
+    attn_out, grad_queries = both[0], both[1]
     key_gradient, value_gradient = from_heads(group_layout(key_grads), group_layout(value_grads))
     return attn_out, grad_queries, key_gradient, value_gradient
 

time: 267 us -> 276 us (1.034)
  the two profiles are of different devices: /device:TPU:0 before, /device:TPU:42 now
where the time goes in v8:
time: 276 us; the launch traced here: 271 us
  waiting for transfers between devices  74.7 us (27%)
  starting transfers between devices  61 us (22%)
  Pallas kernels  55.4 us (20%)
  local copies, waits for them, and re-layouts  42.7 us (15%)
  other arithmetic  28 us (10%)
  matrix products  7.5 us (3%)
    pallas_call x2, Pallas kernels, attend(): pl.pallas_call(attention_kernel, grid_spec=grid_spec, out_shape=out_shape...  55.4 us
    ppermute x12, waiting for transfers between devices, exchange(): lax.ppermute(piece, 'head', [(i, (i + k) % size) for i in range(size)])  45.7 us
    ppermute x12, starting transfers between devices, exchange(): lax.ppermute(piece, 'head', [(i, (i + k) % size) for i in range(size)])  22.3 us
    ppermute x3, waiting for transfers between devices, on_device(): lax.ppermute(piece, 'head', [(i, (i + k) % size) for i in range(size)])  21.8 us
    all_to_all x2, starting transfers between devices, on_device(): recv = lax.all_to_all(send, 'blk', split_axis=0, concat_axis=0, tiled=True)  17 us
    all_to_all x2, starting transfers between devices, on_device(): lax.all_to_all(remote, 'blk', split_axis=0, concat_axis=0, tiled=True)  16.6 us
    slice x3, local copies, waits for them, and re-layouts, on_device(): attn_out, grad_queries = (both[0], both[1])  8.36 us
    squeeze x2, local copies, waits for them, and re-layouts, on_device(): attn_out, grad_queries = (both[0], both[1])  7.47 us
  transfers between devices with their start and end apart: 19, of which 11 were waited for; matrix products, arithmetic and copies ran while one was open for 24% of the time, Pallas kernels for 20%

profile of v8, /device:TPU:42, one launch (start us, length us, event | category | flops | bytes accessed | tf_op | source)
XLA Modules:
  0.0 270.6 jit_solution(15911458110141276034)
XLA Ops:
  9.7 6.0 %collective-permute-done.1 = bf16[2,192,2,128]{3,1,2,0:T(8,128)(2,1)S(1)} collective-permute-done((bf16[2,192,2,128]{3,1,2,0:T(8,128)(2,1)S(1)}, bf16[2,192,2,128]{3,1,2,0:T(8,128)(2,1)S(1)}, u32[]{:S(2)}, u32[]{:S(2)}) %collective-permute-start.1) | collective-permute-done | bytes 196640 | tf_op jit(solution)/shard_map/ppermute | solution.py:19
  19.3 9.0 %all-to-all-start = ((bf16[32,2,128,128]{3,2,1,0:T(8,128)(2,1)}), bf16[32,2,128,128]{3,2,1,0:T(8,128)(2,1)S(1)}, u32[]{:S(2)}, u32[]{:S(2)}) async-start(bf16[32,2,128,128]{3,2,1,0:T(8,128)(2,1)} %copy.157), calls=%async_computation | async-start | bytes 4194304 | tf_op jit(solution)/shard_map/all_to_all | solution.py:202
  28.3 3.5 %stack.152 = bf16[1,192,4,1024]{3,2,1,0:T(4,128)(2,1)} reshape(bf16[192,32,128]{2,1,0:T(8,128)(2,1)} %param.7) | data formatting | bytes 3145728 | tf_op jit(solution)/shard_map/stack | solution.py:156
  31.8 3.5 %stack.153 = bf16[1,192,4,1024]{3,2,1,0:T(4,128)(2,1)} reshape(bf16[192,32,128]{2,1,0:T(8,128)(2,1)} %param.11) | data formatting | bytes 3145728 | tf_op jit(solution)/shard_map/stack | solution.py:156
  41.7 2.9 %collective-permute-start.5 = (bf16[2,192,1024]{2,1,0:T(8,128)(2,1)}, bf16[2,192,1024]{2,1,0:T(8,128)(2,1)}, u32[]{:S(2)}, u32[]{:S(2)}) collective-permute-start(bf16[2,192,1024]{2,1,0:T(8,128)(2,1)} %get-tuple-element.26), channel_id=1, source_target_pairs={{0,96},{32,0},{64,32},{96,64},{1,97},{33,1},{65,33},{97,65},{2,98}... | collective-permute-start | bytes 2359304 | tf_op jit(solution)/shard_map/ppermute | solution.py:162
  47.6 7.1 %all-to-all-done = bf16[32,2,128,128]{3,2,1,0:T(8,128)(2,1)S(1)} async-done(((bf16[32,2,128,128]{3,2,1,0:T(8,128)(2,1)}), bf16[32,2,128,128]{3,2,1,0:T(8,128)(2,1)S(1)}, u32[]{:S(2)}, u32[]{:S(2)}) %all-to-all-start) | async-done | bytes 2097184 | tf_op jit(solution)/shard_map/all_to_all | solution.py:202
  54.7 8.0 %all-to-all-start.1 = ((bf16[32,2,128,128]{3,2,1,0:T(8,128)(2,1)}), bf16[32,2,128,128]{3,2,1,0:T(8,128)(2,1)}, u32[]{:S(2)}, u32[]{:S(2)}) async-start(bf16[32,2,128,128]{3,2,1,0:T(8,128)(2,1)} %copy.156), calls=%async_computation.1 | async-start | bytes 4194304 | tf_op jit(solution)/shard_map/all_to_all | solution.py:202
  64.6 7.3 %collective-permute-done.4 = bf16[2,192,1024]{2,1,0:T(8,128)(2,1)} collective-permute-done((bf16[2,192,1024]{2,1,0:T(8,128)(2,1)}, bf16[2,192,1024]{2,1,0:T(8,128)(2,1)}, u32[]{:S(2)}, u32[]{:S(2)}) %collective-permute-start.4) | collective-permute-done | bytes 786464 | tf_op jit(solution)/shard_map/ppermute | solution.py:162
  71.9 14.4 %collective-permute-done.5 = bf16[2,192,1024]{2,1,0:T(8,128)(2,1)} collective-permute-done((bf16[2,192,1024]{2,1,0:T(8,128)(2,1)}, bf16[2,192,1024]{2,1,0:T(8,128)(2,1)}, u32[]{:S(2)}, u32[]{:S(2)}) %collective-permute-start.5) | collective-permute-done | bytes 786464 | tf_op jit(solution)/shard_map/ppermute | solution.py:162
  86.3 3.3 %pad_maximum_fusion.2.refs_16_.refs_17_.refs_18_.refs_19_ = bf16[4,2,192,1024]{3,2,1,0:T(8,128)(2,1)} fusion(bf16[1,2,192,1024]{3,2,1,0:T(8,128)(2,1)} %bitcast.21, bf16[1,2,192,1024]{3,2,1,0:T(8,128)(2,1)} %bitcast.19, bf16[1,2,192,1024]{3,2,1,0:T(8,128)(2,1)} %bitcast.17, bf16[1,2,192,1024]{3,2,1,0:T(8,128)(2,1)} %get-tuple-element.25), kind=kLoop, calls=%fused_computation.6 | loop fusion | flops 4718592 | bytes 6291456 | tf_op jit(solution)/shard_map/stack | solution.py:164
  91.3 27.7 %shard_map.84 = (bf16[768,512]{1,0:T(8,128)(2,1)S(1)}, bf16[768,512]{1,0:T(8,128)(2,1)S(1)}, f32[38,128,128]{2,1,0:T(8,128)S(1)}, f32[38,128,128]{2,1,0:T(8,128)}) custom-call(s32[48]{0:T(128)S(1)} %reshape_squeeze.6.src_ref, s32[6]{0:T(128)S(1)} %add_multiply_fusion.base_ref, s32[4]{0:T(128)S(1)} %and_select_fusion.peer_ref, ...), custom_call_target="tpu_custom_call" | custom-call | tf_op jit(solution)/shard_map/pallas_call | solution.py:137
  119.0 2.2 fusion.1
  122.8 8.2 %all-to-all-start.2 = ((bf16[32,2,128,128]{3,2,1,0:T(8,128)(2,1)}), bf16[32,2,128,128]{3,2,1,0:T(8,128)(2,1)}, u32[]{:S(2)}, u32[]{:S(2)}) async-start(bf16[32,2,128,128]{3,2,1,0:T(8,128)(2,1)} %copy.116), calls=%async_computation.2 | async-start | bytes 4194304 | tf_op jit(solution)/shard_map/all_to_all | solution.py:213
  131.2 2.5 fusion.36
  133.7 3.0 %collective-permute-start.6 = (bf16[2,192,512]{2,1,0:T(8,128)(2,1)}, bf16[2,192,512]{2,1,0:T(8,128)(2,1)}, u32[]{:S(2)}, u32[]{:S(2)}) collective-permute-start(bf16[2,192,512]{2,1,0:T(8,128)(2,1)} %get-tuple-element.33), channel_id=1, source_target_pairs={{0,96},{32,0},{64,32},{96,64},{1,97},{33,1},{65,33},{97,65},{2,98}... | collective-permute-start | bytes 1179656 | tf_op jit(solution)/shard_map/ppermute | solution.py:19
  138.8 3.3 %pad_maximum_fusion.4.refs_0_.refs_1_.refs_2_.refs_3_.refs_4_.refs_5_.refs_6_.refs_7_.refs_8_.refs_9_.refs_10_.refs_11_.refs_12_.refs_13_.refs_14_.refs_15_ = bf16[38,2,128,128]{3,2,1,0:T(8,128)(2,1)} fusion(bf16[6,2,128,128]{3,2,1,0:T(8,128)(2,1)S(1)} %copy-done.6, bf16[32,2,128,128]{3,2,1,0:T(8,128)(2,1)} %all-to-all-done.1), kind=kLoop, calls=%fused_computation.25 | loop fusion | flops 1245184 | bytes 4980736 | tf_op jit(solution)/shard_map/concatenate | solution.py:203
  142.1 27.7 %shard_map.85 = (bf16[768,512]{1,0:T(8,128)(2,1)S(1)}, bf16[768,512]{1,0:T(8,128)(2,1)S(1)}, f32[38,128,128]{2,1,0:T(8,128)S(1)}, f32[38,128,128]{2,1,0:T(8,128)}) custom-call(s32[48]{0:T(128)S(1)} %reshape_squeeze.7.src_ref, s32[6]{0:T(128)S(1)} %add_multiply_fusion.base_ref, s32[4]{0:T(128)S(1)} %and_select_fusion.peer_ref, ...), custom_call_target="tpu_custom_call" | custom-call | tf_op jit(solution)/shard_map/pallas_call | solution.py:137
  169.8 2.8 %fusion = bf16[32,2,128,128]{3,2,0,1:T(8,128)(2,1)S(1)} fusion(f32[38,1,128,128]{3,2,0,1:T(8,128)} %bitcast.141, f32[38,1,128,128]{3,2,0,1:T(8,128)S(1)} %bitcast.131), kind=kLoop, calls=%fused_computation.1 | loop fusion | flops 1048576 | bytes 7077888 | tf_op jit(solution)/shard_map/convert.1
  175.4 3.2 %collective-permute-start.9 = (bf16[2,192,512]{2,1,0:T(8,128)(2,1)}, bf16[2,192,512]{2,1,0:T(8,128)(2,1)}, u32[]{:S(2)}, u32[]{:S(2)}) collective-permute-start(bf16[2,192,512]{2,1,0:T(8,128)(2,1)} %get-tuple-element.37), channel_id=1, source_target_pairs={{0,96},{32,0},{64,32},{96,64},{1,97},{33,1},{65,33},{97,65},{2,98}... | collective-permute-start | bytes 1179656 | tf_op jit(solution)/shard_map/ppermute | solution.py:19
  178.6 9.9 %collective-permute-start.10 = (bf16[2,192,512]{2,1,0:T(8,128)(2,1)}, bf16[2,192,512]{2,1,0:T(8,128)(2,1)}, u32[]{:S(2)}, u32[]{:S(2)}) collective-permute-start(bf16[2,192,512]{2,1,0:T(8,128)(2,1)} %get-tuple-element.38), channel_id=1, source_target_pairs={{0,64},{32,96},{64,0},{96,32},{1,65},{33,97},{65,1},{97,33},{2,66}... | collective-permute-start | bytes 1179656 | tf_op jit(solution)/shard_map/ppermute | solution.py:19
  188.5 8.4 %all-to-all-start.3 = ((bf16[32,2,128,128]{3,2,1,0:T(8,128)(2,1)}), bf16[32,2,128,128]{3,2,1,0:T(8,128)(2,1)}, u32[]{:S(2)}, u32[]{:S(2)}) async-start(bf16[32,2,128,128]{3,2,1,0:T(8,128)(2,1)} %copy.119), calls=%async_computation.3 | async-start | bytes 4194304 | tf_op jit(solution)/shard_map/all_to_all | solution.py:213
  197.0 3.3 %fusion.18 = bf16[1,2,4,192,512]{4,3,2,1,0:T(8,128)(2,1)S(1)} fusion(s32[]{:T(128)S(6)} %select_n.177, bf16[2,1,192,512]{3,2,1,0:T(8,128)(2,1)S(1)} %copy-done.7, bf16[2,1,192,512]{3,2,1,0:T(8,128)(2,1)} %bitcast.26, bf16[2,1,192,512]{3,2,1,0:T(8,128)(2,1)} %bitcast.28, bf16[2,1,192,512]{3,2,1,0:T(8,128)(2,1)} %bitcast.30), kind=kLoop, calls=%fused_computation.58 | loop fusion | flops 5505024 | bytes 3145732 | tf_op jit(solution)/shard_map/stack | solution.py:227
  200.3 29.0 %collective-permute-done.11 = bf16[2,192,512]{2,1,0:T(8,128)(2,1)S(1)} collective-permute-done((bf16[2,192,512]{2,1,0:T(8,128)(2,1)S(1)}, bf16[2,192,512]{2,1,0:T(8,128)(2,1)S(1)}, u32[]{:S(2)}, u32[]{:S(2)}) %collective-permute-start.11) | collective-permute-done | bytes 393248 | tf_op jit(solution)/shard_map/ppermute | solution.py:19
  229.3 3.0 %fusion.10 = bf16[1,2,4,192,512]{4,3,2,1,0:T(8,128)(2,1)S(1)} fusion(s32[]{:T(128)S(6)} %select_n.177, bf16[2,1,192,512]{3,2,1,0:T(8,128)(2,1)S(1)} %copy-done.8, bf16[2,1,192,512]{3,2,1,0:T(8,128)(2,1)} %bitcast.40, bf16[2,1,192,512]{3,2,1,0:T(8,128)(2,1)} %bitcast.42, bf16[2,1,192,512]{3,2,1,0:T(8,128)(2,1)S(1)} %bitcast.154), kind=kLoop, calls=%fused_computation.50 | loop fusion | flops 5505024 | bytes 3145732 | tf_op jit(solution)/shard_map/stack | solution.py:227
  234.1 2.8 %copy.114 = bf16[1,192,4,2,512]{4,3,2,1,0:T(2,128)(2,1)} copy(bf16[1,192,4,2,512]{4,1,2,0,3:T(8,128)(2,1)S(1)} %get-tuple-element.24) | data formatting | bytes 3145728 | tf_op jit(solution)/shard_map/slice | solution.py:229
  236.8 3.7 %squeeze.110 = bf16[192,32,128]{2,1,0:T(8,128)(2,1)} reshape(bf16[1,192,4,2,512]{4,3,2,1,0:T(2,128)(2,1)} %copy.114) | data formatting | bytes 3145728 | tf_op jit(solution)/shard_map/squeeze | solution.py:229
  240.6 4.2 %copy.115 = bf16[1,192,4,2,512]{4,3,2,1,0:T(2,128)(2,1)} copy(bf16[1,192,4,2,512]{4,1,2,0,3:T(8,128)(2,1)} %get-tuple-element.23) | data formatting | bytes 3145728 | tf_op jit(solution)/shard_map/slice | solution.py:229
  244.7 3.7 %squeeze.111 = bf16[192,32,128]{2,1,0:T(8,128)(2,1)} reshape(bf16[1,192,4,2,512]{4,3,2,1,0:T(2,128)(2,1)} %copy.115) | data formatting | bytes 3145728 | tf_op jit(solution)/shard_map/squeeze | solution.py:229
  248.5 3.0 %fusion.4 = f32[6,2,128,128]{3,0,2,1:T(8,128)S(1)} fusion(bf16[32,2,128,128]{3,2,1,0:T(8,128)(2,1)} %all-to-all-done.2, bf16[2,32,6]{1,2,0:T(8,128)(2,1)S(1)} %broadcast_select_fusion), kind=kOutput, calls=%fused_computation.44 | convolution fusion | flops 12582912 | bytes 2885632 | tf_op jit(solution)/shard_map/rl,rktd->lktd/dot_general | solution.py:221
  251.7 3.0 %fusion.2 = f32[6,2,128,128]{3,0,2,1:T(8,128)S(1)} fusion(bf16[32,2,128,128]{3,2,1,0:T(8,128)(2,1)} %all-to-all-done.3, bf16[2,32,6]{1,2,0:T(8,128)(2,1)S(1)} %broadcast_select_fusion), kind=kOutput, calls=%fused_computation.42 | convolution fusion | flops 12582912 | bytes 2885632 | tf_op jit(solution)/shard_map/rl,rktd->lktd/dot_general | solution.py:221
  257.8 3.7 %collective-permute-done.12 = bf16[2,192,2,128]{3,2,1,0:T(2,128)(2,1)S(1)} collective-permute-done((bf16[2,192,2,128]{3,2,1,0:T(2,128)(2,1)S(1)}, bf16[2,192,2,128]{3,2,1,0:T(2,128)(2,1)S(1)}, u32[]{:S(2)}, u32[]{:S(2)}) %collective-permute-start.12) | collective-permute-done | bytes 196640 | tf_op jit(solution)/shard_map/ppermute | solution.py:19
  261.8 4.0 %collective-permute-done.13 = bf16[2,192,2,128]{3,2,1,0:T(2,128)(2,1)S(1)} collective-permute-done((bf16[2,192,2,128]{3,2,1,0:T(2,128)(2,1)S(1)}, bf16[2,192,2,128]{3,2,1,0:T(2,128)(2,1)S(1)}, u32[]{:S(2)}, u32[]{:S(2)}) %collective-permute-start.13) | collective-permute-done | bytes 196640 | tf_op jit(solution)/shard_map/ppermute | solution.py:19
  (110 shorter events, 41.8 us)
Async XLA Ops:
  2.9 6.8 %collective-permute-start = (bf16[2,192,2,128]{3,1,2,0:T(8,128)(2,1)S(1)}, bf16[2,192,2,128]{3,1,2,0:T(8,128)(2,1)S(1)}, u32[]{:S(2)}, u32[]{:S(2)}) collective-permute-start(bf16[2,192,2,128]{3,1,2,0:T(8,128)(2,1)S(1)} %get-tuple-element.47), channel_id=1, source_target_pairs={{0,96},{32,0},{64,32},{96,64},{1,97},{33,1},{65,33},{97,65},{2,98}... | collective-permute-start | bytes 589832 | tf_op jit(solution)/shard_map/ppermute | solution.py:19
  4.5 11.3 %collective-permute-start.1 = (bf16[2,192,2,128]{3,1,2,0:T(8,128)(2,1)S(1)}, bf16[2,192,2,128]{3,1,2,0:T(8,128)(2,1)S(1)}, u32[]{:S(2)}, u32[]{:S(2)}) collective-permute-start(bf16[2,192,2,128]{3,1,2,0:T(8,128)(2,1)S(1)} %get-tuple-element.46), channel_id=1, source_target_pairs={{0,64},{32,96},{64,0},{96,32},{1,65},{33,97},{65,1},{97,33},{2,66}... | collective-permute-start | bytes 589832 | tf_op jit(solution)/shard_map/ppermute | solution.py:19
  5.9 10.0 %collective-permute-start.2 = (bf16[2,192,2,128]{3,1,2,0:T(8,128)(2,1)S(1)}, bf16[2,192,2,128]{3,1,2,0:T(8,128)(2,1)S(1)}, u32[]{:S(2)}, u32[]{:S(2)}) collective-permute-start(bf16[2,192,2,128]{3,1,2,0:T(8,128)(2,1)S(1)} %get-tuple-element.45), channel_id=1, source_target_pairs={{0,32},{32,64},{64,96},{96,0},{1,33},{33,65},{65,97},{97,1},{2,34}... | collective-permute-start | bytes 589832 | tf_op jit(solution)/shard_map/ppermute | solution.py:19
  16.3 28.4 %copy-start.5 = (bf16[6,2,128,128]{3,2,1,0:T(8,128)(2,1)}, bf16[6,2,128,128]{3,2,1,0:T(8,128)(2,1)S(1)}, u32[]{:S(2)}) copy-start(bf16[6,2,128,128]{3,2,1,0:T(8,128)(2,1)S(1)} %get-tuple-element.44) | copy-start | bytes 1179652
  19.3 35.5 %all-to-all-start = ((bf16[32,2,128,128]{3,2,1,0:T(8,128)(2,1)}), bf16[32,2,128,128]{3,2,1,0:T(8,128)(2,1)S(1)}, u32[]{:S(2)}, u32[]{:S(2)}) async-start(bf16[32,2,128,128]{3,2,1,0:T(8,128)(2,1)} %copy.157), calls=%async_computation | async-start | bytes 4194304 | tf_op jit(solution)/shard_map/all_to_all | solution.py:202
  35.3 2.0 copy-start.4
  39.5 25.1 %collective-permute-start.3 = (bf16[2,192,1024]{2,1,0:T(8,128)(2,1)}, bf16[2,192,1024]{2,1,0:T(8,128)(2,1)}, u32[]{:S(2)}, u32[]{:S(2)}) collective-permute-start(bf16[2,192,1024]{2,1,0:T(8,128)(2,1)} %get-tuple-element.28), channel_id=1, source_target_pairs={{0,32},{32,64},{64,96},{96,0},{1,33},{33,65},{65,97},{97,1},{2,34}... | collective-permute-start | bytes 2359304 | tf_op jit(solution)/shard_map/ppermute | solution.py:162
  39.5 32.3 %collective-permute-start.4 = (bf16[2,192,1024]{2,1,0:T(8,128)(2,1)}, bf16[2,192,1024]{2,1,0:T(8,128)(2,1)}, u32[]{:S(2)}, u32[]{:S(2)}) collective-permute-start(bf16[2,192,1024]{2,1,0:T(8,128)(2,1)} %get-tuple-element.27), channel_id=1, source_target_pairs={{0,64},{32,96},{64,0},{96,32},{1,65},{33,97},{65,1},{97,33},{2,66}... | collective-permute-start | bytes 2359304 | tf_op jit(solution)/shard_map/ppermute | solution.py:162
  41.7 44.6 %collective-permute-start.5 = (bf16[2,192,1024]{2,1,0:T(8,128)(2,1)}, bf16[2,192,1024]{2,1,0:T(8,128)(2,1)}, u32[]{:S(2)}, u32[]{:S(2)}) collective-permute-start(bf16[2,192,1024]{2,1,0:T(8,128)(2,1)} %get-tuple-element.26), channel_id=1, source_target_pairs={{0,96},{32,0},{64,32},{96,64},{1,97},{33,1},{65,33},{97,65},{2,98}... | collective-permute-start | bytes 2359304 | tf_op jit(solution)/shard_map/ppermute | solution.py:162
  54.7 68.1 %all-to-all-start.1 = ((bf16[32,2,128,128]{3,2,1,0:T(8,128)(2,1)}), bf16[32,2,128,128]{3,2,1,0:T(8,128)(2,1)}, u32[]{:S(2)}, u32[]{:S(2)}) async-start(bf16[32,2,128,128]{3,2,1,0:T(8,128)(2,1)} %copy.156), calls=%async_computation.1 | async-start | bytes 4194304 | tf_op jit(solution)/shard_map/all_to_all | solution.py:202
  119.0 2.3 copy-start.2
  122.8 65.7 %all-to-all-start.2 = ((bf16[32,2,128,128]{3,2,1,0:T(8,128)(2,1)}), bf16[32,2,128,128]{3,2,1,0:T(8,128)(2,1)}, u32[]{:S(2)}, u32[]{:S(2)}) async-start(bf16[32,2,128,128]{3,2,1,0:T(8,128)(2,1)} %copy.116), calls=%async_computation.2 | async-start | bytes 4194304 | tf_op jit(solution)/shard_map/all_to_all | solution.py:213
  131.2 7.6 %copy-start.6 = (bf16[6,2,128,128]{3,2,1,0:T(8,128)(2,1)S(1)}, bf16[6,2,128,128]{3,2,1,0:T(8,128)(2,1)}, u32[]{:S(2)}) copy-start(bf16[6,2,128,128]{3,2,1,0:T(8,128)(2,1)} %copy-done.5) | copy-start | bytes 1179652
  133.7 63.2 %collective-permute-start.6 = (bf16[2,192,512]{2,1,0:T(8,128)(2,1)}, bf16[2,192,512]{2,1,0:T(8,128)(2,1)}, u32[]{:S(2)}, u32[]{:S(2)}) collective-permute-start(bf16[2,192,512]{2,1,0:T(8,128)(2,1)} %get-tuple-element.33), channel_id=1, source_target_pairs={{0,96},{32,0},{64,32},{96,64},{1,97},{33,1},{65,33},{97,65},{2,98}... | collective-permute-start | bytes 1179656 | tf_op jit(solution)/shard_map/ppermute | solution.py:19
  136.7 60.3 %collective-permute-start.7 = (bf16[2,192,512]{2,1,0:T(8,128)(2,1)}, bf16[2,192,512]{2,1,0:T(8,128)(2,1)}, u32[]{:S(2)}, u32[]{:S(2)}) collective-permute-start(bf16[2,192,512]{2,1,0:T(8,128)(2,1)} %get-tuple-element.34), channel_id=1, source_target_pairs={{0,64},{32,96},{64,0},{96,32},{1,65},{33,97},{65,1},{97,33},{2,66}... | collective-permute-start | bytes 1179656 | tf_op jit(solution)/shard_map/ppermute | solution.py:19
  138.8 58.2 %collective-permute-start.8 = (bf16[2,192,512]{2,1,0:T(8,128)(2,1)}, bf16[2,192,512]{2,1,0:T(8,128)(2,1)}, u32[]{:S(2)}, u32[]{:S(2)}) collective-permute-start(bf16[2,192,512]{2,1,0:T(8,128)(2,1)} %get-tuple-element.31), channel_id=1, source_target_pairs={{0,32},{32,64},{64,96},{96,0},{1,33},{33,65},{65,97},{97,1},{2,34}... | collective-permute-start | bytes 1179656 | tf_op jit(solution)/shard_map/ppermute | solution.py:19
  169.8 2.9 %copy-start = (f32[38,128,128]{2,1,0:T(8,128)}, f32[38,128,128]{2,1,0:T(8,128)S(1)}, u32[]{:S(2)}) copy-start(f32[38,128,128]{2,1,0:T(8,128)S(1)} %get-tuple-element.19) | copy-start | bytes 7471108
  175.4 24.9 %collective-permute-start.9 = (bf16[2,192,512]{2,1,0:T(8,128)(2,1)}, bf16[2,192,512]{2,1,0:T(8,128)(2,1)}, u32[]{:S(2)}, u32[]{:S(2)}) collective-permute-start(bf16[2,192,512]{2,1,0:T(8,128)(2,1)} %get-tuple-element.37), channel_id=1, source_target_pairs={{0,96},{32,0},{64,32},{96,64},{1,97},{33,1},{65,33},{97,65},{2,98}... | collective-permute-start | bytes 1179656 | tf_op jit(solution)/shard_map/ppermute | solution.py:19
  178.6 18.3 %copy-start.9 = (bf16[2,192,512]{2,1,0:T(8,128)(2,1)S(1)}, bf16[2,192,512]{2,1,0:T(8,128)(2,1)}, u32[]{:S(2)}) copy-start(bf16[2,192,512]{2,1,0:T(8,128)(2,1)} %get-tuple-element.35) | copy-start | bytes 1179652
  178.6 18.4 %copy-start.7 = (bf16[2,1,192,512]{3,2,1,0:T(8,128)(2,1)S(1)}, bf16[2,1,192,512]{3,2,1,0:T(8,128)(2,1)}, u32[]{:S(2)}) copy-start(bf16[2,1,192,512]{3,2,1,0:T(8,128)(2,1)} %get-tuple-element.32) | copy-start | bytes 1179652
  178.6 21.7 %collective-permute-start.10 = (bf16[2,192,512]{2,1,0:T(8,128)(2,1)}, bf16[2,192,512]{2,1,0:T(8,128)(2,1)}, u32[]{:S(2)}, u32[]{:S(2)}) collective-permute-start(bf16[2,192,512]{2,1,0:T(8,128)(2,1)} %get-tuple-element.38), channel_id=1, source_target_pairs={{0,64},{32,96},{64,0},{96,32},{1,65},{33,97},{65,1},{97,33},{2,66}... | collective-permute-start | bytes 1179656 | tf_op jit(solution)/shard_map/ppermute | solution.py:19
  188.5 63.2 %all-to-all-start.3 = ((bf16[32,2,128,128]{3,2,1,0:T(8,128)(2,1)}), bf16[32,2,128,128]{3,2,1,0:T(8,128)(2,1)}, u32[]{:S(2)}, u32[]{:S(2)}) async-start(bf16[32,2,128,128]{3,2,1,0:T(8,128)(2,1)} %copy.119), calls=%async_computation.3 | async-start | bytes 4194304 | tf_op jit(solution)/shard_map/all_to_all | solution.py:213
  196.9 32.4 %collective-permute-start.11 = (bf16[2,192,512]{2,1,0:T(8,128)(2,1)S(1)}, bf16[2,192,512]{2,1,0:T(8,128)(2,1)S(1)}, u32[]{:S(2)}, u32[]{:S(2)}) collective-permute-start(bf16[2,192,512]{2,1,0:T(8,128)(2,1)S(1)} %copy-done.9), channel_id=1, source_target_pairs={{0,32},{32,64},{64,96},{96,0},{1,33},{33,65},{65,97},{97,1},{2,34}... | collective-permute-start | bytes 1179656 | tf_op jit(solution)/shard_map/ppermute | solution.py:19
  197.0 32.3 %copy-start.8 = (bf16[2,1,192,512]{3,2,1,0:T(8,128)(2,1)S(1)}, bf16[2,1,192,512]{3,2,1,0:T(8,128)(2,1)}, u32[]{:S(2)}) copy-start(bf16[2,1,192,512]{3,2,1,0:T(8,128)(2,1)} %get-tuple-element.36) | copy-start | bytes 1179652
  248.5 3.0 %copy-start.3 = (f32[38,128,128]{2,1,0:T(8,128)S(1)}, f32[38,128,128]{2,1,0:T(8,128)}, u32[]{:S(2)}) copy-start(f32[38,128,128]{2,1,0:T(8,128)} %get-tuple-element.18) | copy-start | bytes 7471108
  251.7 3.0 %copy-start.1 = (f32[38,128,128]{2,1,0:T(8,128)S(1)}, f32[38,128,128]{2,1,0:T(8,128)}, u32[]{:S(2)}) copy-start(f32[38,128,128]{2,1,0:T(8,128)} %copy-done) | copy-start | bytes 7471108
  256.3 5.3 %collective-permute-start.12 = (bf16[2,192,2,128]{3,2,1,0:T(2,128)(2,1)S(1)}, bf16[2,192,2,128]{3,2,1,0:T(2,128)(2,1)S(1)}, u32[]{:S(2)}, u32[]{:S(2)}) collective-permute-start(bf16[2,192,2,128]{3,2,1,0:T(2,128)(2,1)S(1)} %bitcast.155), channel_id=1, source_target_pairs={{0,96},{32,0},{64,32},{96,64},{1,97},{33,1},{65,33},{97,65},{2,98}... | collective-permute-start | bytes 589832 | tf_op jit(solution)/shard_map/ppermute | solution.py:19
  256.5 9.3 %collective-permute-start.13 = (bf16[2,192,2,128]{3,2,1,0:T(2,128)(2,1)S(1)}, bf16[2,192,2,128]{3,2,1,0:T(2,128)(2,1)S(1)}, u32[]{:S(2)}, u32[]{:S(2)}) collective-permute-start(bf16[2,192,2,128]{3,2,1,0:T(2,128)(2,1)S(1)} %bitcast.156), channel_id=1, source_target_pairs={{0,64},{32,96},{64,0},{96,32},{1,65},{33,97},{65,1},{97,33},{2,66}... | collective-permute-start | bytes 589832 | tf_op jit(solution)/shard_map/ppermute | solution.py:19
  256.9 10.7 %collective-permute-start.14 = (bf16[2,192,2,128]{3,2,1,0:T(2,128)(2,1)S(1)}, bf16[2,192,2,128]{3,2,1,0:T(2,128)(2,1)S(1)}, u32[]{:S(2)}, u32[]{:S(2)}) collective-permute-start(bf16[2,192,2,128]{3,2,1,0:T(2,128)(2,1)S(1)} %bitcast.157), channel_id=1, source_target_pairs={{0,32},{32,64},{64,96},{96,0},{1,33},{33,65},{65,97},{97,1},{2,34}... | collective-permute-start | bytes 589832 | tf_op jit(solution)/shard_map/ppermute | solution.py:19

commit v9 on v5

--- a/solution.py
+++ b/solution.py
@@ -40,10 +40,8 @@
 
 
 def attention_kernel(src_ref, base_ref, peer_ref, *refs):
-    k_refs = refs[:TOPK]
-    v_refs = refs[TOPK:2 * TOPK]
-    q_lo, q_hi, do_lo, do_hi, kpos_ref = refs[2 * TOPK:2 * TOPK + 5]
-    o_ref, dq_ref, dk_ref, dv_ref = refs[2 * TOPK + 5:]
+    table_ref, q_lo, q_hi, do_lo, do_hi, kpos_ref = refs[:6]
+    o_ref, dq_ref, dk_ref, dv_ref = refs[6:]
     b = pl.program_id(0)
 
     @pl.when(b == 0)
@@ -51,11 +49,12 @@
         dk_ref[...] = jnp.zeros_like(dk_ref)
         dv_ref[...] = jnp.zeros_like(dv_ref)
 
-    head_width = k_refs[0].shape[-1]
+    head_width = table_ref.shape[-1]
     group_width = q_lo.shape[-1] // head_width
     scale = head_width ** (-0.5)
-    keys = jnp.concatenate([r[...] for r in k_refs], axis=0)
-    values = jnp.concatenate([r[...] for r in v_refs], axis=0)
+    slots = [src_ref[b * TOPK + s] for s in range(TOPK)]
+    keys = jnp.concatenate([table_ref[t, 0] for t in slots], axis=0)
+    values = jnp.concatenate([table_ref[t, 1] for t in slots], axis=0)
     query_pos = base_ref[b] + lax.broadcasted_iota(jnp.int32, (BLOCK_TOKENS, 1), 0)
     allowed = kpos_ref[...] <= query_pos
     nt = (((1,), (1,)), ((), ()))
@@ -108,18 +107,13 @@
 
         return pl.BlockSpec((None, None, half, row_width), index)
 
-    def slot_spec(s, kv):
-        def index(b, src, base, peer):
-            return (src[b * TOPK + s], kv, 0, 0)
-
-        return pl.BlockSpec((None, None, BLOCK_TOKENS, head_width), index)
+    table_spec = pl.BlockSpec(table.shape, lambda b, src, base, peer: (0, 0, 0, 0))
 
     out_row = pl.BlockSpec((BLOCK_TOKENS, row_width), lambda b, src, base, peer: (b, 0))
     pos_spec = pl.BlockSpec((None, 1, TOPK * BLOCK_TOKENS), lambda b, src, base, peer: (b, 0, 0))
     acc_spec = pl.BlockSpec((targets, BLOCK_TOKENS, head_width), lambda b, src, base, peer: (0, 0, 0))
     in_specs = (
-        [slot_spec(s, 0) for s in range(TOPK)]
-        + [slot_spec(s, 1) for s in range(TOPK)]
+        [table_spec]
         + [half_spec(0, 0), half_spec(0, 1), half_spec(1, 0), half_spec(1, 1), pos_spec]
     )
     out_shape = (
@@ -142,7 +136,7 @@
             dimension_semantics=("arbitrary",),
             vmem_limit_bytes=48 * 1024 * 1024,
         ),
-    )(slot_src, query_base, peer_of, *([table] * (2 * TOPK)), *([pieces] * 4), key_pos)
+    )(slot_src, query_base, peer_of, table, *([pieces] * 4), key_pos)
 
 
 def on_device(queries, rotated_keys, value_vectors, block_list, grad_out):

time: 267 us -> 265 us (level)
  Pallas kernels: 56 us -> 53.3 us
    pallas_call x2, Pallas kernels: 56 us -> 53.3 us  [attend(): pl.pallas_call(attention_kernel, grid_spec=grid_spec, out_shape=out_shape...]
  transfers between devices with their start and end apart: 16 -> 16, of which waited for: 10 -> 10; matrix products, arithmetic and copies ran while one was open for 17% -> 18% of each run, Pallas kernels for 21% -> 20%
where the time goes in v9:
time: 265 us; the launch traced here: 261 us
  waiting for transfers between devices  95.1 us (36%)
  Pallas kernels  53.3 us (20%)
  starting transfers between devices  47.9 us (18%)
  local copies, waits for them, and re-layouts  32.4 us (12%)
  other arithmetic  23.8 us (9%)
  matrix products  7.5 us (3%)
    pallas_call x2, Pallas kernels, attend(): pl.pallas_call(attention_kernel, grid_spec=grid_spec, out_shape=out_shape...  53.3 us
    ppermute x9, waiting for transfers between devices, exchange(): lax.ppermute(piece, 'head', [(i, (i + k) % size) for i in range(size)])  36.4 us
    all_to_all x2, waiting for transfers between devices, on_device(): lax.all_to_all(remote, 'blk', split_axis=0, concat_axis=0, tiled=True)  22.7 us
    ppermute x3, waiting for transfers between devices, on_device(): lax.ppermute(piece, 'head', [(i, (i + k) % size) for i in range(size)])  22.3 us
    all_to_all x2, starting transfers between devices, on_device(): lax.all_to_all(remote, 'blk', split_axis=0, concat_axis=0, tiled=True)  16.5 us
    all_to_all x2, waiting for transfers between devices, on_device(): recv = lax.all_to_all(send, 'blk', split_axis=0, concat_axis=0, tiled=True)  13.7 us
    ppermute x9, starting transfers between devices, exchange(): lax.ppermute(piece, 'head', [(i, (i + k) % size) for i in range(size)])  13.6 us
    all_to_all x2, starting transfers between devices, on_device(): recv = lax.all_to_all(send, 'blk', split_axis=0, concat_axis=0, tiled=True)  13.3 us
  transfers between devices with their start and end apart: 16, of which 10 were waited for; matrix products, arithmetic and copies ran while one was open for 18% of the time, Pallas kernels for 20%

profile of v9, /device:TPU:0, one launch (start us, length us, event | category | flops | bytes accessed | tf_op | source)
XLA Modules:
  0.0 261.2 jit_solution(13581363499878917067)
XLA Ops:
  3.0 3.2 %collective-permute-start.1 = (bf16[2,192,2,128]{3,1,2,0:T(8,128)(2,1)S(1)}, bf16[2,192,2,128]{3,1,2,0:T(8,128)(2,1)S(1)}, u32[]{:S(2)}, u32[]{:S(2)}) collective-permute-start(bf16[2,192,2,128]{3,1,2,0:T(8,128)(2,1)S(1)} %get-tuple-element.46), channel_id=1, source_target_pairs={{0,64},{32,96},{64,0},{96,32},{1,65},{33,97},{65,1},{97,33},{2,66}... | collective-permute-start | bytes 589832 | tf_op jit(solution)/shard_map/ppermute | solution.py:19
  6.2 2.9 %collective-permute-start = (bf16[2,192,2,128]{3,1,2,0:T(8,128)(2,1)S(1)}, bf16[2,192,2,128]{3,1,2,0:T(8,128)(2,1)S(1)}, u32[]{:S(2)}, u32[]{:S(2)}) collective-permute-start(bf16[2,192,2,128]{3,1,2,0:T(8,128)(2,1)S(1)} %get-tuple-element.47), channel_id=1, source_target_pairs={{0,96},{32,0},{64,32},{96,64},{1,97},{33,1},{65,33},{97,65},{2,98}... | collective-permute-start | bytes 589832 | tf_op jit(solution)/shard_map/ppermute | solution.py:19
  11.4 3.6 %collective-permute-done = bf16[2,192,2,128]{3,1,2,0:T(8,128)(2,1)S(1)} collective-permute-done((bf16[2,192,2,128]{3,1,2,0:T(8,128)(2,1)S(1)}, bf16[2,192,2,128]{3,1,2,0:T(8,128)(2,1)S(1)}, u32[]{:S(2)}, u32[]{:S(2)}) %collective-permute-start) | collective-permute-done | bytes 196640 | tf_op jit(solution)/shard_map/ppermute | solution.py:19
  16.3 2.2 copy.130
  18.5 8.4 %all-to-all-start.1 = ((bf16[32,2,128,128]{3,2,1,0:T(8,128)(2,1)}), bf16[32,2,128,128]{3,2,1,0:T(8,128)(2,1)S(1)}, u32[]{:S(2)}, u32[]{:S(2)}) async-start(bf16[32,2,128,128]{3,2,1,0:T(8,128)(2,1)} %copy.130), calls=%async_computation.1 | async-start | bytes 4194304 | tf_op jit(solution)/shard_map/all_to_all | solution.py:196
  26.8 3.5 %stack.121 = bf16[1,192,4,1024]{3,2,1,0:T(4,128)(2,1)} reshape(bf16[192,32,128]{2,1,0:T(8,128)(2,1)} %param.5) | data formatting | bytes 3145728 | tf_op jit(solution)/shard_map/stack | solution.py:150
  30.3 3.5 %stack.122 = bf16[1,192,4,1024]{3,2,1,0:T(4,128)(2,1)} reshape(bf16[192,32,128]{2,1,0:T(8,128)(2,1)} %param.9) | data formatting | bytes 3145728 | tf_op jit(solution)/shard_map/stack | solution.py:150
  33.8 2.0 copy_dynamic-update-slice_fusion.1
  38.0 3.7 %collective-permute-start.5 = (bf16[2,192,1024]{2,1,0:T(8,128)(2,1)}, bf16[2,192,1024]{2,1,0:T(8,128)(2,1)}, u32[]{:S(2)}, u32[]{:S(2)}) collective-permute-start(bf16[2,192,1024]{2,1,0:T(8,128)(2,1)} %get-tuple-element.34), channel_id=1, source_target_pairs={{0,96},{32,0},{64,32},{96,64},{1,97},{33,1},{65,33},{97,65},{2,98}... | collective-permute-start | bytes 2359304 | tf_op jit(solution)/shard_map/ppermute | solution.py:156
  43.3 2.2 copy.131
  45.6 13.7 %all-to-all-done.1 = bf16[32,2,128,128]{3,2,1,0:T(8,128)(2,1)S(1)} async-done(((bf16[32,2,128,128]{3,2,1,0:T(8,128)(2,1)}), bf16[32,2,128,128]{3,2,1,0:T(8,128)(2,1)S(1)}, u32[]{:S(2)}, u32[]{:S(2)}) %all-to-all-start.1) | async-done | bytes 2097184 | tf_op jit(solution)/shard_map/all_to_all | solution.py:196
  59.3 4.9 %all-to-all-start = ((bf16[32,2,128,128]{3,2,1,0:T(8,128)(2,1)}), bf16[32,2,128,128]{3,2,1,0:T(8,128)(2,1)}, u32[]{:S(2)}, u32[]{:S(2)}) async-start(bf16[32,2,128,128]{3,2,1,0:T(8,128)(2,1)} %copy.131), calls=%async_computation | async-start | bytes 4194304 | tf_op jit(solution)/shard_map/all_to_all | solution.py:196
  66.7 18.5 %collective-permute-done.4 = bf16[2,192,1024]{2,1,0:T(8,128)(2,1)} collective-permute-done((bf16[2,192,1024]{2,1,0:T(8,128)(2,1)}, bf16[2,192,1024]{2,1,0:T(8,128)(2,1)}, u32[]{:S(2)}, u32[]{:S(2)}) %collective-permute-start.4) | collective-permute-done | bytes 786464 | tf_op jit(solution)/shard_map/ppermute | solution.py:156
  85.2 3.0 %collective-permute-done.3 = bf16[2,192,1024]{2,1,0:T(8,128)(2,1)} collective-permute-done((bf16[2,192,1024]{2,1,0:T(8,128)(2,1)}, bf16[2,192,1024]{2,1,0:T(8,128)(2,1)}, u32[]{:S(2)}, u32[]{:S(2)}) %collective-permute-start.3) | collective-permute-done | bytes 786464 | tf_op jit(solution)/shard_map/ppermute | solution.py:156
  88.2 3.2 %pad_maximum_fusion.1.refs_1_.refs_2_.refs_3_.refs_4_ = bf16[4,2,192,1024]{3,2,1,0:T(8,128)(2,1)} fusion(bf16[1,2,192,1024]{3,2,1,0:T(8,128)(2,1)} %bitcast.21, bf16[1,2,192,1024]{3,2,1,0:T(8,128)(2,1)} %bitcast.19, bf16[1,2,192,1024]{3,2,1,0:T(8,128)(2,1)} %bitcast.17, bf16[1,2,192,1024]{3,2,1,0:T(8,128)(2,1)} %get-tuple-element.33), kind=kLoop, calls=%fused_computation.13 | loop fusion | flops 4718592 | bytes 6291456 | tf_op jit(solution)/shard_map/stack | solution.py:158
  93.1 26.7 %shard_map.85 = (bf16[768,512]{1,0:T(8,128)(2,1)S(1)}, bf16[768,512]{1,0:T(8,128)(2,1)S(1)}, f32[38,128,128]{2,1,0:T(8,128)S(1)}, f32[38,128,128]{2,1,0:T(8,128)}) custom-call(s32[48]{0:T(128)S(1)} %reshape_squeeze.7.src_ref, s32[6]{0:T(128)S(1)} %add_multiply_fusion.base_ref, s32[4]{0:T(128)S(1)} %and_select_fusion.peer_ref, ...), custom_call_target="tpu_custom_call" | custom-call | tf_op jit(solution)/shard_map/pallas_call | solution.py:131
  119.7 2.4 maximum_convert_fusion
  123.9 7.9 %all-to-all-start.2 = ((bf16[32,2,128,128]{3,2,1,0:T(8,128)(2,1)}), bf16[32,2,128,128]{3,2,1,0:T(8,128)(2,1)}, u32[]{:S(2)}, u32[]{:S(2)}) async-start(bf16[32,2,128,128]{3,2,1,0:T(8,128)(2,1)} %copy.88), calls=%async_computation.2 | async-start | bytes 4194304 | tf_op jit(solution)/shard_map/all_to_all | solution.py:206
  132.0 3.4 %pad_maximum_fusion.2.refs_0_ = bf16[38,2,128,128]{3,2,1,0:T(8,128)(2,1)} fusion(bf16[6,2,128,128]{3,2,1,0:T(8,128)(2,1)} %copy-done.11, bf16[32,2,128,128]{3,2,1,0:T(8,128)(2,1)} %all-to-all-done), kind=kLoop, calls=%fused_computation.14 | loop fusion | flops 1245184 | bytes 4980736 | tf_op jit(solution)/shard_map/concatenate | solution.py:197
  135.4 26.6 %shard_map.84 = (bf16[768,512]{1,0:T(8,128)(2,1)S(1)}, bf16[768,512]{1,0:T(8,128)(2,1)S(1)}, f32[38,128,128]{2,1,0:T(8,128)S(1)}, f32[38,128,128]{2,1,0:T(8,128)}) custom-call(s32[48]{0:T(128)S(1)} %reshape_squeeze.6.src_ref, s32[6]{0:T(128)S(1)} %add_multiply_fusion.base_ref, s32[4]{0:T(128)S(1)} %and_select_fusion.peer_ref, ...), custom_call_target="tpu_custom_call" | custom-call | tf_op jit(solution)/shard_map/pallas_call | solution.py:131
  162.0 3.4 %fusion = bf16[32,2,128,128]{3,2,0,1:T(8,128)(2,1)S(1)} fusion(f32[38,1,128,128]{3,2,0,1:T(8,128)} %bitcast.148, f32[38,1,128,128]{3,2,0,1:T(8,128)S(1)} %bitcast.136), kind=kLoop, calls=%fused_computation.10 | loop fusion | flops 1048576 | bytes 7077888 | tf_op jit(solution)/shard_map/convert.2
  167.0 8.6 %all-to-all-start.3 = ((bf16[32,2,128,128]{3,2,1,0:T(8,128)(2,1)}), bf16[32,2,128,128]{3,2,1,0:T(8,128)(2,1)}, u32[]{:S(2)}, u32[]{:S(2)}) async-start(bf16[32,2,128,128]{3,2,1,0:T(8,128)(2,1)} %copy.89), calls=%async_computation.3 | async-start | bytes 4194304 | tf_op jit(solution)/shard_map/all_to_all | solution.py:206
  175.6 2.6 maximum_bitcast_fusion
  181.9 22.7 %all-to-all-done.3 = bf16[32,2,128,128]{3,2,1,0:T(8,128)(2,1)} async-done(((bf16[32,2,128,128]{3,2,1,0:T(8,128)(2,1)}), bf16[32,2,128,128]{3,2,1,0:T(8,128)(2,1)}, u32[]{:S(2)}, u32[]{:S(2)}) %all-to-all-start.3) | async-done | bytes 2097184 | tf_op jit(solution)/shard_map/all_to_all | solution.py:206
  204.7 3.0 %fusion.3 = f32[6,2,128,128]{3,0,2,1:T(8,128)S(1)} fusion(bf16[32,2,128,128]{3,2,1,0:T(8,128)(2,1)} %all-to-all-done.3, bf16[2,32,6]{1,2,0:T(8,128)(2,1)S(1)} %broadcast_select_fusion), kind=kOutput, calls=%fused_computation.18 | convolution fusion | flops 12582912 | bytes 2885632 | tf_op jit(solution)/shard_map/rl,rktd->lktd/dot_general | solution.py:220
  208.9 3.0 %fusion.1 = f32[6,2,128,128]{3,0,2,1:T(8,128)S(1)} fusion(bf16[32,2,128,128]{3,2,1,0:T(8,128)(2,1)} %all-to-all-done.2, bf16[2,32,6]{1,2,0:T(8,128)(2,1)S(1)} %broadcast_select_fusion), kind=kOutput, calls=%fused_computation.16 | convolution fusion | flops 12582912 | bytes 2885632 | tf_op jit(solution)/shard_map/rl,rktd->lktd/dot_general | solution.py:220
  218.3 2.3 collective-permute-start.7
  220.8 2.5 collective-permute-done.10
  223.7 2.4 collective-permute-done.11
  228.9 10.4 %collective-permute-done.6 = bf16[2,192,8,128]{3,2,1,0:T(8,128)(2,1)S(1)} collective-permute-done((bf16[2,192,8,128]{3,2,1,0:T(8,128)(2,1)S(1)}, bf16[2,192,8,128]{3,2,1,0:T(8,128)(2,1)S(1)}, u32[]{:S(2)}, u32[]{:S(2)}) %collective-permute-start.6) | collective-permute-done | bytes 786464 | tf_op jit(solution)/shard_map/ppermute | solution.py:19
  239.6 17.5 %collective-permute-done.7 = bf16[2,192,8,128]{3,2,1,0:T(8,128)(2,1)S(1)} collective-permute-done((bf16[2,192,8,128]{3,2,1,0:T(8,128)(2,1)S(1)}, bf16[2,192,8,128]{3,2,1,0:T(8,128)(2,1)S(1)}, u32[]{:S(2)}, u32[]{:S(2)}) %collective-permute-start.7) | collective-permute-done | bytes 786464 | tf_op jit(solution)/shard_map/ppermute | solution.py:19
  258.8 2.4 dynamic-slice_bitcast_fusion
  (121 shorter events, 33.7 us)
Async XLA Ops:
  2.9 12.2 %collective-permute-start.2 = (bf16[2,192,2,128]{3,1,2,0:T(8,128)(2,1)S(1)}, bf16[2,192,2,128]{3,1,2,0:T(8,128)(2,1)S(1)}, u32[]{:S(2)}, u32[]{:S(2)}) collective-permute-start(bf16[2,192,2,128]{3,1,2,0:T(8,128)(2,1)S(1)} %get-tuple-element.45), channel_id=1, source_target_pairs={{0,32},{32,64},{64,96},{96,0},{1,33},{33,65},{65,97},{97,1},{2,34}... | collective-permute-start | bytes 589832 | tf_op jit(solution)/shard_map/ppermute | solution.py:19
  3.0 12.1 %collective-permute-start.1 = (bf16[2,192,2,128]{3,1,2,0:T(8,128)(2,1)S(1)}, bf16[2,192,2,128]{3,1,2,0:T(8,128)(2,1)S(1)}, u32[]{:S(2)}, u32[]{:S(2)}) collective-permute-start(bf16[2,192,2,128]{3,1,2,0:T(8,128)(2,1)S(1)} %get-tuple-element.46), channel_id=1, source_target_pairs={{0,64},{32,96},{64,0},{96,32},{1,65},{33,97},{65,1},{97,33},{2,66}... | collective-permute-start | bytes 589832 | tf_op jit(solution)/shard_map/ppermute | solution.py:19
  6.2 8.8 %collective-permute-start = (bf16[2,192,2,128]{3,1,2,0:T(8,128)(2,1)S(1)}, bf16[2,192,2,128]{3,1,2,0:T(8,128)(2,1)S(1)}, u32[]{:S(2)}, u32[]{:S(2)}) collective-permute-start(bf16[2,192,2,128]{3,1,2,0:T(8,128)(2,1)S(1)} %get-tuple-element.47), channel_id=1, source_target_pairs={{0,96},{32,0},{64,32},{96,64},{1,97},{33,1},{65,33},{97,65},{2,98}... | collective-permute-start | bytes 589832 | tf_op jit(solution)/shard_map/ppermute | solution.py:19
  15.5 27.1 %copy-start.11 = (bf16[6,2,128,128]{3,2,1,0:T(8,128)(2,1)}, bf16[6,2,128,128]{3,2,1,0:T(8,128)(2,1)S(1)}, u32[]{:S(2)}) copy-start(bf16[6,2,128,128]{3,2,1,0:T(8,128)(2,1)S(1)} %get-tuple-element.43) | copy-start | bytes 1179652
  18.5 40.8 %all-to-all-start.1 = ((bf16[32,2,128,128]{3,2,1,0:T(8,128)(2,1)}), bf16[32,2,128,128]{3,2,1,0:T(8,128)(2,1)S(1)}, u32[]{:S(2)}, u32[]{:S(2)}) async-start(bf16[32,2,128,128]{3,2,1,0:T(8,128)(2,1)} %copy.130), calls=%async_computation.1 | async-start | bytes 4194304 | tf_op jit(solution)/shard_map/all_to_all | solution.py:196
  33.8 2.0 copy-start.10
  38.0 28.7 %collective-permute-start.5 = (bf16[2,192,1024]{2,1,0:T(8,128)(2,1)}, bf16[2,192,1024]{2,1,0:T(8,128)(2,1)}, u32[]{:S(2)}, u32[]{:S(2)}) collective-permute-start(bf16[2,192,1024]{2,1,0:T(8,128)(2,1)} %get-tuple-element.34), channel_id=1, source_target_pairs={{0,96},{32,0},{64,32},{96,64},{1,97},{33,1},{65,33},{97,65},{2,98}... | collective-permute-start | bytes 2359304 | tf_op jit(solution)/shard_map/ppermute | solution.py:156
  41.8 43.4 %collective-permute-start.4 = (bf16[2,192,1024]{2,1,0:T(8,128)(2,1)}, bf16[2,192,1024]{2,1,0:T(8,128)(2,1)}, u32[]{:S(2)}, u32[]{:S(2)}) collective-permute-start(bf16[2,192,1024]{2,1,0:T(8,128)(2,1)} %get-tuple-element.35), channel_id=1, source_target_pairs={{0,64},{32,96},{64,0},{96,32},{1,65},{33,97},{65,1},{97,33},{2,66}... | collective-permute-start | bytes 2359304 | tf_op jit(solution)/shard_map/ppermute | solution.py:156
  42.6 45.6 %collective-permute-start.3 = (bf16[2,192,1024]{2,1,0:T(8,128)(2,1)}, bf16[2,192,1024]{2,1,0:T(8,128)(2,1)}, u32[]{:S(2)}, u32[]{:S(2)}) collective-permute-start(bf16[2,192,1024]{2,1,0:T(8,128)(2,1)} %get-tuple-element.36), channel_id=1, source_target_pairs={{0,32},{32,64},{64,96},{96,0},{1,33},{33,65},{65,97},{97,1},{2,34}... | collective-permute-start | bytes 2359304 | tf_op jit(solution)/shard_map/ppermute | solution.py:156
  59.3 64.6 %all-to-all-start = ((bf16[32,2,128,128]{3,2,1,0:T(8,128)(2,1)}), bf16[32,2,128,128]{3,2,1,0:T(8,128)(2,1)}, u32[]{:S(2)}, u32[]{:S(2)}) async-start(bf16[32,2,128,128]{3,2,1,0:T(8,128)(2,1)} %copy.131), calls=%async_computation | async-start | bytes 4194304 | tf_op jit(solution)/shard_map/all_to_all | solution.py:196
  119.7 2.4 copy-start.2
  123.9 43.1 %all-to-all-start.2 = ((bf16[32,2,128,128]{3,2,1,0:T(8,128)(2,1)}), bf16[32,2,128,128]{3,2,1,0:T(8,128)(2,1)}, u32[]{:S(2)}, u32[]{:S(2)}) async-start(bf16[32,2,128,128]{3,2,1,0:T(8,128)(2,1)} %copy.88), calls=%async_computation.2 | async-start | bytes 4194304 | tf_op jit(solution)/shard_map/all_to_all | solution.py:206
  162.0 3.4 %copy-start = (f32[38,128,128]{2,1,0:T(8,128)}, f32[38,128,128]{2,1,0:T(8,128)S(1)}, u32[]{:S(2)}) copy-start(f32[38,128,128]{2,1,0:T(8,128)S(1)} %get-tuple-element.23) | copy-start | bytes 7471108
  162.0 3.4 %copy-start.3 = (bf16[768,512]{1,0:T(8,128)(2,1)}, bf16[768,512]{1,0:T(8,128)(2,1)S(1)}, u32[]{:S(2)}) copy-start(bf16[768,512]{1,0:T(8,128)(2,1)S(1)} %get-tuple-element.15) | copy-start | bytes 2359300
  162.0 3.4 %copy-start.4 = (bf16[768,512]{1,0:T(8,128)(2,1)}, bf16[768,512]{1,0:T(8,128)(2,1)S(1)}, u32[]{:S(2)}) copy-start(bf16[768,512]{1,0:T(8,128)(2,1)S(1)} %get-tuple-element.17) | copy-start | bytes 2359300
  167.0 37.7 %all-to-all-start.3 = ((bf16[32,2,128,128]{3,2,1,0:T(8,128)(2,1)}), bf16[32,2,128,128]{3,2,1,0:T(8,128)(2,1)}, u32[]{:S(2)}, u32[]{:S(2)}) async-start(bf16[32,2,128,128]{3,2,1,0:T(8,128)(2,1)} %copy.89), calls=%async_computation.3 | async-start | bytes 4194304 | tf_op jit(solution)/shard_map/all_to_all | solution.py:206
  178.7 1.5 copy-start.5
  179.1 1.5 copy-start.7
  204.7 3.0 %copy-start.1 = (f32[38,128,128]{2,1,0:T(8,128)S(1)}, f32[38,128,128]{2,1,0:T(8,128)}, u32[]{:S(2)}) copy-start(f32[38,128,128]{2,1,0:T(8,128)} %copy-done) | copy-start | bytes 7471108
  208.8 3.0 %copy-start.9 = (f32[38,128,128]{2,1,0:T(8,128)S(1)}, f32[38,128,128]{2,1,0:T(8,128)}, u32[]{:S(2)}) copy-start(f32[38,128,128]{2,1,0:T(8,128)} %get-tuple-element.20) | copy-start | bytes 7471108
  211.9 27.5 %slice-start = ((s8[6291456]{0:T(1024)(128)(4,1)}), s8[4194304]{0:T(1024)(128)(4,1)S(1)}, s32[]{:S(2)}) async-start(s8[6291456]{0:T(1024)(128)(4,1)} %bitcast.153), calls=%async_computation.4 | async-start | bytes 8388608
  212.1 4.6 %copy-start.13 = (bf16[2,192,8,128]{3,2,1,0:T(8,128)(2,1)S(1)}, bf16[2,192,8,128]{3,2,1,0:T(8,128)(2,1)}, u32[]{:S(2)}) copy-start(bf16[2,192,8,128]{3,2,1,0:T(8,128)(2,1)} %get-tuple-element.31) | copy-start | bytes 2359300
  212.1 6.2 %copy-start.12 = (bf16[2,192,8,128]{3,2,1,0:T(8,128)(2,1)S(1)}, bf16[2,192,8,128]{3,2,1,0:T(8,128)(2,1)}, u32[]{:S(2)}) copy-start(bf16[2,192,8,128]{3,2,1,0:T(8,128)(2,1)} %get-tuple-element.32) | copy-start | bytes 2359300
  212.1 27.2 %slice-start.1 = ((s8[6291456]{0:T(1024)(128)(4,1)}), s8[2097152]{0:T(1024)(128)(4,1)S(1)}, s32[]{:S(2)}) async-start(s8[6291456]{0:T(1024)(128)(4,1)} %bitcast.153), calls=%async_computation.5 | async-start | bytes 4194304
  212.9 5.4 %collective-permute-start.9 = (bf16[2,192,2,128]{3,2,1,0:T(2,128)(2,1)S(1)}, bf16[2,192,2,128]{3,2,1,0:T(2,128)(2,1)S(1)}, u32[]{:S(2)}, u32[]{:S(2)}) collective-permute-start(bf16[2,192,2,128]{3,2,1,0:T(2,128)(2,1)S(1)} %bitcast.165), channel_id=1, source_target_pairs={{0,96},{32,0},{64,32},{96,64},{1,97},{33,1},{65,33},{97,65},{2,98}... | collective-permute-start | bytes 589832 | tf_op jit(solution)/shard_map/ppermute | solution.py:19
  213.0 10.4 %collective-permute-start.10 = (bf16[2,192,2,128]{3,2,1,0:T(2,128)(2,1)S(1)}, bf16[2,192,2,128]{3,2,1,0:T(2,128)(2,1)S(1)}, u32[]{:S(2)}, u32[]{:S(2)}) collective-permute-start(bf16[2,192,2,128]{3,2,1,0:T(2,128)(2,1)S(1)} %bitcast.164), channel_id=1, source_target_pairs={{0,64},{32,96},{64,0},{96,32},{1,65},{33,97},{65,1},{97,33},{2,66}... | collective-permute-start | bytes 589832 | tf_op jit(solution)/shard_map/ppermute | solution.py:19
  214.8 11.3 %collective-permute-start.11 = (bf16[2,192,2,128]{3,2,1,0:T(2,128)(2,1)S(1)}, bf16[2,192,2,128]{3,2,1,0:T(2,128)(2,1)S(1)}, u32[]{:S(2)}, u32[]{:S(2)}) collective-permute-start(bf16[2,192,2,128]{3,2,1,0:T(2,128)(2,1)S(1)} %bitcast.163), channel_id=1, source_target_pairs={{0,32},{32,64},{64,96},{96,0},{1,33},{33,65},{65,97},{97,1},{2,34}... | collective-permute-start | bytes 589832 | tf_op jit(solution)/shard_map/ppermute | solution.py:19
  214.8 42.6 %collective-permute-start.8 = (bf16[2,192,8,128]{3,2,1,0:T(8,128)(2,1)S(1)}, bf16[2,192,8,128]{3,2,1,0:T(8,128)(2,1)S(1)}, u32[]{:S(2)}, u32[]{:S(2)}) collective-permute-start(bf16[2,192,8,128]{3,2,1,0:T(8,128)(2,1)S(1)} %get-tuple-element.30), channel_id=1, source_target_pairs={{0,32},{32,64},{64,96},{96,0},{1,33},{33,65},{65,97},{97,1},{2,34}... | collective-permute-start | bytes 2359304 | tf_op jit(solution)/shard_map/ppermute | solution.py:19
  216.7 22.6 %collective-permute-start.6 = (bf16[2,192,8,128]{3,2,1,0:T(8,128)(2,1)S(1)}, bf16[2,192,8,128]{3,2,1,0:T(8,128)(2,1)S(1)}, u32[]{:S(2)}, u32[]{:S(2)}) collective-permute-start(bf16[2,192,8,128]{3,2,1,0:T(8,128)(2,1)S(1)} %copy-done.13), channel_id=1, source_target_pairs={{0,96},{32,0},{64,32},{96,64},{1,97},{33,1},{65,33},{97,65},{2,98}... | collective-permute-start | bytes 2359304 | tf_op jit(solution)/shard_map/ppermute | solution.py:19
  218.3 38.8 %collective-permute-start.7 = (bf16[2,192,8,128]{3,2,1,0:T(8,128)(2,1)S(1)}, bf16[2,192,8,128]{3,2,1,0:T(8,128)(2,1)S(1)}, u32[]{:S(2)}, u32[]{:S(2)}) collective-permute-start(bf16[2,192,8,128]{3,2,1,0:T(8,128)(2,1)S(1)} %copy-done.12), channel_id=1, source_target_pairs={{0,64},{32,96},{64,0},{96,32},{1,65},{33,97},{65,1},{97,33},{2,66}... | collective-permute-start | bytes 2359304 | tf_op jit(solution)/shard_map/ppermute | solution.py:19
  228.9 28.7 %copy-start.6 = (bf16[96,8,8,128]{3,2,1,0:T(8,128)(2,1)S(1)}, bf16[96,8,8,128]{3,2,1,0:T(8,128)(2,1)}, u32[]{:S(2)}) copy-start(bf16[96,8,8,128]{3,2,1,0:T(8,128)(2,1)} %copy-done.5) | copy-start | bytes 4718596
  228.9 28.7 %copy-start.8 = (bf16[96,8,8,128]{3,2,1,0:T(8,128)(2,1)S(1)}, bf16[96,8,8,128]{3,2,1,0:T(8,128)(2,1)}, u32[]{:S(2)}) copy-start(bf16[96,8,8,128]{3,2,1,0:T(8,128)(2,1)} %copy-done.7) | copy-start | bytes 4718596

commit v10 on v9

--- a/solution.py
+++ b/solution.py
@@ -58,7 +58,6 @@
     query_pos = base_ref[b] + lax.broadcasted_iota(jnp.int32, (BLOCK_TOKENS, 1), 0)
     allowed = kpos_ref[...] <= query_pos
     nt = (((1,), (1,)), ((), ()))
-    tn = (((0,), (0,)), ((), ()))
     dk = None
     dv = None
     for j in range(group_width):
@@ -78,16 +77,16 @@
         ds = (p * (dp - rd)).astype(jnp.bfloat16)
         dq = jnp.dot(ds, keys, preferred_element_type=jnp.float32) * scale
         dq_ref[:, cols] = dq.astype(jnp.bfloat16)
-        dkj = lax.dot_general(ds, qj, tn, preferred_element_type=jnp.float32)
-        dvj = lax.dot_general(pb, gj, tn, preferred_element_type=jnp.float32)
+        dkj = jnp.dot(qj.T, ds, preferred_element_type=jnp.float32)
+        dvj = jnp.dot(gj.T, pb, preferred_element_type=jnp.float32)
         dk = dkj if dk is None else dk + dkj
         dv = dvj if dv is None else dv + dvj
     dk = dk * scale
     for s in range(TOPK):
         t = src_ref[b * TOPK + s]
-        rows = slice(s * BLOCK_TOKENS, (s + 1) * BLOCK_TOKENS)
-        dk_ref[t] = dk_ref[t] + dk[rows]
-        dv_ref[t] = dv_ref[t] + dv[rows]
+        cols = slice(s * BLOCK_TOKENS, (s + 1) * BLOCK_TOKENS)
+        dk_ref[t] = dk_ref[t] + dk[:, cols]
+        dv_ref[t] = dv_ref[t] + dv[:, cols]
 
 
 def attend(slot_src, query_base, peer_of, table, pieces, key_pos, group, groups):
@@ -200,7 +199,7 @@
         )
         outs.append(o_g)
         query_grads.append(dq_g)
-        acc = jnp.stack([dk_acc, dv_acc], axis=1)
+        acc = jnp.swapaxes(jnp.stack([dk_acc, dv_acc], axis=1), 2, 3)
         remote = acc[:peers].astype(jnp.bfloat16)
         local = acc[peers:].astype(jnp.bfloat16)
         backs.append(lax.all_to_all(remote, "blk", split_axis=0, concat_axis=0, tiled=True))

time: 265 us -> 275 us (1.038)
  local copies, waits for them, and re-layouts: 32.4 us -> 54 us
  waiting for transfers between devices: 95.1 us -> 84.7 us
  starting transfers between devices: 47.9 us -> 51.1 us
  other arithmetic: 23.8 us -> 21 us
    all_to_all x2, waiting for transfers between devices: 22.7 us -> 13.6 us  [on_device(): lax.all_to_all(remote, 'blk', split_axis=0, concat_axis=0, tiled=True)]
    dot_general x0 -> x2, local copies, waits for them, and re-layouts: none -> 4.75 us  [on_device(): jnp.einsum('rl,rktd->lktd', take_back[g], backs[g], preferred_element_typ...]
    all_to_all x0 -> x1, local copies, waits for them, and re-layouts: none -> 4.56 us  [on_device(): lax.all_to_all(remote, 'blk', split_axis=0, concat_axis=0, tiled=True)]
    optimization_barrier x0 -> x1, local copies, waits for them, and re-layouts: none -> 4.55 us  [on_device(): lax.optimization_barrier((heads_layout(outs), heads_layout(query_grads),...]
    unnamed x55 -> x35, local copies, waits for them, and re-layouts: 7.81 us -> 11.4 us
    ppermute x9, starting transfers between devices: 13.6 us -> 16.9 us  [exchange(): lax.ppermute(piece, 'head', [(i, (i + k) % size) for i in range(size)])]
    slice x2 -> x4, local copies, waits for them, and re-layouts: 0.06 us -> 3.38 us  [on_device(): key_grads.append(total[:, 0])]
    slice x0 -> x2, local copies, waits for them, and re-layouts: none -> 2.84 us  [on_device(): value_grads.append(total[:, 1])]
  transfers between devices with their start and end apart: 16 -> 16, of which waited for: 10 -> 8; matrix products, arithmetic and copies ran while one was open for 18% -> 19% of each run, Pallas kernels for 20% -> 20%
where the time goes in v10:
time: 275 us; the launch traced here: 273 us
  waiting for transfers between devices  84.7 us (31%)
  local copies, waits for them, and re-layouts  54 us (20%)
  Pallas kernels  53.3 us (19%)
  starting transfers between devices  51.1 us (19%)
  other arithmetic  21 us (8%)
  matrix products  7.45 us (3%)
    pallas_call x2, Pallas kernels, attend(): pl.pallas_call(attention_kernel, grid_spec=grid_spec, out_shape=out_shape...  53.3 us
    ppermute x9, waiting for transfers between devices, exchange(): lax.ppermute(piece, 'head', [(i, (i + k) % size) for i in range(size)])  36.4 us
    ppermute x3, waiting for transfers between devices, on_device(): lax.ppermute(piece, 'head', [(i, (i + k) % size) for i in range(size)])  20.9 us
    ppermute x9, starting transfers between devices, exchange(): lax.ppermute(piece, 'head', [(i, (i + k) % size) for i in range(size)])  16.9 us
    all_to_all x2, starting transfers between devices, on_device(): lax.all_to_all(remote, 'blk', split_axis=0, concat_axis=0, tiled=True)  16.4 us
    all_to_all x2, waiting for transfers between devices, on_device(): recv = lax.all_to_all(send, 'blk', split_axis=0, concat_axis=0, tiled=True)  13.7 us
    all_to_all x2, waiting for transfers between devices, on_device(): lax.all_to_all(remote, 'blk', split_axis=0, concat_axis=0, tiled=True)  13.6 us
    all_to_all x2, starting transfers between devices, on_device(): recv = lax.all_to_all(send, 'blk', split_axis=0, concat_axis=0, tiled=True)  13.3 us
  transfers between devices with their start and end apart: 16, of which 8 were waited for; matrix products, arithmetic and copies ran while one was open for 19% of the time, Pallas kernels for 20%

profile of v10, /device:TPU:0, one launch (start us, length us, event | category | flops | bytes accessed | tf_op | source)
XLA Modules:
  0.0 272.8 jit_solution(17259128042538082248)
XLA Ops:
  3.0 3.2 %collective-permute-start.1 = (bf16[2,192,2,128]{3,1,2,0:T(8,128)(2,1)S(1)}, bf16[2,192,2,128]{3,1,2,0:T(8,128)(2,1)S(1)}, u32[]{:S(2)}, u32[]{:S(2)}) collective-permute-start(bf16[2,192,2,128]{3,1,2,0:T(8,128)(2,1)S(1)} %get-tuple-element.57), channel_id=1, source_target_pairs={{0,64},{32,96},{64,0},{96,32},{1,65},{33,97},{65,1},{97,33},{2,66}... | collective-permute-start | bytes 589832 | tf_op jit(solution)/shard_map/ppermute | solution.py:19
  6.2 2.9 %collective-permute-start = (bf16[2,192,2,128]{3,1,2,0:T(8,128)(2,1)S(1)}, bf16[2,192,2,128]{3,1,2,0:T(8,128)(2,1)S(1)}, u32[]{:S(2)}, u32[]{:S(2)}) collective-permute-start(bf16[2,192,2,128]{3,1,2,0:T(8,128)(2,1)S(1)} %get-tuple-element.58), channel_id=1, source_target_pairs={{0,96},{32,0},{64,32},{96,64},{1,97},{33,1},{65,33},{97,65},{2,98}... | collective-permute-start | bytes 589832 | tf_op jit(solution)/shard_map/ppermute | solution.py:19
  11.4 3.6 %collective-permute-done = bf16[2,192,2,128]{3,1,2,0:T(8,128)(2,1)S(1)} collective-permute-done((bf16[2,192,2,128]{3,1,2,0:T(8,128)(2,1)S(1)}, bf16[2,192,2,128]{3,1,2,0:T(8,128)(2,1)S(1)}, u32[]{:S(2)}, u32[]{:S(2)}) %collective-permute-start) | collective-permute-done | bytes 196640 | tf_op jit(solution)/shard_map/ppermute | solution.py:19
  16.3 2.2 copy.144
  18.4 8.4 %all-to-all-start = ((bf16[32,2,128,128]{3,2,1,0:T(8,128)(2,1)}), bf16[32,2,128,128]{3,2,1,0:T(8,128)(2,1)S(1)}, u32[]{:S(2)}, u32[]{:S(2)}) async-start(bf16[32,2,128,128]{3,2,1,0:T(8,128)(2,1)} %copy.144), calls=%async_computation | async-start | bytes 4194304 | tf_op jit(solution)/shard_map/all_to_all | solution.py:195
  26.8 3.5 %stack.121 = bf16[1,192,4,1024]{3,2,1,0:T(4,128)(2,1)} reshape(bf16[192,32,128]{2,1,0:T(8,128)(2,1)} %param.5) | data formatting | bytes 3145728 | tf_op jit(solution)/shard_map/stack | solution.py:149
  30.3 3.5 %stack.122 = bf16[1,192,4,1024]{3,2,1,0:T(4,128)(2,1)} reshape(bf16[192,32,128]{2,1,0:T(8,128)(2,1)} %param.9) | data formatting | bytes 3145728 | tf_op jit(solution)/shard_map/stack | solution.py:149
  38.1 3.7 %collective-permute-start.5 = (bf16[2,192,1024]{2,1,0:T(8,128)(2,1)}, bf16[2,192,1024]{2,1,0:T(8,128)(2,1)}, u32[]{:S(2)}, u32[]{:S(2)}) collective-permute-start(bf16[2,192,1024]{2,1,0:T(8,128)(2,1)} %get-tuple-element.46), channel_id=1, source_target_pairs={{0,96},{32,0},{64,32},{96,64},{1,97},{33,1},{65,33},{97,65},{2,98}... | collective-permute-start | bytes 2359304 | tf_op jit(solution)/shard_map/ppermute | solution.py:155
  45.5 13.7 %all-to-all-done = bf16[32,2,128,128]{3,2,1,0:T(8,128)(2,1)S(1)} async-done(((bf16[32,2,128,128]{3,2,1,0:T(8,128)(2,1)}), bf16[32,2,128,128]{3,2,1,0:T(8,128)(2,1)S(1)}, u32[]{:S(2)}, u32[]{:S(2)}) %all-to-all-start) | async-done | bytes 2097184 | tf_op jit(solution)/shard_map/all_to_all | solution.py:195
  60.6 4.9 %all-to-all-start.1 = ((bf16[32,2,128,128]{3,2,1,0:T(8,128)(2,1)}), bf16[32,2,128,128]{3,2,1,0:T(8,128)(2,1)}, u32[]{:S(2)}, u32[]{:S(2)}) async-start(bf16[32,2,128,128]{3,2,1,0:T(8,128)(2,1)} %copy.143), calls=%async_computation.1 | async-start | bytes 4194304 | tf_op jit(solution)/shard_map/all_to_all | solution.py:195
  67.2 17.9 %collective-permute-done.4 = bf16[2,192,1024]{2,1,0:T(8,128)(2,1)} collective-permute-done((bf16[2,192,1024]{2,1,0:T(8,128)(2,1)}, bf16[2,192,1024]{2,1,0:T(8,128)(2,1)}, u32[]{:S(2)}, u32[]{:S(2)}) %collective-permute-start.4) | collective-permute-done | bytes 786464 | tf_op jit(solution)/shard_map/ppermute | solution.py:155
  85.2 3.0 %collective-permute-done.3 = bf16[2,192,1024]{2,1,0:T(8,128)(2,1)} collective-permute-done((bf16[2,192,1024]{2,1,0:T(8,128)(2,1)}, bf16[2,192,1024]{2,1,0:T(8,128)(2,1)}, u32[]{:S(2)}, u32[]{:S(2)}) %collective-permute-start.3) | collective-permute-done | bytes 786464 | tf_op jit(solution)/shard_map/ppermute | solution.py:155
  88.2 3.3 %pad_maximum_fusion.refs_1_.refs_2_.refs_3_.refs_4_ = bf16[4,2,192,1024]{3,2,1,0:T(8,128)(2,1)} fusion(bf16[1,2,192,1024]{3,2,1,0:T(8,128)(2,1)} %bitcast.21, bf16[1,2,192,1024]{3,2,1,0:T(8,128)(2,1)} %bitcast.19, bf16[1,2,192,1024]{3,2,1,0:T(8,128)(2,1)} %bitcast.17, bf16[1,2,192,1024]{3,2,1,0:T(8,128)(2,1)} %get-tuple-element.45), kind=kLoop, calls=%fused_computation.12 | loop fusion | flops 4718592 | bytes 6291456 | tf_op jit(solution)/shard_map/stack | solution.py:157
  93.2 26.6 %shard_map.84 = (bf16[768,512]{1,0:T(8,128)(2,1)S(1)}, bf16[768,512]{1,0:T(8,128)(2,1)S(1)}, f32[38,128,128]{2,1,0:T(8,128)S(1)}, f32[38,128,128]{2,1,0:T(8,128)}) custom-call(s32[48]{0:T(128)S(1)} %reshape_squeeze.6.src_ref, s32[6]{0:T(128)S(1)} %add_multiply_fusion.base_ref, s32[4]{0:T(128)S(1)} %and_select_fusion.peer_ref, ...), custom_call_target="tpu_custom_call" | custom-call | tf_op jit(solution)/shard_map/pallas_call | solution.py:130
  119.8 2.2 fusion
  124.9 7.9 %all-to-all-start.3 = ((bf16[32,2,128,128]{2,3,1,0:T(8,128)(2,1)}), bf16[32,2,128,128]{2,3,1,0:T(8,128)(2,1)}, u32[]{:S(2)}, u32[]{:S(2)}) async-start(bf16[32,2,128,128]{2,3,1,0:T(8,128)(2,1)} %copy.115), calls=%async_computation.3 | async-start | bytes 4194304 | tf_op jit(solution)/shard_map/all_to_all | solution.py:205
  132.9 3.3 %pad_maximum_fusion.2.refs_0_ = bf16[38,2,128,128]{3,2,1,0:T(8,128)(2,1)} fusion(bf16[6,2,128,128]{3,2,1,0:T(8,128)(2,1)S(1)} %get-tuple-element.55, bf16[32,2,128,128]{3,2,1,0:T(8,128)(2,1)} %all-to-all-done.1), kind=kLoop, calls=%fused_computation.16 | loop fusion | flops 1245184 | bytes 4980736 | tf_op jit(solution)/shard_map/concatenate | solution.py:196
  136.1 26.7 %shard_map.85 = (bf16[768,512]{1,0:T(8,128)(2,1)S(1)}, bf16[768,512]{1,0:T(8,128)(2,1)S(1)}, f32[38,128,128]{2,1,0:T(8,128)S(1)}, f32[38,128,128]{2,1,0:T(8,128)}) custom-call(s32[48]{0:T(128)S(1)} %reshape_squeeze.7.src_ref, s32[6]{0:T(128)S(1)} %add_multiply_fusion.base_ref, s32[4]{0:T(128)S(1)} %and_select_fusion.peer_ref, ...), custom_call_target="tpu_custom_call" | custom-call | tf_op jit(solution)/shard_map/pallas_call | solution.py:130
  168.1 8.5 %all-to-all-start.2 = ((bf16[32,2,128,128]{2,3,1,0:T(8,128)(2,1)}), bf16[32,2,128,128]{2,3,1,0:T(8,128)(2,1)}, u32[]{:S(2)}, u32[]{:S(2)}) async-start(bf16[32,2,128,128]{2,3,1,0:T(8,128)(2,1)} %copy.114), calls=%async_computation.2 | async-start | bytes 4194304 | tf_op jit(solution)/shard_map/all_to_all | solution.py:205
  178.5 4.6 %copy.116 = bf16[32,2,128,128]{3,0,2,1:T(8,128)(2,1)} copy(bf16[32,2,128,128]{2,3,1,0:T(8,128)(2,1)} %all-to-all-done.3) | data formatting | bytes 4194304 | tf_op jit(solution)/shard_map/all_to_all | solution.py:205
  183.1 2.9 %fusion.21 = f32[6,2,128,128]{3,0,2,1:T(8,128)} fusion(bf16[32,2,128,128]{3,0,2,1:T(8,128)(2,1)} %copy.116, bf16[2,32,6]{1,2,0:T(8,128)(2,1)S(1)} %broadcast_select_fusion), kind=kOutput, calls=%fused_computation.108 | convolution fusion | flops 12582912 | bytes 2885632 | tf_op jit(solution)/shard_map/rl,rktd->lktd/dot_general | solution.py:219
  186.0 2.4 copy.117
  191.7 13.6 %all-to-all-done.2 = bf16[32,2,128,128]{2,3,1,0:T(8,128)(2,1)} async-done(((bf16[32,2,128,128]{2,3,1,0:T(8,128)(2,1)}), bf16[32,2,128,128]{2,3,1,0:T(8,128)(2,1)}, u32[]{:S(2)}, u32[]{:S(2)}) %all-to-all-start.2) | async-done | bytes 2097184 | tf_op jit(solution)/shard_map/all_to_all | solution.py:205
  205.4 4.5 %copy.119 = bf16[32,2,128,128]{3,0,2,1:T(8,128)(2,1)} copy(bf16[32,2,128,128]{2,3,1,0:T(8,128)(2,1)} %all-to-all-done.2) | data formatting | bytes 4194304 | tf_op jit(solution)/shard_map/optimization_barrier | solution.py:214
  209.9 2.9 %fusion.20 = f32[6,2,128,128]{3,0,2,1:T(8,128)} fusion(bf16[32,2,128,128]{3,0,2,1:T(8,128)(2,1)} %copy.119, bf16[2,32,6]{1,2,0:T(8,128)(2,1)S(1)} %broadcast_select_fusion), kind=kOutput, calls=%fused_computation.106 | convolution fusion | flops 12582912 | bytes 2885632 | tf_op jit(solution)/shard_map/rl,rktd->lktd/dot_general | solution.py:219
  212.9 2.4 copy.120
  222.1 3.2 %collective-permute-start.9 = (bf16[2,192,2,128]{3,1,2,0:T(8,128)(2,1)S(1)}, bf16[2,192,2,128]{3,1,2,0:T(8,128)(2,1)S(1)}, u32[]{:S(2)}, u32[]{:S(2)}) collective-permute-start(bf16[2,192,2,128]{3,1,2,0:T(8,128)(2,1)S(1)} %get-tuple-element.53), channel_id=1, source_target_pairs={{0,96},{32,0},{64,32},{96,64},{1,97},{33,1},{65,33},{97,65},{2,98}... | collective-permute-start | bytes 589832 | tf_op jit(solution)/shard_map/ppermute | solution.py:19
  225.7 3.2 %collective-permute-start.6 = (bf16[2,192,8,128]{3,2,1,0:T(8,128)(2,1)S(1)}, bf16[2,192,8,128]{3,2,1,0:T(8,128)(2,1)S(1)}, u32[]{:S(2)}, u32[]{:S(2)}) collective-permute-start(bf16[2,192,8,128]{3,2,1,0:T(8,128)(2,1)S(1)} %get-tuple-element.43), channel_id=1, source_target_pairs={{0,96},{32,0},{64,32},{96,64},{1,97},{33,1},{65,33},{97,65},{2,98}... | collective-permute-start | bytes 2359304 | tf_op jit(solution)/shard_map/ppermute | solution.py:19
  231.0 4.1 %collective-permute-start.7 = (bf16[2,192,8,128]{3,2,1,0:T(8,128)(2,1)S(1)}, bf16[2,192,8,128]{3,2,1,0:T(8,128)(2,1)S(1)}, u32[]{:S(2)}, u32[]{:S(2)}) collective-permute-start(bf16[2,192,8,128]{3,2,1,0:T(8,128)(2,1)S(1)} %get-tuple-element.44), channel_id=1, source_target_pairs={{0,64},{32,96},{64,0},{96,32},{1,65},{33,97},{65,1},{97,33},{2,66}... | collective-permute-start | bytes 2359304 | tf_op jit(solution)/shard_map/ppermute | solution.py:19
  237.5 10.4 %collective-permute-done.6 = bf16[2,192,8,128]{3,2,1,0:T(8,128)(2,1)S(1)} collective-permute-done((bf16[2,192,8,128]{3,2,1,0:T(8,128)(2,1)S(1)}, bf16[2,192,8,128]{3,2,1,0:T(8,128)(2,1)S(1)}, u32[]{:S(2)}, u32[]{:S(2)}) %collective-permute-start.6) | collective-permute-done | bytes 786464 | tf_op jit(solution)/shard_map/ppermute | solution.py:19
  248.1 20.5 %collective-permute-done.7 = bf16[2,192,8,128]{3,2,1,0:T(8,128)(2,1)S(1)} collective-permute-done((bf16[2,192,8,128]{3,2,1,0:T(8,128)(2,1)S(1)}, bf16[2,192,8,128]{3,2,1,0:T(8,128)(2,1)S(1)}, u32[]{:S(2)}, u32[]{:S(2)}) %collective-permute-start.7) | collective-permute-done | bytes 786464 | tf_op jit(solution)/shard_map/ppermute | solution.py:19
  270.3 2.4 dynamic-slice_bitcast_fusion
  (106 shorter events, 45.4 us)
Async XLA Ops:
  2.9 12.2 %collective-permute-start.2 = (bf16[2,192,2,128]{3,1,2,0:T(8,128)(2,1)S(1)}, bf16[2,192,2,128]{3,1,2,0:T(8,128)(2,1)S(1)}, u32[]{:S(2)}, u32[]{:S(2)}) collective-permute-start(bf16[2,192,2,128]{3,1,2,0:T(8,128)(2,1)S(1)} %get-tuple-element.56), channel_id=1, source_target_pairs={{0,32},{32,64},{64,96},{96,0},{1,33},{33,65},{65,97},{97,1},{2,34}... | collective-permute-start | bytes 589832 | tf_op jit(solution)/shard_map/ppermute | solution.py:19
  3.0 12.1 %collective-permute-start.1 = (bf16[2,192,2,128]{3,1,2,0:T(8,128)(2,1)S(1)}, bf16[2,192,2,128]{3,1,2,0:T(8,128)(2,1)S(1)}, u32[]{:S(2)}, u32[]{:S(2)}) collective-permute-start(bf16[2,192,2,128]{3,1,2,0:T(8,128)(2,1)S(1)} %get-tuple-element.57), channel_id=1, source_target_pairs={{0,64},{32,96},{64,0},{96,32},{1,65},{33,97},{65,1},{97,33},{2,66}... | collective-permute-start | bytes 589832 | tf_op jit(solution)/shard_map/ppermute | solution.py:19
  6.2 8.8 %collective-permute-start = (bf16[2,192,2,128]{3,1,2,0:T(8,128)(2,1)S(1)}, bf16[2,192,2,128]{3,1,2,0:T(8,128)(2,1)S(1)}, u32[]{:S(2)}, u32[]{:S(2)}) collective-permute-start(bf16[2,192,2,128]{3,1,2,0:T(8,128)(2,1)S(1)} %get-tuple-element.58), channel_id=1, source_target_pairs={{0,96},{32,0},{64,32},{96,64},{1,97},{33,1},{65,33},{97,65},{2,98}... | collective-permute-start | bytes 589832 | tf_op jit(solution)/shard_map/ppermute | solution.py:19
  18.4 40.8 %all-to-all-start = ((bf16[32,2,128,128]{3,2,1,0:T(8,128)(2,1)}), bf16[32,2,128,128]{3,2,1,0:T(8,128)(2,1)S(1)}, u32[]{:S(2)}, u32[]{:S(2)}) async-start(bf16[32,2,128,128]{3,2,1,0:T(8,128)(2,1)} %copy.144), calls=%async_computation | async-start | bytes 4194304 | tf_op jit(solution)/shard_map/all_to_all | solution.py:195
  33.8 2.0 copy-start.4
  38.1 29.1 %collective-permute-start.5 = (bf16[2,192,1024]{2,1,0:T(8,128)(2,1)}, bf16[2,192,1024]{2,1,0:T(8,128)(2,1)}, u32[]{:S(2)}, u32[]{:S(2)}) collective-permute-start(bf16[2,192,1024]{2,1,0:T(8,128)(2,1)} %get-tuple-element.46), channel_id=1, source_target_pairs={{0,96},{32,0},{64,32},{96,64},{1,97},{33,1},{65,33},{97,65},{2,98}... | collective-permute-start | bytes 2359304 | tf_op jit(solution)/shard_map/ppermute | solution.py:155
  41.8 43.4 %collective-permute-start.4 = (bf16[2,192,1024]{2,1,0:T(8,128)(2,1)}, bf16[2,192,1024]{2,1,0:T(8,128)(2,1)}, u32[]{:S(2)}, u32[]{:S(2)}) collective-permute-start(bf16[2,192,1024]{2,1,0:T(8,128)(2,1)} %get-tuple-element.47), channel_id=1, source_target_pairs={{0,64},{32,96},{64,0},{96,32},{1,65},{33,97},{65,1},{97,33},{2,66}... | collective-permute-start | bytes 2359304 | tf_op jit(solution)/shard_map/ppermute | solution.py:155
  42.6 45.5 %collective-permute-start.3 = (bf16[2,192,1024]{2,1,0:T(8,128)(2,1)}, bf16[2,192,1024]{2,1,0:T(8,128)(2,1)}, u32[]{:S(2)}, u32[]{:S(2)}) collective-permute-start(bf16[2,192,1024]{2,1,0:T(8,128)(2,1)} %get-tuple-element.48), channel_id=1, source_target_pairs={{0,32},{32,64},{64,96},{96,0},{1,33},{33,65},{65,97},{97,1},{2,34}... | collective-permute-start | bytes 2359304 | tf_op jit(solution)/shard_map/ppermute | solution.py:155
  59.2 1.3 copy-start.2
  60.6 64.3 %all-to-all-start.1 = ((bf16[32,2,128,128]{3,2,1,0:T(8,128)(2,1)}), bf16[32,2,128,128]{3,2,1,0:T(8,128)(2,1)}, u32[]{:S(2)}, u32[]{:S(2)}) async-start(bf16[32,2,128,128]{3,2,1,0:T(8,128)(2,1)} %copy.143), calls=%async_computation.1 | async-start | bytes 4194304 | tf_op jit(solution)/shard_map/all_to_all | solution.py:195
  88.2 3.3 %copy-start.3 = (bf16[32,2,128,128]{3,2,1,0:T(8,128)(2,1)S(1)}, bf16[32,2,128,128]{3,2,1,0:T(8,128)(2,1)}, u32[]{:S(2)}) copy-start(bf16[32,2,128,128]{3,2,1,0:T(8,128)(2,1)} %copy-done.2) | copy-start | bytes 6291460
  122.0 1.5 copy-start
  124.9 43.2 %all-to-all-start.3 = ((bf16[32,2,128,128]{2,3,1,0:T(8,128)(2,1)}), bf16[32,2,128,128]{2,3,1,0:T(8,128)(2,1)}, u32[]{:S(2)}, u32[]{:S(2)}) async-start(bf16[32,2,128,128]{2,3,1,0:T(8,128)(2,1)} %copy.115), calls=%async_computation.3 | async-start | bytes 4194304 | tf_op jit(solution)/shard_map/all_to_all | solution.py:205
  165.0 1.5 copy-start.1
  168.1 37.3 %all-to-all-start.2 = ((bf16[32,2,128,128]{2,3,1,0:T(8,128)(2,1)}), bf16[32,2,128,128]{2,3,1,0:T(8,128)(2,1)}, u32[]{:S(2)}, u32[]{:S(2)}) async-start(bf16[32,2,128,128]{2,3,1,0:T(8,128)(2,1)} %copy.114), calls=%async_computation.2 | async-start | bytes 4194304 | tf_op jit(solution)/shard_map/all_to_all | solution.py:205
  222.0 13.2 %collective-permute-start.11 = (bf16[2,192,2,128]{3,1,2,0:T(8,128)(2,1)S(1)}, bf16[2,192,2,128]{3,1,2,0:T(8,128)(2,1)S(1)}, u32[]{:S(2)}, u32[]{:S(2)}) collective-permute-start(bf16[2,192,2,128]{3,1,2,0:T(8,128)(2,1)S(1)} %get-tuple-element.51), channel_id=1, source_target_pairs={{0,32},{32,64},{64,96},{96,0},{1,33},{33,65},{65,97},{97,1},{2,34}... | collective-permute-start | bytes 589832 | tf_op jit(solution)/shard_map/ppermute | solution.py:19
  222.0 13.1 %collective-permute-start.10 = (bf16[2,192,2,128]{3,1,2,0:T(8,128)(2,1)S(1)}, bf16[2,192,2,128]{3,1,2,0:T(8,128)(2,1)S(1)}, u32[]{:S(2)}, u32[]{:S(2)}) collective-permute-start(bf16[2,192,2,128]{3,1,2,0:T(8,128)(2,1)S(1)} %get-tuple-element.52), channel_id=1, source_target_pairs={{0,64},{32,96},{64,0},{96,32},{1,65},{33,97},{65,1},{97,33},{2,66}... | collective-permute-start | bytes 589832 | tf_op jit(solution)/shard_map/ppermute | solution.py:19
  222.1 8.9 %collective-permute-start.9 = (bf16[2,192,2,128]{3,1,2,0:T(8,128)(2,1)S(1)}, bf16[2,192,2,128]{3,1,2,0:T(8,128)(2,1)S(1)}, u32[]{:S(2)}, u32[]{:S(2)}) collective-permute-start(bf16[2,192,2,128]{3,1,2,0:T(8,128)(2,1)S(1)} %get-tuple-element.53), channel_id=1, source_target_pairs={{0,96},{32,0},{64,32},{96,64},{1,97},{33,1},{65,33},{97,65},{2,98}... | collective-permute-start | bytes 589832 | tf_op jit(solution)/shard_map/ppermute | solution.py:19
  225.5 43.4 %collective-permute-start.8 = (bf16[2,192,8,128]{3,2,1,0:T(8,128)(2,1)S(1)}, bf16[2,192,8,128]{3,2,1,0:T(8,128)(2,1)S(1)}, u32[]{:S(2)}, u32[]{:S(2)}) collective-permute-start(bf16[2,192,8,128]{3,2,1,0:T(8,128)(2,1)S(1)} %get-tuple-element.42), channel_id=1, source_target_pairs={{0,32},{32,64},{64,96},{96,0},{1,33},{33,65},{65,97},{97,1},{2,34}... | collective-permute-start | bytes 2359304 | tf_op jit(solution)/shard_map/ppermute | solution.py:19
  225.7 22.2 %collective-permute-start.6 = (bf16[2,192,8,128]{3,2,1,0:T(8,128)(2,1)S(1)}, bf16[2,192,8,128]{3,2,1,0:T(8,128)(2,1)S(1)}, u32[]{:S(2)}, u32[]{:S(2)}) collective-permute-start(bf16[2,192,8,128]{3,2,1,0:T(8,128)(2,1)S(1)} %get-tuple-element.43), channel_id=1, source_target_pairs={{0,96},{32,0},{64,32},{96,64},{1,97},{33,1},{65,33},{97,65},{2,98}... | collective-permute-start | bytes 2359304 | tf_op jit(solution)/shard_map/ppermute | solution.py:19
  231.0 37.7 %collective-permute-start.7 = (bf16[2,192,8,128]{3,2,1,0:T(8,128)(2,1)S(1)}, bf16[2,192,8,128]{3,2,1,0:T(8,128)(2,1)S(1)}, u32[]{:S(2)}, u32[]{:S(2)}) collective-permute-start(bf16[2,192,8,128]{3,2,1,0:T(8,128)(2,1)S(1)} %get-tuple-element.44), channel_id=1, source_target_pairs={{0,64},{32,96},{64,0},{96,32},{1,65},{33,97},{65,1},{97,33},{2,66}... | collective-permute-start | bytes 2359304 | tf_op jit(solution)/shard_map/ppermute | solution.py:19

commit v11 on v9

--- a/solution.py
+++ b/solution.py
@@ -189,6 +189,10 @@
     query_base = (rank * block_ids + block_range) * BLOCK_TOKENS
 
     outs, query_grads, backs, locals_ = [], [], [], []
+
+    def heads_layout(parts):
+        return jnp.concatenate(parts, axis=1).reshape(run_len, head_count, head_width)
+
     for g in range(groups):
         send = jnp.einsum(
             "rb,bktd->rktd", pick_send[g], kv_local[g], preferred_element_type=jnp.float32
@@ -203,18 +207,16 @@
         acc = jnp.stack([dk_acc, dv_acc], axis=1)
         remote = acc[:peers].astype(jnp.bfloat16)
         local = acc[peers:].astype(jnp.bfloat16)
+        if g == groups - 1:
+            attn_all, query_grad_all, remote, backs[0] = lax.optimization_barrier(
+                (heads_layout(outs), heads_layout(query_grads), remote, backs[0])
+            )
         backs.append(lax.all_to_all(remote, "blk", split_axis=0, concat_axis=0, tiled=True))
         locals_.append(local)
 
-    def heads_layout(parts):
-        return jnp.concatenate(parts, axis=1).reshape(run_len, head_count, head_width)
-
     def group_layout(parts):
         return jnp.stack(parts, axis=2).reshape(run_len, groups, head_width)
 
-    attn_all, query_grad_all, backs[-1] = lax.optimization_barrier(
-        (heads_layout(outs), heads_layout(query_grads), backs[-1])
-    )
     key_grads, value_grads = [], []
     for g in range(groups):
         total = locals_[g].astype(jnp.float32) + jnp.einsum(

time: 265 us -> 265 us (level)
  local copies, waits for them, and re-layouts: 32.4 us -> 39.8 us
  waiting for transfers between devices: 95.1 us -> 89.4 us
  other arithmetic: 23.8 us -> 18.8 us
  starting transfers between devices: 47.9 us -> 52.8 us
    all_to_all x2, waiting for transfers between devices: 22.7 us -> 0.01 us  [on_device(): lax.all_to_all(remote, 'blk', split_axis=0, concat_axis=0, tiled=True)]
    ppermute x9, waiting for transfers between devices: 36.4 us -> 53.4 us  [exchange(): lax.ppermute(piece, 'head', [(i, (i + k) % size) for i in range(size)])]
    ppermute x9, starting transfers between devices: 13.6 us -> 18.6 us  [exchange(): lax.ppermute(piece, 'head', [(i, (i + k) % size) for i in range(size)])]
    unnamed x55 -> x47, local copies, waits for them, and re-layouts: 7.81 us -> 12 us
    optimization_barrier x0 -> x1, local copies, waits for them, and re-layouts: none -> 3.25 us  [on_device(): lax.optimization_barrier((heads_layout(outs), heads_layout(query_grads),...]
  transfers between devices with their start and end apart: 16 -> 16, of which waited for: 10 -> 9; matrix products, arithmetic and copies ran while one was open for 18% -> 18% of each run, Pallas kernels for 20% -> 20%
where the time goes in v11:
time: 265 us; the launch traced here: 263 us
  waiting for transfers between devices  89.4 us (34%)
  Pallas kernels  53.3 us (20%)
  starting transfers between devices  52.8 us (20%)
  local copies, waits for them, and re-layouts  39.8 us (15%)
  other arithmetic  18.8 us (7%)
  matrix products  7.34 us (3%)
    ppermute x9, waiting for transfers between devices, exchange(): lax.ppermute(piece, 'head', [(i, (i + k) % size) for i in range(size)])  53.4 us
    pallas_call x2, Pallas kernels, attend(): pl.pallas_call(attention_kernel, grid_spec=grid_spec, out_shape=out_shape...  53.3 us
    ppermute x3, waiting for transfers between devices, on_device(): lax.ppermute(piece, 'head', [(i, (i + k) % size) for i in range(size)])  22.3 us
    ppermute x9, starting transfers between devices, exchange(): lax.ppermute(piece, 'head', [(i, (i + k) % size) for i in range(size)])  18.6 us
    all_to_all x2, starting transfers between devices, on_device(): lax.all_to_all(remote, 'blk', split_axis=0, concat_axis=0, tiled=True)  16.4 us
    all_to_all x2, waiting for transfers between devices, on_device(): recv = lax.all_to_all(send, 'blk', split_axis=0, concat_axis=0, tiled=True)  13.8 us
    all_to_all x2, starting transfers between devices, on_device(): recv = lax.all_to_all(send, 'blk', split_axis=0, concat_axis=0, tiled=True)  13.3 us
    unnamed x47, local copies, waits for them, and re-layouts  12 us
  transfers between devices with their start and end apart: 16, of which 9 were waited for; matrix products, arithmetic and copies ran while one was open for 18% of the time, Pallas kernels for 20%

profile of v11, /device:TPU:0, one launch (start us, length us, event | category | flops | bytes accessed | tf_op | source)
XLA Modules:
  0.0 262.8 jit_solution(10535132855249665906)
XLA Ops:
  3.0 3.2 %collective-permute-start.1 = (bf16[2,192,2,128]{3,1,2,0:T(8,128)(2,1)S(1)}, bf16[2,192,2,128]{3,1,2,0:T(8,128)(2,1)S(1)}, u32[]{:S(2)}, u32[]{:S(2)}) collective-permute-start(bf16[2,192,2,128]{3,1,2,0:T(8,128)(2,1)S(1)} %get-tuple-element.48), channel_id=1, source_target_pairs={{0,64},{32,96},{64,0},{96,32},{1,65},{33,97},{65,1},{97,33},{2,66}... | collective-permute-start | bytes 589832 | tf_op jit(solution)/shard_map/ppermute | solution.py:19
  6.2 2.9 %collective-permute-start = (bf16[2,192,2,128]{3,1,2,0:T(8,128)(2,1)S(1)}, bf16[2,192,2,128]{3,1,2,0:T(8,128)(2,1)S(1)}, u32[]{:S(2)}, u32[]{:S(2)}) collective-permute-start(bf16[2,192,2,128]{3,1,2,0:T(8,128)(2,1)S(1)} %get-tuple-element.49), channel_id=1, source_target_pairs={{0,96},{32,0},{64,32},{96,64},{1,97},{33,1},{65,33},{97,65},{2,98}... | collective-permute-start | bytes 589832 | tf_op jit(solution)/shard_map/ppermute | solution.py:19
  11.4 3.6 %collective-permute-done = bf16[2,192,2,128]{3,1,2,0:T(8,128)(2,1)S(1)} collective-permute-done((bf16[2,192,2,128]{3,1,2,0:T(8,128)(2,1)S(1)}, bf16[2,192,2,128]{3,1,2,0:T(8,128)(2,1)S(1)}, u32[]{:S(2)}, u32[]{:S(2)}) %collective-permute-start) | collective-permute-done | bytes 196640 | tf_op jit(solution)/shard_map/ppermute | solution.py:19
  16.3 2.2 copy.131
  18.5 8.4 %all-to-all-start = ((bf16[32,2,128,128]{3,2,1,0:T(8,128)(2,1)}), bf16[32,2,128,128]{3,2,1,0:T(8,128)(2,1)S(1)}, u32[]{:S(2)}, u32[]{:S(2)}) async-start(bf16[32,2,128,128]{3,2,1,0:T(8,128)(2,1)} %copy.131), calls=%async_computation | async-start | bytes 4194304 | tf_op jit(solution)/shard_map/all_to_all | solution.py:200
  26.8 3.5 %stack.121 = bf16[1,192,4,1024]{3,2,1,0:T(4,128)(2,1)} reshape(bf16[192,32,128]{2,1,0:T(8,128)(2,1)} %param.5) | data formatting | bytes 3145728 | tf_op jit(solution)/shard_map/stack | solution.py:150
  30.3 3.5 %stack.122 = bf16[1,192,4,1024]{3,2,1,0:T(4,128)(2,1)} reshape(bf16[192,32,128]{2,1,0:T(8,128)(2,1)} %param.9) | data formatting | bytes 3145728 | tf_op jit(solution)/shard_map/stack | solution.py:150
  33.8 2.0 copy_dynamic-update-slice_fusion.1
  38.0 3.7 %collective-permute-start.5 = (bf16[2,192,1024]{2,1,0:T(8,128)(2,1)}, bf16[2,192,1024]{2,1,0:T(8,128)(2,1)}, u32[]{:S(2)}, u32[]{:S(2)}) collective-permute-start(bf16[2,192,1024]{2,1,0:T(8,128)(2,1)} %get-tuple-element.36), channel_id=1, source_target_pairs={{0,96},{32,0},{64,32},{96,64},{1,97},{33,1},{65,33},{97,65},{2,98}... | collective-permute-start | bytes 2359304 | tf_op jit(solution)/shard_map/ppermute | solution.py:156
  43.4 2.1 copy.130
  45.5 13.8 %all-to-all-done = bf16[32,2,128,128]{3,2,1,0:T(8,128)(2,1)S(1)} async-done(((bf16[32,2,128,128]{3,2,1,0:T(8,128)(2,1)}), bf16[32,2,128,128]{3,2,1,0:T(8,128)(2,1)S(1)}, u32[]{:S(2)}, u32[]{:S(2)}) %all-to-all-start) | async-done | bytes 2097184 | tf_op jit(solution)/shard_map/all_to_all | solution.py:200
  59.3 5.0 %all-to-all-start.1 = ((bf16[32,2,128,128]{3,2,1,0:T(8,128)(2,1)}), bf16[32,2,128,128]{3,2,1,0:T(8,128)(2,1)}, u32[]{:S(2)}, u32[]{:S(2)}) async-start(bf16[32,2,128,128]{3,2,1,0:T(8,128)(2,1)} %copy.130), calls=%async_computation.1 | async-start | bytes 4194304 | tf_op jit(solution)/shard_map/all_to_all | solution.py:200
  66.7 18.5 %collective-permute-done.4 = bf16[2,192,1024]{2,1,0:T(8,128)(2,1)} collective-permute-done((bf16[2,192,1024]{2,1,0:T(8,128)(2,1)}, bf16[2,192,1024]{2,1,0:T(8,128)(2,1)}, u32[]{:S(2)}, u32[]{:S(2)}) %collective-permute-start.4) | collective-permute-done | bytes 786464 | tf_op jit(solution)/shard_map/ppermute | solution.py:156
  85.2 3.0 %collective-permute-done.3 = bf16[2,192,1024]{2,1,0:T(8,128)(2,1)} collective-permute-done((bf16[2,192,1024]{2,1,0:T(8,128)(2,1)}, bf16[2,192,1024]{2,1,0:T(8,128)(2,1)}, u32[]{:S(2)}, u32[]{:S(2)}) %collective-permute-start.3) | collective-permute-done | bytes 786464 | tf_op jit(solution)/shard_map/ppermute | solution.py:156
  88.2 3.2 %pad_maximum_fusion.refs_1_.refs_2_.refs_3_.refs_4_ = bf16[4,2,192,1024]{3,2,1,0:T(8,128)(2,1)} fusion(bf16[1,2,192,1024]{3,2,1,0:T(8,128)(2,1)} %bitcast.21, bf16[1,2,192,1024]{3,2,1,0:T(8,128)(2,1)} %bitcast.19, bf16[1,2,192,1024]{3,2,1,0:T(8,128)(2,1)} %bitcast.17, bf16[1,2,192,1024]{3,2,1,0:T(8,128)(2,1)} %get-tuple-element.35), kind=kLoop, calls=%fused_computation.12 | loop fusion | flops 4718592 | bytes 6291456 | tf_op jit(solution)/shard_map/stack | solution.py:158
  93.1 26.6 %shard_map.84 = (bf16[768,512]{1,0:T(8,128)(2,1)S(1)}, bf16[768,512]{1,0:T(8,128)(2,1)S(1)}, f32[38,128,128]{2,1,0:T(8,128)S(1)}, f32[38,128,128]{2,1,0:T(8,128)}) custom-call(s32[48]{0:T(128)S(1)} %reshape_squeeze.6.src_ref, s32[6]{0:T(128)S(1)} %add_multiply_fusion.base_ref, s32[4]{0:T(128)S(1)} %and_select_fusion.peer_ref, ...), custom_call_target="tpu_custom_call" | custom-call | tf_op jit(solution)/shard_map/pallas_call | solution.py:131
  119.7 3.3 %maximum_convert_fusion.1 = bf16[38,2,128,128]{3,2,0,1:T(8,128)(2,1)S(1)} fusion(f32[38,1,128,128]{3,2,0,1:T(8,128)} %bitcast.148, f32[38,1,128,128]{3,2,0,1:T(8,128)S(1)} %bitcast.136), kind=kLoop, calls=%fused_computation.1 | loop fusion | flops 1245184 | bytes 7471104 | tf_op jit(solution)/shard_map/convert.2
  124.8 8.0 %all-to-all-start.2 = ((bf16[32,2,128,128]{3,2,1,0:T(8,128)(2,1)}), bf16[32,2,128,128]{3,2,1,0:T(8,128)(2,1)}, u32[]{:S(2)}, u32[]{:S(2)}) async-start(bf16[32,2,128,128]{3,2,1,0:T(8,128)(2,1)} %copy.88), calls=%async_computation.2 | async-start | bytes 4194304 | tf_op jit(solution)/shard_map/all_to_all | solution.py:214
  133.1 3.4 %pad_maximum_fusion.2.refs_0_ = bf16[38,2,128,128]{3,2,1,0:T(8,128)(2,1)} fusion(bf16[6,2,128,128]{3,2,1,0:T(8,128)(2,1)S(1)} %copy-done.11, bf16[32,2,128,128]{3,2,1,0:T(8,128)(2,1)} %all-to-all-done.1), kind=kLoop, calls=%fused_computation.14 | loop fusion | flops 1245184 | bytes 4980736 | tf_op jit(solution)/shard_map/concatenate | solution.py:201
  136.4 26.7 %shard_map.85 = (bf16[768,512]{1,0:T(8,128)(2,1)S(1)}, bf16[768,512]{1,0:T(8,128)(2,1)S(1)}, f32[38,128,128]{2,1,0:T(8,128)S(1)}, f32[38,128,128]{2,1,0:T(8,128)}) custom-call(s32[48]{0:T(128)S(1)} %reshape_squeeze.7.src_ref, s32[6]{0:T(128)S(1)} %add_multiply_fusion.base_ref, s32[4]{0:T(128)S(1)} %and_select_fusion.peer_ref, ...), custom_call_target="tpu_custom_call" | custom-call | tf_op jit(solution)/shard_map/pallas_call | solution.py:131
  170.0 3.2 %copy.91 = bf16[32,2,128,128]{3,2,1,0:T(8,128)(2,1)} copy(bf16[32,2,128,128]{3,2,0,1:T(8,128)(2,1)} %slice.108) | data formatting | bytes 4194304 | tf_op jit(solution)/shard_map/optimization_barrier | solution.py:211
  173.2 8.4 %all-to-all-start.3 = ((bf16[32,2,128,128]{3,2,1,0:T(8,128)(2,1)}), bf16[32,2,128,128]{3,2,1,0:T(8,128)(2,1)}, u32[]{:S(2)}, u32[]{:S(2)}) async-start(bf16[32,2,128,128]{3,2,1,0:T(8,128)(2,1)} %copy.91), calls=%async_computation.3 | async-start | bytes 4194304 | tf_op jit(solution)/shard_map/all_to_all | solution.py:214
  183.9 3.2 %collective-permute-start.6 = (bf16[2,192,8,128]{3,2,1,0:T(8,128)(2,1)S(1)}, bf16[2,192,8,128]{3,2,1,0:T(8,128)(2,1)S(1)}, u32[]{:S(2)}, u32[]{:S(2)}) collective-permute-start(bf16[2,192,8,128]{3,2,1,0:T(8,128)(2,1)S(1)} %get-tuple-element.33), channel_id=1, source_target_pairs={{0,96},{32,0},{64,32},{96,64},{1,97},{33,1},{65,33},{97,65},{2,98}... | collective-permute-start | bytes 2359304 | tf_op jit(solution)/shard_map/ppermute | solution.py:19
  187.1 5.0 %collective-permute-start.7 = (bf16[2,192,8,128]{3,2,1,0:T(8,128)(2,1)S(1)}, bf16[2,192,8,128]{3,2,1,0:T(8,128)(2,1)S(1)}, u32[]{:S(2)}, u32[]{:S(2)}) collective-permute-start(bf16[2,192,8,128]{3,2,1,0:T(8,128)(2,1)S(1)} %get-tuple-element.34), channel_id=1, source_target_pairs={{0,64},{32,96},{64,0},{96,32},{1,65},{33,97},{65,1},{97,33},{2,66}... | collective-permute-start | bytes 2359304 | tf_op jit(solution)/shard_map/ppermute | solution.py:19
  192.1 2.8 %fusion.2 = f32[6,2,128,128]{3,0,2,1:T(8,128)S(1)} fusion(bf16[32,2,128,128]{3,2,1,0:T(8,128)(2,1)} %all-to-all-done.2, bf16[2,32,6]{1,2,0:T(8,128)(2,1)S(1)} %broadcast_select_fusion), kind=kOutput, calls=%fused_computation.17 | convolution fusion | flops 12582912 | bytes 2885632 | tf_op jit(solution)/shard_map/rl,rktd->lktd/dot_general | solution.py:222
  197.0 24.8 %collective-permute-done.6 = bf16[2,192,8,128]{3,2,1,0:T(8,128)(2,1)S(1)} collective-permute-done((bf16[2,192,8,128]{3,2,1,0:T(8,128)(2,1)S(1)}, bf16[2,192,8,128]{3,2,1,0:T(8,128)(2,1)S(1)}, u32[]{:S(2)}, u32[]{:S(2)}) %collective-permute-start.6) | collective-permute-done | bytes 786464 | tf_op jit(solution)/shard_map/ppermute | solution.py:19
  222.1 15.9 %collective-permute-done.7 = bf16[2,192,8,128]{3,2,1,0:T(8,128)(2,1)S(1)} collective-permute-done((bf16[2,192,8,128]{3,2,1,0:T(8,128)(2,1)S(1)}, bf16[2,192,8,128]{3,2,1,0:T(8,128)(2,1)S(1)}, u32[]{:S(2)}, u32[]{:S(2)}) %collective-permute-start.7) | collective-permute-done | bytes 786464 | tf_op jit(solution)/shard_map/ppermute | solution.py:19
  239.7 2.4 dynamic-slice_bitcast_fusion
  242.1 3.0 %fusion = f32[6,2,128,128]{3,0,2,1:T(8,128)S(1)} fusion(bf16[32,2,128,128]{3,2,1,0:T(8,128)(2,1)} %all-to-all-done.3, bf16[2,32,6]{1,2,0:T(8,128)(2,1)S(1)} %broadcast_select_fusion), kind=kOutput, calls=%fused_computation.15 | convolution fusion | flops 12582912 | bytes 2885632 | tf_op jit(solution)/shard_map/rl,rktd->lktd/dot_general | solution.py:222
  246.1 2.3 collective-permute-start.9
  250.3 2.6 collective-permute-done.9
  253.1 6.5 %collective-permute-done.10 = bf16[2,192,2,128]{3,2,1,0:T(2,128)(2,1)S(1)} collective-permute-done((bf16[2,192,2,128]{3,2,1,0:T(2,128)(2,1)S(1)}, bf16[2,192,2,128]{3,2,1,0:T(2,128)(2,1)S(1)}, u32[]{:S(2)}, u32[]{:S(2)}) %collective-permute-start.10) | collective-permute-done | bytes 196640 | tf_op jit(solution)/shard_map/ppermute | solution.py:19
  (113 shorter events, 34.9 us)
Async XLA Ops:
  2.9 12.2 %collective-permute-start.2 = (bf16[2,192,2,128]{3,1,2,0:T(8,128)(2,1)S(1)}, bf16[2,192,2,128]{3,1,2,0:T(8,128)(2,1)S(1)}, u32[]{:S(2)}, u32[]{:S(2)}) collective-permute-start(bf16[2,192,2,128]{3,1,2,0:T(8,128)(2,1)S(1)} %get-tuple-element.47), channel_id=1, source_target_pairs={{0,32},{32,64},{64,96},{96,0},{1,33},{33,65},{65,97},{97,1},{2,34}... | collective-permute-start | bytes 589832 | tf_op jit(solution)/shard_map/ppermute | solution.py:19
  3.0 12.1 %collective-permute-start.1 = (bf16[2,192,2,128]{3,1,2,0:T(8,128)(2,1)S(1)}, bf16[2,192,2,128]{3,1,2,0:T(8,128)(2,1)S(1)}, u32[]{:S(2)}, u32[]{:S(2)}) collective-permute-start(bf16[2,192,2,128]{3,1,2,0:T(8,128)(2,1)S(1)} %get-tuple-element.48), channel_id=1, source_target_pairs={{0,64},{32,96},{64,0},{96,32},{1,65},{33,97},{65,1},{97,33},{2,66}... | collective-permute-start | bytes 589832 | tf_op jit(solution)/shard_map/ppermute | solution.py:19
  6.2 8.8 %collective-permute-start = (bf16[2,192,2,128]{3,1,2,0:T(8,128)(2,1)S(1)}, bf16[2,192,2,128]{3,1,2,0:T(8,128)(2,1)S(1)}, u32[]{:S(2)}, u32[]{:S(2)}) collective-permute-start(bf16[2,192,2,128]{3,1,2,0:T(8,128)(2,1)S(1)} %get-tuple-element.49), channel_id=1, source_target_pairs={{0,96},{32,0},{64,32},{96,64},{1,97},{33,1},{65,33},{97,65},{2,98}... | collective-permute-start | bytes 589832 | tf_op jit(solution)/shard_map/ppermute | solution.py:19
  15.5 27.1 %copy-start.10 = (bf16[6,2,128,128]{3,2,1,0:T(8,128)(2,1)}, bf16[6,2,128,128]{3,2,1,0:T(8,128)(2,1)S(1)}, u32[]{:S(2)}) copy-start(bf16[6,2,128,128]{3,2,1,0:T(8,128)(2,1)S(1)} %get-tuple-element.46) | copy-start | bytes 1179652
  18.5 40.8 %all-to-all-start = ((bf16[32,2,128,128]{3,2,1,0:T(8,128)(2,1)}), bf16[32,2,128,128]{3,2,1,0:T(8,128)(2,1)S(1)}, u32[]{:S(2)}, u32[]{:S(2)}) async-start(bf16[32,2,128,128]{3,2,1,0:T(8,128)(2,1)} %copy.131), calls=%async_computation | async-start | bytes 4194304 | tf_op jit(solution)/shard_map/all_to_all | solution.py:200
  33.8 2.0 copy-start.9
  38.0 28.7 %collective-permute-start.5 = (bf16[2,192,1024]{2,1,0:T(8,128)(2,1)}, bf16[2,192,1024]{2,1,0:T(8,128)(2,1)}, u32[]{:S(2)}, u32[]{:S(2)}) collective-permute-start(bf16[2,192,1024]{2,1,0:T(8,128)(2,1)} %get-tuple-element.36), channel_id=1, source_target_pairs={{0,96},{32,0},{64,32},{96,64},{1,97},{33,1},{65,33},{97,65},{2,98}... | collective-permute-start | bytes 2359304 | tf_op jit(solution)/shard_map/ppermute | solution.py:156
  41.8 43.4 %collective-permute-start.4 = (bf16[2,192,1024]{2,1,0:T(8,128)(2,1)}, bf16[2,192,1024]{2,1,0:T(8,128)(2,1)}, u32[]{:S(2)}, u32[]{:S(2)}) collective-permute-start(bf16[2,192,1024]{2,1,0:T(8,128)(2,1)} %get-tuple-element.37), channel_id=1, source_target_pairs={{0,64},{32,96},{64,0},{96,32},{1,65},{33,97},{65,1},{97,33},{2,66}... | collective-permute-start | bytes 2359304 | tf_op jit(solution)/shard_map/ppermute | solution.py:156
  42.6 45.6 %collective-permute-start.3 = (bf16[2,192,1024]{2,1,0:T(8,128)(2,1)}, bf16[2,192,1024]{2,1,0:T(8,128)(2,1)}, u32[]{:S(2)}, u32[]{:S(2)}) collective-permute-start(bf16[2,192,1024]{2,1,0:T(8,128)(2,1)} %get-tuple-element.38), channel_id=1, source_target_pairs={{0,32},{32,64},{64,96},{96,0},{1,33},{33,65},{65,97},{97,1},{2,34}... | collective-permute-start | bytes 2359304 | tf_op jit(solution)/shard_map/ppermute | solution.py:156
  59.3 65.5 %all-to-all-start.1 = ((bf16[32,2,128,128]{3,2,1,0:T(8,128)(2,1)}), bf16[32,2,128,128]{3,2,1,0:T(8,128)(2,1)}, u32[]{:S(2)}, u32[]{:S(2)}) async-start(bf16[32,2,128,128]{3,2,1,0:T(8,128)(2,1)} %copy.130), calls=%async_computation.1 | async-start | bytes 4194304 | tf_op jit(solution)/shard_map/all_to_all | solution.py:200
  119.7 3.3 %copy-start = (f32[38,128,128]{2,1,0:T(8,128)}, f32[38,128,128]{2,1,0:T(8,128)S(1)}, u32[]{:S(2)}) copy-start(f32[38,128,128]{2,1,0:T(8,128)S(1)} %get-tuple-element.22) | copy-start | bytes 7471108
  119.7 3.3 %copy-start.2 = (bf16[768,512]{1,0:T(8,128)(2,1)}, bf16[768,512]{1,0:T(8,128)(2,1)S(1)}, u32[]{:S(2)}) copy-start(bf16[768,512]{1,0:T(8,128)(2,1)S(1)} %get-tuple-element.18) | copy-start | bytes 2359300
  124.8 8.3 %copy-start.11 = (bf16[6,2,128,128]{3,2,1,0:T(8,128)(2,1)S(1)}, bf16[6,2,128,128]{3,2,1,0:T(8,128)(2,1)}, u32[]{:S(2)}) copy-start(bf16[6,2,128,128]{3,2,1,0:T(8,128)(2,1)} %copy-done.10) | copy-start | bytes 1179652
  124.8 45.2 %all-to-all-start.2 = ((bf16[32,2,128,128]{3,2,1,0:T(8,128)(2,1)}), bf16[32,2,128,128]{3,2,1,0:T(8,128)(2,1)}, u32[]{:S(2)}, u32[]{:S(2)}) async-start(bf16[32,2,128,128]{3,2,1,0:T(8,128)(2,1)} %copy.88), calls=%async_computation.2 | async-start | bytes 4194304 | tf_op jit(solution)/shard_map/all_to_all | solution.py:214
  136.4 26.7 %copy-start.3 = (bf16[768,512]{1,0:T(8,128)(2,1)S(1)}, bf16[768,512]{1,0:T(8,128)(2,1)}, u32[]{:S(2)}) copy-start(bf16[768,512]{1,0:T(8,128)(2,1)} %copy-done.2) | copy-start | bytes 2359300
  165.7 2.3 copy-start.6
  173.2 68.9 %all-to-all-start.3 = ((bf16[32,2,128,128]{3,2,1,0:T(8,128)(2,1)}), bf16[32,2,128,128]{3,2,1,0:T(8,128)(2,1)}, u32[]{:S(2)}, u32[]{:S(2)}) async-start(bf16[32,2,128,128]{3,2,1,0:T(8,128)(2,1)} %copy.91), calls=%async_computation.3 | async-start | bytes 4194304 | tf_op jit(solution)/shard_map/all_to_all | solution.py:214
  181.6 13.3 %copy-start.8 = (f32[38,128,128]{2,1,0:T(8,128)S(1)}, f32[38,128,128]{2,1,0:T(8,128)}, u32[]{:S(2)}) copy-start(f32[38,128,128]{2,1,0:T(8,128)} %get-tuple-element.23) | copy-start | bytes 7471108
  183.6 11.3 %copy-start.1 = (f32[38,128,128]{2,1,0:T(8,128)S(1)}, f32[38,128,128]{2,1,0:T(8,128)}, u32[]{:S(2)}) copy-start(f32[38,128,128]{2,1,0:T(8,128)} %copy-done) | copy-start | bytes 7471108
  183.6 54.7 %collective-permute-start.8 = (bf16[2,192,8,128]{3,2,1,0:T(8,128)(2,1)S(1)}, bf16[2,192,8,128]{3,2,1,0:T(8,128)(2,1)S(1)}, u32[]{:S(2)}, u32[]{:S(2)}) collective-permute-start(bf16[2,192,8,128]{3,2,1,0:T(8,128)(2,1)S(1)} %get-tuple-element.32), channel_id=1, source_target_pairs={{0,32},{32,64},{64,96},{96,0},{1,33},{33,65},{65,97},{97,1},{2,34}... | collective-permute-start | bytes 2359304 | tf_op jit(solution)/shard_map/ppermute | solution.py:19
  183.9 38.0 %collective-permute-start.6 = (bf16[2,192,8,128]{3,2,1,0:T(8,128)(2,1)S(1)}, bf16[2,192,8,128]{3,2,1,0:T(8,128)(2,1)S(1)}, u32[]{:S(2)}, u32[]{:S(2)}) collective-permute-start(bf16[2,192,8,128]{3,2,1,0:T(8,128)(2,1)S(1)} %get-tuple-element.33), channel_id=1, source_target_pairs={{0,96},{32,0},{64,32},{96,64},{1,97},{33,1},{65,33},{97,65},{2,98}... | collective-permute-start | bytes 2359304 | tf_op jit(solution)/shard_map/ppermute | solution.py:19
  187.1 50.9 %collective-permute-start.7 = (bf16[2,192,8,128]{3,2,1,0:T(8,128)(2,1)S(1)}, bf16[2,192,8,128]{3,2,1,0:T(8,128)(2,1)S(1)}, u32[]{:S(2)}, u32[]{:S(2)}) collective-permute-start(bf16[2,192,8,128]{3,2,1,0:T(8,128)(2,1)S(1)} %get-tuple-element.34), channel_id=1, source_target_pairs={{0,64},{32,96},{64,0},{96,32},{1,65},{33,97},{65,1},{97,33},{2,66}... | collective-permute-start | bytes 2359304 | tf_op jit(solution)/shard_map/ppermute | solution.py:19
  194.9 1.4 copy-start.4
  194.9 1.9 copy-start.5
  242.1 3.0 %copy-start.7 = (f32[38,128,128]{2,1,0:T(8,128)S(1)}, f32[38,128,128]{2,1,0:T(8,128)}, u32[]{:S(2)}) copy-start(f32[38,128,128]{2,1,0:T(8,128)} %get-tuple-element.21) | copy-start | bytes 7471108
  246.1 6.7 %collective-permute-start.9 = (bf16[2,192,2,128]{3,2,1,0:T(2,128)(2,1)S(1)}, bf16[2,192,2,128]{3,2,1,0:T(2,128)(2,1)S(1)}, u32[]{:S(2)}, u32[]{:S(2)}) collective-permute-start(bf16[2,192,2,128]{3,2,1,0:T(2,128)(2,1)S(1)} %bitcast.163), channel_id=1, source_target_pairs={{0,96},{32,0},{64,32},{96,64},{1,97},{33,1},{65,33},{97,65},{2,98}... | collective-permute-start | bytes 589832 | tf_op jit(solution)/shard_map/ppermute | solution.py:19
  248.5 11.1 %collective-permute-start.10 = (bf16[2,192,2,128]{3,2,1,0:T(2,128)(2,1)S(1)}, bf16[2,192,2,128]{3,2,1,0:T(2,128)(2,1)S(1)}, u32[]{:S(2)}, u32[]{:S(2)}) collective-permute-start(bf16[2,192,2,128]{3,2,1,0:T(2,128)(2,1)S(1)} %bitcast.162), channel_id=1, source_target_pairs={{0,64},{32,96},{64,0},{96,32},{1,65},{33,97},{65,1},{97,33},{2,66}... | collective-permute-start | bytes 589832 | tf_op jit(solution)/shard_map/ppermute | solution.py:19
  249.9 10.0 %collective-permute-start.11 = (bf16[2,192,2,128]{3,2,1,0:T(2,128)(2,1)S(1)}, bf16[2,192,2,128]{3,2,1,0:T(2,128)(2,1)S(1)}, u32[]{:S(2)}, u32[]{:S(2)}) collective-permute-start(bf16[2,192,2,128]{3,2,1,0:T(2,128)(2,1)S(1)} %bitcast.161), channel_id=1, source_target_pairs={{0,32},{32,64},{64,96},{96,0},{1,33},{33,65},{65,97},{97,1},{2,34}... | collective-permute-start | bytes 589832 | tf_op jit(solution)/shard_map/ppermute | solution.py:19

commit v12 on v11

--- a/solution.py
+++ b/solution.py
@@ -26,8 +26,7 @@
     size = lax.axis_size("head")
     x = jnp.stack(xs)
     n, tok, heads, d = x.shape
-    x = x.reshape(n, tok, size, heads // size, d)
-    return exchange(x, 2, 1).reshape(n, size * tok, heads // size, d)
+    return lax.all_to_all(x, "head", split_axis=2, concat_axis=1, tiled=True)
 
 
 def from_heads(*xs):

time: 265 us -> 263 us (level)
  waiting for transfers between devices: 89.4 us -> 94.9 us
  starting transfers between devices: 52.8 us -> 48.7 us
    all_to_all x0 -> x1, waiting for transfers between devices: none -> 12.2 us  [to_heads(): return lax.all_to_all(x, 'head', split_axis=2, concat_axis=1, tiled=True)]
    ppermute x9 -> x6, starting transfers between devices: 18.6 us -> 11.4 us  [exchange(): lax.ppermute(piece, 'head', [(i, (i + k) % size) for i in range(size)])]
    ppermute x9 -> x6, waiting for transfers between devices: 53.4 us -> 47.4 us  [exchange(): lax.ppermute(piece, 'head', [(i, (i + k) % size) for i in range(size)])]
    all_to_all x0 -> x1, starting transfers between devices: none -> 4.38 us  [to_heads(): return lax.all_to_all(x, 'head', split_axis=2, concat_axis=1, tiled=True)]
    unnamed x47 -> x35, local copies, waits for them, and re-layouts: 12 us -> 10.3 us
  transfers between devices with their start and end apart: 16 -> 14, of which waited for: 9 -> 7; matrix products, arithmetic and copies ran while one was open for 18% -> 17% of each run, Pallas kernels for 20% -> 20%
where the time goes in v12:
time: 263 us; the launch traced here: 261 us
  waiting for transfers between devices  94.9 us (36%)
  Pallas kernels  53.3 us (20%)
  starting transfers between devices  48.7 us (19%)
  local copies, waits for them, and re-layouts  37.4 us (14%)
  other arithmetic  18.5 us (7%)
  matrix products  7.34 us (3%)
    pallas_call x2, Pallas kernels, attend(): pl.pallas_call(attention_kernel, grid_spec=grid_spec, out_shape=out_shape...  53.3 us
    ppermute x6, waiting for transfers between devices, exchange(): lax.ppermute(piece, 'head', [(i, (i + k) % size) for i in range(size)])  47.4 us
    ppermute x3, waiting for transfers between devices, on_device(): lax.ppermute(piece, 'head', [(i, (i + k) % size) for i in range(size)])  19.8 us
    all_to_all x2, starting transfers between devices, on_device(): lax.all_to_all(remote, 'blk', split_axis=0, concat_axis=0, tiled=True)  17.1 us
    all_to_all x2, waiting for transfers between devices, on_device(): recv = lax.all_to_all(send, 'blk', split_axis=0, concat_axis=0, tiled=True)  15.6 us
    all_to_all x2, starting transfers between devices, on_device(): recv = lax.all_to_all(send, 'blk', split_axis=0, concat_axis=0, tiled=True)  13.4 us
    all_to_all x1, waiting for transfers between devices, to_heads(): return lax.all_to_all(x, 'head', split_axis=2, concat_axis=1, tiled=True)  12.2 us
    ppermute x6, starting transfers between devices, exchange(): lax.ppermute(piece, 'head', [(i, (i + k) % size) for i in range(size)])  11.4 us
  transfers between devices with their start and end apart: 14, of which 7 were waited for; matrix products, arithmetic and copies ran while one was open for 17% of the time, Pallas kernels for 20%

profile of v12, /device:TPU:0, one launch (start us, length us, event | category | flops | bytes accessed | tf_op | source)
XLA Modules:
  0.0 261.5 jit_solution(9827971186577067604)
XLA Ops:
  2.8 4.4 %all-to-all-start = ((bf16[2,192,8,128]{3,1,0,2:T(8,128)(2,1)}), bf16[2,192,8,128]{3,1,0,2:T(8,128)(2,1)S(1)}, u32[]{:S(2)}, u32[]{:S(2)}) async-start(bf16[2,192,8,128]{3,1,0,2:T(8,128)(2,1)} %pad_maximum_fusion.3), calls=%async_computation | async-start | bytes 1572864 | tf_op jit(solution)/shard_map/all_to_all | solution.py:29
  8.2 12.2 %all-to-all-done = bf16[2,192,8,128]{3,1,0,2:T(8,128)(2,1)S(1)} async-done(((bf16[2,192,8,128]{3,1,0,2:T(8,128)(2,1)}), bf16[2,192,8,128]{3,1,0,2:T(8,128)(2,1)S(1)}, u32[]{:S(2)}, u32[]{:S(2)}) %all-to-all-start) | async-done | bytes 786464 | tf_op jit(solution)/shard_map/all_to_all | solution.py:29
  21.4 2.1 copy.157
  23.5 8.4 %all-to-all-start.1 = ((bf16[32,2,128,128]{3,2,1,0:T(8,128)(2,1)}), bf16[32,2,128,128]{3,2,1,0:T(8,128)(2,1)S(1)}, u32[]{:S(2)}, u32[]{:S(2)}) async-start(bf16[32,2,128,128]{3,2,1,0:T(8,128)(2,1)} %copy.157), calls=%async_computation.1 | async-start | bytes 4194304 | tf_op jit(solution)/shard_map/all_to_all | solution.py:199
  32.0 3.5 %stack.104 = bf16[1,192,4,1024]{3,2,1,0:T(4,128)(2,1)} reshape(bf16[192,32,128]{2,1,0:T(8,128)(2,1)} %param.5) | data formatting | bytes 3145728 | tf_op jit(solution)/shard_map/stack | solution.py:149
  35.5 3.5 %stack.105 = bf16[1,192,4,1024]{3,2,1,0:T(4,128)(2,1)} reshape(bf16[192,32,128]{2,1,0:T(8,128)(2,1)} %param.9) | data formatting | bytes 3145728 | tf_op jit(solution)/shard_map/stack | solution.py:149
  39.0 2.0 copy_dynamic-update-slice_fusion.1
  41.5 1.7 dynamic-slice_bitcast_fusion.5
  43.4 2.3 collective-permute-start.1
  46.5 2.2 copy.156
  48.7 15.6 %all-to-all-done.1 = bf16[32,2,128,128]{3,2,1,0:T(8,128)(2,1)S(1)} async-done(((bf16[32,2,128,128]{3,2,1,0:T(8,128)(2,1)}), bf16[32,2,128,128]{3,2,1,0:T(8,128)(2,1)S(1)}, u32[]{:S(2)}, u32[]{:S(2)}) %all-to-all-start.1) | async-done | bytes 2097184 | tf_op jit(solution)/shard_map/all_to_all | solution.py:199
  64.3 5.0 %all-to-all-start.2 = ((bf16[32,2,128,128]{3,2,1,0:T(8,128)(2,1)}), bf16[32,2,128,128]{3,2,1,0:T(8,128)(2,1)}, u32[]{:S(2)}, u32[]{:S(2)}) async-start(bf16[32,2,128,128]{3,2,1,0:T(8,128)(2,1)} %copy.156), calls=%async_computation.2 | async-start | bytes 4194304 | tf_op jit(solution)/shard_map/all_to_all | solution.py:199
  72.5 18.2 %collective-permute-done.1 = bf16[2,192,1024]{2,1,0:T(8,128)(2,1)} collective-permute-done((bf16[2,192,1024]{2,1,0:T(8,128)(2,1)}, bf16[2,192,1024]{2,1,0:T(8,128)(2,1)}, u32[]{:S(2)}, u32[]{:S(2)}) %collective-permute-start.1) | collective-permute-done | bytes 786464 | tf_op jit(solution)/shard_map/ppermute | solution.py:155
  90.7 3.2 %pad_maximum_fusion.refs_1_.refs_2_.refs_3_.refs_4_ = bf16[4,2,192,1024]{3,2,1,0:T(8,128)(2,1)} fusion(bf16[1,2,192,1024]{3,2,1,0:T(8,128)(2,1)} %bitcast.17, bf16[1,2,192,1024]{3,2,1,0:T(8,128)(2,1)} %bitcast.15, bf16[1,2,192,1024]{3,2,1,0:T(8,128)(2,1)} %bitcast.13, bf16[1,2,192,1024]{3,2,1,0:T(8,128)(2,1)} %get-tuple-element.35), kind=kLoop, calls=%fused_computation.12 | loop fusion | flops 4718592 | bytes 6291456 | tf_op jit(solution)/shard_map/stack | solution.py:157
  94.0 1.7 pad_maximum_fusion.1.refs_0_
  95.7 26.6 %shard_map.84 = (bf16[768,512]{1,0:T(8,128)(2,1)S(1)}, bf16[768,512]{1,0:T(8,128)(2,1)S(1)}, f32[38,128,128]{2,1,0:T(8,128)S(1)}, f32[38,128,128]{2,1,0:T(8,128)}) custom-call(s32[48]{0:T(128)S(1)} %reshape_squeeze.6.src_ref, s32[6]{0:T(128)S(1)} %add_multiply_fusion.base_ref, s32[4]{0:T(128)S(1)} %and_select_fusion.peer_ref, ...), custom_call_target="tpu_custom_call" | custom-call | tf_op jit(solution)/shard_map/pallas_call | solution.py:130
  122.3 2.4 maximum_convert_fusion.1
  126.5 8.7 %all-to-all-start.3 = ((bf16[32,2,128,128]{3,2,1,0:T(8,128)(2,1)}), bf16[32,2,128,128]{3,2,1,0:T(8,128)(2,1)}, u32[]{:S(2)}, u32[]{:S(2)}) async-start(bf16[32,2,128,128]{3,2,1,0:T(8,128)(2,1)} %copy.113), calls=%async_computation.3 | async-start | bytes 4194304 | tf_op jit(solution)/shard_map/all_to_all | solution.py:213
  135.4 3.4 %pad_maximum_fusion.2.refs_0_ = bf16[38,2,128,128]{3,2,1,0:T(8,128)(2,1)} fusion(bf16[6,2,128,128]{3,2,1,0:T(8,128)(2,1)} %copy-done.9, bf16[32,2,128,128]{3,2,1,0:T(8,128)(2,1)} %all-to-all-done.2), kind=kLoop, calls=%fused_computation.14 | loop fusion | flops 1245184 | bytes 4980736 | tf_op jit(solution)/shard_map/concatenate | solution.py:200
  138.8 26.7 %shard_map.85 = (bf16[768,512]{1,0:T(8,128)(2,1)S(1)}, bf16[768,512]{1,0:T(8,128)(2,1)S(1)}, f32[38,128,128]{2,1,0:T(8,128)S(1)}, f32[38,128,128]{2,1,0:T(8,128)}) custom-call(s32[48]{0:T(128)S(1)} %reshape_squeeze.7.src_ref, s32[6]{0:T(128)S(1)} %add_multiply_fusion.base_ref, s32[4]{0:T(128)S(1)} %and_select_fusion.peer_ref, ...), custom_call_target="tpu_custom_call" | custom-call | tf_op jit(solution)/shard_map/pallas_call | solution.py:130
  171.3 3.2 %copy.116 = bf16[32,2,128,128]{3,2,1,0:T(8,128)(2,1)} copy(bf16[32,2,128,128]{3,2,0,1:T(8,128)(2,1)} %slice.108) | data formatting | bytes 4194304 | tf_op jit(solution)/shard_map/optimization_barrier | solution.py:210
  174.5 8.4 %all-to-all-start.4 = ((bf16[32,2,128,128]{3,2,1,0:T(8,128)(2,1)}), bf16[32,2,128,128]{3,2,1,0:T(8,128)(2,1)}, u32[]{:S(2)}, u32[]{:S(2)}) async-start(bf16[32,2,128,128]{3,2,1,0:T(8,128)(2,1)} %copy.116), calls=%async_computation.4 | async-start | bytes 4194304 | tf_op jit(solution)/shard_map/all_to_all | solution.py:213
  182.8 1.8 fusion.5
  184.7 3.2 %collective-permute-start.3 = (bf16[2,192,8,128]{3,2,1,0:T(8,128)(2,1)S(1)}, bf16[2,192,8,128]{3,2,1,0:T(8,128)(2,1)S(1)}, u32[]{:S(2)}, u32[]{:S(2)}) collective-permute-start(bf16[2,192,8,128]{3,2,1,0:T(8,128)(2,1)S(1)} %get-tuple-element.33), channel_id=1, source_target_pairs={{0,96},{32,0},{64,32},{96,64},{1,97},{33,1},{65,33},{97,65},{2,98}... | collective-permute-start | bytes 2359304 | tf_op jit(solution)/shard_map/ppermute | solution.py:19
  188.0 4.6 %collective-permute-start.4 = (bf16[2,192,8,128]{3,2,1,0:T(8,128)(2,1)S(1)}, bf16[2,192,8,128]{3,2,1,0:T(8,128)(2,1)S(1)}, u32[]{:S(2)}, u32[]{:S(2)}) collective-permute-start(bf16[2,192,8,128]{3,2,1,0:T(8,128)(2,1)S(1)} %get-tuple-element.34), channel_id=1, source_target_pairs={{0,64},{32,96},{64,0},{96,32},{1,65},{33,97},{65,1},{97,33},{2,66}... | collective-permute-start | bytes 2359304 | tf_op jit(solution)/shard_map/ppermute | solution.py:19
  192.6 2.8 %fusion.2 = f32[6,2,128,128]{3,0,2,1:T(8,128)S(1)} fusion(bf16[32,2,128,128]{3,2,1,0:T(8,128)(2,1)} %all-to-all-done.3, bf16[2,32,6]{1,2,0:T(8,128)(2,1)S(1)} %broadcast_select_fusion), kind=kOutput, calls=%fused_computation.17 | convolution fusion | flops 12582912 | bytes 2885632 | tf_op jit(solution)/shard_map/rl,rktd->lktd/dot_general | solution.py:221
  197.5 25.7 %collective-permute-done.3 = bf16[2,192,8,128]{3,2,1,0:T(8,128)(2,1)S(1)} collective-permute-done((bf16[2,192,8,128]{3,2,1,0:T(8,128)(2,1)S(1)}, bf16[2,192,8,128]{3,2,1,0:T(8,128)(2,1)S(1)}, u32[]{:S(2)}, u32[]{:S(2)}) %collective-permute-start.3) | collective-permute-done | bytes 786464 | tf_op jit(solution)/shard_map/ppermute | solution.py:19
  223.5 12.6 %collective-permute-done.4 = bf16[2,192,8,128]{3,2,1,0:T(8,128)(2,1)S(1)} collective-permute-done((bf16[2,192,8,128]{3,2,1,0:T(8,128)(2,1)S(1)}, bf16[2,192,8,128]{3,2,1,0:T(8,128)(2,1)S(1)}, u32[]{:S(2)}, u32[]{:S(2)}) %collective-permute-start.4) | collective-permute-done | bytes 786464 | tf_op jit(solution)/shard_map/ppermute | solution.py:19
  237.7 2.4 dynamic-slice_bitcast_fusion
  240.2 3.0 %fusion = f32[6,2,128,128]{3,0,2,1:T(8,128)S(1)} fusion(bf16[32,2,128,128]{3,2,1,0:T(8,128)(2,1)} %all-to-all-done.4, bf16[2,32,6]{1,2,0:T(8,128)(2,1)S(1)} %broadcast_select_fusion), kind=kOutput, calls=%fused_computation.15 | convolution fusion | flops 12582912 | bytes 2885632 | tf_op jit(solution)/shard_map/rl,rktd->lktd/dot_general | solution.py:221
  245.2 3.3 %collective-permute-start.7 = (bf16[2,192,2,128]{3,2,1,0:T(2,128)(2,1)S(1)}, bf16[2,192,2,128]{3,2,1,0:T(2,128)(2,1)S(1)}, u32[]{:S(2)}, u32[]{:S(2)}) collective-permute-start(bf16[2,192,2,128]{3,2,1,0:T(2,128)(2,1)S(1)} %bitcast.148), channel_id=1, source_target_pairs={{0,64},{32,96},{64,0},{96,32},{1,65},{33,97},{65,1},{97,33},{2,66}... | collective-permute-start | bytes 589832 | tf_op jit(solution)/shard_map/ppermute | solution.py:19
  249.2 9.1 %collective-permute-done.7 = bf16[2,192,2,128]{3,2,1,0:T(2,128)(2,1)S(1)} collective-permute-done((bf16[2,192,2,128]{3,2,1,0:T(2,128)(2,1)S(1)}, bf16[2,192,2,128]{3,2,1,0:T(2,128)(2,1)S(1)}, u32[]{:S(2)}, u32[]{:S(2)}) %collective-permute-start.7) | collective-permute-done | bytes 196640 | tf_op jit(solution)/shard_map/ppermute | solution.py:19
  (97 shorter events, 26.4 us)
Async XLA Ops:
  2.8 17.5 %all-to-all-start = ((bf16[2,192,8,128]{3,1,0,2:T(8,128)(2,1)}), bf16[2,192,8,128]{3,1,0,2:T(8,128)(2,1)S(1)}, u32[]{:S(2)}, u32[]{:S(2)}) async-start(bf16[2,192,8,128]{3,1,0,2:T(8,128)(2,1)} %pad_maximum_fusion.3), calls=%async_computation | async-start | bytes 1572864 | tf_op jit(solution)/shard_map/all_to_all | solution.py:29
  20.6 25.2 %copy-start.9 = (bf16[6,2,128,128]{3,2,1,0:T(8,128)(2,1)}, bf16[6,2,128,128]{3,2,1,0:T(8,128)(2,1)S(1)}, u32[]{:S(2)}) copy-start(bf16[6,2,128,128]{3,2,1,0:T(8,128)(2,1)S(1)} %get-tuple-element.46) | copy-start | bytes 1179652
  23.5 40.8 %all-to-all-start.1 = ((bf16[32,2,128,128]{3,2,1,0:T(8,128)(2,1)}), bf16[32,2,128,128]{3,2,1,0:T(8,128)(2,1)S(1)}, u32[]{:S(2)}, u32[]{:S(2)}) async-start(bf16[32,2,128,128]{3,2,1,0:T(8,128)(2,1)} %copy.157), calls=%async_computation.1 | async-start | bytes 4194304 | tf_op jit(solution)/shard_map/all_to_all | solution.py:199
  39.0 2.0 copy-start.8
  43.2 29.2 %collective-permute-start.2 = (bf16[2,192,1024]{2,1,0:T(8,128)(2,1)}, bf16[2,192,1024]{2,1,0:T(8,128)(2,1)}, u32[]{:S(2)}, u32[]{:S(2)}) collective-permute-start(bf16[2,192,1024]{2,1,0:T(8,128)(2,1)} %get-tuple-element.36), channel_id=1, source_target_pairs={{0,96},{32,0},{64,32},{96,64},{1,97},{33,1},{65,33},{97,65},{2,98}... | collective-permute-start | bytes 2359304 | tf_op jit(solution)/shard_map/ppermute | solution.py:155
  43.4 47.3 %collective-permute-start.1 = (bf16[2,192,1024]{2,1,0:T(8,128)(2,1)}, bf16[2,192,1024]{2,1,0:T(8,128)(2,1)}, u32[]{:S(2)}, u32[]{:S(2)}) collective-permute-start(bf16[2,192,1024]{2,1,0:T(8,128)(2,1)} %get-tuple-element.37), channel_id=1, source_target_pairs={{0,64},{32,96},{64,0},{96,32},{1,65},{33,97},{65,1},{97,33},{2,66}... | collective-permute-start | bytes 2359304 | tf_op jit(solution)/shard_map/ppermute | solution.py:155
  45.7 45.0 %collective-permute-start = (bf16[2,192,1024]{2,1,0:T(8,128)(2,1)}, bf16[2,192,1024]{2,1,0:T(8,128)(2,1)}, u32[]{:S(2)}, u32[]{:S(2)}) collective-permute-start(bf16[2,192,1024]{2,1,0:T(8,128)(2,1)} %get-tuple-element.38), channel_id=1, source_target_pairs={{0,32},{32,64},{64,96},{96,0},{1,33},{33,65},{65,97},{97,1},{2,34}... | collective-permute-start | bytes 2359304 | tf_op jit(solution)/shard_map/ppermute | solution.py:155
  64.3 62.2 %all-to-all-start.2 = ((bf16[32,2,128,128]{3,2,1,0:T(8,128)(2,1)}), bf16[32,2,128,128]{3,2,1,0:T(8,128)(2,1)}, u32[]{:S(2)}, u32[]{:S(2)}) async-start(bf16[32,2,128,128]{3,2,1,0:T(8,128)(2,1)} %copy.156), calls=%async_computation.2 | async-start | bytes 4194304 | tf_op jit(solution)/shard_map/all_to_all | solution.py:199
  122.3 2.4 copy-start.2
  126.5 44.8 %all-to-all-start.3 = ((bf16[32,2,128,128]{3,2,1,0:T(8,128)(2,1)}), bf16[32,2,128,128]{3,2,1,0:T(8,128)(2,1)}, u32[]{:S(2)}, u32[]{:S(2)}) async-start(bf16[32,2,128,128]{3,2,1,0:T(8,128)(2,1)} %copy.113), calls=%async_computation.3 | async-start | bytes 4194304 | tf_op jit(solution)/shard_map/all_to_all | solution.py:213
  138.8 26.7 %copy-start.3 = (bf16[768,512]{1,0:T(8,128)(2,1)S(1)}, bf16[768,512]{1,0:T(8,128)(2,1)}, u32[]{:S(2)}) copy-start(bf16[768,512]{1,0:T(8,128)(2,1)} %copy-done.2) | copy-start | bytes 2359300
  165.5 3.8 %copy-start = (f32[38,128,128]{2,1,0:T(8,128)}, f32[38,128,128]{2,1,0:T(8,128)S(1)}, u32[]{:S(2)}) copy-start(f32[38,128,128]{2,1,0:T(8,128)S(1)} %get-tuple-element.20) | copy-start | bytes 7471108
  167.4 1.8 copy-start.7
  174.5 65.7 %all-to-all-start.4 = ((bf16[32,2,128,128]{3,2,1,0:T(8,128)(2,1)}), bf16[32,2,128,128]{3,2,1,0:T(8,128)(2,1)}, u32[]{:S(2)}, u32[]{:S(2)}) async-start(bf16[32,2,128,128]{3,2,1,0:T(8,128)(2,1)} %copy.116), calls=%async_computation.4 | async-start | bytes 4194304 | tf_op jit(solution)/shard_map/all_to_all | solution.py:213
  184.6 10.7 %copy-start.6 = (f32[38,128,128]{2,1,0:T(8,128)S(1)}, f32[38,128,128]{2,1,0:T(8,128)}, u32[]{:S(2)}) copy-start(f32[38,128,128]{2,1,0:T(8,128)} %get-tuple-element.23) | copy-start | bytes 7471108
  184.6 51.7 %collective-permute-start.5 = (bf16[2,192,8,128]{3,2,1,0:T(8,128)(2,1)S(1)}, bf16[2,192,8,128]{3,2,1,0:T(8,128)(2,1)S(1)}, u32[]{:S(2)}, u32[]{:S(2)}) collective-permute-start(bf16[2,192,8,128]{3,2,1,0:T(8,128)(2,1)S(1)} %get-tuple-element.32), channel_id=1, source_target_pairs={{0,32},{32,64},{64,96},{96,0},{1,33},{33,65},{65,97},{97,1},{2,34}... | collective-permute-start | bytes 2359304 | tf_op jit(solution)/shard_map/ppermute | solution.py:19
  184.7 38.5 %collective-permute-start.3 = (bf16[2,192,8,128]{3,2,1,0:T(8,128)(2,1)S(1)}, bf16[2,192,8,128]{3,2,1,0:T(8,128)(2,1)S(1)}, u32[]{:S(2)}, u32[]{:S(2)}) collective-permute-start(bf16[2,192,8,128]{3,2,1,0:T(8,128)(2,1)S(1)} %get-tuple-element.33), channel_id=1, source_target_pairs={{0,96},{32,0},{64,32},{96,64},{1,97},{33,1},{65,33},{97,65},{2,98}... | collective-permute-start | bytes 2359304 | tf_op jit(solution)/shard_map/ppermute | solution.py:19
  188.0 48.1 %collective-permute-start.4 = (bf16[2,192,8,128]{3,2,1,0:T(8,128)(2,1)S(1)}, bf16[2,192,8,128]{3,2,1,0:T(8,128)(2,1)S(1)}, u32[]{:S(2)}, u32[]{:S(2)}) collective-permute-start(bf16[2,192,8,128]{3,2,1,0:T(8,128)(2,1)S(1)} %get-tuple-element.34), channel_id=1, source_target_pairs={{0,64},{32,96},{64,0},{96,32},{1,65},{33,97},{65,1},{97,33},{2,66}... | collective-permute-start | bytes 2359304 | tf_op jit(solution)/shard_map/ppermute | solution.py:19
  195.4 1.4 copy-start.4
  195.4 1.9 copy-start.5
  240.2 3.0 %copy-start.1 = (f32[38,128,128]{2,1,0:T(8,128)S(1)}, f32[38,128,128]{2,1,0:T(8,128)}, u32[]{:S(2)}) copy-start(f32[38,128,128]{2,1,0:T(8,128)} %copy-done) | copy-start | bytes 7471108
  245.2 3.7 %collective-permute-start.6 = (bf16[2,192,2,128]{3,2,1,0:T(2,128)(2,1)S(1)}, bf16[2,192,2,128]{3,2,1,0:T(2,128)(2,1)S(1)}, u32[]{:S(2)}, u32[]{:S(2)}) collective-permute-start(bf16[2,192,2,128]{3,2,1,0:T(2,128)(2,1)S(1)} %bitcast.149), channel_id=1, source_target_pairs={{0,96},{32,0},{64,32},{96,64},{1,97},{33,1},{65,33},{97,65},{2,98}... | collective-permute-start | bytes 589832 | tf_op jit(solution)/shard_map/ppermute | solution.py:19
  245.2 13.0 %collective-permute-start.7 = (bf16[2,192,2,128]{3,2,1,0:T(2,128)(2,1)S(1)}, bf16[2,192,2,128]{3,2,1,0:T(2,128)(2,1)S(1)}, u32[]{:S(2)}, u32[]{:S(2)}) collective-permute-start(bf16[2,192,2,128]{3,2,1,0:T(2,128)(2,1)S(1)} %bitcast.148), channel_id=1, source_target_pairs={{0,64},{32,96},{64,0},{96,32},{1,65},{33,97},{65,1},{97,33},{2,66}... | collective-permute-start | bytes 589832 | tf_op jit(solution)/shard_map/ppermute | solution.py:19
  248.5 10.0 %collective-permute-start.8 = (bf16[2,192,2,128]{3,2,1,0:T(2,128)(2,1)S(1)}, bf16[2,192,2,128]{3,2,1,0:T(2,128)(2,1)S(1)}, u32[]{:S(2)}, u32[]{:S(2)}) collective-permute-start(bf16[2,192,2,128]{3,2,1,0:T(2,128)(2,1)S(1)} %bitcast.147), channel_id=1, source_target_pairs={{0,32},{32,64},{64,96},{96,0},{1,33},{33,65},{65,97},{97,1},{2,34}... | collective-permute-start | bytes 589832 | tf_op jit(solution)/shard_map/ppermute | solution.py:19

commit v13 on v12

--- a/solution.py
+++ b/solution.py
@@ -225,7 +225,11 @@
         key_grads.append(total[:, 0])
         value_grads.append(total[:, 1])
     attn_out, grad_queries = from_heads(attn_all, query_grad_all)
-    key_gradient, value_gradient = from_heads(group_layout(key_grads), group_layout(value_grads))
+    grads = lax.all_to_all(
+        jnp.stack([group_layout(key_grads), group_layout(value_grads)]),
+        "head", split_axis=1, concat_axis=2, tiled=True,
+    )
+    key_gradient, value_gradient = grads[0], grads[1]
     return attn_out, grad_queries, key_gradient, value_gradient
 
 

time: 263 us -> 271 us (1.030)
  local copies, waits for them, and re-layouts: 37.4 us -> 43.2 us
  other arithmetic: 18.5 us -> 23.6 us
  waiting for transfers between devices: 94.9 us -> 90.9 us
    ppermute x6 -> x3, waiting for transfers between devices: 47.4 us -> 36.3 us  [exchange(): lax.ppermute(piece, 'head', [(i, (i + k) % size) for i in range(size)])]
    all_to_all x0 -> x1, waiting for transfers between devices: none -> 7.05 us  [on_device(): lax.all_to_all(jnp.stack([group_layout(key_grads), group_layout(value_gra...]
    all_to_all x0 -> x1, starting transfers between devices: none -> 4.49 us  [on_device(): lax.all_to_all(jnp.stack([group_layout(key_grads), group_layout(value_gra...]
    another operation x3, other arithmetic: 2.93 us -> 6.53 us  [the longest x1 3.67 us: on_device(): jnp.stack([group_layout(key_grads), group_layout(value_grads)])]
    ppermute x6 -> x3, starting transfers between devices: 11.4 us -> 7.91 us  [exchange(): lax.ppermute(piece, 'head', [(i, (i + k) % size) for i in range(size)])]
    unnamed x35 -> x36, local copies, waits for them, and re-layouts: 10.3 us -> 10.5 us
  transfers between devices with their start and end apart: 14 -> 12, of which waited for: 7 -> 7; matrix products, arithmetic and copies ran while one was open for 17% -> 20% of each run, Pallas kernels for 20% -> 20%
where the time goes in v13:
time: 271 us; the launch traced here: 269 us
  waiting for transfers between devices  90.9 us (34%)
  Pallas kernels  53.3 us (20%)
  starting transfers between devices  49.7 us (18%)
  local copies, waits for them, and re-layouts  43.2 us (16%)
  other arithmetic  23.6 us (9%)
  matrix products  7.19 us (3%)
    pallas_call x2, Pallas kernels, attend(): pl.pallas_call(attention_kernel, grid_spec=grid_spec, out_shape=out_shape...  53.3 us
    ppermute x3, waiting for transfers between devices, exchange(): lax.ppermute(piece, 'head', [(i, (i + k) % size) for i in range(size)])  36.3 us
    ppermute x3, waiting for transfers between devices, on_device(): lax.ppermute(piece, 'head', [(i, (i + k) % size) for i in range(size)])  19.8 us
    all_to_all x2, starting transfers between devices, on_device(): lax.all_to_all(remote, 'blk', split_axis=0, concat_axis=0, tiled=True)  17.1 us
    all_to_all x2, waiting for transfers between devices, on_device(): recv = lax.all_to_all(send, 'blk', split_axis=0, concat_axis=0, tiled=True)  15.5 us
    all_to_all x2, starting transfers between devices, on_device(): recv = lax.all_to_all(send, 'blk', split_axis=0, concat_axis=0, tiled=True)  13.4 us
    all_to_all x1, waiting for transfers between devices, to_heads(): return lax.all_to_all(x, 'head', split_axis=2, concat_axis=1, tiled=True)  12.2 us
    unnamed x36, local copies, waits for them, and re-layouts  10.5 us
  transfers between devices with their start and end apart: 12, of which 7 were waited for; matrix products, arithmetic and copies ran while one was open for 20% of the time, Pallas kernels for 20%

profile of v13, /device:TPU:0, one launch (start us, length us, event | category | flops | bytes accessed | tf_op | source)
XLA Modules:
  0.0 268.9 jit_solution(14205059620605117038)
XLA Ops:
  2.8 4.4 %all-to-all-start = ((bf16[2,192,8,128]{3,1,0,2:T(8,128)(2,1)}), bf16[2,192,8,128]{3,1,0,2:T(8,128)(2,1)S(1)}, u32[]{:S(2)}, u32[]{:S(2)}) async-start(bf16[2,192,8,128]{3,1,0,2:T(8,128)(2,1)} %pad_maximum_fusion.3), calls=%async_computation | async-start | bytes 1572864 | tf_op jit(solution)/shard_map/all_to_all | solution.py:29
  8.2 12.2 %all-to-all-done = bf16[2,192,8,128]{3,1,0,2:T(8,128)(2,1)S(1)} async-done(((bf16[2,192,8,128]{3,1,0,2:T(8,128)(2,1)}), bf16[2,192,8,128]{3,1,0,2:T(8,128)(2,1)S(1)}, u32[]{:S(2)}, u32[]{:S(2)}) %all-to-all-start) | async-done | bytes 786464 | tf_op jit(solution)/shard_map/all_to_all | solution.py:29
  21.4 2.2 copy.147
  23.5 8.4 %all-to-all-start.1 = ((bf16[32,2,128,128]{3,2,1,0:T(8,128)(2,1)}), bf16[32,2,128,128]{3,2,1,0:T(8,128)(2,1)S(1)}, u32[]{:S(2)}, u32[]{:S(2)}) async-start(bf16[32,2,128,128]{3,2,1,0:T(8,128)(2,1)} %copy.147), calls=%async_computation.1 | async-start | bytes 4194304 | tf_op jit(solution)/shard_map/all_to_all | solution.py:199
  32.0 3.5 %stack.91 = bf16[1,192,4,1024]{3,2,1,0:T(4,128)(2,1)} reshape(bf16[192,32,128]{2,1,0:T(8,128)(2,1)} %param.5) | data formatting | bytes 3145728 | tf_op jit(solution)/shard_map/stack | solution.py:149
  35.5 3.5 %stack.92 = bf16[1,192,4,1024]{3,2,1,0:T(4,128)(2,1)} reshape(bf16[192,32,128]{2,1,0:T(8,128)(2,1)} %param.9) | data formatting | bytes 3145728 | tf_op jit(solution)/shard_map/stack | solution.py:149
  39.0 2.0 copy_dynamic-update-slice_fusion.1
  41.5 1.8 dynamic-slice_bitcast_fusion.5
  43.5 2.3 collective-permute-start.1
  46.6 2.2 copy.146
  48.8 15.5 %all-to-all-done.1 = bf16[32,2,128,128]{3,2,1,0:T(8,128)(2,1)S(1)} async-done(((bf16[32,2,128,128]{3,2,1,0:T(8,128)(2,1)}), bf16[32,2,128,128]{3,2,1,0:T(8,128)(2,1)S(1)}, u32[]{:S(2)}, u32[]{:S(2)}) %all-to-all-start.1) | async-done | bytes 2097184 | tf_op jit(solution)/shard_map/all_to_all | solution.py:199
  64.3 5.0 %all-to-all-start.2 = ((bf16[32,2,128,128]{3,2,1,0:T(8,128)(2,1)}), bf16[32,2,128,128]{3,2,1,0:T(8,128)(2,1)}, u32[]{:S(2)}, u32[]{:S(2)}) async-start(bf16[32,2,128,128]{3,2,1,0:T(8,128)(2,1)} %copy.146), calls=%async_computation.2 | async-start | bytes 4194304 | tf_op jit(solution)/shard_map/all_to_all | solution.py:199
  72.5 18.2 %collective-permute-done.1 = bf16[2,192,1024]{2,1,0:T(8,128)(2,1)} collective-permute-done((bf16[2,192,1024]{2,1,0:T(8,128)(2,1)}, bf16[2,192,1024]{2,1,0:T(8,128)(2,1)}, u32[]{:S(2)}, u32[]{:S(2)}) %collective-permute-start.1) | collective-permute-done | bytes 786464 | tf_op jit(solution)/shard_map/ppermute | solution.py:155
  90.7 3.2 %pad_maximum_fusion.refs_1_.refs_2_.refs_3_.refs_4_ = bf16[4,2,192,1024]{3,2,1,0:T(8,128)(2,1)} fusion(bf16[1,2,192,1024]{3,2,1,0:T(8,128)(2,1)} %bitcast.17, bf16[1,2,192,1024]{3,2,1,0:T(8,128)(2,1)} %bitcast.15, bf16[1,2,192,1024]{3,2,1,0:T(8,128)(2,1)} %bitcast.13, bf16[1,2,192,1024]{3,2,1,0:T(8,128)(2,1)} %get-tuple-element.35), kind=kLoop, calls=%fused_computation.12 | loop fusion | flops 4718592 | bytes 6291456 | tf_op jit(solution)/shard_map/stack | solution.py:157
  95.6 26.6 %shard_map.84 = (bf16[768,512]{1,0:T(8,128)(2,1)S(1)}, bf16[768,512]{1,0:T(8,128)(2,1)S(1)}, f32[38,128,128]{2,1,0:T(8,128)S(1)}, f32[38,128,128]{2,1,0:T(8,128)}) custom-call(s32[48]{0:T(128)S(1)} %reshape_squeeze.6.src_ref, s32[6]{0:T(128)S(1)} %add_multiply_fusion.base_ref, s32[4]{0:T(128)S(1)} %and_select_fusion.peer_ref, ...), custom_call_target="tpu_custom_call" | custom-call | tf_op jit(solution)/shard_map/pallas_call | solution.py:130
  122.2 2.4 maximum_convert_fusion.1
  126.4 8.7 %all-to-all-start.3 = ((bf16[32,2,128,128]{3,2,1,0:T(8,128)(2,1)}), bf16[32,2,128,128]{3,2,1,0:T(8,128)(2,1)}, u32[]{:S(2)}, u32[]{:S(2)}) async-start(bf16[32,2,128,128]{3,2,1,0:T(8,128)(2,1)} %copy.106), calls=%async_computation.3 | async-start | bytes 4194304 | tf_op jit(solution)/shard_map/all_to_all | solution.py:213
  135.3 3.4 %pad_maximum_fusion.2.refs_0_ = bf16[38,2,128,128]{3,2,1,0:T(8,128)(2,1)} fusion(bf16[6,2,128,128]{3,2,1,0:T(8,128)(2,1)} %copy-done.9, bf16[32,2,128,128]{3,2,1,0:T(8,128)(2,1)} %all-to-all-done.2), kind=kLoop, calls=%fused_computation.14 | loop fusion | flops 1245184 | bytes 4980736 | tf_op jit(solution)/shard_map/concatenate | solution.py:200
  138.7 26.7 %shard_map.85 = (bf16[768,512]{1,0:T(8,128)(2,1)S(1)}, bf16[768,512]{1,0:T(8,128)(2,1)S(1)}, f32[38,128,128]{2,1,0:T(8,128)S(1)}, f32[38,128,128]{2,1,0:T(8,128)}) custom-call(s32[48]{0:T(128)S(1)} %reshape_squeeze.7.src_ref, s32[6]{0:T(128)S(1)} %add_multiply_fusion.base_ref, s32[4]{0:T(128)S(1)} %and_select_fusion.peer_ref, ...), custom_call_target="tpu_custom_call" | custom-call | tf_op jit(solution)/shard_map/pallas_call | solution.py:130
  171.2 3.3 %copy.109 = bf16[32,2,128,128]{3,2,1,0:T(8,128)(2,1)} copy(bf16[32,2,128,128]{3,2,0,1:T(8,128)(2,1)} %slice.108) | data formatting | bytes 4194304 | tf_op jit(solution)/shard_map/optimization_barrier | solution.py:210
  174.5 8.3 %all-to-all-start.4 = ((bf16[32,2,128,128]{3,2,1,0:T(8,128)(2,1)}), bf16[32,2,128,128]{3,2,1,0:T(8,128)(2,1)}, u32[]{:S(2)}, u32[]{:S(2)}) async-start(bf16[32,2,128,128]{3,2,1,0:T(8,128)(2,1)} %copy.109), calls=%async_computation.4 | async-start | bytes 4194304 | tf_op jit(solution)/shard_map/all_to_all | solution.py:213
  182.8 1.8 fusion.5
  184.7 3.2 %collective-permute-start.3 = (bf16[2,192,8,128]{3,2,1,0:T(8,128)(2,1)S(1)}, bf16[2,192,8,128]{3,2,1,0:T(8,128)(2,1)S(1)}, u32[]{:S(2)}, u32[]{:S(2)}) collective-permute-start(bf16[2,192,8,128]{3,2,1,0:T(8,128)(2,1)S(1)} %get-tuple-element.33), channel_id=1, source_target_pairs={{0,96},{32,0},{64,32},{96,64},{1,97},{33,1},{65,33},{97,65},{2,98}... | collective-permute-start | bytes 2359304 | tf_op jit(solution)/shard_map/ppermute | solution.py:19
  188.0 4.6 %collective-permute-start.4 = (bf16[2,192,8,128]{3,2,1,0:T(8,128)(2,1)S(1)}, bf16[2,192,8,128]{3,2,1,0:T(8,128)(2,1)S(1)}, u32[]{:S(2)}, u32[]{:S(2)}) collective-permute-start(bf16[2,192,8,128]{3,2,1,0:T(8,128)(2,1)S(1)} %get-tuple-element.34), channel_id=1, source_target_pairs={{0,64},{32,96},{64,0},{96,32},{1,65},{33,97},{65,1},{97,33},{2,66}... | collective-permute-start | bytes 2359304 | tf_op jit(solution)/shard_map/ppermute | solution.py:19
  192.5 2.8 %fusion.2 = f32[6,2,128,128]{3,0,2,1:T(8,128)S(1)} fusion(bf16[32,2,128,128]{3,2,1,0:T(8,128)(2,1)} %all-to-all-done.3, bf16[2,32,6]{1,2,0:T(8,128)(2,1)S(1)} %broadcast_select_fusion), kind=kOutput, calls=%fused_computation.17 | convolution fusion | flops 12582912 | bytes 2885632 | tf_op jit(solution)/shard_map/rl,rktd->lktd/dot_general | solution.py:221
  198.7 24.5 %collective-permute-done.3 = bf16[2,192,8,128]{3,2,1,0:T(8,128)(2,1)S(1)} collective-permute-done((bf16[2,192,8,128]{3,2,1,0:T(8,128)(2,1)S(1)}, bf16[2,192,8,128]{3,2,1,0:T(8,128)(2,1)S(1)}, u32[]{:S(2)}, u32[]{:S(2)}) %collective-permute-start.3) | collective-permute-done | bytes 786464 | tf_op jit(solution)/shard_map/ppermute | solution.py:19
  224.2 11.8 %collective-permute-done.4 = bf16[2,192,8,128]{3,2,1,0:T(8,128)(2,1)S(1)} collective-permute-done((bf16[2,192,8,128]{3,2,1,0:T(8,128)(2,1)S(1)}, bf16[2,192,8,128]{3,2,1,0:T(8,128)(2,1)S(1)}, u32[]{:S(2)}, u32[]{:S(2)}) %collective-permute-start.4) | collective-permute-done | bytes 786464 | tf_op jit(solution)/shard_map/ppermute | solution.py:19
  240.2 2.8 %fusion = f32[6,2,128,128]{3,0,2,1:T(8,128)S(1)} fusion(bf16[32,2,128,128]{3,2,1,0:T(8,128)(2,1)} %all-to-all-done.4, bf16[2,32,6]{1,2,0:T(8,128)(2,1)S(1)} %broadcast_select_fusion), kind=kOutput, calls=%fused_computation.15 | convolution fusion | flops 12582912 | bytes 2885632 | tf_op jit(solution)/shard_map/rl,rktd->lktd/dot_general | solution.py:221
  245.0 3.7 %maximum_maximum_fusion = bf16[2,768,2,128]{3,2,0,1:T(2,128)(2,1)} fusion(bf16[1,768,1,128]{3,2,0,1:T(2,128)(2,1)S(1)} %copy.115, bf16[1,768,1,128]{3,2,0,1:T(2,128)(2,1)S(1)} %copy-done.12, bf16[1,768,1,128]{3,2,0,1:T(2,128)(2,1)S(1)} %copy.113, bf16[1,768,1,128]{3,2,0,1:T(2,128)(2,1)S(1)} %copy-done.13), kind=kLoop, calls=%fused_computation.36 | loop fusion | flops 3145728 | bytes 1572864 | tf_op jit(solution)/shard_map/stack | solution.py:229
  248.7 4.5 %all-to-all-start.5 = ((bf16[2,768,2,128]{3,2,0,1:T(2,128)(2,1)}), bf16[2,768,2,128]{3,2,0,1:T(2,128)(2,1)S(1)}, u32[]{:S(2)}, u32[]{:S(2)}) async-start(bf16[2,768,2,128]{3,2,0,1:T(2,128)(2,1)} %maximum_maximum_fusion), calls=%async_computation.5 | async-start | bytes 1572864 | tf_op jit(solution)/shard_map/all_to_all | solution.py:228
  255.1 4.1 %dynamic-slice_bitcast_fusion = (bf16[192,32,128]{2,1,0:T(8,128)(2,1)}, bf16[192,32,128]{2,1,0:T(8,128)(2,1)}) fusion(bf16[2,192,8,8,128]{4,3,2,1,0:T(8,128)(2,1)} %bitcast_dynamic-update-slice_fusion.1, s32[]{:T(128)S(6)} %add.143, s32[]{:T(128)S(6)} %select_n.127), kind=kLoop, calls=%fused_computation.19 | loop fusion | bytes 6291464 | tf_op jit(solution)/shard_map/squeeze | solution.py:38
  259.3 7.0 %all-to-all-done.5 = bf16[2,768,2,128]{3,2,0,1:T(2,128)(2,1)S(1)} async-done(((bf16[2,768,2,128]{3,2,0,1:T(2,128)(2,1)}), bf16[2,768,2,128]{3,2,0,1:T(2,128)(2,1)S(1)}, u32[]{:S(2)}, u32[]{:S(2)}) %all-to-all-start.5) | async-done | bytes 786464 | tf_op jit(solution)/shard_map/all_to_all | solution.py:228
  (95 shorter events, 33.2 us)
Async XLA Ops:
  2.8 17.5 %all-to-all-start = ((bf16[2,192,8,128]{3,1,0,2:T(8,128)(2,1)}), bf16[2,192,8,128]{3,1,0,2:T(8,128)(2,1)S(1)}, u32[]{:S(2)}, u32[]{:S(2)}) async-start(bf16[2,192,8,128]{3,1,0,2:T(8,128)(2,1)} %pad_maximum_fusion.3), calls=%async_computation | async-start | bytes 1572864 | tf_op jit(solution)/shard_map/all_to_all | solution.py:29
  20.6 25.2 %copy-start.9 = (bf16[6,2,128,128]{3,2,1,0:T(8,128)(2,1)}, bf16[6,2,128,128]{3,2,1,0:T(8,128)(2,1)S(1)}, u32[]{:S(2)}) copy-start(bf16[6,2,128,128]{3,2,1,0:T(8,128)(2,1)S(1)} %get-tuple-element.42) | copy-start | bytes 1179652
  23.5 40.8 %all-to-all-start.1 = ((bf16[32,2,128,128]{3,2,1,0:T(8,128)(2,1)}), bf16[32,2,128,128]{3,2,1,0:T(8,128)(2,1)S(1)}, u32[]{:S(2)}, u32[]{:S(2)}) async-start(bf16[32,2,128,128]{3,2,1,0:T(8,128)(2,1)} %copy.147), calls=%async_computation.1 | async-start | bytes 4194304 | tf_op jit(solution)/shard_map/all_to_all | solution.py:199
  39.0 2.0 copy-start.8
  43.3 29.2 %collective-permute-start.2 = (bf16[2,192,1024]{2,1,0:T(8,128)(2,1)}, bf16[2,192,1024]{2,1,0:T(8,128)(2,1)}, u32[]{:S(2)}, u32[]{:S(2)}) collective-permute-start(bf16[2,192,1024]{2,1,0:T(8,128)(2,1)} %get-tuple-element.36), channel_id=1, source_target_pairs={{0,96},{32,0},{64,32},{96,64},{1,97},{33,1},{65,33},{97,65},{2,98}... | collective-permute-start | bytes 2359304 | tf_op jit(solution)/shard_map/ppermute | solution.py:155
  43.5 47.3 %collective-permute-start.1 = (bf16[2,192,1024]{2,1,0:T(8,128)(2,1)}, bf16[2,192,1024]{2,1,0:T(8,128)(2,1)}, u32[]{:S(2)}, u32[]{:S(2)}) collective-permute-start(bf16[2,192,1024]{2,1,0:T(8,128)(2,1)} %get-tuple-element.37), channel_id=1, source_target_pairs={{0,64},{32,96},{64,0},{96,32},{1,65},{33,97},{65,1},{97,33},{2,66}... | collective-permute-start | bytes 2359304 | tf_op jit(solution)/shard_map/ppermute | solution.py:155
  45.8 45.0 %collective-permute-start = (bf16[2,192,1024]{2,1,0:T(8,128)(2,1)}, bf16[2,192,1024]{2,1,0:T(8,128)(2,1)}, u32[]{:S(2)}, u32[]{:S(2)}) collective-permute-start(bf16[2,192,1024]{2,1,0:T(8,128)(2,1)} %get-tuple-element.38), channel_id=1, source_target_pairs={{0,32},{32,64},{64,96},{96,0},{1,33},{33,65},{65,97},{97,1},{2,34}... | collective-permute-start | bytes 2359304 | tf_op jit(solution)/shard_map/ppermute | solution.py:155
  64.3 62.1 %all-to-all-start.2 = ((bf16[32,2,128,128]{3,2,1,0:T(8,128)(2,1)}), bf16[32,2,128,128]{3,2,1,0:T(8,128)(2,1)}, u32[]{:S(2)}, u32[]{:S(2)}) async-start(bf16[32,2,128,128]{3,2,1,0:T(8,128)(2,1)} %copy.146), calls=%async_computation.2 | async-start | bytes 4194304 | tf_op jit(solution)/shard_map/all_to_all | solution.py:199
  122.2 2.4 copy-start.2
  126.4 44.8 %all-to-all-start.3 = ((bf16[32,2,128,128]{3,2,1,0:T(8,128)(2,1)}), bf16[32,2,128,128]{3,2,1,0:T(8,128)(2,1)}, u32[]{:S(2)}, u32[]{:S(2)}) async-start(bf16[32,2,128,128]{3,2,1,0:T(8,128)(2,1)} %copy.106), calls=%async_computation.3 | async-start | bytes 4194304 | tf_op jit(solution)/shard_map/all_to_all | solution.py:213
  138.7 26.7 %copy-start.3 = (bf16[768,512]{1,0:T(8,128)(2,1)S(1)}, bf16[768,512]{1,0:T(8,128)(2,1)}, u32[]{:S(2)}) copy-start(bf16[768,512]{1,0:T(8,128)(2,1)} %copy-done.2) | copy-start | bytes 2359300
  165.3 3.8 %copy-start = (f32[38,128,128]{2,1,0:T(8,128)}, f32[38,128,128]{2,1,0:T(8,128)S(1)}, u32[]{:S(2)}) copy-start(f32[38,128,128]{2,1,0:T(8,128)S(1)} %get-tuple-element.20) | copy-start | bytes 7471108
  167.3 1.8 copy-start.7
  174.5 65.8 %all-to-all-start.4 = ((bf16[32,2,128,128]{3,2,1,0:T(8,128)(2,1)}), bf16[32,2,128,128]{3,2,1,0:T(8,128)(2,1)}, u32[]{:S(2)}, u32[]{:S(2)}) async-start(bf16[32,2,128,128]{3,2,1,0:T(8,128)(2,1)} %copy.109), calls=%async_computation.4 | async-start | bytes 4194304 | tf_op jit(solution)/shard_map/all_to_all | solution.py:213
  184.6 10.7 %copy-start.6 = (f32[38,128,128]{2,1,0:T(8,128)S(1)}, f32[38,128,128]{2,1,0:T(8,128)}, u32[]{:S(2)}) copy-start(f32[38,128,128]{2,1,0:T(8,128)} %get-tuple-element.23) | copy-start | bytes 7471108
  184.6 52.5 %collective-permute-start.5 = (bf16[2,192,8,128]{3,2,1,0:T(8,128)(2,1)S(1)}, bf16[2,192,8,128]{3,2,1,0:T(8,128)(2,1)S(1)}, u32[]{:S(2)}, u32[]{:S(2)}) collective-permute-start(bf16[2,192,8,128]{3,2,1,0:T(8,128)(2,1)S(1)} %get-tuple-element.32), channel_id=1, source_target_pairs={{0,32},{32,64},{64,96},{96,0},{1,33},{33,65},{65,97},{97,1},{2,34}... | collective-permute-start | bytes 2359304 | tf_op jit(solution)/shard_map/ppermute | solution.py:19
  184.7 38.5 %collective-permute-start.3 = (bf16[2,192,8,128]{3,2,1,0:T(8,128)(2,1)S(1)}, bf16[2,192,8,128]{3,2,1,0:T(8,128)(2,1)S(1)}, u32[]{:S(2)}, u32[]{:S(2)}) collective-permute-start(bf16[2,192,8,128]{3,2,1,0:T(8,128)(2,1)S(1)} %get-tuple-element.33), channel_id=1, source_target_pairs={{0,96},{32,0},{64,32},{96,64},{1,97},{33,1},{65,33},{97,65},{2,98}... | collective-permute-start | bytes 2359304 | tf_op jit(solution)/shard_map/ppermute | solution.py:19
  188.0 48.1 %collective-permute-start.4 = (bf16[2,192,8,128]{3,2,1,0:T(8,128)(2,1)S(1)}, bf16[2,192,8,128]{3,2,1,0:T(8,128)(2,1)S(1)}, u32[]{:S(2)}, u32[]{:S(2)}) collective-permute-start(bf16[2,192,8,128]{3,2,1,0:T(8,128)(2,1)S(1)} %get-tuple-element.34), channel_id=1, source_target_pairs={{0,64},{32,96},{64,0},{96,32},{1,65},{33,97},{65,1},{97,33},{2,66}... | collective-permute-start | bytes 2359304 | tf_op jit(solution)/shard_map/ppermute | solution.py:19
  195.4 2.3 copy-start.5
  195.6 2.2 copy-start.4
  236.0 3.1 %copy-start.10 = (bf16[2,192,8,128]{3,2,1,0:T(8,128)(2,1)}, bf16[2,192,8,128]{3,2,1,0:T(8,128)(2,1)S(1)}, u32[]{:S(2)}) copy-start(bf16[2,192,8,128]{3,2,1,0:T(8,128)(2,1)S(1)} %collective-permute-done.4) | copy-start | bytes 2359300
  239.2 3.9 %copy-start.1 = (f32[38,128,128]{2,1,0:T(8,128)S(1)}, f32[38,128,128]{2,1,0:T(8,128)}, u32[]{:S(2)}) copy-start(f32[38,128,128]{2,1,0:T(8,128)} %copy-done) | copy-start | bytes 7471108
  243.0 1.9 copy-start.12
  243.0 1.9 copy-start.13
  244.3 8.8 %copy-start.11 = (bf16[2,192,8,128]{3,2,1,0:T(8,128)(2,1)S(1)}, bf16[2,192,8,128]{3,2,1,0:T(8,128)(2,1)}, u32[]{:S(2)}) copy-start(bf16[2,192,8,128]{3,2,1,0:T(8,128)(2,1)} %copy-done.10) | copy-start | bytes 2359300
  248.7 17.6 %all-to-all-start.5 = ((bf16[2,768,2,128]{3,2,0,1:T(2,128)(2,1)}), bf16[2,768,2,128]{3,2,0,1:T(2,128)(2,1)S(1)}, u32[]{:S(2)}, u32[]{:S(2)}) async-start(bf16[2,768,2,128]{3,2,0,1:T(2,128)(2,1)} %maximum_maximum_fusion), calls=%async_computation.5 | async-start | bytes 1572864 | tf_op jit(solution)/shard_map/all_to_all | solution.py:228

commit v14 on v12

--- a/solution.py
+++ b/solution.py
@@ -39,8 +39,8 @@
 
 
 def attention_kernel(src_ref, base_ref, peer_ref, *refs):
-    table_ref, q_lo, q_hi, do_lo, do_hi, kpos_ref = refs[:6]
-    o_ref, dq_ref, dk_ref, dv_ref = refs[6:]
+    recv_ref, local_ref, q_lo, q_hi, do_lo, do_hi, kpos_ref = refs[:7]
+    o_ref, dq_ref, dk_ref, dv_ref = refs[7:]
     b = pl.program_id(0)
 
     @pl.when(b == 0)
@@ -48,12 +48,19 @@
         dk_ref[...] = jnp.zeros_like(dk_ref)
         dv_ref[...] = jnp.zeros_like(dv_ref)
 
-    head_width = table_ref.shape[-1]
+    head_width = recv_ref.shape[-1]
     group_width = q_lo.shape[-1] // head_width
     scale = head_width ** (-0.5)
     slots = [src_ref[b * TOPK + s] for s in range(TOPK)]
-    keys = jnp.concatenate([table_ref[t, 0] for t in slots], axis=0)
-    values = jnp.concatenate([table_ref[t, 1] for t in slots], axis=0)
+    peers = recv_ref.shape[0]
+
+    def pick(t, kv):
+        there = recv_ref[jnp.minimum(t, peers - 1), kv]
+        here = local_ref[jnp.maximum(t - peers, 0), kv]
+        return jnp.where(t < peers, there, here)
+
+    keys = jnp.concatenate([pick(t, 0) for t in slots], axis=0)
+    values = jnp.concatenate([pick(t, 1) for t in slots], axis=0)
     query_pos = base_ref[b] + lax.broadcasted_iota(jnp.int32, (BLOCK_TOKENS, 1), 0)
     allowed = kpos_ref[...] <= query_pos
     nt = (((1,), (1,)), ((), ()))
@@ -89,12 +96,12 @@
         dv_ref[t] = dv_ref[t] + dv[rows]
 
 
-def attend(slot_src, query_base, peer_of, table, pieces, key_pos, group, groups):
+def attend(slot_src, query_base, peer_of, recv, local, pieces, key_pos, group, groups):
     piece_len = pieces.shape[2]
     run_len = pieces.shape[0] * piece_len
     block_ids = run_len // BLOCK_TOKENS
-    targets = table.shape[0]
-    head_width = table.shape[-1]
+    targets = recv.shape[0] + local.shape[0]
+    head_width = recv.shape[-1]
     row_width = pieces.shape[-1] // groups
     half = BLOCK_TOKENS // 2
     per_piece = piece_len // half
@@ -106,13 +113,14 @@
 
         return pl.BlockSpec((None, None, half, row_width), index)
 
-    table_spec = pl.BlockSpec(table.shape, lambda b, src, base, peer: (0, 0, 0, 0))
+    recv_spec = pl.BlockSpec(recv.shape, lambda b, src, base, peer: (0, 0, 0, 0))
+    local_spec = pl.BlockSpec(local.shape, lambda b, src, base, peer: (0, 0, 0, 0))
 
     out_row = pl.BlockSpec((BLOCK_TOKENS, row_width), lambda b, src, base, peer: (b, 0))
     pos_spec = pl.BlockSpec((None, 1, TOPK * BLOCK_TOKENS), lambda b, src, base, peer: (b, 0, 0))
     acc_spec = pl.BlockSpec((targets, BLOCK_TOKENS, head_width), lambda b, src, base, peer: (0, 0, 0))
     in_specs = (
-        [table_spec]
+        [recv_spec, local_spec]
         + [half_spec(0, 0), half_spec(0, 1), half_spec(1, 0), half_spec(1, 1), pos_spec]
     )
     out_shape = (
@@ -135,7 +143,7 @@
             dimension_semantics=("arbitrary",),
             vmem_limit_bytes=48 * 1024 * 1024,
         ),
-    )(slot_src, query_base, peer_of, table, *([pieces] * 4), key_pos)
+    )(slot_src, query_base, peer_of, recv, local, *([pieces] * 4), key_pos)
 
 
 def on_device(queries, rotated_keys, value_vectors, block_list, grad_out):
@@ -197,9 +205,8 @@
             "rb,bktd->rktd", pick_send[g], kv_local[g], preferred_element_type=jnp.float32
         ).astype(jnp.bfloat16)
         recv = lax.all_to_all(send, "blk", split_axis=0, concat_axis=0, tiled=True)
-        table = jnp.concatenate([recv, kv_local[g]], axis=0)
         o_g, dq_g, dk_acc, dv_acc = attend(
-            slot_src[g].reshape(-1), query_base, peer_of, table, qg_pieces, key_pos[g], g, groups
+            slot_src[g].reshape(-1), query_base, peer_of, recv, kv_local[g], qg_pieces, key_pos[g], g, groups
         )
         outs.append(o_g)
         query_grads.append(dq_g)

time: 263 us -> 293 us (1.11)
  waiting for transfers between devices: 94.9 us -> 133 us
  starting transfers between devices: 48.7 us -> 43 us
  other arithmetic: 18.5 us -> 12.8 us
    ppermute x3, waiting for transfers between devices: 19.8 us -> 49.5 us  [on_device(): lax.ppermute(piece, 'head', [(i, (i + k) % size) for i in range(size)])]
    ppermute x6, waiting for transfers between devices: 47.4 us -> 55.1 us  [exchange(): lax.ppermute(piece, 'head', [(i, (i + k) % size) for i in range(size)])]
    ppermute x6, starting transfers between devices: 11.4 us -> 5.84 us  [exchange(): lax.ppermute(piece, 'head', [(i, (i + k) % size) for i in range(size)])]
    concatenate x2 -> x0, other arithmetic: 5.12 us -> none  [on_device(): table = jnp.concatenate([recv, kv_local[g]], axis=0)]
    unnamed x35 -> x37, local copies, waits for them, and re-layouts: 10.3 us -> 10.3 us
  transfers between devices with their start and end apart: 14 -> 14, of which waited for: 7 -> 9; matrix products, arithmetic and copies ran while one was open for 17% -> 13% of each run, Pallas kernels for 20% -> 19%
where the time goes in v14:
time: 293 us; the launch traced here: 291 us
  waiting for transfers between devices  133 us (45%)
  Pallas kernels  54 us (18%)
  starting transfers between devices  43 us (15%)
  local copies, waits for them, and re-layouts  39.2 us (13%)
  other arithmetic  12.8 us (4%)
  matrix products  7.34 us (3%)
    ppermute x6, waiting for transfers between devices, exchange(): lax.ppermute(piece, 'head', [(i, (i + k) % size) for i in range(size)])  55.1 us
    pallas_call x2, Pallas kernels, attend(): pl.pallas_call(attention_kernel, grid_spec=grid_spec, out_shape=out_shape...  54 us
    ppermute x3, waiting for transfers between devices, on_device(): lax.ppermute(piece, 'head', [(i, (i + k) % size) for i in range(size)])  49.5 us
    all_to_all x2, starting transfers between devices, on_device(): lax.all_to_all(remote, 'blk', split_axis=0, concat_axis=0, tiled=True)  18.3 us
    all_to_all x2, waiting for transfers between devices, on_device(): recv = lax.all_to_all(send, 'blk', split_axis=0, concat_axis=0, tiled=True)  16.4 us
    all_to_all x2, starting transfers between devices, on_device(): recv = lax.all_to_all(send, 'blk', split_axis=0, concat_axis=0, tiled=True)  13.2 us
    all_to_all x1, waiting for transfers between devices, to_heads(): return lax.all_to_all(x, 'head', split_axis=2, concat_axis=1, tiled=True)  12.2 us
    unnamed x37, local copies, waits for them, and re-layouts  10.3 us
  transfers between devices with their start and end apart: 14, of which 9 were waited for; matrix products, arithmetic and copies ran while one was open for 13% of the time, Pallas kernels for 19%

profile of v14, /device:TPU:0, one launch (start us, length us, event | category | flops | bytes accessed | tf_op | source)
XLA Modules:
  0.0 290.7 jit_solution(3574921801122654092)
XLA Ops:
  2.8 4.4 %all-to-all-start = ((bf16[2,192,8,128]{3,1,0,2:T(8,128)(2,1)}), bf16[2,192,8,128]{3,1,0,2:T(8,128)(2,1)S(1)}, u32[]{:S(2)}, u32[]{:S(2)}) async-start(bf16[2,192,8,128]{3,1,0,2:T(8,128)(2,1)} %pad_maximum_fusion.1), calls=%async_computation | async-start | bytes 1572864 | tf_op jit(solution)/shard_map/all_to_all | solution.py:29
  8.2 12.2 %all-to-all-done = bf16[2,192,8,128]{3,1,0,2:T(8,128)(2,1)S(1)} async-done(((bf16[2,192,8,128]{3,1,0,2:T(8,128)(2,1)}), bf16[2,192,8,128]{3,1,0,2:T(8,128)(2,1)S(1)}, u32[]{:S(2)}, u32[]{:S(2)}) %all-to-all-start) | async-done | bytes 786464 | tf_op jit(solution)/shard_map/all_to_all | solution.py:29
  21.4 2.2 copy.157
  23.5 8.4 %all-to-all-start.1 = ((bf16[32,2,128,128]{3,2,1,0:T(8,128)(2,1)}), bf16[32,2,128,128]{3,2,1,0:T(8,128)(2,1)S(1)}, u32[]{:S(2)}, u32[]{:S(2)}) async-start(bf16[32,2,128,128]{3,2,1,0:T(8,128)(2,1)} %copy.157), calls=%async_computation.1 | async-start | bytes 4194304 | tf_op jit(solution)/shard_map/all_to_all | solution.py:207
  32.0 3.5 %stack.104 = bf16[1,192,4,1024]{3,2,1,0:T(4,128)(2,1)} reshape(bf16[192,32,128]{2,1,0:T(8,128)(2,1)} %param.5) | data formatting | bytes 3145728 | tf_op jit(solution)/shard_map/stack | solution.py:157
  35.5 3.5 %stack.105 = bf16[1,192,4,1024]{3,2,1,0:T(4,128)(2,1)} reshape(bf16[192,32,128]{2,1,0:T(8,128)(2,1)} %param.9) | data formatting | bytes 3145728 | tf_op jit(solution)/shard_map/stack | solution.py:157
  39.0 2.0 copy_dynamic-update-slice_fusion.1
  41.5 1.6 copy-done.9
  43.9 2.2 copy.156
  46.1 16.4 %all-to-all-done.1.refs_0_ = bf16[32,2,128,128]{3,2,1,0:T(8,128)(2,1)S(1)} async-done(((bf16[32,2,128,128]{3,2,1,0:T(8,128)(2,1)}), bf16[32,2,128,128]{3,2,1,0:T(8,128)(2,1)S(1)}, u32[]{:S(2)}, u32[]{:S(2)}) %all-to-all-start.1) | async-done | bytes 2097184 | tf_op jit(solution)/shard_map/all_to_all | solution.py:207
  62.5 4.8 %all-to-all-start.2 = ((bf16[32,2,128,128]{3,2,1,0:T(8,128)(2,1)}), bf16[32,2,128,128]{3,2,1,0:T(8,128)(2,1)}, u32[]{:S(2)}, u32[]{:S(2)}) async-start(bf16[32,2,128,128]{3,2,1,0:T(8,128)(2,1)} %copy.156), calls=%async_computation.2 | async-start | bytes 4194304 | tf_op jit(solution)/shard_map/all_to_all | solution.py:207
  67.3 3.7 %dynamic-slice_bitcast_fusion.5 = (bf16[1,2,192,1024]{3,2,1,0:T(8,128)(2,1)}, bf16[2,192,1024]{2,1,0:T(8,128)(2,1)}, bf16[2,192,1024]{2,1,0:T(8,128)(2,1)}, bf16[2,192,1024]{2,1,0:T(8,128)(2,1)}) fusion(bf16[2,192,4,1024]{3,1,0,2:T(8,128)(2,1)} %copy-done.9, s32[]{:T(128)S(6)} %select_n.138, s32[]{:T(128)S(6)} %select_n.144, s32[]{:T(128)S(6)} %select_n.142, ...), kind=kLoop, calls=%fused_computation.49 | loop fusion | bytes 6291472 | tf_op jit(solution)/shard_map/jit(dynamic_index_in_dim)/dynamic_slice | solution.py:161
  73.9 33.8 %collective-permute-done.2 = bf16[2,192,1024]{2,1,0:T(8,128)(2,1)} collective-permute-done((bf16[2,192,1024]{2,1,0:T(8,128)(2,1)}, bf16[2,192,1024]{2,1,0:T(8,128)(2,1)}, u32[]{:S(2)}, u32[]{:S(2)}) %collective-permute-start.2) | collective-permute-done | bytes 786464 | tf_op jit(solution)/shard_map/ppermute | solution.py:163
  107.8 15.6 %collective-permute-done.1 = bf16[2,192,1024]{2,1,0:T(8,128)(2,1)} collective-permute-done((bf16[2,192,1024]{2,1,0:T(8,128)(2,1)}, bf16[2,192,1024]{2,1,0:T(8,128)(2,1)}, u32[]{:S(2)}, u32[]{:S(2)}) %collective-permute-start.1) | collective-permute-done | bytes 786464 | tf_op jit(solution)/shard_map/ppermute | solution.py:163
  123.4 3.2 %pad_maximum_fusion.refs_2_.refs_3_.refs_4_.refs_5_ = bf16[4,2,192,1024]{3,2,1,0:T(8,128)(2,1)} fusion(bf16[1,2,192,1024]{3,2,1,0:T(8,128)(2,1)} %bitcast.17, bf16[1,2,192,1024]{3,2,1,0:T(8,128)(2,1)} %bitcast.15, bf16[1,2,192,1024]{3,2,1,0:T(8,128)(2,1)} %bitcast.13, bf16[1,2,192,1024]{3,2,1,0:T(8,128)(2,1)} %get-tuple-element.35), kind=kLoop, calls=%fused_computation.12 | loop fusion | flops 4718592 | bytes 6291456 | tf_op jit(solution)/shard_map/stack | solution.py:165
  126.6 26.6 %shard_map.84 = (bf16[768,512]{1,0:T(8,128)(2,1)S(1)}, bf16[768,512]{1,0:T(8,128)(2,1)S(1)}, f32[38,128,128]{2,1,0:T(8,128)}, f32[38,128,128]{2,1,0:T(8,128)}) custom-call(s32[48]{0:T(128)S(1)} %reshape_squeeze.6.src_ref, s32[6]{0:T(128)S(1)} %add_multiply_fusion.base_ref, s32[4]{0:T(128)S(1)} %and_select_fusion.peer_ref, ...), custom_call_target="tpu_custom_call" | custom-call | tf_op jit(solution)/shard_map/pallas_call | solution.py:138
  153.1 3.5 %maximum_convert_fusion.1 = bf16[38,2,128,128]{3,2,0,1:T(8,128)(2,1)S(1)} fusion(f32[38,1,128,128]{3,2,0,1:T(8,128)} %bitcast.135, f32[38,1,128,128]{3,2,0,1:T(8,128)} %bitcast.133), kind=kLoop, calls=%fused_computation.1 | loop fusion | flops 1245184 | bytes 7471104 | tf_op jit(solution)/shard_map/convert.2
  156.8 1.5 copy.113
  158.2 10.0 %all-to-all-start.3 = ((bf16[32,2,128,128]{3,2,1,0:T(8,128)(2,1)}), bf16[32,2,128,128]{3,2,1,0:T(8,128)(2,1)}, u32[]{:S(2)}, u32[]{:S(2)}) async-start(bf16[32,2,128,128]{3,2,1,0:T(8,128)(2,1)} %copy.113), calls=%async_computation.3 | async-start | bytes 4194304 | tf_op jit(solution)/shard_map/all_to_all | solution.py:220
  168.4 27.5 %shard_map.85 = (bf16[768,512]{1,0:T(8,128)(2,1)S(1)}, bf16[768,512]{1,0:T(8,128)(2,1)S(1)}, f32[38,128,128]{2,1,0:T(8,128)}, f32[38,128,128]{2,1,0:T(8,128)}) custom-call(s32[48]{0:T(128)S(1)} %reshape_squeeze.7.src_ref, s32[6]{0:T(128)S(1)} %add_multiply_fusion.base_ref, s32[4]{0:T(128)S(1)} %and_select_fusion.peer_ref, ...), custom_call_target="tpu_custom_call" | custom-call | tf_op jit(solution)/shard_map/pallas_call | solution.py:138
  200.2 1.5 slice.108
  201.7 3.1 %copy.116 = bf16[32,2,128,128]{3,2,1,0:T(8,128)(2,1)} copy(bf16[32,2,128,128]{3,2,0,1:T(8,128)(2,1)} %slice.108) | data formatting | bytes 4194304 | tf_op jit(solution)/shard_map/optimization_barrier | solution.py:217
  204.9 8.3 %all-to-all-start.4 = ((bf16[32,2,128,128]{3,2,1,0:T(8,128)(2,1)}), bf16[32,2,128,128]{3,2,1,0:T(8,128)(2,1)}, u32[]{:S(2)}, u32[]{:S(2)}) async-start(bf16[32,2,128,128]{3,2,1,0:T(8,128)(2,1)} %copy.116), calls=%async_computation.4 | async-start | bytes 4194304 | tf_op jit(solution)/shard_map/all_to_all | solution.py:220
  213.5 3.2 %collective-permute-start.3 = (bf16[2,192,8,128]{3,2,1,0:T(8,128)(2,1)S(1)}, bf16[2,192,8,128]{3,2,1,0:T(8,128)(2,1)S(1)}, u32[]{:S(2)}, u32[]{:S(2)}) collective-permute-start(bf16[2,192,8,128]{3,2,1,0:T(8,128)(2,1)S(1)} %get-tuple-element.33), channel_id=1, source_target_pairs={{0,96},{32,0},{64,32},{96,64},{1,97},{33,1},{65,33},{97,65},{2,98}... | collective-permute-start | bytes 2359304 | tf_op jit(solution)/shard_map/ppermute | solution.py:19
  216.8 2.0 collective-permute-start.4
  218.7 2.8 fusion.2
  222.0 32.0 %collective-permute-done.3 = bf16[2,192,8,128]{3,2,1,0:T(8,128)(2,1)S(1)} collective-permute-done((bf16[2,192,8,128]{3,2,1,0:T(8,128)(2,1)S(1)}, bf16[2,192,8,128]{3,2,1,0:T(8,128)(2,1)S(1)}, u32[]{:S(2)}, u32[]{:S(2)}) %collective-permute-start.3) | collective-permute-done | bytes 786464 | tf_op jit(solution)/shard_map/ppermute | solution.py:19
  254.3 13.4 %collective-permute-done.4 = bf16[2,192,8,128]{3,2,1,0:T(8,128)(2,1)S(1)} collective-permute-done((bf16[2,192,8,128]{3,2,1,0:T(8,128)(2,1)S(1)}, bf16[2,192,8,128]{3,2,1,0:T(8,128)(2,1)S(1)}, u32[]{:S(2)}, u32[]{:S(2)}) %collective-permute-start.4) | collective-permute-done | bytes 786464 | tf_op jit(solution)/shard_map/ppermute | solution.py:19
  269.4 2.4 dynamic-slice_bitcast_fusion
  271.8 3.0 %fusion = f32[6,2,128,128]{3,0,2,1:T(8,128)S(1)} fusion(bf16[32,2,128,128]{3,2,1,0:T(8,128)(2,1)} %all-to-all-done.4, bf16[2,32,6]{1,2,0:T(8,128)(2,1)S(1)} %broadcast_select_fusion), kind=kOutput, calls=%fused_computation.13 | convolution fusion | flops 12582912 | bytes 2885632 | tf_op jit(solution)/shard_map/rl,rktd->lktd/dot_general | solution.py:228
  277.6 4.6 %collective-permute-done.6 = bf16[2,192,2,128]{3,2,1,0:T(2,128)(2,1)S(1)} collective-permute-done((bf16[2,192,2,128]{3,2,1,0:T(2,128)(2,1)S(1)}, bf16[2,192,2,128]{3,2,1,0:T(2,128)(2,1)S(1)}, u32[]{:S(2)}, u32[]{:S(2)}) %collective-permute-start.6) | collective-permute-done | bytes 196640 | tf_op jit(solution)/shard_map/ppermute | solution.py:19
  282.4 3.8 %collective-permute-done.7 = bf16[2,192,2,128]{3,2,1,0:T(2,128)(2,1)S(1)} collective-permute-done((bf16[2,192,2,128]{3,2,1,0:T(2,128)(2,1)S(1)}, bf16[2,192,2,128]{3,2,1,0:T(2,128)(2,1)S(1)}, u32[]{:S(2)}, u32[]{:S(2)}) %collective-permute-start.7) | collective-permute-done | bytes 196640 | tf_op jit(solution)/shard_map/ppermute | solution.py:19
  (97 shorter events, 23.0 us)
Async XLA Ops:
  2.8 17.5 %all-to-all-start = ((bf16[2,192,8,128]{3,1,0,2:T(8,128)(2,1)}), bf16[2,192,8,128]{3,1,0,2:T(8,128)(2,1)S(1)}, u32[]{:S(2)}, u32[]{:S(2)}) async-start(bf16[2,192,8,128]{3,1,0,2:T(8,128)(2,1)} %pad_maximum_fusion.1), calls=%async_computation | async-start | bytes 1572864 | tf_op jit(solution)/shard_map/all_to_all | solution.py:29
  23.5 39.0 %all-to-all-start.1 = ((bf16[32,2,128,128]{3,2,1,0:T(8,128)(2,1)}), bf16[32,2,128,128]{3,2,1,0:T(8,128)(2,1)S(1)}, u32[]{:S(2)}, u32[]{:S(2)}) async-start(bf16[32,2,128,128]{3,2,1,0:T(8,128)(2,1)} %copy.157), calls=%async_computation.1 | async-start | bytes 4194304 | tf_op jit(solution)/shard_map/all_to_all | solution.py:207
  39.0 2.0 copy-start.10
  41.5 1.6 copy-start.9
  62.5 95.7 %all-to-all-start.2 = ((bf16[32,2,128,128]{3,2,1,0:T(8,128)(2,1)}), bf16[32,2,128,128]{3,2,1,0:T(8,128)(2,1)}, u32[]{:S(2)}, u32[]{:S(2)}) async-start(bf16[32,2,128,128]{3,2,1,0:T(8,128)(2,1)} %copy.156), calls=%async_computation.2 | async-start | bytes 4194304 | tf_op jit(solution)/shard_map/all_to_all | solution.py:207
  71.0 36.8 %collective-permute-start.2 = (bf16[2,192,1024]{2,1,0:T(8,128)(2,1)}, bf16[2,192,1024]{2,1,0:T(8,128)(2,1)}, u32[]{:S(2)}, u32[]{:S(2)}) collective-permute-start(bf16[2,192,1024]{2,1,0:T(8,128)(2,1)} %get-tuple-element.36), channel_id=1, source_target_pairs={{0,96},{32,0},{64,32},{96,64},{1,97},{33,1},{65,33},{97,65},{2,98}... | collective-permute-start | bytes 2359304 | tf_op jit(solution)/shard_map/ppermute | solution.py:163
  71.0 52.4 %collective-permute-start.1 = (bf16[2,192,1024]{2,1,0:T(8,128)(2,1)}, bf16[2,192,1024]{2,1,0:T(8,128)(2,1)}, u32[]{:S(2)}, u32[]{:S(2)}) collective-permute-start(bf16[2,192,1024]{2,1,0:T(8,128)(2,1)} %get-tuple-element.37), channel_id=1, source_target_pairs={{0,64},{32,96},{64,0},{96,32},{1,65},{33,97},{65,1},{97,33},{2,66}... | collective-permute-start | bytes 2359304 | tf_op jit(solution)/shard_map/ppermute | solution.py:163
  72.3 51.1 %collective-permute-start = (bf16[2,192,1024]{2,1,0:T(8,128)(2,1)}, bf16[2,192,1024]{2,1,0:T(8,128)(2,1)}, u32[]{:S(2)}, u32[]{:S(2)}) collective-permute-start(bf16[2,192,1024]{2,1,0:T(8,128)(2,1)} %get-tuple-element.38), channel_id=1, source_target_pairs={{0,32},{32,64},{64,96},{96,0},{1,33},{33,65},{65,97},{97,1},{2,34}... | collective-permute-start | bytes 2359304 | tf_op jit(solution)/shard_map/ppermute | solution.py:163
  153.1 3.5 %copy-start = (bf16[768,512]{1,0:T(8,128)(2,1)}, bf16[768,512]{1,0:T(8,128)(2,1)S(1)}, u32[]{:S(2)}) copy-start(bf16[768,512]{1,0:T(8,128)(2,1)S(1)} %get-tuple-element.18) | copy-start | bytes 2359300
  153.1 3.5 %copy-start.2 = (bf16[768,512]{1,0:T(8,128)(2,1)}, bf16[768,512]{1,0:T(8,128)(2,1)S(1)}, u32[]{:S(2)}) copy-start(bf16[768,512]{1,0:T(8,128)(2,1)S(1)} %get-tuple-element.16) | copy-start | bytes 2359300
  158.2 43.5 %all-to-all-start.3 = ((bf16[32,2,128,128]{3,2,1,0:T(8,128)(2,1)}), bf16[32,2,128,128]{3,2,1,0:T(8,128)(2,1)}, u32[]{:S(2)}, u32[]{:S(2)}) async-start(bf16[32,2,128,128]{3,2,1,0:T(8,128)(2,1)} %copy.113), calls=%async_computation.3 | async-start | bytes 4194304 | tf_op jit(solution)/shard_map/all_to_all | solution.py:220
  168.4 27.5 %copy-start.3 = (bf16[768,512]{1,0:T(8,128)(2,1)S(1)}, bf16[768,512]{1,0:T(8,128)(2,1)}, u32[]{:S(2)}) copy-start(bf16[768,512]{1,0:T(8,128)(2,1)} %copy-done.2) | copy-start | bytes 2359300
  196.1 1.1 copy-start.1
  197.2 1.7 copy-start.6
  197.5 2.3 copy-start.4
  204.9 67.0 %all-to-all-start.4 = ((bf16[32,2,128,128]{3,2,1,0:T(8,128)(2,1)}), bf16[32,2,128,128]{3,2,1,0:T(8,128)(2,1)}, u32[]{:S(2)}, u32[]{:S(2)}) async-start(bf16[32,2,128,128]{3,2,1,0:T(8,128)(2,1)} %copy.116), calls=%async_computation.4 | async-start | bytes 4194304 | tf_op jit(solution)/shard_map/all_to_all | solution.py:220
  213.2 8.3 %copy-start.8 = (f32[38,128,128]{2,1,0:T(8,128)S(1)}, f32[38,128,128]{2,1,0:T(8,128)}, u32[]{:S(2)}) copy-start(f32[38,128,128]{2,1,0:T(8,128)} %get-tuple-element.23) | copy-start | bytes 7471108
  213.4 8.1 %copy-start.7 = (f32[38,128,128]{2,1,0:T(8,128)S(1)}, f32[38,128,128]{2,1,0:T(8,128)}, u32[]{:S(2)}) copy-start(f32[38,128,128]{2,1,0:T(8,128)} %get-tuple-element.22) | copy-start | bytes 7471108
  213.4 54.5 %collective-permute-start.5 = (bf16[2,192,8,128]{3,2,1,0:T(8,128)(2,1)S(1)}, bf16[2,192,8,128]{3,2,1,0:T(8,128)(2,1)S(1)}, u32[]{:S(2)}, u32[]{:S(2)}) collective-permute-start(bf16[2,192,8,128]{3,2,1,0:T(8,128)(2,1)S(1)} %get-tuple-element.32), channel_id=1, source_target_pairs={{0,32},{32,64},{64,96},{96,0},{1,33},{33,65},{65,97},{97,1},{2,34}... | collective-permute-start | bytes 2359304 | tf_op jit(solution)/shard_map/ppermute | solution.py:19
  213.5 40.5 %collective-permute-start.3 = (bf16[2,192,8,128]{3,2,1,0:T(8,128)(2,1)S(1)}, bf16[2,192,8,128]{3,2,1,0:T(8,128)(2,1)S(1)}, u32[]{:S(2)}, u32[]{:S(2)}) collective-permute-start(bf16[2,192,8,128]{3,2,1,0:T(8,128)(2,1)S(1)} %get-tuple-element.33), channel_id=1, source_target_pairs={{0,96},{32,0},{64,32},{96,64},{1,97},{33,1},{65,33},{97,65},{2,98}... | collective-permute-start | bytes 2359304 | tf_op jit(solution)/shard_map/ppermute | solution.py:19
  216.8 50.9 %collective-permute-start.4 = (bf16[2,192,8,128]{3,2,1,0:T(8,128)(2,1)S(1)}, bf16[2,192,8,128]{3,2,1,0:T(8,128)(2,1)S(1)}, u32[]{:S(2)}, u32[]{:S(2)}) collective-permute-start(bf16[2,192,8,128]{3,2,1,0:T(8,128)(2,1)S(1)} %get-tuple-element.34), channel_id=1, source_target_pairs={{0,64},{32,96},{64,0},{96,32},{1,65},{33,97},{65,1},{97,33},{2,66}... | collective-permute-start | bytes 2359304 | tf_op jit(solution)/shard_map/ppermute | solution.py:19
  271.8 3.0 %copy-start.5 = (f32[38,128,128]{2,1,0:T(8,128)S(1)}, f32[38,128,128]{2,1,0:T(8,128)}, u32[]{:S(2)}) copy-start(f32[38,128,128]{2,1,0:T(8,128)} %get-tuple-element.20) | copy-start | bytes 7471108
  276.8 5.4 %collective-permute-start.6 = (bf16[2,192,2,128]{3,2,1,0:T(2,128)(2,1)S(1)}, bf16[2,192,2,128]{3,2,1,0:T(2,128)(2,1)S(1)}, u32[]{:S(2)}, u32[]{:S(2)}) collective-permute-start(bf16[2,192,2,128]{3,2,1,0:T(2,128)(2,1)S(1)} %bitcast.149), channel_id=1, source_target_pairs={{0,96},{32,0},{64,32},{96,64},{1,97},{33,1},{65,33},{97,65},{2,98}... | collective-permute-start | bytes 589832 | tf_op jit(solution)/shard_map/ppermute | solution.py:19
  276.9 9.3 %collective-permute-start.7 = (bf16[2,192,2,128]{3,2,1,0:T(2,128)(2,1)S(1)}, bf16[2,192,2,128]{3,2,1,0:T(2,128)(2,1)S(1)}, u32[]{:S(2)}, u32[]{:S(2)}) collective-permute-start(bf16[2,192,2,128]{3,2,1,0:T(2,128)(2,1)S(1)} %bitcast.148), channel_id=1, source_target_pairs={{0,64},{32,96},{64,0},{96,32},{1,65},{33,97},{65,1},{97,33},{2,66}... | collective-permute-start | bytes 589832 | tf_op jit(solution)/shard_map/ppermute | solution.py:19
  277.2 10.6 %collective-permute-start.8 = (bf16[2,192,2,128]{3,2,1,0:T(2,128)(2,1)S(1)}, bf16[2,192,2,128]{3,2,1,0:T(2,128)(2,1)S(1)}, u32[]{:S(2)}, u32[]{:S(2)}) collective-permute-start(bf16[2,192,2,128]{3,2,1,0:T(2,128)(2,1)S(1)} %bitcast.147), channel_id=1, source_target_pairs={{0,32},{32,64},{64,96},{96,0},{1,33},{33,65},{65,97},{97,1},{2,34}... | collective-permute-start | bytes 589832 | tf_op jit(solution)/shard_map/ppermute | solution.py:19

commit v15 on v12

--- a/solution.py
+++ b/solution.py
@@ -40,7 +40,7 @@
 
 def attention_kernel(src_ref, base_ref, peer_ref, *refs):
     table_ref, q_lo, q_hi, do_lo, do_hi, kpos_ref = refs[:6]
-    o_ref, dq_ref, dk_ref, dv_ref = refs[6:]
+    o_ref, dq_ref, part_ref, dk_ref, dv_ref = refs[6:]
     b = pl.program_id(0)
 
     @pl.when(b == 0)
@@ -88,6 +88,11 @@
         dk_ref[t] = dk_ref[t] + dk[rows]
         dv_ref[t] = dv_ref[t] + dv[rows]
 
+    @pl.when(b == pl.num_programs(0) - 1)
+    def _():
+        part_ref[:, 0] = dk_ref[...].astype(part_ref.dtype)
+        part_ref[:, 1] = dv_ref[...].astype(part_ref.dtype)
+
 
 def attend(slot_src, query_base, peer_of, table, pieces, key_pos, group, groups):
     piece_len = pieces.shape[2]
@@ -110,7 +115,9 @@
 
     out_row = pl.BlockSpec((BLOCK_TOKENS, row_width), lambda b, src, base, peer: (b, 0))
     pos_spec = pl.BlockSpec((None, 1, TOPK * BLOCK_TOKENS), lambda b, src, base, peer: (b, 0, 0))
-    acc_spec = pl.BlockSpec((targets, BLOCK_TOKENS, head_width), lambda b, src, base, peer: (0, 0, 0))
+    part_spec = pl.BlockSpec(
+        (targets, 2, BLOCK_TOKENS, head_width), lambda b, src, base, peer: (0, 0, 0, 0)
+    )
     in_specs = (
         [table_spec]
         + [half_spec(0, 0), half_spec(0, 1), half_spec(1, 0), half_spec(1, 1), pos_spec]
@@ -118,14 +125,14 @@
     out_shape = (
         jax.ShapeDtypeStruct((run_len, row_width), jnp.bfloat16),
         jax.ShapeDtypeStruct((run_len, row_width), jnp.bfloat16),
-        jax.ShapeDtypeStruct((targets, BLOCK_TOKENS, head_width), jnp.float32),
-        jax.ShapeDtypeStruct((targets, BLOCK_TOKENS, head_width), jnp.float32),
+        jax.ShapeDtypeStruct((targets, 2, BLOCK_TOKENS, head_width), jnp.bfloat16),
     )
     grid_spec = pltpu.PrefetchScalarGridSpec(
         num_scalar_prefetch=3,
         grid=(block_ids,),
         in_specs=in_specs,
-        out_specs=(out_row, out_row, acc_spec, acc_spec),
+        out_specs=(out_row, out_row, part_spec),
+        scratch_shapes=[pltpu.VMEM((targets, BLOCK_TOKENS, head_width), jnp.float32)] * 2,
     )
     return pl.pallas_call(
         attention_kernel,
@@ -198,14 +205,13 @@
         ).astype(jnp.bfloat16)
         recv = lax.all_to_all(send, "blk", split_axis=0, concat_axis=0, tiled=True)
         table = jnp.concatenate([recv, kv_local[g]], axis=0)
-        o_g, dq_g, dk_acc, dv_acc = attend(
+        o_g, dq_g, part = attend(
             slot_src[g].reshape(-1), query_base, peer_of, table, qg_pieces, key_pos[g], g, groups
         )
         outs.append(o_g)
         query_grads.append(dq_g)
-        acc = jnp.stack([dk_acc, dv_acc], axis=1)
-        remote = acc[:peers].astype(jnp.bfloat16)
-        local = acc[peers:].astype(jnp.bfloat16)
+        remote = part[:peers]
+        local = part[peers:]
         if g == groups - 1:
             attn_all, query_grad_all, remote, backs[0] = lax.optimization_barrier(
                 (heads_layout(outs), heads_layout(query_grads), remote, backs[0])

time: 263 us -> 288 us (1.095)
  waiting for transfers between devices: 94.9 us -> 130 us
  starting transfers between devices: 48.7 us -> 43.2 us
  other arithmetic: 18.5 us -> 15.5 us
    ppermute x3, waiting for transfers between devices: 19.8 us -> 49.4 us  [on_device(): lax.ppermute(piece, 'head', [(i, (i + k) % size) for i in range(size)])]
    ppermute x6, starting transfers between devices: 11.4 us -> 5.9 us  [exchange(): lax.ppermute(piece, 'head', [(i, (i + k) % size) for i in range(size)])]
    ppermute x6, waiting for transfers between devices: 47.4 us -> 52 us  [exchange(): lax.ppermute(piece, 'head', [(i, (i + k) % size) for i in range(size)])]
    optimization_barrier x1 -> x0, local copies, waits for them, and re-layouts: 3.17 us -> none  [on_device(): lax.optimization_barrier((heads_layout(outs), heads_layout(query_grads),...]
    unnamed x35 -> x33, local copies, waits for them, and re-layouts: 10.3 us -> 12.6 us
  transfers between devices with their start and end apart: 14 -> 14, of which waited for: 7 -> 9; matrix products, arithmetic and copies ran while one was open for 17% -> 16% of each run, Pallas kernels for 20% -> 18%
where the time goes in v15:
time: 288 us; the launch traced here: 287 us
  waiting for transfers between devices  130 us (45%)
  Pallas kernels  51 us (18%)
  starting transfers between devices  43.2 us (15%)
  local copies, waits for them, and re-layouts  38.3 us (13%)
  other arithmetic  15.5 us (5%)
  matrix products  7.31 us (3%)
    ppermute x6, waiting for transfers between devices, exchange(): lax.ppermute(piece, 'head', [(i, (i + k) % size) for i in range(size)])  52 us
    pallas_call x2, Pallas kernels, attend(): pl.pallas_call(attention_kernel, grid_spec=grid_spec, out_shape=out_shape...  51 us
    ppermute x3, waiting for transfers between devices, on_device(): lax.ppermute(piece, 'head', [(i, (i + k) % size) for i in range(size)])  49.4 us
    all_to_all x2, starting transfers between devices, on_device(): lax.all_to_all(remote, 'blk', split_axis=0, concat_axis=0, tiled=True)  18.4 us
    all_to_all x2, waiting for transfers between devices, on_device(): recv = lax.all_to_all(send, 'blk', split_axis=0, concat_axis=0, tiled=True)  16.5 us
    all_to_all x2, starting transfers between devices, on_device(): recv = lax.all_to_all(send, 'blk', split_axis=0, concat_axis=0, tiled=True)  13.2 us
    unnamed x33, local copies, waits for them, and re-layouts  12.6 us
    all_to_all x1, waiting for transfers between devices, to_heads(): return lax.all_to_all(x, 'head', split_axis=2, concat_axis=1, tiled=True)  12.2 us
  transfers between devices with their start and end apart: 14, of which 9 were waited for; matrix products, arithmetic and copies ran while one was open for 16% of the time, Pallas kernels for 18%

profile of v15, /device:TPU:0, one launch (start us, length us, event | category | flops | bytes accessed | tf_op | source)
XLA Modules:
  0.0 286.6 jit_solution(3467890280491637609)
XLA Ops:
  2.8 4.4 %all-to-all-start = ((bf16[2,192,8,128]{3,1,0,2:T(8,128)(2,1)}), bf16[2,192,8,128]{3,1,0,2:T(8,128)(2,1)S(1)}, u32[]{:S(2)}, u32[]{:S(2)}) async-start(bf16[2,192,8,128]{3,1,0,2:T(8,128)(2,1)} %pad_maximum_fusion.3), calls=%async_computation | async-start | bytes 1572864 | tf_op jit(solution)/shard_map/all_to_all | solution.py:29
  8.2 12.2 %all-to-all-done = bf16[2,192,8,128]{3,1,0,2:T(8,128)(2,1)S(1)} async-done(((bf16[2,192,8,128]{3,1,0,2:T(8,128)(2,1)}), bf16[2,192,8,128]{3,1,0,2:T(8,128)(2,1)S(1)}, u32[]{:S(2)}, u32[]{:S(2)}) %all-to-all-start) | async-done | bytes 786464 | tf_op jit(solution)/shard_map/all_to_all | solution.py:29
  21.4 2.2 copy.153
  23.5 8.4 %all-to-all-start.1 = ((bf16[32,2,128,128]{3,2,1,0:T(8,128)(2,1)}), bf16[32,2,128,128]{3,2,1,0:T(8,128)(2,1)S(1)}, u32[]{:S(2)}, u32[]{:S(2)}) async-start(bf16[32,2,128,128]{3,2,1,0:T(8,128)(2,1)} %copy.153), calls=%async_computation.1 | async-start | bytes 4194304 | tf_op jit(solution)/shard_map/all_to_all | solution.py:206
  32.0 3.5 %stack.86 = bf16[1,192,4,1024]{3,2,1,0:T(4,128)(2,1)} reshape(bf16[192,32,128]{2,1,0:T(8,128)(2,1)} %param.5) | data formatting | bytes 3145728 | tf_op jit(solution)/shard_map/stack | solution.py:156
  35.5 3.5 %stack.87 = bf16[1,192,4,1024]{3,2,1,0:T(4,128)(2,1)} reshape(bf16[192,32,128]{2,1,0:T(8,128)(2,1)} %param.9) | data formatting | bytes 3145728 | tf_op jit(solution)/shard_map/stack | solution.py:156
  39.0 2.0 copy_dynamic-update-slice_fusion.1
  41.5 1.6 copy-done.5
  43.9 2.1 copy.152
  46.1 16.5 %all-to-all-done.1 = bf16[32,2,128,128]{3,2,1,0:T(8,128)(2,1)S(1)} async-done(((bf16[32,2,128,128]{3,2,1,0:T(8,128)(2,1)}), bf16[32,2,128,128]{3,2,1,0:T(8,128)(2,1)S(1)}, u32[]{:S(2)}, u32[]{:S(2)}) %all-to-all-start.1) | async-done | bytes 2097184 | tf_op jit(solution)/shard_map/all_to_all | solution.py:206
  62.6 4.8 %all-to-all-start.2 = ((bf16[32,2,128,128]{3,2,1,0:T(8,128)(2,1)}), bf16[32,2,128,128]{3,2,1,0:T(8,128)(2,1)}, u32[]{:S(2)}, u32[]{:S(2)}) async-start(bf16[32,2,128,128]{3,2,1,0:T(8,128)(2,1)} %copy.152), calls=%async_computation.2 | async-start | bytes 4194304 | tf_op jit(solution)/shard_map/all_to_all | solution.py:206
  67.4 3.7 %dynamic-slice_bitcast_fusion.5 = (bf16[1,2,192,1024]{3,2,1,0:T(8,128)(2,1)}, bf16[2,192,1024]{2,1,0:T(8,128)(2,1)}, bf16[2,192,1024]{2,1,0:T(8,128)(2,1)}, bf16[2,192,1024]{2,1,0:T(8,128)(2,1)}) fusion(bf16[2,192,4,1024]{3,1,0,2:T(8,128)(2,1)} %copy-done.5, s32[]{:T(128)S(6)} %select_n.138, s32[]{:T(128)S(6)} %select_n.144, s32[]{:T(128)S(6)} %select_n.142, ...), kind=kLoop, calls=%fused_computation.47 | loop fusion | bytes 6291472 | tf_op jit(solution)/shard_map/jit(dynamic_index_in_dim)/dynamic_slice | solution.py:160
  74.0 33.8 %collective-permute-done.2 = bf16[2,192,1024]{2,1,0:T(8,128)(2,1)} collective-permute-done((bf16[2,192,1024]{2,1,0:T(8,128)(2,1)}, bf16[2,192,1024]{2,1,0:T(8,128)(2,1)}, u32[]{:S(2)}, u32[]{:S(2)}) %collective-permute-start.2) | collective-permute-done | bytes 786464 | tf_op jit(solution)/shard_map/ppermute | solution.py:162
  107.8 15.5 %collective-permute-done.1 = bf16[2,192,1024]{2,1,0:T(8,128)(2,1)} collective-permute-done((bf16[2,192,1024]{2,1,0:T(8,128)(2,1)}, bf16[2,192,1024]{2,1,0:T(8,128)(2,1)}, u32[]{:S(2)}, u32[]{:S(2)}) %collective-permute-start.1) | collective-permute-done | bytes 786464 | tf_op jit(solution)/shard_map/ppermute | solution.py:162
  123.4 3.2 %pad_maximum_fusion.refs_1_.refs_2_.refs_3_.refs_4_ = bf16[4,2,192,1024]{3,2,1,0:T(8,128)(2,1)} fusion(bf16[1,2,192,1024]{3,2,1,0:T(8,128)(2,1)} %bitcast.17, bf16[1,2,192,1024]{3,2,1,0:T(8,128)(2,1)} %bitcast.15, bf16[1,2,192,1024]{3,2,1,0:T(8,128)(2,1)} %bitcast.13, bf16[1,2,192,1024]{3,2,1,0:T(8,128)(2,1)} %get-tuple-element.31), kind=kLoop, calls=%fused_computation.10 | loop fusion | flops 4718592 | bytes 6291456 | tf_op jit(solution)/shard_map/stack | solution.py:164
  126.6 1.7 pad_maximum_fusion.1.refs_0_
  128.2 25.5 %shard_map.84 = (bf16[768,512]{1,0:T(8,128)(2,1)S(1)}, bf16[768,512]{1,0:T(8,128)(2,1)S(1)}, bf16[38,2,128,128]{3,2,1,0:T(8,128)(2,1)S(1)}) custom-call(s32[48]{0:T(128)S(1)} %reshape_squeeze.6.src_ref, s32[6]{0:T(128)S(1)} %add_multiply_fusion.base_ref, s32[4]{0:T(128)S(1)} %and_select_fusion.peer_ref, bf16[38,2,128,128]{3,2,1,0:T(8,128)(2,1)} %pad_maximum_fusion.1.refs_0_, ...), custom_call_target="tpu_custom_call" | custom-call | tf_op jit(solution)/shard_map/pallas_call | solution.py:137
  157.7 10.1 %all-to-all-start.3 = ((bf16[32,2,128,128]{3,2,1,0:T(8,128)(2,1)}), bf16[32,2,128,128]{3,2,1,0:T(8,128)(2,1)}, u32[]{:S(2)}, u32[]{:S(2)}) async-start(bf16[32,2,128,128]{3,2,1,0:T(8,128)(2,1)} %slice.83), calls=%async_computation.3 | async-start | bytes 4194304 | tf_op jit(solution)/shard_map/all_to_all | solution.py:219
  168.0 3.3 %pad_maximum_fusion.2.refs_0_ = bf16[38,2,128,128]{3,2,1,0:T(8,128)(2,1)} fusion(bf16[6,2,128,128]{3,2,1,0:T(8,128)(2,1)S(1)} %copy-done.8, bf16[32,2,128,128]{3,2,1,0:T(8,128)(2,1)} %all-to-all-done.2), kind=kLoop, calls=%fused_computation.12 | loop fusion | flops 1245184 | bytes 4980736 | tf_op jit(solution)/shard_map/concatenate | solution.py:207
  171.2 25.5 %shard_map.85 = (bf16[768,512]{1,0:T(8,128)(2,1)S(1)}, bf16[768,512]{1,0:T(8,128)(2,1)S(1)}, bf16[38,2,128,128]{3,2,1,0:T(8,128)(2,1)S(1)}) custom-call(s32[48]{0:T(128)S(1)} %reshape_squeeze.7.src_ref, s32[6]{0:T(128)S(1)} %add_multiply_fusion.base_ref, s32[4]{0:T(128)S(1)} %and_select_fusion.peer_ref, bf16[38,2,128,128]{3,2,1,0:T(8,128)(2,1)} %pad_maximum_fusion.2.refs_0_, ...), custom_call_target="tpu_custom_call" | custom-call | tf_op jit(solution)/shard_map/pallas_call | solution.py:137
  198.8 1.6 copy.125
  201.9 8.3 %all-to-all-start.4 = ((bf16[32,2,128,128]{3,2,1,0:T(8,128)(2,1)}), bf16[32,2,128,128]{3,2,1,0:T(8,128)(2,1)}, u32[]{:S(2)}, u32[]{:S(2)}) async-start(bf16[32,2,128,128]{3,2,1,0:T(8,128)(2,1)} %slice.82), calls=%async_computation.4 | async-start | bytes 4194304 | tf_op jit(solution)/shard_map/all_to_all | solution.py:219
  210.3 1.8 fusion.5
  212.2 3.2 %collective-permute-start.3 = (bf16[2,192,8,128]{3,2,1,0:T(8,128)(2,1)S(1)}, bf16[2,192,8,128]{3,2,1,0:T(8,128)(2,1)S(1)}, u32[]{:S(2)}, u32[]{:S(2)}) collective-permute-start(bf16[2,192,8,128]{3,2,1,0:T(8,128)(2,1)S(1)} %get-tuple-element.29), channel_id=1, source_target_pairs={{0,96},{32,0},{64,32},{96,64},{1,97},{33,1},{65,33},{97,65},{2,98}... | collective-permute-start | bytes 2359304 | tf_op jit(solution)/shard_map/ppermute | solution.py:19
  215.4 2.0 collective-permute-start.4
  217.4 2.9 %fusion.2 = f32[6,2,128,128]{3,0,2,1:T(8,128)S(1)} fusion(bf16[32,2,128,128]{3,2,1,0:T(8,128)(2,1)} %all-to-all-done.3, bf16[2,32,6]{1,2,0:T(8,128)(2,1)S(1)} %broadcast_select_fusion), kind=kOutput, calls=%fused_computation.15 | convolution fusion | flops 12582912 | bytes 2885632 | tf_op jit(solution)/shard_map/rl,rktd->lktd/dot_general | solution.py:227
  222.1 28.9 %collective-permute-done.3 = bf16[2,192,8,128]{3,2,1,0:T(8,128)(2,1)S(1)} collective-permute-done((bf16[2,192,8,128]{3,2,1,0:T(8,128)(2,1)S(1)}, bf16[2,192,8,128]{3,2,1,0:T(8,128)(2,1)S(1)}, u32[]{:S(2)}, u32[]{:S(2)}) %collective-permute-start.3) | collective-permute-done | bytes 786464 | tf_op jit(solution)/shard_map/ppermute | solution.py:19
  251.3 13.4 %collective-permute-done.4 = bf16[2,192,8,128]{3,2,1,0:T(8,128)(2,1)S(1)} collective-permute-done((bf16[2,192,8,128]{3,2,1,0:T(8,128)(2,1)S(1)}, bf16[2,192,8,128]{3,2,1,0:T(8,128)(2,1)S(1)}, u32[]{:S(2)}, u32[]{:S(2)}) %collective-permute-start.4) | collective-permute-done | bytes 786464 | tf_op jit(solution)/shard_map/ppermute | solution.py:19
  266.4 2.4 dynamic-slice_bitcast_fusion
  268.8 2.8 fusion
  273.5 4.6 %collective-permute-done.6 = bf16[2,192,2,128]{3,2,1,0:T(2,128)(2,1)S(1)} collective-permute-done((bf16[2,192,2,128]{3,2,1,0:T(2,128)(2,1)S(1)}, bf16[2,192,2,128]{3,2,1,0:T(2,128)(2,1)S(1)}, u32[]{:S(2)}, u32[]{:S(2)}) %collective-permute-start.6) | collective-permute-done | bytes 196640 | tf_op jit(solution)/shard_map/ppermute | solution.py:19
  278.3 3.8 %collective-permute-done.7 = bf16[2,192,2,128]{3,2,1,0:T(2,128)(2,1)S(1)} collective-permute-done((bf16[2,192,2,128]{3,2,1,0:T(2,128)(2,1)S(1)}, bf16[2,192,2,128]{3,2,1,0:T(2,128)(2,1)S(1)}, u32[]{:S(2)}, u32[]{:S(2)}) %collective-permute-start.7) | collective-permute-done | bytes 196640 | tf_op jit(solution)/shard_map/ppermute | solution.py:19
  (91 shorter events, 26.1 us)
Async XLA Ops:
  2.8 17.5 %all-to-all-start = ((bf16[2,192,8,128]{3,1,0,2:T(8,128)(2,1)}), bf16[2,192,8,128]{3,1,0,2:T(8,128)(2,1)S(1)}, u32[]{:S(2)}, u32[]{:S(2)}) async-start(bf16[2,192,8,128]{3,1,0,2:T(8,128)(2,1)} %pad_maximum_fusion.3), calls=%async_computation | async-start | bytes 1572864 | tf_op jit(solution)/shard_map/all_to_all | solution.py:29
  20.6 22.6 %copy-start.7 = (bf16[6,2,128,128]{3,2,1,0:T(8,128)(2,1)}, bf16[6,2,128,128]{3,2,1,0:T(8,128)(2,1)S(1)}, u32[]{:S(2)}) copy-start(bf16[6,2,128,128]{3,2,1,0:T(8,128)(2,1)S(1)} %get-tuple-element.42) | copy-start | bytes 1179652
  23.5 39.1 %all-to-all-start.1 = ((bf16[32,2,128,128]{3,2,1,0:T(8,128)(2,1)}), bf16[32,2,128,128]{3,2,1,0:T(8,128)(2,1)S(1)}, u32[]{:S(2)}, u32[]{:S(2)}) async-start(bf16[32,2,128,128]{3,2,1,0:T(8,128)(2,1)} %copy.153), calls=%async_computation.1 | async-start | bytes 4194304 | tf_op jit(solution)/shard_map/all_to_all | solution.py:206
  39.0 2.0 copy-start.6
  41.5 1.6 copy-start.5
  62.6 95.0 %all-to-all-start.2 = ((bf16[32,2,128,128]{3,2,1,0:T(8,128)(2,1)}), bf16[32,2,128,128]{3,2,1,0:T(8,128)(2,1)}, u32[]{:S(2)}, u32[]{:S(2)}) async-start(bf16[32,2,128,128]{3,2,1,0:T(8,128)(2,1)} %copy.152), calls=%async_computation.2 | async-start | bytes 4194304 | tf_op jit(solution)/shard_map/all_to_all | solution.py:206
  71.1 36.8 %collective-permute-start.2 = (bf16[2,192,1024]{2,1,0:T(8,128)(2,1)}, bf16[2,192,1024]{2,1,0:T(8,128)(2,1)}, u32[]{:S(2)}, u32[]{:S(2)}) collective-permute-start(bf16[2,192,1024]{2,1,0:T(8,128)(2,1)} %get-tuple-element.32), channel_id=1, source_target_pairs={{0,96},{32,0},{64,32},{96,64},{1,97},{33,1},{65,33},{97,65},{2,98}... | collective-permute-start | bytes 2359304 | tf_op jit(solution)/shard_map/ppermute | solution.py:162
  71.1 52.3 %collective-permute-start.1 = (bf16[2,192,1024]{2,1,0:T(8,128)(2,1)}, bf16[2,192,1024]{2,1,0:T(8,128)(2,1)}, u32[]{:S(2)}, u32[]{:S(2)}) collective-permute-start(bf16[2,192,1024]{2,1,0:T(8,128)(2,1)} %get-tuple-element.33), channel_id=1, source_target_pairs={{0,64},{32,96},{64,0},{96,32},{1,65},{33,97},{65,1},{97,33},{2,66}... | collective-permute-start | bytes 2359304 | tf_op jit(solution)/shard_map/ppermute | solution.py:162
  72.3 51.0 %collective-permute-start = (bf16[2,192,1024]{2,1,0:T(8,128)(2,1)}, bf16[2,192,1024]{2,1,0:T(8,128)(2,1)}, u32[]{:S(2)}, u32[]{:S(2)}) collective-permute-start(bf16[2,192,1024]{2,1,0:T(8,128)(2,1)} %get-tuple-element.34), channel_id=1, source_target_pairs={{0,32},{32,64},{64,96},{96,0},{1,33},{33,65},{65,97},{97,1},{2,34}... | collective-permute-start | bytes 2359304 | tf_op jit(solution)/shard_map/ppermute | solution.py:162
  153.7 0.9 copy-start.1
  154.6 1.4 copy-start
  157.6 10.3 %copy-start.8 = (bf16[6,2,128,128]{3,2,1,0:T(8,128)(2,1)S(1)}, bf16[6,2,128,128]{3,2,1,0:T(8,128)(2,1)}, u32[]{:S(2)}) copy-start(bf16[6,2,128,128]{3,2,1,0:T(8,128)(2,1)} %copy-done.7) | copy-start | bytes 1179652
  157.7 44.3 %all-to-all-start.3 = ((bf16[32,2,128,128]{3,2,1,0:T(8,128)(2,1)}), bf16[32,2,128,128]{3,2,1,0:T(8,128)(2,1)}, u32[]{:S(2)}, u32[]{:S(2)}) async-start(bf16[32,2,128,128]{3,2,1,0:T(8,128)(2,1)} %slice.83), calls=%async_computation.3 | async-start | bytes 4194304 | tf_op jit(solution)/shard_map/all_to_all | solution.py:219
  171.2 25.5 %copy-start.2 = (bf16[768,512]{1,0:T(8,128)(2,1)S(1)}, bf16[768,512]{1,0:T(8,128)(2,1)}, u32[]{:S(2)}) copy-start(bf16[768,512]{1,0:T(8,128)(2,1)} %copy-done.1) | copy-start | bytes 2359300
  201.9 66.9 %all-to-all-start.4 = ((bf16[32,2,128,128]{3,2,1,0:T(8,128)(2,1)}), bf16[32,2,128,128]{3,2,1,0:T(8,128)(2,1)}, u32[]{:S(2)}, u32[]{:S(2)}) async-start(bf16[32,2,128,128]{3,2,1,0:T(8,128)(2,1)} %slice.82), calls=%async_computation.4 | async-start | bytes 4194304 | tf_op jit(solution)/shard_map/all_to_all | solution.py:219
  212.1 52.9 %collective-permute-start.5 = (bf16[2,192,8,128]{3,2,1,0:T(8,128)(2,1)S(1)}, bf16[2,192,8,128]{3,2,1,0:T(8,128)(2,1)S(1)}, u32[]{:S(2)}, u32[]{:S(2)}) collective-permute-start(bf16[2,192,8,128]{3,2,1,0:T(8,128)(2,1)S(1)} %get-tuple-element.28), channel_id=1, source_target_pairs={{0,32},{32,64},{64,96},{96,0},{1,33},{33,65},{65,97},{97,1},{2,34}... | collective-permute-start | bytes 2359304 | tf_op jit(solution)/shard_map/ppermute | solution.py:19
  212.2 38.8 %collective-permute-start.3 = (bf16[2,192,8,128]{3,2,1,0:T(8,128)(2,1)S(1)}, bf16[2,192,8,128]{3,2,1,0:T(8,128)(2,1)S(1)}, u32[]{:S(2)}, u32[]{:S(2)}) collective-permute-start(bf16[2,192,8,128]{3,2,1,0:T(8,128)(2,1)S(1)} %get-tuple-element.29), channel_id=1, source_target_pairs={{0,96},{32,0},{64,32},{96,64},{1,97},{33,1},{65,33},{97,65},{2,98}... | collective-permute-start | bytes 2359304 | tf_op jit(solution)/shard_map/ppermute | solution.py:19
  215.4 49.3 %collective-permute-start.4 = (bf16[2,192,8,128]{3,2,1,0:T(8,128)(2,1)S(1)}, bf16[2,192,8,128]{3,2,1,0:T(8,128)(2,1)S(1)}, u32[]{:S(2)}, u32[]{:S(2)}) collective-permute-start(bf16[2,192,8,128]{3,2,1,0:T(8,128)(2,1)S(1)} %get-tuple-element.30), channel_id=1, source_target_pairs={{0,64},{32,96},{64,0},{96,32},{1,65},{33,97},{65,1},{97,33},{2,66}... | collective-permute-start | bytes 2359304 | tf_op jit(solution)/shard_map/ppermute | solution.py:19
  217.4 4.3 %copy-start.4 = (bf16[96,8,8,128]{3,2,1,0:T(8,128)(2,1)S(1)}, bf16[96,8,8,128]{3,2,1,0:T(8,128)(2,1)}, u32[]{:S(2)}) copy-start(bf16[96,8,8,128]{3,2,1,0:T(8,128)(2,1)} %copy.125) | copy-start | bytes 4718596
  220.4 1.5 copy-start.3
  272.7 5.4 %collective-permute-start.6 = (bf16[2,192,2,128]{3,2,1,0:T(2,128)(2,1)S(1)}, bf16[2,192,2,128]{3,2,1,0:T(2,128)(2,1)S(1)}, u32[]{:S(2)}, u32[]{:S(2)}) collective-permute-start(bf16[2,192,2,128]{3,2,1,0:T(2,128)(2,1)S(1)} %bitcast.137), channel_id=1, source_target_pairs={{0,96},{32,0},{64,32},{96,64},{1,97},{33,1},{65,33},{97,65},{2,98}... | collective-permute-start | bytes 589832 | tf_op jit(solution)/shard_map/ppermute | solution.py:19
  272.8 9.3 %collective-permute-start.7 = (bf16[2,192,2,128]{3,2,1,0:T(2,128)(2,1)S(1)}, bf16[2,192,2,128]{3,2,1,0:T(2,128)(2,1)S(1)}, u32[]{:S(2)}, u32[]{:S(2)}) collective-permute-start(bf16[2,192,2,128]{3,2,1,0:T(2,128)(2,1)S(1)} %bitcast.136), channel_id=1, source_target_pairs={{0,64},{32,96},{64,0},{96,32},{1,65},{33,97},{65,1},{97,33},{2,66}... | collective-permute-start | bytes 589832 | tf_op jit(solution)/shard_map/ppermute | solution.py:19
  273.1 10.6 %collective-permute-start.8 = (bf16[2,192,2,128]{3,2,1,0:T(2,128)(2,1)S(1)}, bf16[2,192,2,128]{3,2,1,0:T(2,128)(2,1)S(1)}, u32[]{:S(2)}, u32[]{:S(2)}) collective-permute-start(bf16[2,192,2,128]{3,2,1,0:T(2,128)(2,1)S(1)} %bitcast.135), channel_id=1, source_target_pairs={{0,32},{32,64},{64,96},{96,0},{1,33},{33,65},{65,97},{97,1},{2,34}... | collective-permute-start | bytes 589832 | tf_op jit(solution)/shard_map/ppermute | solution.py:19

commit v16 on v12

--- a/solution.py
+++ b/solution.py
@@ -90,21 +90,21 @@
 
 
 def attend(slot_src, query_base, peer_of, table, pieces, key_pos, group, groups):
-    piece_len = pieces.shape[2]
+    piece_len = pieces.shape[1]
     run_len = pieces.shape[0] * piece_len
     block_ids = run_len // BLOCK_TOKENS
     targets = table.shape[0]
     head_width = table.shape[-1]
-    row_width = pieces.shape[-1] // groups
+    row_width = pieces.shape[-1] // 2 // groups
     half = BLOCK_TOKENS // 2
     per_piece = piece_len // half
 
     def half_spec(which, part):
         def index(b, src, base, peer):
             i = 2 * b + part
-            return (peer[i // per_piece], which, i % per_piece, group)
-
-        return pl.BlockSpec((None, None, half, row_width), index)
+            return (peer[i // per_piece], i % per_piece, which * groups + group)
+
+        return pl.BlockSpec((None, half, row_width), index)
 
     table_spec = pl.BlockSpec(table.shape, lambda b, src, base, peer: (0, 0, 0, 0))
 
@@ -146,8 +146,11 @@
     run_len = size * tok
     groups = kv_h.shape[2]
     group_width = head_count // size // groups
-    qg = jnp.stack([queries, grad_out]).reshape(2, tok, size, head_count // size * head_width)
-    qg = jnp.transpose(qg, (2, 0, 1, 3))
+    qg = jnp.concatenate(
+        [x.reshape(tok, size, head_count // size * head_width) for x in (queries, grad_out)],
+        axis=-1,
+    )
+    qg = jnp.transpose(qg, (1, 0, 2))
     pieces = []
     for k in range(size):
         piece = lax.dynamic_index_in_dim(qg, (here + k) % size, axis=0, keepdims=False)

time: 263 us -> 263 us (level)
    another operation x3 -> x0, local copies, waits for them, and re-layouts: 7.45 us -> none  [on_device(): jnp.stack([queries, grad_out])]
    reshape x0 -> x2, local copies, waits for them, and re-layouts: none -> 6.99 us  [on_device(): x.reshape(tok, size, head_count // size * head_width)]
where the time goes in v16:
time: 263 us; the launch traced here: 261 us
  waiting for transfers between devices  94.9 us (36%)
  Pallas kernels  53.3 us (20%)
  starting transfers between devices  48.8 us (19%)
  local copies, waits for them, and re-layouts  37.4 us (14%)
  other arithmetic  18.5 us (7%)
  matrix products  7.34 us (3%)
    pallas_call x2, Pallas kernels, attend(): pl.pallas_call(attention_kernel, grid_spec=grid_spec, out_shape=out_shape...  53.3 us
    ppermute x6, waiting for transfers between devices, exchange(): lax.ppermute(piece, 'head', [(i, (i + k) % size) for i in range(size)])  47.4 us
    ppermute x3, waiting for transfers between devices, on_device(): lax.ppermute(piece, 'head', [(i, (i + k) % size) for i in range(size)])  19.8 us
    all_to_all x2, starting transfers between devices, on_device(): lax.all_to_all(remote, 'blk', split_axis=0, concat_axis=0, tiled=True)  17.1 us
    all_to_all x2, waiting for transfers between devices, on_device(): recv = lax.all_to_all(send, 'blk', split_axis=0, concat_axis=0, tiled=True)  15.6 us
    all_to_all x2, starting transfers between devices, on_device(): recv = lax.all_to_all(send, 'blk', split_axis=0, concat_axis=0, tiled=True)  13.4 us
    all_to_all x1, waiting for transfers between devices, to_heads(): return lax.all_to_all(x, 'head', split_axis=2, concat_axis=1, tiled=True)  12.2 us
    ppermute x6, starting transfers between devices, exchange(): lax.ppermute(piece, 'head', [(i, (i + k) % size) for i in range(size)])  11.4 us
  transfers between devices with their start and end apart: 14, of which 7 were waited for; matrix products, arithmetic and copies ran while one was open for 17% of the time, Pallas kernels for 20%

profile of v16, /device:TPU:0, one launch (start us, length us, event | category | flops | bytes accessed | tf_op | source)
XLA Modules:
  0.0 261.4 jit_solution(5238221911955628655)
XLA Ops:
  2.8 4.4 %all-to-all-start = ((bf16[2,192,8,128]{3,1,0,2:T(8,128)(2,1)}), bf16[2,192,8,128]{3,1,0,2:T(8,128)(2,1)S(1)}, u32[]{:S(2)}, u32[]{:S(2)}) async-start(bf16[2,192,8,128]{3,1,0,2:T(8,128)(2,1)} %pad_maximum_fusion.3), calls=%async_computation | async-start | bytes 1572864 | tf_op jit(solution)/shard_map/all_to_all | solution.py:29
  8.2 12.2 %all-to-all-done = bf16[2,192,8,128]{3,1,0,2:T(8,128)(2,1)S(1)} async-done(((bf16[2,192,8,128]{3,1,0,2:T(8,128)(2,1)}), bf16[2,192,8,128]{3,1,0,2:T(8,128)(2,1)S(1)}, u32[]{:S(2)}, u32[]{:S(2)}) %all-to-all-start) | async-done | bytes 786464 | tf_op jit(solution)/shard_map/all_to_all | solution.py:29
  21.4 2.1 copy.157
  23.5 8.4 %all-to-all-start.1 = ((bf16[32,2,128,128]{3,2,1,0:T(8,128)(2,1)}), bf16[32,2,128,128]{3,2,1,0:T(8,128)(2,1)S(1)}, u32[]{:S(2)}, u32[]{:S(2)}) async-start(bf16[32,2,128,128]{3,2,1,0:T(8,128)(2,1)} %copy.157), calls=%async_computation.1 | async-start | bytes 4194304 | tf_op jit(solution)/shard_map/all_to_all | solution.py:202
  32.0 3.5 %reshape.107 = bf16[192,4,1024]{2,1,0:T(4,128)(2,1)} reshape(bf16[192,32,128]{2,1,0:T(8,128)(2,1)} %param.5) | data formatting | bytes 3145728 | tf_op jit(solution)/shard_map/reshape | solution.py:150
  35.5 3.5 %reshape.108 = bf16[192,4,1024]{2,1,0:T(4,128)(2,1)} reshape(bf16[192,32,128]{2,1,0:T(8,128)(2,1)} %param.9) | data formatting | bytes 3145728 | tf_op jit(solution)/shard_map/reshape | solution.py:150
  39.0 2.0 copy_dynamic-update-slice_fusion.1
  41.5 1.7 dynamic-slice_bitcast_fusion.5
  43.4 2.3 collective-permute-start.1
  46.5 2.2 copy.156
  48.7 15.6 %all-to-all-done.1 = bf16[32,2,128,128]{3,2,1,0:T(8,128)(2,1)S(1)} async-done(((bf16[32,2,128,128]{3,2,1,0:T(8,128)(2,1)}), bf16[32,2,128,128]{3,2,1,0:T(8,128)(2,1)S(1)}, u32[]{:S(2)}, u32[]{:S(2)}) %all-to-all-start.1) | async-done | bytes 2097184 | tf_op jit(solution)/shard_map/all_to_all | solution.py:202
  64.3 5.0 %all-to-all-start.2 = ((bf16[32,2,128,128]{3,2,1,0:T(8,128)(2,1)}), bf16[32,2,128,128]{3,2,1,0:T(8,128)(2,1)}, u32[]{:S(2)}, u32[]{:S(2)}) async-start(bf16[32,2,128,128]{3,2,1,0:T(8,128)(2,1)} %copy.156), calls=%async_computation.2 | async-start | bytes 4194304 | tf_op jit(solution)/shard_map/all_to_all | solution.py:202
  72.5 18.2 %collective-permute-done.1 = bf16[192,2048]{1,0:T(8,128)(2,1)} collective-permute-done((bf16[192,2048]{1,0:T(8,128)(2,1)}, bf16[192,2048]{1,0:T(8,128)(2,1)}, u32[]{:S(2)}, u32[]{:S(2)}) %collective-permute-start.1) | collective-permute-done | bytes 786464 | tf_op jit(solution)/shard_map/ppermute | solution.py:158
  90.7 3.2 %pad_maximum_fusion.refs_1_.refs_2_.refs_3_.refs_4_ = bf16[4,192,2048]{2,1,0:T(8,128)(2,1)} fusion(bf16[1,192,2048]{2,1,0:T(8,128)(2,1)} %bitcast.17, bf16[1,192,2048]{2,1,0:T(8,128)(2,1)} %bitcast.15, bf16[1,192,2048]{2,1,0:T(8,128)(2,1)} %bitcast.13, bf16[1,192,2048]{2,1,0:T(8,128)(2,1)} %get-tuple-element.35), kind=kLoop, calls=%fused_computation.12 | loop fusion | flops 4718592 | bytes 6291456 | tf_op jit(solution)/shard_map/stack | solution.py:160
  94.0 1.7 pad_maximum_fusion.1.refs_0_
  95.7 26.6 %shard_map.84 = (bf16[768,512]{1,0:T(8,128)(2,1)S(1)}, bf16[768,512]{1,0:T(8,128)(2,1)S(1)}, f32[38,128,128]{2,1,0:T(8,128)S(1)}, f32[38,128,128]{2,1,0:T(8,128)}) custom-call(s32[48]{0:T(128)S(1)} %reshape_squeeze.6.src_ref, s32[6]{0:T(128)S(1)} %add_multiply_fusion.base_ref, s32[4]{0:T(128)S(1)} %and_select_fusion.peer_ref, ...), custom_call_target="tpu_custom_call" | custom-call | tf_op jit(solution)/shard_map/pallas_call | solution.py:130
  122.3 2.4 maximum_convert_fusion.1
  126.5 8.7 %all-to-all-start.3 = ((bf16[32,2,128,128]{3,2,1,0:T(8,128)(2,1)}), bf16[32,2,128,128]{3,2,1,0:T(8,128)(2,1)}, u32[]{:S(2)}, u32[]{:S(2)}) async-start(bf16[32,2,128,128]{3,2,1,0:T(8,128)(2,1)} %copy.113), calls=%async_computation.3 | async-start | bytes 4194304 | tf_op jit(solution)/shard_map/all_to_all | solution.py:216
  135.4 3.4 %pad_maximum_fusion.2.refs_0_ = bf16[38,2,128,128]{3,2,1,0:T(8,128)(2,1)} fusion(bf16[6,2,128,128]{3,2,1,0:T(8,128)(2,1)} %copy-done.9, bf16[32,2,128,128]{3,2,1,0:T(8,128)(2,1)} %all-to-all-done.2), kind=kLoop, calls=%fused_computation.14 | loop fusion | flops 1245184 | bytes 4980736 | tf_op jit(solution)/shard_map/concatenate | solution.py:203
  138.8 26.7 %shard_map.85 = (bf16[768,512]{1,0:T(8,128)(2,1)S(1)}, bf16[768,512]{1,0:T(8,128)(2,1)S(1)}, f32[38,128,128]{2,1,0:T(8,128)S(1)}, f32[38,128,128]{2,1,0:T(8,128)}) custom-call(s32[48]{0:T(128)S(1)} %reshape_squeeze.7.src_ref, s32[6]{0:T(128)S(1)} %add_multiply_fusion.base_ref, s32[4]{0:T(128)S(1)} %and_select_fusion.peer_ref, ...), custom_call_target="tpu_custom_call" | custom-call | tf_op jit(solution)/shard_map/pallas_call | solution.py:130
  171.3 3.2 %copy.116 = bf16[32,2,128,128]{3,2,1,0:T(8,128)(2,1)} copy(bf16[32,2,128,128]{3,2,0,1:T(8,128)(2,1)} %slice.108) | data formatting | bytes 4194304 | tf_op jit(solution)/shard_map/optimization_barrier | solution.py:213
  174.5 8.3 %all-to-all-start.4 = ((bf16[32,2,128,128]{3,2,1,0:T(8,128)(2,1)}), bf16[32,2,128,128]{3,2,1,0:T(8,128)(2,1)}, u32[]{:S(2)}, u32[]{:S(2)}) async-start(bf16[32,2,128,128]{3,2,1,0:T(8,128)(2,1)} %copy.116), calls=%async_computation.4 | async-start | bytes 4194304 | tf_op jit(solution)/shard_map/all_to_all | solution.py:216
  182.8 1.8 fusion.5
  184.7 3.2 %collective-permute-start.3 = (bf16[2,192,8,128]{3,2,1,0:T(8,128)(2,1)S(1)}, bf16[2,192,8,128]{3,2,1,0:T(8,128)(2,1)S(1)}, u32[]{:S(2)}, u32[]{:S(2)}) collective-permute-start(bf16[2,192,8,128]{3,2,1,0:T(8,128)(2,1)S(1)} %get-tuple-element.33), channel_id=1, source_target_pairs={{0,96},{32,0},{64,32},{96,64},{1,97},{33,1},{65,33},{97,65},{2,98}... | collective-permute-start | bytes 2359304 | tf_op jit(solution)/shard_map/ppermute | solution.py:19
  188.0 4.6 %collective-permute-start.4 = (bf16[2,192,8,128]{3,2,1,0:T(8,128)(2,1)S(1)}, bf16[2,192,8,128]{3,2,1,0:T(8,128)(2,1)S(1)}, u32[]{:S(2)}, u32[]{:S(2)}) collective-permute-start(bf16[2,192,8,128]{3,2,1,0:T(8,128)(2,1)S(1)} %get-tuple-element.34), channel_id=1, source_target_pairs={{0,64},{32,96},{64,0},{96,32},{1,65},{33,97},{65,1},{97,33},{2,66}... | collective-permute-start | bytes 2359304 | tf_op jit(solution)/shard_map/ppermute | solution.py:19
  192.6 2.8 %fusion.2 = f32[6,2,128,128]{3,0,2,1:T(8,128)S(1)} fusion(bf16[32,2,128,128]{3,2,1,0:T(8,128)(2,1)} %all-to-all-done.3, bf16[2,32,6]{1,2,0:T(8,128)(2,1)S(1)} %broadcast_select_fusion), kind=kOutput, calls=%fused_computation.17 | convolution fusion | flops 12582912 | bytes 2885632 | tf_op jit(solution)/shard_map/rl,rktd->lktd/dot_general | solution.py:224
  197.5 25.7 %collective-permute-done.3 = bf16[2,192,8,128]{3,2,1,0:T(8,128)(2,1)S(1)} collective-permute-done((bf16[2,192,8,128]{3,2,1,0:T(8,128)(2,1)S(1)}, bf16[2,192,8,128]{3,2,1,0:T(8,128)(2,1)S(1)}, u32[]{:S(2)}, u32[]{:S(2)}) %collective-permute-start.3) | collective-permute-done | bytes 786464 | tf_op jit(solution)/shard_map/ppermute | solution.py:19
  223.5 12.5 %collective-permute-done.4 = bf16[2,192,8,128]{3,2,1,0:T(8,128)(2,1)S(1)} collective-permute-done((bf16[2,192,8,128]{3,2,1,0:T(8,128)(2,1)S(1)}, bf16[2,192,8,128]{3,2,1,0:T(8,128)(2,1)S(1)}, u32[]{:S(2)}, u32[]{:S(2)}) %collective-permute-start.4) | collective-permute-done | bytes 786464 | tf_op jit(solution)/shard_map/ppermute | solution.py:19
  237.7 2.4 dynamic-slice_bitcast_fusion
  240.2 3.0 %fusion = f32[6,2,128,128]{3,0,2,1:T(8,128)S(1)} fusion(bf16[32,2,128,128]{3,2,1,0:T(8,128)(2,1)} %all-to-all-done.4, bf16[2,32,6]{1,2,0:T(8,128)(2,1)S(1)} %broadcast_select_fusion), kind=kOutput, calls=%fused_computation.15 | convolution fusion | flops 12582912 | bytes 2885632 | tf_op jit(solution)/shard_map/rl,rktd->lktd/dot_general | solution.py:224
  245.2 3.3 %collective-permute-start.7 = (bf16[2,192,2,128]{3,2,1,0:T(2,128)(2,1)S(1)}, bf16[2,192,2,128]{3,2,1,0:T(2,128)(2,1)S(1)}, u32[]{:S(2)}, u32[]{:S(2)}) collective-permute-start(bf16[2,192,2,128]{3,2,1,0:T(2,128)(2,1)S(1)} %bitcast.148), channel_id=1, source_target_pairs={{0,64},{32,96},{64,0},{96,32},{1,65},{33,97},{65,1},{97,33},{2,66}... | collective-permute-start | bytes 589832 | tf_op jit(solution)/shard_map/ppermute | solution.py:19
  249.2 9.1 %collective-permute-done.7 = bf16[2,192,2,128]{3,2,1,0:T(2,128)(2,1)S(1)} collective-permute-done((bf16[2,192,2,128]{3,2,1,0:T(2,128)(2,1)S(1)}, bf16[2,192,2,128]{3,2,1,0:T(2,128)(2,1)S(1)}, u32[]{:S(2)}, u32[]{:S(2)}) %collective-permute-start.7) | collective-permute-done | bytes 196640 | tf_op jit(solution)/shard_map/ppermute | solution.py:19
  (97 shorter events, 26.4 us)
Async XLA Ops:
  2.8 17.5 %all-to-all-start = ((bf16[2,192,8,128]{3,1,0,2:T(8,128)(2,1)}), bf16[2,192,8,128]{3,1,0,2:T(8,128)(2,1)S(1)}, u32[]{:S(2)}, u32[]{:S(2)}) async-start(bf16[2,192,8,128]{3,1,0,2:T(8,128)(2,1)} %pad_maximum_fusion.3), calls=%async_computation | async-start | bytes 1572864 | tf_op jit(solution)/shard_map/all_to_all | solution.py:29
  20.6 25.2 %copy-start.9 = (bf16[6,2,128,128]{3,2,1,0:T(8,128)(2,1)}, bf16[6,2,128,128]{3,2,1,0:T(8,128)(2,1)S(1)}, u32[]{:S(2)}) copy-start(bf16[6,2,128,128]{3,2,1,0:T(8,128)(2,1)S(1)} %get-tuple-element.46) | copy-start | bytes 1179652
  23.5 40.8 %all-to-all-start.1 = ((bf16[32,2,128,128]{3,2,1,0:T(8,128)(2,1)}), bf16[32,2,128,128]{3,2,1,0:T(8,128)(2,1)S(1)}, u32[]{:S(2)}, u32[]{:S(2)}) async-start(bf16[32,2,128,128]{3,2,1,0:T(8,128)(2,1)} %copy.157), calls=%async_computation.1 | async-start | bytes 4194304 | tf_op jit(solution)/shard_map/all_to_all | solution.py:202
  39.0 2.0 copy-start.8
  43.2 29.2 %collective-permute-start.2 = (bf16[192,2048]{1,0:T(8,128)(2,1)}, bf16[192,2048]{1,0:T(8,128)(2,1)}, u32[]{:S(2)}, u32[]{:S(2)}) collective-permute-start(bf16[192,2048]{1,0:T(8,128)(2,1)} %get-tuple-element.36), channel_id=1, source_target_pairs={{0,96},{32,0},{64,32},{96,64},{1,97},{33,1},{65,33},{97,65},{2,98}... | collective-permute-start | bytes 2359304 | tf_op jit(solution)/shard_map/ppermute | solution.py:158
  43.4 47.3 %collective-permute-start.1 = (bf16[192,2048]{1,0:T(8,128)(2,1)}, bf16[192,2048]{1,0:T(8,128)(2,1)}, u32[]{:S(2)}, u32[]{:S(2)}) collective-permute-start(bf16[192,2048]{1,0:T(8,128)(2,1)} %get-tuple-element.37), channel_id=1, source_target_pairs={{0,64},{32,96},{64,0},{96,32},{1,65},{33,97},{65,1},{97,33},{2,66}... | collective-permute-start | bytes 2359304 | tf_op jit(solution)/shard_map/ppermute | solution.py:158
  45.7 45.0 %collective-permute-start = (bf16[192,2048]{1,0:T(8,128)(2,1)}, bf16[192,2048]{1,0:T(8,128)(2,1)}, u32[]{:S(2)}, u32[]{:S(2)}) collective-permute-start(bf16[192,2048]{1,0:T(8,128)(2,1)} %get-tuple-element.38), channel_id=1, source_target_pairs={{0,32},{32,64},{64,96},{96,0},{1,33},{33,65},{65,97},{97,1},{2,34}... | collective-permute-start | bytes 2359304 | tf_op jit(solution)/shard_map/ppermute | solution.py:158
  64.3 62.2 %all-to-all-start.2 = ((bf16[32,2,128,128]{3,2,1,0:T(8,128)(2,1)}), bf16[32,2,128,128]{3,2,1,0:T(8,128)(2,1)}, u32[]{:S(2)}, u32[]{:S(2)}) async-start(bf16[32,2,128,128]{3,2,1,0:T(8,128)(2,1)} %copy.156), calls=%async_computation.2 | async-start | bytes 4194304 | tf_op jit(solution)/shard_map/all_to_all | solution.py:202
  122.3 2.4 copy-start.2
  126.5 44.8 %all-to-all-start.3 = ((bf16[32,2,128,128]{3,2,1,0:T(8,128)(2,1)}), bf16[32,2,128,128]{3,2,1,0:T(8,128)(2,1)}, u32[]{:S(2)}, u32[]{:S(2)}) async-start(bf16[32,2,128,128]{3,2,1,0:T(8,128)(2,1)} %copy.113), calls=%async_computation.3 | async-start | bytes 4194304 | tf_op jit(solution)/shard_map/all_to_all | solution.py:216
  138.8 26.7 %copy-start.3 = (bf16[768,512]{1,0:T(8,128)(2,1)S(1)}, bf16[768,512]{1,0:T(8,128)(2,1)}, u32[]{:S(2)}) copy-start(bf16[768,512]{1,0:T(8,128)(2,1)} %copy-done.2) | copy-start | bytes 2359300
  165.5 3.8 %copy-start = (f32[38,128,128]{2,1,0:T(8,128)}, f32[38,128,128]{2,1,0:T(8,128)S(1)}, u32[]{:S(2)}) copy-start(f32[38,128,128]{2,1,0:T(8,128)S(1)} %get-tuple-element.20) | copy-start | bytes 7471108
  167.4 1.8 copy-start.7
  174.5 65.7 %all-to-all-start.4 = ((bf16[32,2,128,128]{3,2,1,0:T(8,128)(2,1)}), bf16[32,2,128,128]{3,2,1,0:T(8,128)(2,1)}, u32[]{:S(2)}, u32[]{:S(2)}) async-start(bf16[32,2,128,128]{3,2,1,0:T(8,128)(2,1)} %copy.116), calls=%async_computation.4 | async-start | bytes 4194304 | tf_op jit(solution)/shard_map/all_to_all | solution.py:216
  184.6 10.7 %copy-start.6 = (f32[38,128,128]{2,1,0:T(8,128)S(1)}, f32[38,128,128]{2,1,0:T(8,128)}, u32[]{:S(2)}) copy-start(f32[38,128,128]{2,1,0:T(8,128)} %get-tuple-element.23) | copy-start | bytes 7471108
  184.6 51.7 %collective-permute-start.5 = (bf16[2,192,8,128]{3,2,1,0:T(8,128)(2,1)S(1)}, bf16[2,192,8,128]{3,2,1,0:T(8,128)(2,1)S(1)}, u32[]{:S(2)}, u32[]{:S(2)}) collective-permute-start(bf16[2,192,8,128]{3,2,1,0:T(8,128)(2,1)S(1)} %get-tuple-element.32), channel_id=1, source_target_pairs={{0,32},{32,64},{64,96},{96,0},{1,33},{33,65},{65,97},{97,1},{2,34}... | collective-permute-start | bytes 2359304 | tf_op jit(solution)/shard_map/ppermute | solution.py:19
  184.7 38.5 %collective-permute-start.3 = (bf16[2,192,8,128]{3,2,1,0:T(8,128)(2,1)S(1)}, bf16[2,192,8,128]{3,2,1,0:T(8,128)(2,1)S(1)}, u32[]{:S(2)}, u32[]{:S(2)}) collective-permute-start(bf16[2,192,8,128]{3,2,1,0:T(8,128)(2,1)S(1)} %get-tuple-element.33), channel_id=1, source_target_pairs={{0,96},{32,0},{64,32},{96,64},{1,97},{33,1},{65,33},{97,65},{2,98}... | collective-permute-start | bytes 2359304 | tf_op jit(solution)/shard_map/ppermute | solution.py:19
  188.0 48.1 %collective-permute-start.4 = (bf16[2,192,8,128]{3,2,1,0:T(8,128)(2,1)S(1)}, bf16[2,192,8,128]{3,2,1,0:T(8,128)(2,1)S(1)}, u32[]{:S(2)}, u32[]{:S(2)}) collective-permute-start(bf16[2,192,8,128]{3,2,1,0:T(8,128)(2,1)S(1)} %get-tuple-element.34), channel_id=1, source_target_pairs={{0,64},{32,96},{64,0},{96,32},{1,65},{33,97},{65,1},{97,33},{2,66}... | collective-permute-start | bytes 2359304 | tf_op jit(solution)/shard_map/ppermute | solution.py:19
  195.4 1.4 copy-start.4
  195.4 1.9 copy-start.5
  240.2 3.0 %copy-start.1 = (f32[38,128,128]{2,1,0:T(8,128)S(1)}, f32[38,128,128]{2,1,0:T(8,128)}, u32[]{:S(2)}) copy-start(f32[38,128,128]{2,1,0:T(8,128)} %copy-done) | copy-start | bytes 7471108
  245.2 3.7 %collective-permute-start.6 = (bf16[2,192,2,128]{3,2,1,0:T(2,128)(2,1)S(1)}, bf16[2,192,2,128]{3,2,1,0:T(2,128)(2,1)S(1)}, u32[]{:S(2)}, u32[]{:S(2)}) collective-permute-start(bf16[2,192,2,128]{3,2,1,0:T(2,128)(2,1)S(1)} %bitcast.149), channel_id=1, source_target_pairs={{0,96},{32,0},{64,32},{96,64},{1,97},{33,1},{65,33},{97,65},{2,98}... | collective-permute-start | bytes 589832 | tf_op jit(solution)/shard_map/ppermute | solution.py:19
  245.2 13.0 %collective-permute-start.7 = (bf16[2,192,2,128]{3,2,1,0:T(2,128)(2,1)S(1)}, bf16[2,192,2,128]{3,2,1,0:T(2,128)(2,1)S(1)}, u32[]{:S(2)}, u32[]{:S(2)}) collective-permute-start(bf16[2,192,2,128]{3,2,1,0:T(2,128)(2,1)S(1)} %bitcast.148), channel_id=1, source_target_pairs={{0,64},{32,96},{64,0},{96,32},{1,65},{33,97},{65,1},{97,33},{2,66}... | collective-permute-start | bytes 589832 | tf_op jit(solution)/shard_map/ppermute | solution.py:19
  248.5 10.0 %collective-permute-start.8 = (bf16[2,192,2,128]{3,2,1,0:T(2,128)(2,1)S(1)}, bf16[2,192,2,128]{3,2,1,0:T(2,128)(2,1)S(1)}, u32[]{:S(2)}, u32[]{:S(2)}) collective-permute-start(bf16[2,192,2,128]{3,2,1,0:T(2,128)(2,1)S(1)} %bitcast.147), channel_id=1, source_target_pairs={{0,32},{32,64},{64,96},{96,0},{1,33},{33,65},{65,97},{97,1},{2,34}... | collective-permute-start | bytes 589832 | tf_op jit(solution)/shard_map/ppermute | solution.py:19

commit v17 on v16

--- a/solution.py
+++ b/solution.py
@@ -39,8 +39,8 @@
 
 
 def attention_kernel(src_ref, base_ref, peer_ref, *refs):
-    table_ref, q_lo, q_hi, do_lo, do_hi, kpos_ref = refs[:6]
-    o_ref, dq_ref, dk_ref, dv_ref = refs[6:]
+    table_ref, lo_ref, hi_ref, kpos_ref = refs[:4]
+    o_ref, dq_ref, dk_ref, dv_ref = refs[4:]
     b = pl.program_id(0)
 
     @pl.when(b == 0)
@@ -49,7 +49,8 @@
         dv_ref[...] = jnp.zeros_like(dv_ref)
 
     head_width = table_ref.shape[-1]
-    group_width = q_lo.shape[-1] // head_width
+    width = lo_ref.shape[-1] // 2
+    group_width = width // head_width
     scale = head_width ** (-0.5)
     slots = [src_ref[b * TOPK + s] for s in range(TOPK)]
     keys = jnp.concatenate([table_ref[t, 0] for t in slots], axis=0)
@@ -62,8 +63,9 @@
     dv = None
     for j in range(group_width):
         cols = slice(j * head_width, (j + 1) * head_width)
-        qj = jnp.concatenate([q_lo[:, cols], q_hi[:, cols]], axis=0)
-        gj = jnp.concatenate([do_lo[:, cols], do_hi[:, cols]], axis=0)
+        dcols = slice(width + j * head_width, width + (j + 1) * head_width)
+        qj = jnp.concatenate([lo_ref[:, cols], hi_ref[:, cols]], axis=0)
+        gj = jnp.concatenate([lo_ref[:, dcols], hi_ref[:, dcols]], axis=0)
         s = lax.dot_general(qj, keys, nt, preferred_element_type=jnp.float32) * scale
         s = jnp.where(allowed, s, -jnp.inf)
         m = jnp.max(s, axis=-1, keepdims=True)
@@ -96,15 +98,16 @@
     targets = table.shape[0]
     head_width = table.shape[-1]
     row_width = pieces.shape[-1] // 2 // groups
+    block_width = 2 * row_width
     half = BLOCK_TOKENS // 2
     per_piece = piece_len // half
 
-    def half_spec(which, part):
+    def half_spec(part):
         def index(b, src, base, peer):
             i = 2 * b + part
-            return (peer[i // per_piece], i % per_piece, which * groups + group)
-
-        return pl.BlockSpec((None, half, row_width), index)
+            return (peer[i // per_piece], i % per_piece, group)
+
+        return pl.BlockSpec((None, half, block_width), index)
 
     table_spec = pl.BlockSpec(table.shape, lambda b, src, base, peer: (0, 0, 0, 0))
 
@@ -113,7 +116,7 @@
     acc_spec = pl.BlockSpec((targets, BLOCK_TOKENS, head_width), lambda b, src, base, peer: (0, 0, 0))
     in_specs = (
         [table_spec]
-        + [half_spec(0, 0), half_spec(0, 1), half_spec(1, 0), half_spec(1, 1), pos_spec]
+        + [half_spec(0), half_spec(1), pos_spec]
     )
     out_shape = (
         jax.ShapeDtypeStruct((run_len, row_width), jnp.bfloat16),
@@ -135,7 +138,7 @@
             dimension_semantics=("arbitrary",),
             vmem_limit_bytes=48 * 1024 * 1024,
         ),
-    )(slot_src, query_base, peer_of, table, *([pieces] * 4), key_pos)
+    )(slot_src, query_base, peer_of, table, pieces, pieces, key_pos)
 
 
 def on_device(queries, rotated_keys, value_vectors, block_list, grad_out):
@@ -146,10 +149,10 @@
     run_len = size * tok
     groups = kv_h.shape[2]
     group_width = head_count // size // groups
-    qg = jnp.concatenate(
-        [x.reshape(tok, size, head_count // size * head_width) for x in (queries, grad_out)],
-        axis=-1,
-    )
+    qg = jnp.stack(
+        [x.reshape(tok, size, groups, group_width * head_width) for x in (queries, grad_out)],
+        axis=3,
+    ).reshape(tok, size, 2 * head_count // size * head_width)
     qg = jnp.transpose(qg, (1, 0, 2))
     pieces = []
     for k in range(size):

time: 263 us -> 269 us (1.023); the launches traced: 261 us -> 265 us
  local copies, waits for them, and re-layouts: 37.4 us -> 43.1 us
  other arithmetic: 18.5 us -> 24.2 us
  waiting for transfers between devices: 94.9 us -> 90 us
  starting transfers between devices: 48.8 us -> 45.8 us
    all_to_all x2, waiting for transfers between devices: 15.6 us -> 5.61 us  [on_device(): recv = lax.all_to_all(send, 'blk', split_axis=0, concat_axis=0, tiled=True)]
    another operation x0 -> x3, local copies, waits for them, and re-layouts: none -> 9.65 us  [on_device(): jnp.stack([x.reshape(tok, size, groups, group_width * head_width) for x i...]
    another operation x2 -> x3, other arithmetic: 2.86 us -> 7.3 us  [the longest x1 4.45 us: on_device(): jnp.stack([x.reshape(tok, size, groups, group_width * head_width) for x i...]
    ppermute x6, waiting for transfers between devices: 47.4 us -> 51.6 us  [exchange(): lax.ppermute(piece, 'head', [(i, (i + k) % size) for i in range(size)])]
    ppermute x6, starting transfers between devices: 11.4 us -> 7.96 us  [exchange(): lax.ppermute(piece, 'head', [(i, (i + k) % size) for i in range(size)])]
    reshape x2 -> x1, local copies, waits for them, and re-layouts: 6.99 us -> 4.75 us  [on_device(): qg = jnp.stack([x.reshape(tok, size, groups, group_width * head_width) fo...]
    unnamed x35 -> x40, local copies, waits for them, and re-layouts: 10.3 us -> 9 us
  transfers between devices with their start and end apart: 14 -> 14, of which waited for: 7 -> 10; matrix products, arithmetic and copies ran while one was open for 17% -> 21% of each run, Pallas kernels for 20% -> 20%
where the time goes in v17:
time: 269 us; the launch traced here: 265 us
  waiting for transfers between devices  90 us (33%)
  Pallas kernels  52.8 us (20%)
  starting transfers between devices  45.8 us (17%)
  local copies, waits for them, and re-layouts  43.1 us (16%)
  other arithmetic  24.2 us (9%)
  matrix products  7.35 us (3%)
    pallas_call x2, Pallas kernels, attend(): pl.pallas_call(attention_kernel, grid_spec=grid_spec, out_shape=out_shape...  52.8 us
    ppermute x6, waiting for transfers between devices, exchange(): lax.ppermute(piece, 'head', [(i, (i + k) % size) for i in range(size)])  51.6 us
    ppermute x3, waiting for transfers between devices, on_device(): lax.ppermute(piece, 'head', [(i, (i + k) % size) for i in range(size)])  20.6 us
    all_to_all x2, starting transfers between devices, on_device(): lax.all_to_all(remote, 'blk', split_axis=0, concat_axis=0, tiled=True)  16.9 us
    all_to_all x2, starting transfers between devices, on_device(): recv = lax.all_to_all(send, 'blk', split_axis=0, concat_axis=0, tiled=True)  13.6 us
    all_to_all x1, waiting for transfers between devices, to_heads(): return lax.all_to_all(x, 'head', split_axis=2, concat_axis=1, tiled=True)  12.2 us
    another operation x3, local copies, waits for them, and re-layouts, on_device(): jnp.stack([x.reshape(tok, size, groups, group_width * head_width) for x i...  9.65 us
    unnamed x40, local copies, waits for them, and re-layouts  9 us
  transfers between devices with their start and end apart: 14, of which 10 were waited for; matrix products, arithmetic and copies ran while one was open for 21% of the time, Pallas kernels for 20%

profile of v17, /device:TPU:0, one launch (start us, length us, event | category | flops | bytes accessed | tf_op | source)
XLA Modules:
  0.0 264.7 jit_solution(790268106278339545)
XLA Ops:
  2.8 4.4 %all-to-all-start = ((bf16[2,192,8,128]{3,1,0,2:T(8,128)(2,1)}), bf16[2,192,8,128]{3,1,0,2:T(8,128)(2,1)S(1)}, u32[]{:S(2)}, u32[]{:S(2)}) async-start(bf16[2,192,8,128]{3,1,0,2:T(8,128)(2,1)} %pad_maximum_fusion.4), calls=%async_computation | async-start | bytes 1572864 | tf_op jit(solution)/shard_map/all_to_all | solution.py:29
  8.2 12.2 %all-to-all-done = bf16[2,192,8,128]{3,1,0,2:T(8,128)(2,1)S(1)} async-done(((bf16[2,192,8,128]{3,1,0,2:T(8,128)(2,1)}), bf16[2,192,8,128]{3,1,0,2:T(8,128)(2,1)S(1)}, u32[]{:S(2)}, u32[]{:S(2)}) %all-to-all-start) | async-done | bytes 786464 | tf_op jit(solution)/shard_map/all_to_all | solution.py:29
  22.1 2.1 copy.150
  24.3 8.9 %all-to-all-start.1 = ((bf16[32,2,128,128]{3,2,1,0:T(8,128)(2,1)}), bf16[32,2,128,128]{3,2,1,0:T(8,128)(2,1)}, u32[]{:S(2)}, u32[]{:S(2)}) async-start(bf16[32,2,128,128]{3,2,1,0:T(8,128)(2,1)} %copy.150), calls=%async_computation.1 | async-start | bytes 4194304 | tf_op jit(solution)/shard_map/all_to_all | solution.py:205
  33.9 2.5 stack_reshape.9
  36.4 4.4 %pad_maximum_fusion = bf16[192,4,2,2,512]{4,2,1,0,3:T(2,128)(2,1)S(1)} fusion(bf16[192,4,2,1,512]{4,2,1,0,3:T(2,128)(2,1)S(1)} %stack_reshape.9, bf16[192,4,2,1,512]{4,2,1,0,3:T(2,128)(2,1)S(1)} %stack_reshape.8), kind=kLoop, calls=%fused_computation.12 | loop fusion | flops 1572864 | bytes 6291456 | tf_op jit(solution)/shard_map/stack | solution.py:152
  40.8 6.5 %copy.101 = bf16[192,4,2,2,512]{4,3,2,0,1:T(2,128)(2,1)} copy(bf16[192,4,2,2,512]{4,2,1,0,3:T(2,128)(2,1)S(1)} %pad_maximum_fusion) | data formatting | bytes 6291456 | tf_op jit(solution)/shard_map/stack | solution.py:152
  47.3 4.7 %reshape.104 = bf16[192,4,2048]{2,0,1:T(8,128)(2,1)S(1)} reshape(bf16[192,4,2,2,512]{4,3,2,0,1:T(2,128)(2,1)} %copy.101) | data formatting | bytes 6291456 | tf_op jit(solution)/shard_map/reshape | solution.py:155
  54.0 2.3 collective-permute-start.1
  57.6 2.2 copy.149
  59.8 5.6 %all-to-all-done.1 = bf16[32,2,128,128]{3,2,1,0:T(8,128)(2,1)} async-done(((bf16[32,2,128,128]{3,2,1,0:T(8,128)(2,1)}), bf16[32,2,128,128]{3,2,1,0:T(8,128)(2,1)}, u32[]{:S(2)}, u32[]{:S(2)}) %all-to-all-start.1) | async-done | bytes 2097184 | tf_op jit(solution)/shard_map/all_to_all | solution.py:205
  65.4 4.8 %all-to-all-start.2 = ((bf16[32,2,128,128]{3,2,1,0:T(8,128)(2,1)}), bf16[32,2,128,128]{3,2,1,0:T(8,128)(2,1)}, u32[]{:S(2)}, u32[]{:S(2)}) async-start(bf16[32,2,128,128]{3,2,1,0:T(8,128)(2,1)} %copy.149), calls=%async_computation.2 | async-start | bytes 4194304 | tf_op jit(solution)/shard_map/all_to_all | solution.py:205
  72.0 19.3 %collective-permute-done.1 = bf16[192,2048]{1,0:T(8,128)(2,1)S(1)} collective-permute-done((bf16[192,2048]{1,0:T(8,128)(2,1)}, bf16[192,2048]{1,0:T(8,128)(2,1)S(1)}, u32[]{:S(2)}, u32[]{:S(2)}) %collective-permute-start.1) | collective-permute-done | bytes 786464 | tf_op jit(solution)/shard_map/ppermute | solution.py:161
  92.4 2.9 %pad_maximum_fusion.1.refs_1_.refs_2_ = bf16[4,192,2048]{2,1,0:T(8,128)(2,1)} fusion(bf16[1,192,2048]{2,1,0:T(8,128)(2,1)S(1)} %bitcast.143, bf16[1,192,2048]{2,1,0:T(8,128)(2,1)S(1)} %bitcast.144, bf16[1,192,2048]{2,1,0:T(8,128)(2,1)} %bitcast.13, bf16[1,192,2048]{2,1,0:T(8,128)(2,1)S(1)} %copy-done.11), kind=kLoop, calls=%fused_computation.13 | loop fusion | flops 4718592 | bytes 6291456 | tf_op jit(solution)/shard_map/stack | solution.py:163
  95.3 3.3 %pad_maximum_fusion.2.refs_0_ = bf16[38,2,128,128]{3,2,1,0:T(8,128)(2,1)} fusion(bf16[6,2,128,128]{3,2,1,0:T(8,128)(2,1)S(1)} %copy-done.10, bf16[32,2,128,128]{3,2,1,0:T(8,128)(2,1)} %all-to-all-done.1), kind=kLoop, calls=%fused_computation.14 | loop fusion | flops 1245184 | bytes 4980736 | tf_op jit(solution)/shard_map/concatenate | solution.py:206
  98.7 26.4 %shard_map.84 = (bf16[768,512]{1,0:T(8,128)(2,1)S(1)}, bf16[768,512]{1,0:T(8,128)(2,1)S(1)}, f32[38,128,128]{2,1,0:T(8,128)S(1)}, f32[38,128,128]{2,1,0:T(8,128)}) custom-call(s32[48]{0:T(128)S(1)} %reshape_squeeze.6.src_ref, s32[6]{0:T(128)S(1)} %add_multiply_fusion.base_ref, s32[4]{0:T(128)S(1)} %and_select_fusion.peer_ref, ...), custom_call_target="tpu_custom_call" | custom-call | tf_op jit(solution)/shard_map/pallas_call | solution.py:133
  125.0 2.4 maximum_convert_fusion.1
  129.2 8.6 %all-to-all-start.3 = ((bf16[32,2,128,128]{3,2,1,0:T(8,128)(2,1)}), bf16[32,2,128,128]{3,2,1,0:T(8,128)(2,1)}, u32[]{:S(2)}, u32[]{:S(2)}) async-start(bf16[32,2,128,128]{3,2,1,0:T(8,128)(2,1)} %copy.108), calls=%async_computation.3 | async-start | bytes 4194304 | tf_op jit(solution)/shard_map/all_to_all | solution.py:219
  138.0 3.4 %pad_maximum_fusion.3.refs_0_ = bf16[38,2,128,128]{3,2,1,0:T(8,128)(2,1)} fusion(bf16[6,2,128,128]{3,2,1,0:T(8,128)(2,1)} %copy-done.8, bf16[32,2,128,128]{3,2,1,0:T(8,128)(2,1)} %all-to-all-done.2), kind=kLoop, calls=%fused_computation.15 | loop fusion | flops 1245184 | bytes 4980736 | tf_op jit(solution)/shard_map/concatenate | solution.py:206
  141.4 26.4 %shard_map.85 = (bf16[768,512]{1,0:T(8,128)(2,1)S(1)}, bf16[768,512]{1,0:T(8,128)(2,1)S(1)}, f32[38,128,128]{2,1,0:T(8,128)S(1)}, f32[38,128,128]{2,1,0:T(8,128)}) custom-call(s32[48]{0:T(128)S(1)} %reshape_squeeze.7.src_ref, s32[6]{0:T(128)S(1)} %add_multiply_fusion.base_ref, s32[4]{0:T(128)S(1)} %and_select_fusion.peer_ref, ...), custom_call_target="tpu_custom_call" | custom-call | tf_op jit(solution)/shard_map/pallas_call | solution.py:133
  173.6 3.2 %copy.111 = bf16[32,2,128,128]{3,2,1,0:T(8,128)(2,1)} copy(bf16[32,2,128,128]{3,2,0,1:T(8,128)(2,1)} %slice.108) | data formatting | bytes 4194304 | tf_op jit(solution)/shard_map/optimization_barrier | solution.py:216
  176.8 8.3 %all-to-all-start.4 = ((bf16[32,2,128,128]{3,2,1,0:T(8,128)(2,1)}), bf16[32,2,128,128]{3,2,1,0:T(8,128)(2,1)}, u32[]{:S(2)}, u32[]{:S(2)}) async-start(bf16[32,2,128,128]{3,2,1,0:T(8,128)(2,1)} %copy.111), calls=%async_computation.4 | async-start | bytes 4194304 | tf_op jit(solution)/shard_map/all_to_all | solution.py:219
  185.1 1.8 fusion.5
  187.0 3.2 %collective-permute-start.3 = (bf16[2,192,8,128]{3,2,1,0:T(8,128)(2,1)S(1)}, bf16[2,192,8,128]{3,2,1,0:T(8,128)(2,1)S(1)}, u32[]{:S(2)}, u32[]{:S(2)}) collective-permute-start(bf16[2,192,8,128]{3,2,1,0:T(8,128)(2,1)S(1)} %get-tuple-element.33), channel_id=1, source_target_pairs={{0,96},{32,0},{64,32},{96,64},{1,97},{33,1},{65,33},{97,65},{2,98}... | collective-permute-start | bytes 2359304 | tf_op jit(solution)/shard_map/ppermute | solution.py:19
  190.3 4.1 %collective-permute-start.4 = (bf16[2,192,8,128]{3,2,1,0:T(8,128)(2,1)S(1)}, bf16[2,192,8,128]{3,2,1,0:T(8,128)(2,1)S(1)}, u32[]{:S(2)}, u32[]{:S(2)}) collective-permute-start(bf16[2,192,8,128]{3,2,1,0:T(8,128)(2,1)S(1)} %get-tuple-element.34), channel_id=1, source_target_pairs={{0,64},{32,96},{64,0},{96,32},{1,65},{33,97},{65,1},{97,33},{2,66}... | collective-permute-start | bytes 2359304 | tf_op jit(solution)/shard_map/ppermute | solution.py:19
  194.4 2.8 %fusion.2 = f32[6,2,128,128]{3,0,2,1:T(8,128)S(1)} fusion(bf16[32,2,128,128]{3,2,1,0:T(8,128)(2,1)} %all-to-all-done.3, bf16[2,32,6]{1,2,0:T(8,128)(2,1)S(1)} %broadcast_select_fusion), kind=kOutput, calls=%fused_computation.18 | convolution fusion | flops 12582912 | bytes 2885632 | tf_op jit(solution)/shard_map/rl,rktd->lktd/dot_general | solution.py:227
  199.3 26.2 %collective-permute-done.3 = bf16[2,192,8,128]{3,2,1,0:T(8,128)(2,1)S(1)} collective-permute-done((bf16[2,192,8,128]{3,2,1,0:T(8,128)(2,1)S(1)}, bf16[2,192,8,128]{3,2,1,0:T(8,128)(2,1)S(1)}, u32[]{:S(2)}, u32[]{:S(2)}) %collective-permute-start.3) | collective-permute-done | bytes 786464 | tf_op jit(solution)/shard_map/ppermute | solution.py:19
  225.8 15.7 %collective-permute-done.4 = bf16[2,192,8,128]{3,2,1,0:T(8,128)(2,1)S(1)} collective-permute-done((bf16[2,192,8,128]{3,2,1,0:T(8,128)(2,1)S(1)}, bf16[2,192,8,128]{3,2,1,0:T(8,128)(2,1)S(1)}, u32[]{:S(2)}, u32[]{:S(2)}) %collective-permute-start.4) | collective-permute-done | bytes 786464 | tf_op jit(solution)/shard_map/ppermute | solution.py:19
  243.2 2.4 dynamic-slice_bitcast_fusion
  245.6 3.0 %fusion = f32[6,2,128,128]{3,0,2,1:T(8,128)S(1)} fusion(bf16[32,2,128,128]{3,2,1,0:T(8,128)(2,1)} %all-to-all-done.4, bf16[2,32,6]{1,2,0:T(8,128)(2,1)S(1)} %broadcast_select_fusion), kind=kOutput, calls=%fused_computation.16 | convolution fusion | flops 12582912 | bytes 2885632 | tf_op jit(solution)/shard_map/rl,rktd->lktd/dot_general | solution.py:227
  251.4 4.6 %collective-permute-done.6 = bf16[2,192,2,128]{3,2,1,0:T(2,128)(2,1)S(1)} collective-permute-done((bf16[2,192,2,128]{3,2,1,0:T(2,128)(2,1)S(1)}, bf16[2,192,2,128]{3,2,1,0:T(2,128)(2,1)S(1)}, u32[]{:S(2)}, u32[]{:S(2)}) %collective-permute-start.6) | collective-permute-done | bytes 196640 | tf_op jit(solution)/shard_map/ppermute | solution.py:19
  256.2 3.8 %collective-permute-done.7 = bf16[2,192,2,128]{3,2,1,0:T(2,128)(2,1)S(1)} collective-permute-done((bf16[2,192,2,128]{3,2,1,0:T(2,128)(2,1)S(1)}, bf16[2,192,2,128]{3,2,1,0:T(2,128)(2,1)S(1)}, u32[]{:S(2)}, u32[]{:S(2)}) %collective-permute-start.7) | collective-permute-done | bytes 196640 | tf_op jit(solution)/shard_map/ppermute | solution.py:19
  (104 shorter events, 30.8 us)
Async XLA Ops:
  2.8 17.5 %all-to-all-start = ((bf16[2,192,8,128]{3,1,0,2:T(8,128)(2,1)}), bf16[2,192,8,128]{3,1,0,2:T(8,128)(2,1)S(1)}, u32[]{:S(2)}, u32[]{:S(2)}) async-start(bf16[2,192,8,128]{3,1,0,2:T(8,128)(2,1)} %pad_maximum_fusion.4), calls=%async_computation | async-start | bytes 1572864 | tf_op jit(solution)/shard_map/all_to_all | solution.py:29
  20.6 0.7 copy-start.9
  20.6 36.2 %copy-start.8 = (bf16[6,2,128,128]{3,2,1,0:T(8,128)(2,1)}, bf16[6,2,128,128]{3,2,1,0:T(8,128)(2,1)S(1)}, u32[]{:S(2)}) copy-start(bf16[6,2,128,128]{3,2,1,0:T(8,128)(2,1)S(1)} %get-tuple-element.46) | copy-start | bytes 1179652
  24.3 8.9 %copy-start.12 = (bf16[192,32,128]{2,1,0:T(8,128)(2,1)S(1)}, bf16[192,32,128]{2,1,0:T(8,128)(2,1)}, u32[]{:S(2)}) copy-start(bf16[192,32,128]{2,1,0:T(8,128)(2,1)} %param.5) | copy-start | bytes 4718596
  24.3 41.1 %all-to-all-start.1 = ((bf16[32,2,128,128]{3,2,1,0:T(8,128)(2,1)}), bf16[32,2,128,128]{3,2,1,0:T(8,128)(2,1)}, u32[]{:S(2)}, u32[]{:S(2)}) async-start(bf16[32,2,128,128]{3,2,1,0:T(8,128)(2,1)} %copy.150), calls=%async_computation.1 | async-start | bytes 4194304 | tf_op jit(solution)/shard_map/all_to_all | solution.py:205
  53.9 18.1 %collective-permute-start.2 = (bf16[192,2048]{1,0:T(8,128)(2,1)}, bf16[192,2048]{1,0:T(8,128)(2,1)S(1)}, u32[]{:S(2)}, u32[]{:S(2)}) collective-permute-start(bf16[192,2048]{1,0:T(8,128)(2,1)} %get-tuple-element.36), channel_id=1, source_target_pairs={{0,96},{32,0},{64,32},{96,64},{1,97},{33,1},{65,33},{97,65},{2,98}... | collective-permute-start | bytes 2359304 | tf_op jit(solution)/shard_map/ppermute | solution.py:161
  54.0 37.2 %collective-permute-start.1 = (bf16[192,2048]{1,0:T(8,128)(2,1)}, bf16[192,2048]{1,0:T(8,128)(2,1)S(1)}, u32[]{:S(2)}, u32[]{:S(2)}) collective-permute-start(bf16[192,2048]{1,0:T(8,128)(2,1)} %get-tuple-element.37), channel_id=1, source_target_pairs={{0,64},{32,96},{64,0},{96,32},{1,65},{33,97},{65,1},{97,33},{2,66}... | collective-permute-start | bytes 2359304 | tf_op jit(solution)/shard_map/ppermute | solution.py:161
  56.3 36.1 %collective-permute-start = (bf16[192,2048]{1,0:T(8,128)(2,1)}, bf16[192,2048]{1,0:T(8,128)(2,1)}, u32[]{:S(2)}, u32[]{:S(2)}) collective-permute-start(bf16[192,2048]{1,0:T(8,128)(2,1)} %get-tuple-element.38), channel_id=1, source_target_pairs={{0,32},{32,64},{64,96},{96,0},{1,33},{33,65},{65,97},{97,1},{2,34}... | collective-permute-start | bytes 2359304 | tf_op jit(solution)/shard_map/ppermute | solution.py:161
  59.8 32.7 %copy-start.11 = (bf16[1,192,2048]{2,1,0:T(8,128)(2,1)S(1)}, bf16[1,192,2048]{2,1,0:T(8,128)(2,1)}, u32[]{:S(2)}) copy-start(bf16[1,192,2048]{2,1,0:T(8,128)(2,1)} %get-tuple-element.35) | copy-start | bytes 2359300
  65.4 63.8 %all-to-all-start.2 = ((bf16[32,2,128,128]{3,2,1,0:T(8,128)(2,1)}), bf16[32,2,128,128]{3,2,1,0:T(8,128)(2,1)}, u32[]{:S(2)}, u32[]{:S(2)}) async-start(bf16[32,2,128,128]{3,2,1,0:T(8,128)(2,1)} %copy.149), calls=%async_computation.2 | async-start | bytes 4194304 | tf_op jit(solution)/shard_map/all_to_all | solution.py:205
  92.4 2.9 %copy-start.10 = (bf16[6,2,128,128]{3,2,1,0:T(8,128)(2,1)S(1)}, bf16[6,2,128,128]{3,2,1,0:T(8,128)(2,1)}, u32[]{:S(2)}) copy-start(bf16[6,2,128,128]{3,2,1,0:T(8,128)(2,1)} %copy-done.9) | copy-start | bytes 1179652
  125.0 2.4 copy-start.2
  129.2 44.4 %all-to-all-start.3 = ((bf16[32,2,128,128]{3,2,1,0:T(8,128)(2,1)}), bf16[32,2,128,128]{3,2,1,0:T(8,128)(2,1)}, u32[]{:S(2)}, u32[]{:S(2)}) async-start(bf16[32,2,128,128]{3,2,1,0:T(8,128)(2,1)} %copy.108), calls=%async_computation.3 | async-start | bytes 4194304 | tf_op jit(solution)/shard_map/all_to_all | solution.py:219
  141.4 26.4 %copy-start.3 = (bf16[768,512]{1,0:T(8,128)(2,1)S(1)}, bf16[768,512]{1,0:T(8,128)(2,1)}, u32[]{:S(2)}) copy-start(bf16[768,512]{1,0:T(8,128)(2,1)} %copy-done.2) | copy-start | bytes 2359300
  167.8 3.8 %copy-start = (f32[38,128,128]{2,1,0:T(8,128)}, f32[38,128,128]{2,1,0:T(8,128)S(1)}, u32[]{:S(2)}) copy-start(f32[38,128,128]{2,1,0:T(8,128)S(1)} %get-tuple-element.20) | copy-start | bytes 7471108
  169.7 1.8 copy-start.7
  176.8 68.8 %all-to-all-start.4 = ((bf16[32,2,128,128]{3,2,1,0:T(8,128)(2,1)}), bf16[32,2,128,128]{3,2,1,0:T(8,128)(2,1)}, u32[]{:S(2)}, u32[]{:S(2)}) async-start(bf16[32,2,128,128]{3,2,1,0:T(8,128)(2,1)} %copy.111), calls=%async_computation.4 | async-start | bytes 4194304 | tf_op jit(solution)/shard_map/all_to_all | solution.py:219
  187.0 10.2 %copy-start.6 = (f32[38,128,128]{2,1,0:T(8,128)S(1)}, f32[38,128,128]{2,1,0:T(8,128)}, u32[]{:S(2)}) copy-start(f32[38,128,128]{2,1,0:T(8,128)} %get-tuple-element.23) | copy-start | bytes 7471108
  187.0 54.8 %collective-permute-start.5 = (bf16[2,192,8,128]{3,2,1,0:T(8,128)(2,1)S(1)}, bf16[2,192,8,128]{3,2,1,0:T(8,128)(2,1)S(1)}, u32[]{:S(2)}, u32[]{:S(2)}) collective-permute-start(bf16[2,192,8,128]{3,2,1,0:T(8,128)(2,1)S(1)} %get-tuple-element.32), channel_id=1, source_target_pairs={{0,32},{32,64},{64,96},{96,0},{1,33},{33,65},{65,97},{97,1},{2,34}... | collective-permute-start | bytes 2359304 | tf_op jit(solution)/shard_map/ppermute | solution.py:19
  187.0 38.5 %collective-permute-start.3 = (bf16[2,192,8,128]{3,2,1,0:T(8,128)(2,1)S(1)}, bf16[2,192,8,128]{3,2,1,0:T(8,128)(2,1)S(1)}, u32[]{:S(2)}, u32[]{:S(2)}) collective-permute-start(bf16[2,192,8,128]{3,2,1,0:T(8,128)(2,1)S(1)} %get-tuple-element.33), channel_id=1, source_target_pairs={{0,96},{32,0},{64,32},{96,64},{1,97},{33,1},{65,33},{97,65},{2,98}... | collective-permute-start | bytes 2359304 | tf_op jit(solution)/shard_map/ppermute | solution.py:19
  190.3 51.2 %collective-permute-start.4 = (bf16[2,192,8,128]{3,2,1,0:T(8,128)(2,1)S(1)}, bf16[2,192,8,128]{3,2,1,0:T(8,128)(2,1)S(1)}, u32[]{:S(2)}, u32[]{:S(2)}) collective-permute-start(bf16[2,192,8,128]{3,2,1,0:T(8,128)(2,1)S(1)} %get-tuple-element.34), channel_id=1, source_target_pairs={{0,64},{32,96},{64,0},{96,32},{1,65},{33,97},{65,1},{97,33},{2,66}... | collective-permute-start | bytes 2359304 | tf_op jit(solution)/shard_map/ppermute | solution.py:19
  197.2 1.4 copy-start.4
  197.2 1.9 copy-start.5
  245.6 3.0 %copy-start.1 = (f32[38,128,128]{2,1,0:T(8,128)S(1)}, f32[38,128,128]{2,1,0:T(8,128)}, u32[]{:S(2)}) copy-start(f32[38,128,128]{2,1,0:T(8,128)} %copy-done) | copy-start | bytes 7471108
  250.6 5.4 %collective-permute-start.6 = (bf16[2,192,2,128]{3,2,1,0:T(2,128)(2,1)S(1)}, bf16[2,192,2,128]{3,2,1,0:T(2,128)(2,1)S(1)}, u32[]{:S(2)}, u32[]{:S(2)}) collective-permute-start(bf16[2,192,2,128]{3,2,1,0:T(2,128)(2,1)S(1)} %bitcast.153), channel_id=1, source_target_pairs={{0,96},{32,0},{64,32},{96,64},{1,97},{33,1},{65,33},{97,65},{2,98}... | collective-permute-start | bytes 589832 | tf_op jit(solution)/shard_map/ppermute | solution.py:19
  250.7 9.3 %collective-permute-start.7 = (bf16[2,192,2,128]{3,2,1,0:T(2,128)(2,1)S(1)}, bf16[2,192,2,128]{3,2,1,0:T(2,128)(2,1)S(1)}, u32[]{:S(2)}, u32[]{:S(2)}) collective-permute-start(bf16[2,192,2,128]{3,2,1,0:T(2,128)(2,1)S(1)} %bitcast.152), channel_id=1, source_target_pairs={{0,64},{32,96},{64,0},{96,32},{1,65},{33,97},{65,1},{97,33},{2,66}... | collective-permute-start | bytes 589832 | tf_op jit(solution)/shard_map/ppermute | solution.py:19
  250.8 10.8 %collective-permute-start.8 = (bf16[2,192,2,128]{3,2,1,0:T(2,128)(2,1)S(1)}, bf16[2,192,2,128]{3,2,1,0:T(2,128)(2,1)S(1)}, u32[]{:S(2)}, u32[]{:S(2)}) collective-permute-start(bf16[2,192,2,128]{3,2,1,0:T(2,128)(2,1)S(1)} %bitcast.151), channel_id=1, source_target_pairs={{0,32},{32,64},{64,96},{96,0},{1,33},{33,65},{65,97},{97,1},{2,34}... | collective-permute-start | bytes 589832 | tf_op jit(solution)/shard_map/ppermute | solution.py:19
